TPU v7x, 512 devices: a whole 4x8x8 slice. The times are simulated.
512 devices in a mesh: gz: 64 (over x, z, y_lo), gx: 8 (over y_hi, core).
Axes of the slice: x: 4, y: 8 (y_hi: 4, y_lo: 2; y = y_hi * 2 + y_lo), z: 8, core: 2. Of those that a mesh axis runs over, the one named last changes fastest.
Arguments:
- latent: float32 [8, 128, 32, 128], P(None, 'gz', 'gx'), may hold values from -6 to 6
- condition: bfloat16 [8, 128, 32, 128], P(None, 'gz', 'gx'), may hold values from -6 to 6
- cotangent: float32 [8, 128, 32, 128], P(None, 'gz', 'gx'), may hold values from -6 to 6
- expand_kernel: bfloat16 [27, 64, 12], replicated, may hold values from -0.3125 to 0.3125
- mixing_matrix: bfloat16 [64, 64], replicated, may hold values from -0.75 to 0.75
- project_kernel: bfloat16 [27, 8, 64], replicated, may hold values from -0.15625 to 0.15625
- offsets: float32 [136], replicated, may hold values from -3 to 3
Outputs:
- restored: float32 [256, 64, 256], P('gz', 'gx')
- field_grad: float32 [256, 64, 256], P('gz', 'gx')
- condition_grad: float32 [8, 128, 32, 128], P(None, 'gz', 'gx')
- expand_grad: float32 [27, 64, 12], replicated
- mixing_grad: float32 [64, 64], replicated
- project_grad: float32 [27, 8, 64], replicated
- offset_grad: float32 [136], replicated
All inputs are finite; a program needn't handle non-finite values.
Results may differ from a plain program's by a relative error of at most 0.007.
Values may be sent and summed in bfloat16 or wider, within the bound.
No kernel may reach another device: no remote copies, remote signals or barrier semaphores. Data moves between devices by JAX's collectives and lax.ppermute only.
A program may use at most 64 MiB of HBM per device.

v0:
```python
import math

import jax
import jax.numpy as jnp
import numpy as np
from jax import lax
from jax.sharding import PartitionSpec as P

CH = 4


def extended(cells, sides, width):
    for axis, dim in sides:
        count = lax.axis_size(axis)
        ends = count - 1
        head = lax.slice_in_dim(cells, 0, width, axis=dim)
        tail = lax.slice_in_dim(cells, cells.shape[dim] - width, cells.shape[dim], axis=dim)
        cells = jnp.concatenate(
            [
                lax.ppermute(tail, axis, [(i, (i + 1) % count) for i in range(ends)]),
                cells,
                lax.ppermute(head, axis, [((i + 1) % count, i) for i in range(ends)]),
            ],
            axis=dim,
        )
    return cells


def set_bits(value):
    parity_count = 0
    for bit_place in range(3):
        parity_count = parity_count + (value >> bit_place & 1)
    return parity_count


def haar_table():
    signs = np.zeros((8, 8), np.float32)
    for fine_index in range(8):
        for coef_index in range(8):
            parity = set_bits(fine_index & coef_index)
            signs[fine_index, coef_index] = (-1.0) ** parity / np.sqrt(8.0)
    return signs


def unsqueeze(coarse):
    haar_signs = jnp.asarray(haar_table())
    spread = jnp.einsum("pk,kzxy->pzxy", haar_signs, coarse, precision=lax.Precision.HIGHEST)
    planes, x_rows, y_cols = (coarse.shape[1], coarse.shape[2], coarse.shape[3])
    spread = spread.reshape(2, 2, 2, planes, x_rows, y_cols).transpose(3, 0, 4, 1, 5, 2)
    return spread.reshape(2 * planes, 2 * x_rows, 2 * y_cols)


def silu_slope(preact):
    sigma = jax.nn.sigmoid(preact)
    return sigma * (1.0 + preact * (1.0 - sigma))


def forward_taps(padded, weight, planes, x_rows):
    y_cols = padded.shape[3] - 2
    summed = None
    for tap_index in range(27):
        z_step, x_step, y_step = (tap_index // 9, tap_index // 3 % 3, tap_index % 3)
        sliced = padded[
            :, z_step : z_step + planes, x_step : x_step + x_rows, y_step : y_step + y_cols
        ]
        product = jnp.einsum(
            "oc,czxy->ozxy", weight[tap_index], sliced, preferred_element_type=jnp.float32
        )
        summed = product if summed is None else summed + product
    return summed


def backward_taps(padded, weight, planes, x_rows):
    y_cols = padded.shape[3] - 2
    summed = None
    for tap_index in range(27):
        z_step, x_step, y_step = (tap_index // 9, tap_index // 3 % 3, tap_index % 3)
        sliced = padded[
            :,
            2 - z_step : 2 - z_step + planes,
            2 - x_step : 2 - x_step + x_rows,
            2 - y_step : 2 - y_step + y_cols,
        ]
        product = jnp.einsum(
            "oc,ozxy->czxy", weight[tap_index], sliced, preferred_element_type=jnp.float32
        )
        summed = product if summed is None else summed + product
    return summed


def weight_taps(grad, padded):
    planes, x_rows, y_cols = (grad.shape[1], grad.shape[2], grad.shape[3])
    result = []
    for tap_index in range(27):
        z_step, x_step, y_step = (tap_index // 9, tap_index // 3 % 3, tap_index % 3)
        sliced = padded[
            :, z_step : z_step + planes, x_step : x_step + x_rows, y_step : y_step + y_cols
        ]
        result.append(jnp.einsum("ozxy,czxy->oc", grad, sliced, preferred_element_type=jnp.float32))
    return jnp.stack(result)


def frame_cols(tensor):
    return jnp.pad(tensor, ((0, 0), (0, 0), (0, 0), (1, 1)))


def channel_sums(tensor):
    return jnp.sum(tensor.astype(jnp.float32), axis=(1, 2, 3))


def per_device(latent, condition, cotangent, expand_kernel, mixing_matrix, project_kernel, offsets):
    planes, x_rows, y_cols = (latent.shape[1], latent.shape[2], latent.shape[3])
    hidden_width = mixing_matrix.shape[0]
    upper_half, lower_half = (latent[:CH], latent[CH:])
    cot_upper, cot_lower = (cotangent[:CH], cotangent[CH:])
    expand_offset = offsets[:hidden_width][:, None, None, None]
    mixing_offset = offsets[hidden_width : 2 * hidden_width][:, None, None, None]
    project_offset = offsets[2 * hidden_width :][:, None, None, None]
    inputs = jnp.concatenate([upper_half.astype(jnp.bfloat16), condition], axis=0)
    framed = frame_cols(extended(inputs, (("gz", 1), ("gx", 2)), 1))
    pre_one = forward_taps(framed, expand_kernel, planes, x_rows) + expand_offset
    act_one = jax.nn.silu(pre_one).astype(jnp.bfloat16)
    pre_two = (
        jnp.einsum("oc,czxy->ozxy", mixing_matrix, act_one, preferred_element_type=jnp.float32)
        + mixing_offset
    )
    act_two = jax.nn.silu(pre_two).astype(jnp.bfloat16)
    act_frame = frame_cols(extended(act_two, (("gz", 1), ("gx", 2)), 1))
    scores = forward_taps(act_frame, project_kernel, planes, x_rows) + project_offset
    log_scale = jnp.tanh(scores[:CH])
    centered = lower_half - scores[CH:]
    recovered = centered * jnp.exp(-log_scale)
    score_grad = jnp.concatenate(
        [cot_lower * centered * (1.0 - log_scale * log_scale), cot_lower], axis=0
    ).astype(jnp.bfloat16)
    recovered, score_grad, lower_grad = (recovered, score_grad, cot_lower * jnp.exp(log_scale))
    score_frame = frame_cols(extended(score_grad, (("gz", 1), ("gx", 2)), 1))
    hidden_grad = backward_taps(score_frame, project_kernel, planes, x_rows)
    mix_grad = (hidden_grad * silu_slope(pre_two)).astype(jnp.bfloat16)
    back_one = jnp.einsum(
        "oc,ozxy->czxy", mixing_matrix, mix_grad, preferred_element_type=jnp.float32
    )
    first_grad = (back_one * silu_slope(pre_one)).astype(jnp.bfloat16)
    first_frame = frame_cols(extended(first_grad, (("gz", 1), ("gx", 2)), 1))
    input_grad = backward_taps(first_frame, expand_kernel, planes, x_rows)
    inner_first, inner_mix, inner_act = (first_grad, mix_grad, act_one)
    expand_term = weight_taps(inner_first, framed)
    mixing_term = jnp.einsum(
        "ozxy,czxy->oc", inner_mix, inner_act, preferred_element_type=jnp.float32
    )
    project_term = weight_taps(score_grad, act_frame)
    offset_term = jnp.concatenate(
        [channel_sums(inner_first), channel_sums(inner_mix), channel_sums(score_grad)]
    )
    expand_sum, mixing_sum, project_sum, offset_sum = lax.psum(
        (expand_term, mixing_term, project_term, offset_term), ("gz", "gx")
    )
    restored = unsqueeze(jnp.concatenate([upper_half, recovered], axis=0))
    field_grad = unsqueeze(jnp.concatenate([cot_upper + input_grad[:CH], lower_grad], axis=0))
    condition_grad = input_grad[CH:]
    factor = 1.0 / math.sqrt(float(planes * x_rows * y_cols))
    return (
        restored,
        field_grad,
        condition_grad,
        expand_sum * factor,
        mixing_sum * factor,
        project_sum * factor,
        offset_sum * factor,
    )


def solution(mesh):
    placed = (
        P(None, "gz", "gx", None),
        P(None, "gz", "gx", None),
        P(None, "gz", "gx", None),
        P(),
        P(),
        P(),
        P(),
    )
    return jax.shard_map(
        per_device,
        mesh=mesh,
        in_specs=placed,
        out_specs=(
            P("gz", "gx", None),
            P("gz", "gx", None),
            P(None, "gz", "gx", None),
            P(),
            P(),
            P(),
            P(),
        ),
        check_vma=False,
    )
```

profile of v0, /device:TPU:56, one launch (start us, length us, event | category | flops | bytes accessed | tf_op | source)
XLA Modules:
  0.0 659.7 jit_solution(13013788002436073114)
XLA Ops:
  8.7 5.1 collective-permute-start
  13.8 1.9 collective-permute-start.1
  15.7 1.2 fusion.548
  16.9 1.4 fusion.547
  19.4 0.8 fusion.553
  20.9 1.9 collective-permute-start.2
  22.8 4.5 collective-permute-start.3
  29.0 0.9 fusion.544
  36.4 4.8 collective-permute-start.4
  41.2 1.9 collective-permute-start.5
  44.0 4.3 collective-permute-done.5
  48.3 1.9 collective-permute-start.6
  50.2 4.5 collective-permute-start.7
  54.8 1.8 collective-permute-done.7
  63.1 2.8 collective-permute-start.8
  65.9 3.0 collective-permute-start.9
  73.8 1.8 reshape.30
  75.8 4.0 collective-permute-start.11
  79.9 1.9 collective-permute-start.10
  82.0 3.7 collective-permute-done.10
  92.0 0.8 convolution_bitcast_fusion.34
  93.3 4.1 collective-permute-start.12
  97.5 2.1 collective-permute-start.13
  105.1 273.0 %all-reduce.10.cloned.1.call-done = (f32[64,64]{1,0:T(8,128)}, f32[27,8,64]{2,1,0:T(8,128)}, f32[136]{0:T(256)}) async-done(((f32[64,64]{1,0:T(8,128)}, f32[27,8,64]{2,1,0:T(8,128)}, f32[136]{0:T(256)}), (f32[64,64]{1,0:T(8,128)}, f32[27,8,64]{2,1,0:T(8,128)}, f32[136]{0:T(256)})) %all-reduce.10.cloned.1.call-update) | async-done | bytes 72240 | tf_op jit(solution)/shard_map/psum | solution.py:155
  378.1 1.5 broadcast_multiply_fusion.1
  379.6 1.4 broadcast_multiply_fusion.2
  381.0 1.2 broadcast_multiply_fusion.3
  382.2 3.7 collective-permute-start.15
  386.0 1.9 collective-permute-start.14
  387.9 254.9 %all-reduce.8.cloned.1.call-done = f32[27,64,12]{1,2,0:T(8,128)} async-done(((f32[27,64,12]{1,2,0:T(8,128)}), f32[27,64,12]{1,2,0:T(8,128)}) %all-reduce.8.cloned.1.call-update) | async-done | bytes 82960 | tf_op jit(solution)/shard_map/psum | solution.py:155
  642.8 1.0 broadcast_multiply_fusion
  650.4 1.8 reshape.32
  (294 shorter events, 42.6 us)
Async XLA Ops:
  7.2 29.0 %copy-start = (bf16[64,64]{1,0:T(8,128)(2,1)S(1)}, bf16[64,64]{1,0:T(8,128)(2,1)}, u32[]{:S(2)}) copy-start(bf16[64,64]{1,0:T(8,128)(2,1)} %param.13) | copy-start | bytes 24580
  7.2 370.9 %all-reduce.10.cloned.1.call-start = ((), (), s32[]{:S(2)}) async-start(), calls=%async_computation.1 | async-start | bytes 288768 | tf_op jit(solution)/shard_map/psum | solution.py:155
  8.7 12.2 %collective-permute-start = (bf16[12,1,4,128]{3,0,2,1:T(8,128)(2,1)S(1)}, bf16[12,1,4,128]{3,0,2,1:T(8,128)(2,1)S(1)}, u32[]{:S(2)}, u32[]{:S(2)}) collective-permute-start(bf16[12,1,4,128]{3,0,2,1:T(8,128)(2,1)S(1)} %get-tuple-element.127), channel_id=1, source_target_pairs={{0,8},{8,16},{16,24},{24,32},{32,40},{40,48},{48,56},{56,64},{64,7... | collective-permute-start | bytes 36872 | tf_op jit(solution)/shard_map/ppermute | solution.py:20
  13.8 7.1 %collective-permute-start.1 = (bf16[12,1,4,128]{3,0,2,1:T(8,128)(2,1)S(1)}, bf16[12,1,4,128]{3,0,2,1:T(8,128)(2,1)S(1)}, u32[]{:S(2)}, u32[]{:S(2)}) collective-permute-start(bf16[12,1,4,128]{3,0,2,1:T(8,128)(2,1)S(1)} %get-tuple-element.128), channel_id=1, source_target_pairs={{8,0},{16,8},{24,16},{32,24},{40,32},{48,40},{56,48},{64,56},{72,6... | collective-permute-start | bytes 36872 | tf_op jit(solution)/shard_map/ppermute | solution.py:22
  18.3 16.3 %copy-start.29 = (bf16[1,64,12]{1,0,2:T(2,128)(2,1)}, bf16[1,64,12]{1,0,2:T(2,128)(2,1)S(1)}, u32[]{:S(2)}) copy-start(bf16[1,64,12]{1,0,2:T(2,128)(2,1)S(1)} %get-tuple-element.85) | copy-start | bytes 4612
  18.4 16.8 %copy-start.35 = (bf16[1,64,12]{1,0,2:T(2,128)(2,1)}, bf16[1,64,12]{1,0,2:T(2,128)(2,1)S(1)}, u32[]{:S(2)}) copy-start(bf16[1,64,12]{1,0,2:T(2,128)(2,1)S(1)} %get-tuple-element.96) | copy-start | bytes 4612
  18.4 17.0 %copy-start.33 = (bf16[1,64,12]{1,0,2:T(2,128)(2,1)}, bf16[1,64,12]{1,0,2:T(2,128)(2,1)S(1)}, u32[]{:S(2)}) copy-start(bf16[1,64,12]{1,0,2:T(2,128)(2,1)S(1)} %get-tuple-element.93) | copy-start | bytes 4612
  18.4 17.3 %copy-start.31 = (bf16[1,64,12]{1,0,2:T(2,128)(2,1)}, bf16[1,64,12]{1,0,2:T(2,128)(2,1)S(1)}, u32[]{:S(2)}) copy-start(bf16[1,64,12]{1,0,2:T(2,128)(2,1)S(1)} %get-tuple-element.78) | copy-start | bytes 4612
  20.9 7.4 %collective-permute-start.2 = (bf16[12,4,1,128]{3,0,2,1:T(8,128)(2,1)S(1)}, bf16[12,4,1,128]{3,0,2,1:T(8,128)(2,1)S(1)}, u32[]{:S(2)}, u32[]{:S(2)}) collective-permute-start(bf16[12,4,1,128]{3,0,2,1:T(8,128)(2,1)S(1)} %get-tuple-element.113), channel_id=1, source_target_pairs={{0,1},{1,2},{2,3},{3,4},{4,5},{5,6},{6,7},{8,9},{9,10},{10,11},{11... | collective-permute-start | bytes 36872 | tf_op jit(solution)/shard_map/ppermute | solution.py:20
  22.8 6.0 collective-permute-start.3
  36.4 7.6 %collective-permute-start.4 = (bf16[64,1,4,128]{3,0,2,1:T(8,128)(2,1)S(1)}, bf16[64,1,4,128]{3,0,2,1:T(8,128)(2,1)S(1)}, u32[]{:S(2)}, u32[]{:S(2)}) collective-permute-start(bf16[64,1,4,128]{3,0,2,1:T(8,128)(2,1)S(1)} %get-tuple-element.76), channel_id=1, source_target_pairs={{0,8},{8,16},{16,24},{24,32},{32,40},{40,48},{48,56},{56,64},{64,7... | collective-permute-start | bytes 196616 | tf_op jit(solution)/shard_map/ppermute | solution.py:20
  41.2 7.1 %collective-permute-start.5 = (bf16[64,1,4,128]{3,0,2,1:T(8,128)(2,1)S(1)}, bf16[64,1,4,128]{3,0,2,1:T(8,128)(2,1)S(1)}, u32[]{:S(2)}, u32[]{:S(2)}) collective-permute-start(bf16[64,1,4,128]{3,0,2,1:T(8,128)(2,1)S(1)} %get-tuple-element.77), channel_id=1, source_target_pairs={{8,0},{16,8},{24,16},{32,24},{40,32},{48,40},{56,48},{64,56},{72,6... | collective-permute-start | bytes 196616 | tf_op jit(solution)/shard_map/ppermute | solution.py:22
  48.3 6.5 collective-permute-start.6
  50.2 6.4 collective-permute-start.7
  63.1 12.7 %collective-permute-start.8 = (bf16[8,1,4,128]{3,0,2,1:T(8,128)(2,1)}, bf16[8,1,4,128]{3,0,2,1:T(8,128)(2,1)S(1)}, u32[]{:S(2)}, u32[]{:S(2)}) collective-permute-start(bf16[8,1,4,128]{3,0,2,1:T(8,128)(2,1)} %get-tuple-element.129), channel_id=1, source_target_pairs={{0,8},{8,16},{16,24},{24,32},{32,40},{40,48},{48,56},{56,64},{64,7... | collective-permute-start | bytes 24584 | tf_op jit(solution)/shard_map/ppermute | solution.py:20
  65.9 9.9 %collective-permute-start.9 = (bf16[8,1,4,128]{3,0,2,1:T(8,128)(2,1)}, bf16[8,1,4,128]{3,0,2,1:T(8,128)(2,1)S(1)}, u32[]{:S(2)}, u32[]{:S(2)}) collective-permute-start(bf16[8,1,4,128]{3,0,2,1:T(8,128)(2,1)} %get-tuple-element.130), channel_id=1, source_target_pairs={{8,0},{16,8},{24,16},{32,24},{40,32},{48,40},{56,48},{64,56},{72,6... | collective-permute-start | bytes 24584 | tf_op jit(solution)/shard_map/ppermute | solution.py:22
  75.8 6.2 collective-permute-start.11
  79.9 5.9 collective-permute-start.10
  92.0 8.1 %copy-start.15 = (bf16[12,2,4,128]{3,0,2,1:T(8,128)(2,1)S(1)}, bf16[12,2,4,128]{3,0,2,1:T(8,128)(2,1)}, u32[]{:S(2)}) copy-start(bf16[12,2,4,128]{3,0,2,1:T(8,128)(2,1)} %get-tuple-element.125) | copy-start | bytes 73732
  92.0 8.2 %copy-start.19 = (bf16[12,2,4,128]{3,0,2,1:T(8,128)(2,1)S(1)}, bf16[12,2,4,128]{3,0,2,1:T(8,128)(2,1)}, u32[]{:S(2)}) copy-start(bf16[12,2,4,128]{3,0,2,1:T(8,128)(2,1)} %get-tuple-element.68) | copy-start | bytes 73732
  92.8 8.1 %copy-start.16 = (bf16[12,2,4,128]{3,0,2,1:T(8,128)(2,1)S(1)}, bf16[12,2,4,128]{3,0,2,1:T(8,128)(2,1)}, u32[]{:S(2)}) copy-start(bf16[12,2,4,128]{3,0,2,1:T(8,128)(2,1)} %get-tuple-element.65) | copy-start | bytes 73732
  92.8 8.2 %copy-start.26 = (bf16[12,2,4,128]{3,0,2,1:T(8,128)(2,1)S(1)}, bf16[12,2,4,128]{3,0,2,1:T(8,128)(2,1)}, u32[]{:S(2)}) copy-start(bf16[12,2,4,128]{3,0,2,1:T(8,128)(2,1)} %get-tuple-element.145) | copy-start | bytes 73732
  93.1 8.2 %copy-start.13 = (bf16[12,2,4,128]{3,0,2,1:T(8,128)(2,1)S(1)}, bf16[12,2,4,128]{3,0,2,1:T(8,128)(2,1)}, u32[]{:S(2)}) copy-start(bf16[12,2,4,128]{3,0,2,1:T(8,128)(2,1)} %get-tuple-element.63) | copy-start | bytes 73732
  93.1 8.3 %copy-start.6 = (bf16[12,2,4,128]{3,0,2,1:T(8,128)(2,1)S(1)}, bf16[12,2,4,128]{3,0,2,1:T(8,128)(2,1)}, u32[]{:S(2)}) copy-start(bf16[12,2,4,128]{3,0,2,1:T(8,128)(2,1)} %get-tuple-element.126) | copy-start | bytes 73732
  93.2 8.5 %copy-start.12 = (bf16[12,2,4,128]{3,0,2,1:T(8,128)(2,1)S(1)}, bf16[12,2,4,128]{3,0,2,1:T(8,128)(2,1)}, u32[]{:S(2)}) copy-start(bf16[12,2,4,128]{3,0,2,1:T(8,128)(2,1)} %get-tuple-element.62) | copy-start | bytes 73732
  93.2 8.6 %copy-start.11 = (bf16[12,2,4,128]{3,0,2,1:T(8,128)(2,1)S(1)}, bf16[12,2,4,128]{3,0,2,1:T(8,128)(2,1)}, u32[]{:S(2)}) copy-start(bf16[12,2,4,128]{3,0,2,1:T(8,128)(2,1)} %get-tuple-element.61) | copy-start | bytes 73732
  93.3 8.6 %copy-start.25 = (bf16[12,2,4,128]{3,0,2,1:T(8,128)(2,1)S(1)}, bf16[12,2,4,128]{3,0,2,1:T(8,128)(2,1)}, u32[]{:S(2)}) copy-start(bf16[12,2,4,128]{3,0,2,1:T(8,128)(2,1)} %get-tuple-element.106) | copy-start | bytes 73732
  93.3 288.8 %collective-permute-start.12 = (bf16[64,1,4,128]{3,0,2,1:T(8,128)(2,1)S(1)}, bf16[64,1,4,128]{3,0,2,1:T(8,128)(2,1)S(1)}, u32[]{:S(2)}, u32[]{:S(2)}) collective-permute-start(bf16[64,1,4,128]{3,0,2,1:T(8,128)(2,1)S(1)} %get-tuple-element.74), channel_id=1, source_target_pairs={{0,8},{8,16},{16,24},{24,32},{32,40},{40,48},{48,56},{56,64},{64,7... | collective-permute-start | bytes 196616 | tf_op jit(solution)/shard_map/ppermute | solution.py:20
  97.5 284.7 %collective-permute-start.13 = (bf16[64,1,4,128]{3,0,2,1:T(8,128)(2,1)S(1)}, bf16[64,1,4,128]{3,0,2,1:T(8,128)(2,1)S(1)}, u32[]{:S(2)}, u32[]{:S(2)}) collective-permute-start(bf16[64,1,4,128]{3,0,2,1:T(8,128)(2,1)S(1)} %get-tuple-element.75), channel_id=1, source_target_pairs={{8,0},{16,8},{24,16},{32,24},{40,32},{48,40},{56,48},{64,56},{72,6... | collective-permute-start | bytes 196616 | tf_op jit(solution)/shard_map/ppermute | solution.py:22
  104.2 538.6 %all-reduce.8.cloned.1.call-start = ((), (), s32[]{:S(2)}) async-start(), calls=%async_computation | async-start | bytes 442368 | tf_op jit(solution)/shard_map/psum | solution.py:155
  382.2 262.3 %collective-permute-start.15 = (bf16[64,4,1,128]{3,0,2,1:T(8,128)(2,1)S(1)}, bf16[64,4,1,128]{3,0,2,1:T(8,128)(2,1)S(1)}, u32[]{:S(2)}, u32[]{:S(2)}) collective-permute-start(bf16[64,4,1,128]{3,0,2,1:T(8,128)(2,1)S(1)} %get-tuple-element.49), channel_id=1, source_target_pairs={{1,0},{2,1},{3,2},{4,3},{5,4},{6,5},{7,6},{9,8},{10,9},{11,10},{12... | collective-permute-start | bytes 196616 | tf_op jit(solution)/shard_map/ppermute | solution.py:22
  386.0 258.5 %collective-permute-start.14 = (bf16[64,4,1,128]{3,0,2,1:T(8,128)(2,1)S(1)}, bf16[64,4,1,128]{3,0,2,1:T(8,128)(2,1)S(1)}, u32[]{:S(2)}, u32[]{:S(2)}) collective-permute-start(bf16[64,4,1,128]{3,0,2,1:T(8,128)(2,1)S(1)} %get-tuple-element.48), channel_id=1, source_target_pairs={{0,1},{1,2},{2,3},{3,4},{4,5},{5,6},{6,7},{8,9},{9,10},{10,11},{11... | collective-permute-start | bytes 196616 | tf_op jit(solution)/shard_map/ppermute | solution.py:20
  (24 other events, 93.6 us)
Sparse Core Ops, SparseCore 0:
  104.3 273.7 all-reduce.9
  383.8 258.8 all-reduce.7
where the time goes:
time: 666 us; the launch traced here: 660 us
  waiting for transfers between devices  538 us (81%)
  starting transfers between devices  50.4 us (8%)
  matrix products  31.4 us (5%)
  local copies, waits for them, and re-layouts  15.9 us (2%)
  between operations  15.2 us (2%)
  other arithmetic  8.42 us (1%)
    psum x2, waiting for transfers between devices, per_device(): lax.psum((expand_term, mixing_term, project_term, offset_term), ('gz', 'g...  528 us
    ppermute x8, starting transfers between devices, extended(): lax.ppermute(head, axis, [((i + 1) % count, i) for i in range(ends)])  25.8 us
    ppermute x8, starting transfers between devices, extended(): lax.ppermute(tail, axis, [(i, (i + 1) % count) for i in range(ends)])  24.5 us
  transfers between devices with their start and end apart: 18, of which 6 were waited for; matrix products, arithmetic and copies ran while one was open for 4% of the time, Pallas kernels for 0%

commit v1 on v0

--- a/solution.py
+++ b/solution.py
@@ -108,6 +108,19 @@
     return jnp.sum(tensor.astype(jnp.float32), axis=(1, 2, 3))
 
 
+def butterfly_sum(flat, axes):
+    for axis in axes:
+        count = lax.axis_size(axis)
+        if count & (count - 1):
+            flat = lax.psum(flat, axis)
+            continue
+        bit = 1
+        while bit < count:
+            flat = flat + lax.ppermute(flat, axis, [(i, i ^ bit) for i in range(count)])
+            bit *= 2
+    return flat
+
+
 def per_device(latent, condition, cotangent, expand_kernel, mixing_matrix, project_kernel, offsets):
     planes, x_rows, y_cols = (latent.shape[1], latent.shape[2], latent.shape[3])
     hidden_width = mixing_matrix.shape[0]
@@ -152,9 +165,13 @@
     offset_term = jnp.concatenate(
         [channel_sums(inner_first), channel_sums(inner_mix), channel_sums(score_grad)]
     )
-    expand_sum, mixing_sum, project_sum, offset_sum = lax.psum(
-        (expand_term, mixing_term, project_term, offset_term), ("gz", "gx")
-    )
+    terms = (expand_term, mixing_term, project_term, offset_term)
+    flat = butterfly_sum(jnp.concatenate([t.reshape(-1) for t in terms]), ("gx", "gz"))
+    pieces, start = [], 0
+    for t in terms:
+        pieces.append(flat[start : start + t.size].reshape(t.shape))
+        start += t.size
+    expand_sum, mixing_sum, project_sum, offset_sum = pieces
     restored = unsqueeze(jnp.concatenate([upper_half, recovered], axis=0))
     field_grad = unsqueeze(jnp.concatenate([cot_upper + input_grad[:CH], lower_grad], axis=0))
     condition_grad = input_grad[CH:]

time: 666 us -> 212 us (0.32)
  the two profiles are of different devices: /device:TPU:56 before, /device:TPU:22 now
where the time goes in v1:
time: 212 us; the launch traced here: 210 us
  starting transfers between devices  96.6 us (46%)
  waiting for transfers between devices  58.3 us (28%)
  matrix products  30.8 us (15%)
  local copies, waits for them, and re-layouts  19.1 us (9%)
  other arithmetic  3.5 us (2%)
    ppermute x9, waiting for transfers between devices, butterfly_sum(): flat = flat + lax.ppermute(flat, axis, [(i, i ^ bit) for i in range(count)])  53.1 us
    ppermute x8, starting transfers between devices, extended(): lax.ppermute(head, axis, [((i + 1) % count, i) for i in range(ends)])  45.1 us
    ppermute x9, starting transfers between devices, butterfly_sum(): flat = flat + lax.ppermute(flat, axis, [(i, i ^ bit) for i in range(count)])  27.4 us
    ppermute x8, starting transfers between devices, extended(): lax.ppermute(tail, axis, [(i, (i + 1) % count) for i in range(ends)])  24.1 us
    dot_general x54, matrix products, forward_taps(): jnp.einsum('oc,czxy->ozxy', weight[tap_index], sliced, preferred_element_...  10.8 us
    dot_general x54, matrix products, backward_taps(): jnp.einsum('oc,ozxy->czxy', weight[tap_index], sliced, preferred_element_...  10.8 us
    dot_general x54, matrix products, weight_taps(): jnp.einsum('ozxy,czxy->oc', grad, sliced, preferred_element_type=jnp.floa...  8.13 us
  transfers between devices with their start and end apart: 25, of which 12 were waited for; matrix products, arithmetic and copies ran while one was open for 12% of the time, Pallas kernels for 0%

profile of v1, /device:TPU:22, one launch (start us, length us, event | category | flops | bytes accessed | tf_op | source)
XLA Modules:
  0.0 210.4 jit_solution(12052796860654151432)
XLA Ops:
  2.1 3.5 %collective-permute-start = (bf16[12,1,4,128]{3,0,2,1:T(8,128)(2,1)S(1)}, bf16[12,1,4,128]{3,0,2,1:T(8,128)(2,1)S(1)}, u32[]{:S(2)}, u32[]{:S(2)}) collective-permute-start(bf16[12,1,4,128]{3,0,2,1:T(8,128)(2,1)S(1)} %get-tuple-element.124), channel_id=1, source_target_pairs={{0,8},{8,16},{16,24},{24,32},{32,40},{40,48},{48,56},{56,64},{64,7... | collective-permute-start | bytes 36872 | tf_op jit(solution)/shard_map/ppermute | solution.py:20
  5.6 10.7 %collective-permute-start.1 = (bf16[12,1,4,128]{3,0,2,1:T(8,128)(2,1)S(1)}, bf16[12,1,4,128]{3,0,2,1:T(8,128)(2,1)S(1)}, u32[]{:S(2)}, u32[]{:S(2)}) collective-permute-start(bf16[12,1,4,128]{3,0,2,1:T(8,128)(2,1)S(1)} %get-tuple-element.125), channel_id=1, source_target_pairs={{8,0},{16,8},{24,16},{32,24},{40,32},{48,40},{56,48},{64,56},{72,6... | collective-permute-start | bytes 36872 | tf_op jit(solution)/shard_map/ppermute | solution.py:22
  21.4 1.9 collective-permute-start.2
  23.4 4.5 %collective-permute-start.3 = (bf16[12,4,1,128]{3,0,2,1:T(8,128)(2,1)S(1)}, bf16[12,4,1,128]{3,0,2,1:T(8,128)(2,1)S(1)}, u32[]{:S(2)}, u32[]{:S(2)}) collective-permute-start(bf16[12,4,1,128]{3,0,2,1:T(8,128)(2,1)S(1)} %get-tuple-element.111), channel_id=1, source_target_pairs={{1,0},{2,1},{3,2},{4,3},{5,4},{6,5},{7,6},{9,8},{10,9},{11,10},{12... | collective-permute-start | bytes 36872 | tf_op jit(solution)/shard_map/ppermute | solution.py:22
  36.9 1.9 collective-permute-start.4
  38.8 6.9 %collective-permute-start.5 = (bf16[64,1,4,128]{3,0,2,1:T(8,128)(2,1)S(1)}, bf16[64,1,4,128]{3,0,2,1:T(8,128)(2,1)S(1)}, u32[]{:S(2)}, u32[]{:S(2)}) collective-permute-start(bf16[64,1,4,128]{3,0,2,1:T(8,128)(2,1)S(1)} %get-tuple-element.74), channel_id=1, source_target_pairs={{8,0},{16,8},{24,16},{32,24},{40,32},{48,40},{56,48},{64,56},{72,6... | collective-permute-start | bytes 196616 | tf_op jit(solution)/shard_map/ppermute | solution.py:22
  47.7 5.0 %collective-permute-start.6 = (bf16[64,4,1,128]{3,0,2,1:T(8,128)(2,1)S(1)}, bf16[64,4,1,128]{3,0,2,1:T(8,128)(2,1)S(1)}, u32[]{:S(2)}, u32[]{:S(2)}) collective-permute-start(bf16[64,4,1,128]{3,0,2,1:T(8,128)(2,1)S(1)} %get-tuple-element.49), channel_id=1, source_target_pairs={{0,1},{1,2},{2,3},{3,4},{4,5},{5,6},{6,7},{8,9},{9,10},{10,11},{11... | collective-permute-start | bytes 196616 | tf_op jit(solution)/shard_map/ppermute | solution.py:20
  52.6 1.9 collective-permute-start.7
  65.0 1.9 collective-permute-start.8
  66.9 7.6 %collective-permute-start.9 = (bf16[8,1,4,128]{3,0,2,1:T(8,128)(2,1)}, bf16[8,1,4,128]{3,0,2,1:T(8,128)(2,1)S(1)}, u32[]{:S(2)}, u32[]{:S(2)}) collective-permute-start(bf16[8,1,4,128]{3,0,2,1:T(8,128)(2,1)} %get-tuple-element.127), channel_id=1, source_target_pairs={{8,0},{16,8},{24,16},{32,24},{40,32},{48,40},{56,48},{64,56},{72,6... | collective-permute-start | bytes 24584 | tf_op jit(solution)/shard_map/ppermute | solution.py:22
  79.4 4.4 %collective-permute-start.11 = (bf16[8,4,1,128]{3,0,2,1:T(8,128)(2,1)S(1)}, bf16[8,4,1,128]{3,0,2,1:T(8,128)(2,1)S(1)}, u32[]{:S(2)}, u32[]{:S(2)}) collective-permute-start(bf16[8,4,1,128]{3,0,2,1:T(8,128)(2,1)S(1)} %get-tuple-element.118), channel_id=1, source_target_pairs={{1,0},{2,1},{3,2},{4,3},{5,4},{6,5},{7,6},{9,8},{10,9},{11,10},{12... | collective-permute-start | bytes 24584 | tf_op jit(solution)/shard_map/ppermute | solution.py:22
  83.8 3.9 %collective-permute-start.10 = (bf16[8,4,1,128]{3,0,2,1:T(8,128)(2,1)S(1)}, bf16[8,4,1,128]{3,0,2,1:T(8,128)(2,1)S(1)}, u32[]{:S(2)}, u32[]{:S(2)}) collective-permute-start(bf16[8,4,1,128]{3,0,2,1:T(8,128)(2,1)S(1)} %get-tuple-element.117), channel_id=1, source_target_pairs={{0,1},{1,2},{2,3},{3,4},{4,5},{5,6},{6,7},{8,9},{9,10},{10,11},{11... | collective-permute-start | bytes 24584 | tf_op jit(solution)/shard_map/ppermute | solution.py:20
  96.5 2.1 collective-permute-start.12
  98.6 7.1 %collective-permute-start.13 = (bf16[64,1,4,128]{3,0,2,1:T(8,128)(2,1)S(1)}, bf16[64,1,4,128]{3,0,2,1:T(8,128)(2,1)S(1)}, u32[]{:S(2)}, u32[]{:S(2)}) collective-permute-start(bf16[64,1,4,128]{3,0,2,1:T(8,128)(2,1)S(1)} %get-tuple-element.72), channel_id=1, source_target_pairs={{8,0},{16,8},{24,16},{32,24},{40,32},{48,40},{56,48},{64,56},{72,6... | collective-permute-start | bytes 196616 | tf_op jit(solution)/shard_map/ppermute | solution.py:22
  110.9 1.9 collective-permute-start.15
  112.8 4.0 %collective-permute-start.14 = (bf16[64,4,1,128]{3,0,2,1:T(8,128)(2,1)S(1)}, bf16[64,4,1,128]{3,0,2,1:T(8,128)(2,1)S(1)}, u32[]{:S(2)}, u32[]{:S(2)}) collective-permute-start(bf16[64,4,1,128]{3,0,2,1:T(8,128)(2,1)S(1)} %get-tuple-element.45), channel_id=1, source_target_pairs={{0,1},{1,2},{2,3},{3,4},{4,5},{5,6},{6,7},{8,9},{9,10},{10,11},{11... | collective-permute-start | bytes 196616 | tf_op jit(solution)/shard_map/ppermute | solution.py:20
  117.2 6.9 %collective-permute-start.16 = (f32[38792]{0:T(1024)S(1)}, f32[38792]{0:T(1024)S(1)}, u32[]{:S(2)}, u32[]{:S(2)}) collective-permute-start(f32[38792]{0:T(1024)S(1)} %concatenate.132), channel_id=1, source_target_pairs={{0,1},{1,0},{2,3},{3,2},{4,5},{5,4},{6,7},{7,6},{8,9},{9,8},{10,11... | collective-permute-start | bytes 465512 | tf_op jit(solution)/shard_map/ppermute | solution.py:119
  128.2 1.9 collective-permute-start.17
  130.2 6.6 %collective-permute-done.17 = f32[38792]{0:T(1024)S(1)} collective-permute-done((f32[38792]{0:T(1024)S(1)}, f32[38792]{0:T(1024)S(1)}, u32[]{:S(2)}, u32[]{:S(2)}) %collective-permute-start.17) | collective-permute-done | bytes 155200 | tf_op jit(solution)/shard_map/ppermute | solution.py:119
  136.9 4.0 %collective-permute-start.18 = (f32[38792]{0:T(1024)S(1)}, f32[38792]{0:T(1024)S(1)}, u32[]{:S(2)}, u32[]{:S(2)}) collective-permute-start(f32[38792]{0:T(1024)S(1)} %add.537), channel_id=1, source_target_pairs={{0,4},{1,5},{2,6},{3,7},{4,0},{5,1},{6,2},{7,3},{8,12},{9,13},{10,... | collective-permute-start | bytes 465512 | tf_op jit(solution)/shard_map/ppermute | solution.py:119
  141.1 10.9 %collective-permute-done.18 = f32[38792]{0:T(1024)S(1)} collective-permute-done((f32[38792]{0:T(1024)S(1)}, f32[38792]{0:T(1024)S(1)}, u32[]{:S(2)}, u32[]{:S(2)}) %collective-permute-start.18) | collective-permute-done | bytes 155200 | tf_op jit(solution)/shard_map/ppermute | solution.py:119
  152.1 1.9 collective-permute-start.19
  154.2 5.0 %collective-permute-done.19 = f32[38792]{0:T(1024)S(1)} collective-permute-done((f32[38792]{0:T(1024)S(1)}, f32[38792]{0:T(1024)S(1)}, u32[]{:S(2)}, u32[]{:S(2)}) %collective-permute-start.19) | collective-permute-done | bytes 155200 | tf_op jit(solution)/shard_map/ppermute | solution.py:119
  159.2 1.9 collective-permute-start.20
  161.3 5.5 %collective-permute-done.20 = f32[38792]{0:T(1024)S(1)} collective-permute-done((f32[38792]{0:T(1024)S(1)}, f32[38792]{0:T(1024)S(1)}, u32[]{:S(2)}, u32[]{:S(2)}) %collective-permute-start.20) | collective-permute-done | bytes 155200 | tf_op jit(solution)/shard_map/ppermute | solution.py:119
  168.9 10.5 %collective-permute-done.21 = f32[38792]{0:T(1024)S(1)} collective-permute-done((f32[38792]{0:T(1024)S(1)}, f32[38792]{0:T(1024)S(1)}, u32[]{:S(2)}, u32[]{:S(2)}) %collective-permute-start.21) | collective-permute-done | bytes 155200 | tf_op jit(solution)/shard_map/ppermute | solution.py:119
  179.4 3.7 %collective-permute-start.22 = (f32[38792]{0:T(1024)S(1)}, f32[38792]{0:T(1024)S(1)}, u32[]{:S(2)}, u32[]{:S(2)}) collective-permute-start(f32[38792]{0:T(1024)S(1)} %add.541), channel_id=1, source_target_pairs={{0,64},{8,72},{16,80},{24,88},{32,96},{40,104},{48,112},{56,120},{... | collective-permute-start | bytes 465512 | tf_op jit(solution)/shard_map/ppermute | solution.py:119
  183.3 7.2 %collective-permute-done.22 = f32[38792]{0:T(1024)S(1)} collective-permute-done((f32[38792]{0:T(1024)S(1)}, f32[38792]{0:T(1024)S(1)}, u32[]{:S(2)}, u32[]{:S(2)}) %collective-permute-start.22) | collective-permute-done | bytes 155200 | tf_op jit(solution)/shard_map/ppermute | solution.py:119
  190.5 2.3 %collective-permute-start.23 = (f32[38792]{0:T(1024)S(1)}, f32[38792]{0:T(1024)S(1)}, u32[]{:S(2)}, u32[]{:S(2)}) collective-permute-start(f32[38792]{0:T(1024)S(1)} %add.542), channel_id=1, source_target_pairs={{0,128},{8,136},{16,144},{24,152},{32,160},{40,168},{48,176},{56,1... | collective-permute-start | bytes 465512 | tf_op jit(solution)/shard_map/ppermute | solution.py:119
  192.9 4.8 %collective-permute-done.23 = f32[38792]{0:T(1024)S(1)} collective-permute-done((f32[38792]{0:T(1024)S(1)}, f32[38792]{0:T(1024)S(1)}, u32[]{:S(2)}, u32[]{:S(2)}) %collective-permute-start.23) | collective-permute-done | bytes 155200 | tf_op jit(solution)/shard_map/ppermute | solution.py:119
  197.7 2.9 %collective-permute-start.24 = (f32[38792]{0:T(1024)S(1)}, f32[38792]{0:T(1024)S(1)}, u32[]{:S(2)}, u32[]{:S(2)}) collective-permute-start(f32[38792]{0:T(1024)S(1)} %add.543), channel_id=1, source_target_pairs={{0,256},{8,264},{16,272},{24,280},{32,288},{40,296},{48,304},{56,3... | collective-permute-start | bytes 465512 | tf_op jit(solution)/shard_map/ppermute | solution.py:119
  203.9 2.5 %collective-permute-done.24 = f32[38792]{0:T(1024)S(1)} collective-permute-done((f32[38792]{0:T(1024)S(1)}, f32[38792]{0:T(1024)S(1)}, u32[]{:S(2)}, u32[]{:S(2)}) %collective-permute-start.24) | collective-permute-done | bytes 155200 | tf_op jit(solution)/shard_map/ppermute | solution.py:119
  (320 shorter events, 60.6 us)
Async XLA Ops:
  0.6 36.0 %copy-start = (bf16[64,64]{1,0:T(8,128)(2,1)S(1)}, bf16[64,64]{1,0:T(8,128)(2,1)}, u32[]{:S(2)}) copy-start(bf16[64,64]{1,0:T(8,128)(2,1)} %param.13) | copy-start | bytes 24580
  2.1 19.3 %collective-permute-start = (bf16[12,1,4,128]{3,0,2,1:T(8,128)(2,1)S(1)}, bf16[12,1,4,128]{3,0,2,1:T(8,128)(2,1)S(1)}, u32[]{:S(2)}, u32[]{:S(2)}) collective-permute-start(bf16[12,1,4,128]{3,0,2,1:T(8,128)(2,1)S(1)} %get-tuple-element.124), channel_id=1, source_target_pairs={{0,8},{8,16},{16,24},{24,32},{32,40},{40,48},{48,56},{56,64},{64,7... | collective-permute-start | bytes 36872 | tf_op jit(solution)/shard_map/ppermute | solution.py:20
  5.6 15.8 %collective-permute-start.1 = (bf16[12,1,4,128]{3,0,2,1:T(8,128)(2,1)S(1)}, bf16[12,1,4,128]{3,0,2,1:T(8,128)(2,1)S(1)}, u32[]{:S(2)}, u32[]{:S(2)}) collective-permute-start(bf16[12,1,4,128]{3,0,2,1:T(8,128)(2,1)S(1)} %get-tuple-element.125), channel_id=1, source_target_pairs={{8,0},{16,8},{24,16},{32,24},{40,32},{48,40},{56,48},{64,56},{72,6... | collective-permute-start | bytes 36872 | tf_op jit(solution)/shard_map/ppermute | solution.py:22
  18.9 16.3 %copy-start.27 = (bf16[1,64,12]{1,0,2:T(2,128)(2,1)}, bf16[1,64,12]{1,0,2:T(2,128)(2,1)S(1)}, u32[]{:S(2)}) copy-start(bf16[1,64,12]{1,0,2:T(2,128)(2,1)S(1)} %get-tuple-element.82) | copy-start | bytes 4612
  18.9 16.8 %copy-start.33 = (bf16[1,64,12]{1,0,2:T(2,128)(2,1)}, bf16[1,64,12]{1,0,2:T(2,128)(2,1)S(1)}, u32[]{:S(2)}) copy-start(bf16[1,64,12]{1,0,2:T(2,128)(2,1)S(1)} %get-tuple-element.93) | copy-start | bytes 4612
  18.9 17.0 %copy-start.31 = (bf16[1,64,12]{1,0,2:T(2,128)(2,1)}, bf16[1,64,12]{1,0,2:T(2,128)(2,1)S(1)}, u32[]{:S(2)}) copy-start(bf16[1,64,12]{1,0,2:T(2,128)(2,1)S(1)} %get-tuple-element.90) | copy-start | bytes 4612
  18.9 17.3 %copy-start.29 = (bf16[1,64,12]{1,0,2:T(2,128)(2,1)}, bf16[1,64,12]{1,0,2:T(2,128)(2,1)S(1)}, u32[]{:S(2)}) copy-start(bf16[1,64,12]{1,0,2:T(2,128)(2,1)S(1)} %get-tuple-element.75) | copy-start | bytes 4612
  21.4 7.3 %collective-permute-start.2 = (bf16[12,4,1,128]{3,0,2,1:T(8,128)(2,1)S(1)}, bf16[12,4,1,128]{3,0,2,1:T(8,128)(2,1)S(1)}, u32[]{:S(2)}, u32[]{:S(2)}) collective-permute-start(bf16[12,4,1,128]{3,0,2,1:T(8,128)(2,1)S(1)} %get-tuple-element.110), channel_id=1, source_target_pairs={{0,1},{1,2},{2,3},{3,4},{4,5},{5,6},{6,7},{8,9},{9,10},{10,11},{11... | collective-permute-start | bytes 36872 | tf_op jit(solution)/shard_map/ppermute | solution.py:20
  23.4 6.0 %collective-permute-start.3 = (bf16[12,4,1,128]{3,0,2,1:T(8,128)(2,1)S(1)}, bf16[12,4,1,128]{3,0,2,1:T(8,128)(2,1)S(1)}, u32[]{:S(2)}, u32[]{:S(2)}) collective-permute-start(bf16[12,4,1,128]{3,0,2,1:T(8,128)(2,1)S(1)} %get-tuple-element.111), channel_id=1, source_target_pairs={{1,0},{2,1},{3,2},{4,3},{5,4},{6,5},{7,6},{9,8},{10,9},{11,10},{12... | collective-permute-start | bytes 36872 | tf_op jit(solution)/shard_map/ppermute | solution.py:22
  36.9 9.7 %collective-permute-start.4 = (bf16[64,1,4,128]{3,0,2,1:T(8,128)(2,1)S(1)}, bf16[64,1,4,128]{3,0,2,1:T(8,128)(2,1)S(1)}, u32[]{:S(2)}, u32[]{:S(2)}) collective-permute-start(bf16[64,1,4,128]{3,0,2,1:T(8,128)(2,1)S(1)} %get-tuple-element.73), channel_id=1, source_target_pairs={{0,8},{8,16},{16,24},{24,32},{32,40},{40,48},{48,56},{56,64},{64,7... | collective-permute-start | bytes 196616 | tf_op jit(solution)/shard_map/ppermute | solution.py:20
  38.8 8.8 %collective-permute-start.5 = (bf16[64,1,4,128]{3,0,2,1:T(8,128)(2,1)S(1)}, bf16[64,1,4,128]{3,0,2,1:T(8,128)(2,1)S(1)}, u32[]{:S(2)}, u32[]{:S(2)}) collective-permute-start(bf16[64,1,4,128]{3,0,2,1:T(8,128)(2,1)S(1)} %get-tuple-element.74), channel_id=1, source_target_pairs={{8,0},{16,8},{24,16},{32,24},{40,32},{48,40},{56,48},{64,56},{72,6... | collective-permute-start | bytes 196616 | tf_op jit(solution)/shard_map/ppermute | solution.py:22
  47.7 7.0 %collective-permute-start.6 = (bf16[64,4,1,128]{3,0,2,1:T(8,128)(2,1)S(1)}, bf16[64,4,1,128]{3,0,2,1:T(8,128)(2,1)S(1)}, u32[]{:S(2)}, u32[]{:S(2)}) collective-permute-start(bf16[64,4,1,128]{3,0,2,1:T(8,128)(2,1)S(1)} %get-tuple-element.49), channel_id=1, source_target_pairs={{0,1},{1,2},{2,3},{3,4},{4,5},{5,6},{6,7},{8,9},{9,10},{10,11},{11... | collective-permute-start | bytes 196616 | tf_op jit(solution)/shard_map/ppermute | solution.py:20
  52.6 3.8 %collective-permute-start.7 = (bf16[64,4,1,128]{3,0,2,1:T(8,128)(2,1)S(1)}, bf16[64,4,1,128]{3,0,2,1:T(8,128)(2,1)S(1)}, u32[]{:S(2)}, u32[]{:S(2)}) collective-permute-start(bf16[64,4,1,128]{3,0,2,1:T(8,128)(2,1)S(1)} %get-tuple-element.50), channel_id=1, source_target_pairs={{1,0},{2,1},{3,2},{4,3},{5,4},{6,5},{7,6},{9,8},{10,9},{11,10},{12... | collective-permute-start | bytes 196616 | tf_op jit(solution)/shard_map/ppermute | solution.py:22
  65.0 14.4 %collective-permute-start.8 = (bf16[8,1,4,128]{3,0,2,1:T(8,128)(2,1)}, bf16[8,1,4,128]{3,0,2,1:T(8,128)(2,1)S(1)}, u32[]{:S(2)}, u32[]{:S(2)}) collective-permute-start(bf16[8,1,4,128]{3,0,2,1:T(8,128)(2,1)} %get-tuple-element.126), channel_id=1, source_target_pairs={{0,8},{8,16},{16,24},{24,32},{32,40},{40,48},{48,56},{56,64},{64,7... | collective-permute-start | bytes 24584 | tf_op jit(solution)/shard_map/ppermute | solution.py:20
  66.9 12.5 %collective-permute-start.9 = (bf16[8,1,4,128]{3,0,2,1:T(8,128)(2,1)}, bf16[8,1,4,128]{3,0,2,1:T(8,128)(2,1)S(1)}, u32[]{:S(2)}, u32[]{:S(2)}) collective-permute-start(bf16[8,1,4,128]{3,0,2,1:T(8,128)(2,1)} %get-tuple-element.127), channel_id=1, source_target_pairs={{8,0},{16,8},{24,16},{32,24},{40,32},{48,40},{56,48},{64,56},{72,6... | collective-permute-start | bytes 24584 | tf_op jit(solution)/shard_map/ppermute | solution.py:22
  79.4 8.5 %collective-permute-start.11 = (bf16[8,4,1,128]{3,0,2,1:T(8,128)(2,1)S(1)}, bf16[8,4,1,128]{3,0,2,1:T(8,128)(2,1)S(1)}, u32[]{:S(2)}, u32[]{:S(2)}) collective-permute-start(bf16[8,4,1,128]{3,0,2,1:T(8,128)(2,1)S(1)} %get-tuple-element.118), channel_id=1, source_target_pairs={{1,0},{2,1},{3,2},{4,3},{5,4},{6,5},{7,6},{9,8},{10,9},{11,10},{12... | collective-permute-start | bytes 24584 | tf_op jit(solution)/shard_map/ppermute | solution.py:22
  83.8 5.9 %collective-permute-start.10 = (bf16[8,4,1,128]{3,0,2,1:T(8,128)(2,1)S(1)}, bf16[8,4,1,128]{3,0,2,1:T(8,128)(2,1)S(1)}, u32[]{:S(2)}, u32[]{:S(2)}) collective-permute-start(bf16[8,4,1,128]{3,0,2,1:T(8,128)(2,1)S(1)} %get-tuple-element.117), channel_id=1, source_target_pairs={{0,1},{1,2},{2,3},{3,4},{4,5},{5,6},{6,7},{8,9},{9,10},{10,11},{11... | collective-permute-start | bytes 24584 | tf_op jit(solution)/shard_map/ppermute | solution.py:20
  96.5 14.3 %collective-permute-start.12 = (bf16[64,1,4,128]{3,0,2,1:T(8,128)(2,1)S(1)}, bf16[64,1,4,128]{3,0,2,1:T(8,128)(2,1)S(1)}, u32[]{:S(2)}, u32[]{:S(2)}) collective-permute-start(bf16[64,1,4,128]{3,0,2,1:T(8,128)(2,1)S(1)} %get-tuple-element.71), channel_id=1, source_target_pairs={{0,8},{8,16},{16,24},{24,32},{32,40},{40,48},{48,56},{56,64},{64,7... | collective-permute-start | bytes 196616 | tf_op jit(solution)/shard_map/ppermute | solution.py:20
  98.6 12.3 %collective-permute-start.13 = (bf16[64,1,4,128]{3,0,2,1:T(8,128)(2,1)S(1)}, bf16[64,1,4,128]{3,0,2,1:T(8,128)(2,1)S(1)}, u32[]{:S(2)}, u32[]{:S(2)}) collective-permute-start(bf16[64,1,4,128]{3,0,2,1:T(8,128)(2,1)S(1)} %get-tuple-element.72), channel_id=1, source_target_pairs={{8,0},{16,8},{24,16},{32,24},{40,32},{48,40},{56,48},{64,56},{72,6... | collective-permute-start | bytes 196616 | tf_op jit(solution)/shard_map/ppermute | solution.py:22
  110.9 13.1 %collective-permute-start.15 = (bf16[64,4,1,128]{3,0,2,1:T(8,128)(2,1)S(1)}, bf16[64,4,1,128]{3,0,2,1:T(8,128)(2,1)S(1)}, u32[]{:S(2)}, u32[]{:S(2)}) collective-permute-start(bf16[64,4,1,128]{3,0,2,1:T(8,128)(2,1)S(1)} %get-tuple-element.46), channel_id=1, source_target_pairs={{1,0},{2,1},{3,2},{4,3},{5,4},{6,5},{7,6},{9,8},{10,9},{11,10},{12... | collective-permute-start | bytes 196616 | tf_op jit(solution)/shard_map/ppermute | solution.py:22
  112.8 11.2 %collective-permute-start.14 = (bf16[64,4,1,128]{3,0,2,1:T(8,128)(2,1)S(1)}, bf16[64,4,1,128]{3,0,2,1:T(8,128)(2,1)S(1)}, u32[]{:S(2)}, u32[]{:S(2)}) collective-permute-start(bf16[64,4,1,128]{3,0,2,1:T(8,128)(2,1)S(1)} %get-tuple-element.45), channel_id=1, source_target_pairs={{0,1},{1,2},{2,3},{3,4},{4,5},{5,6},{6,7},{8,9},{9,10},{10,11},{11... | collective-permute-start | bytes 196616 | tf_op jit(solution)/shard_map/ppermute | solution.py:20
  117.2 11.0 %collective-permute-start.16 = (f32[38792]{0:T(1024)S(1)}, f32[38792]{0:T(1024)S(1)}, u32[]{:S(2)}, u32[]{:S(2)}) collective-permute-start(f32[38792]{0:T(1024)S(1)} %concatenate.132), channel_id=1, source_target_pairs={{0,1},{1,0},{2,3},{3,2},{4,5},{5,4},{6,7},{7,6},{8,9},{9,8},{10,11... | collective-permute-start | bytes 465512 | tf_op jit(solution)/shard_map/ppermute | solution.py:119
  128.2 8.7 %collective-permute-start.17 = (f32[38792]{0:T(1024)S(1)}, f32[38792]{0:T(1024)S(1)}, u32[]{:S(2)}, u32[]{:S(2)}) collective-permute-start(f32[38792]{0:T(1024)S(1)} %add.536), channel_id=1, source_target_pairs={{0,2},{1,3},{2,0},{3,1},{4,6},{5,7},{6,4},{7,5},{8,10},{9,11},{10,... | collective-permute-start | bytes 465512 | tf_op jit(solution)/shard_map/ppermute | solution.py:119
  136.9 46.2 %copy-start.26 = (bf16[1,64,12]{1,0,2:T(2,128)(2,1)S(1)}, bf16[1,64,12]{1,0,2:T(2,128)(2,1)}, u32[]{:S(2)}) copy-start(bf16[1,64,12]{1,0,2:T(2,128)(2,1)} %copy-done.25) | copy-start | bytes 4612
  136.9 15.1 %collective-permute-start.18 = (f32[38792]{0:T(1024)S(1)}, f32[38792]{0:T(1024)S(1)}, u32[]{:S(2)}, u32[]{:S(2)}) collective-permute-start(f32[38792]{0:T(1024)S(1)} %add.537), channel_id=1, source_target_pairs={{0,4},{1,5},{2,6},{3,7},{4,0},{5,1},{6,2},{7,3},{8,12},{9,13},{10,... | collective-permute-start | bytes 465512 | tf_op jit(solution)/shard_map/ppermute | solution.py:119
  152.1 7.1 %collective-permute-start.19 = (f32[38792]{0:T(1024)S(1)}, f32[38792]{0:T(1024)S(1)}, u32[]{:S(2)}, u32[]{:S(2)}) collective-permute-start(f32[38792]{0:T(1024)S(1)} %add.538), channel_id=1, source_target_pairs={{0,8},{8,0},{16,24},{24,16},{32,40},{40,32},{48,56},{56,48},{64,72... | collective-permute-start | bytes 465512 | tf_op jit(solution)/shard_map/ppermute | solution.py:119
  159.2 7.6 %collective-permute-start.20 = (f32[38792]{0:T(1024)S(1)}, f32[38792]{0:T(1024)S(1)}, u32[]{:S(2)}, u32[]{:S(2)}) collective-permute-start(f32[38792]{0:T(1024)S(1)} %add.539), channel_id=1, source_target_pairs={{0,16},{8,24},{16,0},{24,8},{32,48},{40,56},{48,32},{56,40},{64,80... | collective-permute-start | bytes 465512 | tf_op jit(solution)/shard_map/ppermute | solution.py:119
  161.3 39.3 %copy-start.36 = (f32[8,8,1,1]{1,0,3,2:T(8,128)S(1)}, f32[8,8,1,1]{1,0,3,2:T(8,128)}, u32[]{:S(2)}) copy-start(f32[8,8,1,1]{1,0,3,2:T(8,128)} %constant.30) | copy-start | bytes 772
  166.9 12.6 %collective-permute-start.21 = (f32[38792]{0:T(1024)S(1)}, f32[38792]{0:T(1024)S(1)}, u32[]{:S(2)}, u32[]{:S(2)}) collective-permute-start(f32[38792]{0:T(1024)S(1)} %add.540), channel_id=1, source_target_pairs={{0,32},{8,40},{16,48},{24,56},{32,0},{40,8},{48,16},{56,24},{64,96... | collective-permute-start | bytes 465512 | tf_op jit(solution)/shard_map/ppermute | solution.py:119
  179.4 11.1 %collective-permute-start.22 = (f32[38792]{0:T(1024)S(1)}, f32[38792]{0:T(1024)S(1)}, u32[]{:S(2)}, u32[]{:S(2)}) collective-permute-start(f32[38792]{0:T(1024)S(1)} %add.541), channel_id=1, source_target_pairs={{0,64},{8,72},{16,80},{24,88},{32,96},{40,104},{48,112},{56,120},{... | collective-permute-start | bytes 465512 | tf_op jit(solution)/shard_map/ppermute | solution.py:119
  190.5 7.1 %collective-permute-start.23 = (f32[38792]{0:T(1024)S(1)}, f32[38792]{0:T(1024)S(1)}, u32[]{:S(2)}, u32[]{:S(2)}) collective-permute-start(f32[38792]{0:T(1024)S(1)} %add.542), channel_id=1, source_target_pairs={{0,128},{8,136},{16,144},{24,152},{32,160},{40,168},{48,176},{56,1... | collective-permute-start | bytes 465512 | tf_op jit(solution)/shard_map/ppermute | solution.py:119
  197.7 8.6 %collective-permute-start.24 = (f32[38792]{0:T(1024)S(1)}, f32[38792]{0:T(1024)S(1)}, u32[]{:S(2)}, u32[]{:S(2)}) collective-permute-start(f32[38792]{0:T(1024)S(1)} %add.543), channel_id=1, source_target_pairs={{0,256},{8,264},{16,272},{24,280},{32,288},{40,296},{48,304},{56,3... | collective-permute-start | bytes 465512 | tf_op jit(solution)/shard_map/ppermute | solution.py:119
  (30 other events, 233.1 us)

commit v2 on v1

--- a/solution.py
+++ b/solution.py
@@ -121,6 +121,16 @@
     return flat
 
 
+def replicated_sum(flat, scatter_axis, other_axes):
+    total = flat.shape[0]
+    count = lax.axis_size(scatter_axis)
+    chunks = jnp.pad(flat, (0, (-total) % count)).reshape(count, -1)
+    owned = lax.all_to_all(chunks, scatter_axis, 0, 0, tiled=False).sum(0)
+    owned = butterfly_sum(owned, other_axes)
+    spread = lax.all_to_all(jnp.broadcast_to(owned, (count,) + owned.shape), scatter_axis, 0, 0, tiled=False)
+    return spread.reshape(-1)[:total]
+
+
 def per_device(latent, condition, cotangent, expand_kernel, mixing_matrix, project_kernel, offsets):
     planes, x_rows, y_cols = (latent.shape[1], latent.shape[2], latent.shape[3])
     hidden_width = mixing_matrix.shape[0]
@@ -166,7 +176,7 @@
         [channel_sums(inner_first), channel_sums(inner_mix), channel_sums(score_grad)]
     )
     terms = (expand_term, mixing_term, project_term, offset_term)
-    flat = butterfly_sum(jnp.concatenate([t.reshape(-1) for t in terms]), ("gx", "gz"))
+    flat = replicated_sum(jnp.concatenate([t.reshape(-1) for t in terms]), "gz", ("gx",))
     pieces, start = [], 0
     for t in terms:
         pieces.append(flat[start : start + t.size].reshape(t.shape))

time: 212 us -> 181 us (0.85)
  the two profiles are of different devices: /device:TPU:22 before, /device:TPU:56 now
where the time goes in v2:
time: 181 us; the launch traced here: 177 us
  starting transfers between devices  90.5 us (50%)
  matrix products  30.8 us (17%)
  waiting for transfers between devices  29 us (16%)
  local copies, waits for them, and re-layouts  20.7 us (11%)
  other arithmetic  4.46 us (2%)
  between operations  2 us (1%)
    ppermute x8, starting transfers between devices, extended(): lax.ppermute(head, axis, [((i + 1) % count, i) for i in range(ends)])  26.3 us
    ppermute x8, starting transfers between devices, extended(): lax.ppermute(tail, axis, [(i, (i + 1) % count) for i in range(ends)])  24.6 us
    all_to_all x1, starting transfers between devices, replicated_sum(): owned = lax.all_to_all(chunks, scatter_axis, 0, 0, tiled=False).sum(0)  18.1 us
    ppermute x3, starting transfers between devices, butterfly_sum(): flat = flat + lax.ppermute(flat, axis, [(i, i ^ bit) for i in range(count)])  16 us
    dot_general x54, matrix products, forward_taps(): jnp.einsum('oc,czxy->ozxy', weight[tap_index], sliced, preferred_element_...  10.8 us
    dot_general x54, matrix products, backward_taps(): jnp.einsum('oc,ozxy->czxy', weight[tap_index], sliced, preferred_element_...  10.8 us
    dot_general x54, matrix products, weight_taps(): jnp.einsum('ozxy,czxy->oc', grad, sliced, preferred_element_type=jnp.floa...  8.14 us
    all_to_all x1, waiting for transfers between devices, replicated_sum(): lax.all_to_all(jnp.broadcast_to(owned, (count,) + owned.shape), scatter_a...  7.14 us
  transfers between devices with their start and end apart: 21, of which 9 were waited for; matrix products, arithmetic and copies ran while one was open for 14% of the time, Pallas kernels for 0%

profile of v2, /device:TPU:56, one launch (start us, length us, event | category | flops | bytes accessed | tf_op | source)
XLA Modules:
  0.0 177.5 jit_solution(431727433100290144)
XLA Ops:
  2.1 5.1 %collective-permute-start = (bf16[12,1,4,128]{3,0,2,1:T(8,128)(2,1)S(1)}, bf16[12,1,4,128]{3,0,2,1:T(8,128)(2,1)S(1)}, u32[]{:S(2)}, u32[]{:S(2)}) collective-permute-start(bf16[12,1,4,128]{3,0,2,1:T(8,128)(2,1)S(1)} %get-tuple-element.145), channel_id=1, source_target_pairs={{0,8},{8,16},{16,24},{24,32},{32,40},{40,48},{48,56},{56,64},{64,7... | collective-permute-start | bytes 36872 | tf_op jit(solution)/shard_map/ppermute | solution.py:20
  7.2 1.9 %collective-permute-start.1 = (bf16[12,1,4,128]{3,0,2,1:T(8,128)(2,1)S(1)}, bf16[12,1,4,128]{3,0,2,1:T(8,128)(2,1)S(1)}, u32[]{:S(2)}, u32[]{:S(2)}) collective-permute-start(bf16[12,1,4,128]{3,0,2,1:T(8,128)(2,1)S(1)} %get-tuple-element.146), channel_id=1, source_target_pairs={{8,0},{16,8},{24,16},{32,24},{40,32},{48,40},{56,48},{64,56},{72,6... | collective-permute-start | bytes 36872 | tf_op jit(solution)/shard_map/ppermute | solution.py:22
  9.1 1.2 fusion.548
  10.3 1.4 fusion.547
  14.3 1.9 %collective-permute-start.2 = (bf16[12,4,1,128]{3,0,2,1:T(8,128)(2,1)S(1)}, bf16[12,4,1,128]{3,0,2,1:T(8,128)(2,1)S(1)}, u32[]{:S(2)}, u32[]{:S(2)}) collective-permute-start(bf16[12,4,1,128]{3,0,2,1:T(8,128)(2,1)S(1)} %get-tuple-element.131), channel_id=1, source_target_pairs={{0,1},{1,2},{2,3},{3,4},{4,5},{5,6},{6,7},{8,9},{9,10},{10,11},{11... | collective-permute-start | bytes 36872 | tf_op jit(solution)/shard_map/ppermute | solution.py:20
  16.2 4.5 %collective-permute-start.3 = (bf16[12,4,1,128]{3,0,2,1:T(8,128)(2,1)S(1)}, bf16[12,4,1,128]{3,0,2,1:T(8,128)(2,1)S(1)}, u32[]{:S(2)}, u32[]{:S(2)}) collective-permute-start(bf16[12,4,1,128]{3,0,2,1:T(8,128)(2,1)S(1)} %get-tuple-element.132), channel_id=1, source_target_pairs={{1,0},{2,1},{3,2},{4,3},{5,4},{6,5},{7,6},{9,8},{10,9},{11,10},{12... | collective-permute-start | bytes 36872 | tf_op jit(solution)/shard_map/ppermute | solution.py:22
  29.7 4.8 %collective-permute-start.4 = (bf16[64,1,4,128]{3,0,2,1:T(8,128)(2,1)S(1)}, bf16[64,1,4,128]{3,0,2,1:T(8,128)(2,1)S(1)}, u32[]{:S(2)}, u32[]{:S(2)}) collective-permute-start(bf16[64,1,4,128]{3,0,2,1:T(8,128)(2,1)S(1)} %get-tuple-element.94), channel_id=1, source_target_pairs={{0,8},{8,16},{16,24},{24,32},{32,40},{40,48},{48,56},{56,64},{64,7... | collective-permute-start | bytes 196616 | tf_op jit(solution)/shard_map/ppermute | solution.py:20
  34.6 1.9 %collective-permute-start.5 = (bf16[64,1,4,128]{3,0,2,1:T(8,128)(2,1)S(1)}, bf16[64,1,4,128]{3,0,2,1:T(8,128)(2,1)S(1)}, u32[]{:S(2)}, u32[]{:S(2)}) collective-permute-start(bf16[64,1,4,128]{3,0,2,1:T(8,128)(2,1)S(1)} %get-tuple-element.95), channel_id=1, source_target_pairs={{8,0},{16,8},{24,16},{32,24},{40,32},{48,40},{56,48},{64,56},{72,6... | collective-permute-start | bytes 196616 | tf_op jit(solution)/shard_map/ppermute | solution.py:22
  37.4 4.3 %collective-permute-done.5 = bf16[64,1,4,128]{3,0,2,1:T(8,128)(2,1)S(1)} collective-permute-done((bf16[64,1,4,128]{3,0,2,1:T(8,128)(2,1)S(1)}, bf16[64,1,4,128]{3,0,2,1:T(8,128)(2,1)S(1)}, u32[]{:S(2)}, u32[]{:S(2)}) %collective-permute-start.5) | collective-permute-done | bytes 65568 | tf_op jit(solution)/shard_map/ppermute | solution.py:22
  41.6 1.9 %collective-permute-start.6 = (bf16[64,4,1,128]{3,0,2,1:T(8,128)(2,1)S(1)}, bf16[64,4,1,128]{3,0,2,1:T(8,128)(2,1)S(1)}, u32[]{:S(2)}, u32[]{:S(2)}) collective-permute-start(bf16[64,4,1,128]{3,0,2,1:T(8,128)(2,1)S(1)} %get-tuple-element.70), channel_id=1, source_target_pairs={{0,1},{1,2},{2,3},{3,4},{4,5},{5,6},{6,7},{8,9},{9,10},{10,11},{11... | collective-permute-start | bytes 196616 | tf_op jit(solution)/shard_map/ppermute | solution.py:20
  43.6 4.5 %collective-permute-start.7 = (bf16[64,4,1,128]{3,0,2,1:T(8,128)(2,1)S(1)}, bf16[64,4,1,128]{3,0,2,1:T(8,128)(2,1)S(1)}, u32[]{:S(2)}, u32[]{:S(2)}) collective-permute-start(bf16[64,4,1,128]{3,0,2,1:T(8,128)(2,1)S(1)} %get-tuple-element.71), channel_id=1, source_target_pairs={{1,0},{2,1},{3,2},{4,3},{5,4},{6,5},{7,6},{9,8},{10,9},{11,10},{12... | collective-permute-start | bytes 196616 | tf_op jit(solution)/shard_map/ppermute | solution.py:22
  48.2 1.8 %collective-permute-done.7 = bf16[64,4,1,128]{3,0,2,1:T(8,128)(2,1)S(1)} collective-permute-done((bf16[64,4,1,128]{3,0,2,1:T(8,128)(2,1)S(1)}, bf16[64,4,1,128]{3,0,2,1:T(8,128)(2,1)S(1)}, u32[]{:S(2)}, u32[]{:S(2)}) %collective-permute-start.7) | collective-permute-done | bytes 65568 | tf_op jit(solution)/shard_map/ppermute | solution.py:22
  58.5 2.8 %collective-permute-start.8 = (bf16[8,1,4,128]{3,0,2,1:T(8,128)(2,1)}, bf16[8,1,4,128]{3,0,2,1:T(8,128)(2,1)S(1)}, u32[]{:S(2)}, u32[]{:S(2)}) collective-permute-start(bf16[8,1,4,128]{3,0,2,1:T(8,128)(2,1)} %get-tuple-element.147), channel_id=1, source_target_pairs={{0,8},{8,16},{16,24},{24,32},{32,40},{40,48},{48,56},{56,64},{64,7... | collective-permute-start | bytes 24584 | tf_op jit(solution)/shard_map/ppermute | solution.py:20
  61.4 3.0 %collective-permute-start.9 = (bf16[8,1,4,128]{3,0,2,1:T(8,128)(2,1)}, bf16[8,1,4,128]{3,0,2,1:T(8,128)(2,1)S(1)}, u32[]{:S(2)}, u32[]{:S(2)}) collective-permute-start(bf16[8,1,4,128]{3,0,2,1:T(8,128)(2,1)} %get-tuple-element.148), channel_id=1, source_target_pairs={{8,0},{16,8},{24,16},{32,24},{40,32},{48,40},{56,48},{64,56},{72,6... | collective-permute-start | bytes 24584 | tf_op jit(solution)/shard_map/ppermute | solution.py:22
  67.3 1.8 %reshape.60 = f32[4,8,256]{2,1,0:T(8,128)} reshape(f32[2,2,4,2,128,2]{5,4,3,2,1,0:T(8,128)S(1)} %bitcast.1118) | data formatting | bytes 65536 | tf_op jit(solution)/shard_map/reshape | solution.py:50
  69.3 4.0 %collective-permute-start.11 = (bf16[8,4,1,128]{3,0,2,1:T(8,128)(2,1)S(1)}, bf16[8,4,1,128]{3,0,2,1:T(8,128)(2,1)S(1)}, u32[]{:S(2)}, u32[]{:S(2)}) collective-permute-start(bf16[8,4,1,128]{3,0,2,1:T(8,128)(2,1)S(1)} %get-tuple-element.139), channel_id=1, source_target_pairs={{1,0},{2,1},{3,2},{4,3},{5,4},{6,5},{7,6},{9,8},{10,9},{11,10},{12... | collective-permute-start | bytes 24584 | tf_op jit(solution)/shard_map/ppermute | solution.py:22
  73.3 1.9 %collective-permute-start.10 = (bf16[8,4,1,128]{3,0,2,1:T(8,128)(2,1)S(1)}, bf16[8,4,1,128]{3,0,2,1:T(8,128)(2,1)S(1)}, u32[]{:S(2)}, u32[]{:S(2)}) collective-permute-start(bf16[8,4,1,128]{3,0,2,1:T(8,128)(2,1)S(1)} %get-tuple-element.138), channel_id=1, source_target_pairs={{0,1},{1,2},{2,3},{3,4},{4,5},{5,6},{6,7},{8,9},{9,10},{10,11},{11... | collective-permute-start | bytes 24584 | tf_op jit(solution)/shard_map/ppermute | solution.py:20
  75.5 3.7 %collective-permute-done.10 = bf16[8,4,1,128]{3,0,2,1:T(8,128)(2,1)S(1)} collective-permute-done((bf16[8,4,1,128]{3,0,2,1:T(8,128)(2,1)S(1)}, bf16[8,4,1,128]{3,0,2,1:T(8,128)(2,1)S(1)}, u32[]{:S(2)}, u32[]{:S(2)}) %collective-permute-start.10) | collective-permute-done | bytes 8224 | tf_op jit(solution)/shard_map/ppermute | solution.py:20
  86.0 4.1 %collective-permute-start.12 = (bf16[64,1,4,128]{3,0,2,1:T(8,128)(2,1)S(1)}, bf16[64,1,4,128]{3,0,2,1:T(8,128)(2,1)S(1)}, u32[]{:S(2)}, u32[]{:S(2)}) collective-permute-start(bf16[64,1,4,128]{3,0,2,1:T(8,128)(2,1)S(1)} %get-tuple-element.92), channel_id=1, source_target_pairs={{0,8},{8,16},{16,24},{24,32},{32,40},{40,48},{48,56},{56,64},{64,7... | collective-permute-start | bytes 196616 | tf_op jit(solution)/shard_map/ppermute | solution.py:20
  90.2 2.1 %collective-permute-start.13 = (bf16[64,1,4,128]{3,0,2,1:T(8,128)(2,1)S(1)}, bf16[64,1,4,128]{3,0,2,1:T(8,128)(2,1)S(1)}, u32[]{:S(2)}, u32[]{:S(2)}) collective-permute-start(bf16[64,1,4,128]{3,0,2,1:T(8,128)(2,1)S(1)} %get-tuple-element.93), channel_id=1, source_target_pairs={{8,0},{16,8},{24,16},{32,24},{40,32},{48,40},{56,48},{64,56},{72,6... | collective-permute-start | bytes 196616 | tf_op jit(solution)/shard_map/ppermute | solution.py:22
  97.5 4.2 %collective-permute-start.15 = (bf16[64,4,1,128]{3,0,2,1:T(8,128)(2,1)S(1)}, bf16[64,4,1,128]{3,0,2,1:T(8,128)(2,1)S(1)}, u32[]{:S(2)}, u32[]{:S(2)}) collective-permute-start(bf16[64,4,1,128]{3,0,2,1:T(8,128)(2,1)S(1)} %get-tuple-element.67), channel_id=1, source_target_pairs={{1,0},{2,1},{3,2},{4,3},{5,4},{6,5},{7,6},{9,8},{10,9},{11,10},{12... | collective-permute-start | bytes 196616 | tf_op jit(solution)/shard_map/ppermute | solution.py:22
  101.7 1.9 %collective-permute-start.14 = (bf16[64,4,1,128]{3,0,2,1:T(8,128)(2,1)S(1)}, bf16[64,4,1,128]{3,0,2,1:T(8,128)(2,1)S(1)}, u32[]{:S(2)}, u32[]{:S(2)}) collective-permute-start(bf16[64,4,1,128]{3,0,2,1:T(8,128)(2,1)S(1)} %get-tuple-element.66), channel_id=1, source_target_pairs={{0,1},{1,2},{2,3},{3,4},{4,5},{5,6},{6,7},{8,9},{9,10},{10,11},{11... | collective-permute-start | bytes 196616 | tf_op jit(solution)/shard_map/ppermute | solution.py:20
  105.0 18.1 %all-to-all-start = ((f32[64,1,607]{2,1,0:T(1,128)}), f32[64,1,607]{2,1,0:T(1,128)S(1)}, u32[]{:S(2)}, u32[]{:S(2)}) async-start(f32[64,1,607]{2,1,0:T(1,128)} %all_to_all.10), calls=%async_computation | async-start | bytes 327680 | tf_op jit(solution)/shard_map/all_to_all | solution.py:128
  127.8 5.9 %all-to-all-done = f32[64,1,607]{2,1,0:T(1,128)S(1)} async-done(((f32[64,1,607]{2,1,0:T(1,128)}), f32[64,1,607]{2,1,0:T(1,128)S(1)}, u32[]{:S(2)}, u32[]{:S(2)}) %all-to-all-start) | async-done | bytes 155424 | tf_op jit(solution)/shard_map/all_to_all | solution.py:128
  133.8 1.9 %collective-permute-start.16 = (f32[607]{0:T(1024)S(1)}, f32[607]{0:T(1024)S(1)}, u32[]{:S(2)}, u32[]{:S(2)}) collective-permute-start(f32[607]{0:T(1024)S(1)} %reduce_sum.39), channel_id=1, source_target_pairs={{0,1},{1,0},{2,3},{3,2},{4,5},{5,4},{6,7},{7,6},{8,9},{9,8},{10,11... | collective-permute-start | bytes 7292 | tf_op jit(solution)/shard_map/ppermute | solution.py:119
  136.8 8.1 %collective-permute-start.17 = (f32[607]{0:T(1024)S(1)}, f32[607]{0:T(1024)S(1)}, u32[]{:S(2)}, u32[]{:S(2)}) collective-permute-start(f32[607]{0:T(1024)S(1)} %add.520), channel_id=1, source_target_pairs={{0,2},{1,3},{2,0},{3,1},{4,6},{5,7},{6,4},{7,5},{8,10},{9,11},{10,... | collective-permute-start | bytes 7292 | tf_op jit(solution)/shard_map/ppermute | solution.py:119
  145.0 1.4 collective-permute-done.17
  146.5 6.0 %collective-permute-start.18 = (f32[607]{0:T(1024)S(1)}, f32[607]{0:T(1024)S(1)}, u32[]{:S(2)}, u32[]{:S(2)}) collective-permute-start(f32[607]{0:T(1024)S(1)} %add.521), channel_id=1, source_target_pairs={{0,4},{1,5},{2,6},{3,7},{4,0},{5,1},{6,2},{7,3},{8,12},{9,13},{10,... | collective-permute-start | bytes 7292 | tf_op jit(solution)/shard_map/ppermute | solution.py:119
  152.6 3.2 %collective-permute-done.18 = f32[607]{0:T(1024)S(1)} collective-permute-done((f32[607]{0:T(1024)S(1)}, f32[607]{0:T(1024)S(1)}, u32[]{:S(2)}, u32[]{:S(2)}) %collective-permute-start.18) | collective-permute-done | bytes 2460 | tf_op jit(solution)/shard_map/ppermute | solution.py:119
  156.6 5.5 %all-to-all-start.1 = ((f32[64,1,607]{2,1,0:T(1,128)}), f32[64,1,607]{2,1,0:T(1,128)S(1)}, u32[]{:S(2)}, u32[]{:S(2)}) async-start(f32[64,1,607]{2,1,0:T(1,128)} %broadcast_in_dim.2), calls=%async_computation.1 | async-start | bytes 327680 | tf_op jit(solution)/shard_map/all_to_all | solution.py:130
  163.0 1.8 %reshape.62 = f32[4,8,256]{2,1,0:T(8,128)} reshape(f32[2,2,4,2,128,2]{5,4,3,2,1,0:T(8,128)S(1)} %bitcast.1119) | data formatting | bytes 65536 | tf_op jit(solution)/shard_map/reshape | solution.py:50
  165.5 7.1 %all-to-all-done.1 = f32[64,1,607]{2,1,0:T(1,128)S(1)} async-done(((f32[64,1,607]{2,1,0:T(1,128)}), f32[64,1,607]{2,1,0:T(1,128)S(1)}, u32[]{:S(2)}, u32[]{:S(2)}) %all-to-all-start.1) | async-done | bytes 155424 | tf_op jit(solution)/shard_map/all_to_all | solution.py:130
  (312 shorter events, 51.3 us)
Async XLA Ops:
  0.6 28.8 %copy-start = (bf16[64,64]{1,0:T(8,128)(2,1)S(1)}, bf16[64,64]{1,0:T(8,128)(2,1)}, u32[]{:S(2)}) copy-start(bf16[64,64]{1,0:T(8,128)(2,1)} %param.13) | copy-start | bytes 24580
  2.1 12.1 %collective-permute-start = (bf16[12,1,4,128]{3,0,2,1:T(8,128)(2,1)S(1)}, bf16[12,1,4,128]{3,0,2,1:T(8,128)(2,1)S(1)}, u32[]{:S(2)}, u32[]{:S(2)}) collective-permute-start(bf16[12,1,4,128]{3,0,2,1:T(8,128)(2,1)S(1)} %get-tuple-element.145), channel_id=1, source_target_pairs={{0,8},{8,16},{16,24},{24,32},{32,40},{40,48},{48,56},{56,64},{64,7... | collective-permute-start | bytes 36872 | tf_op jit(solution)/shard_map/ppermute | solution.py:20
  7.2 7.0 %collective-permute-start.1 = (bf16[12,1,4,128]{3,0,2,1:T(8,128)(2,1)S(1)}, bf16[12,1,4,128]{3,0,2,1:T(8,128)(2,1)S(1)}, u32[]{:S(2)}, u32[]{:S(2)}) collective-permute-start(bf16[12,1,4,128]{3,0,2,1:T(8,128)(2,1)S(1)} %get-tuple-element.146), channel_id=1, source_target_pairs={{8,0},{16,8},{24,16},{32,24},{40,32},{48,40},{56,48},{64,56},{72,6... | collective-permute-start | bytes 36872 | tf_op jit(solution)/shard_map/ppermute | solution.py:22
  11.7 16.1 %copy-start.25 = (bf16[1,64,12]{1,0,2:T(2,128)(2,1)}, bf16[1,64,12]{1,0,2:T(2,128)(2,1)S(1)}, u32[]{:S(2)}) copy-start(bf16[1,64,12]{1,0,2:T(2,128)(2,1)S(1)} %get-tuple-element.97) | copy-start | bytes 4612
  11.7 16.3 %copy-start.27 = (bf16[1,64,12]{1,0,2:T(2,128)(2,1)}, bf16[1,64,12]{1,0,2:T(2,128)(2,1)S(1)}, u32[]{:S(2)}) copy-start(bf16[1,64,12]{1,0,2:T(2,128)(2,1)S(1)} %get-tuple-element.103) | copy-start | bytes 4612
  11.7 16.8 %copy-start.33 = (bf16[1,64,12]{1,0,2:T(2,128)(2,1)}, bf16[1,64,12]{1,0,2:T(2,128)(2,1)S(1)}, u32[]{:S(2)}) copy-start(bf16[1,64,12]{1,0,2:T(2,128)(2,1)S(1)} %get-tuple-element.114) | copy-start | bytes 4612
  11.7 17.0 %copy-start.31 = (bf16[1,64,12]{1,0,2:T(2,128)(2,1)}, bf16[1,64,12]{1,0,2:T(2,128)(2,1)S(1)}, u32[]{:S(2)}) copy-start(bf16[1,64,12]{1,0,2:T(2,128)(2,1)S(1)} %get-tuple-element.111) | copy-start | bytes 4612
  11.7 17.3 %copy-start.29 = (bf16[1,64,12]{1,0,2:T(2,128)(2,1)}, bf16[1,64,12]{1,0,2:T(2,128)(2,1)S(1)}, u32[]{:S(2)}) copy-start(bf16[1,64,12]{1,0,2:T(2,128)(2,1)S(1)} %get-tuple-element.96) | copy-start | bytes 4612
  14.3 7.4 %collective-permute-start.2 = (bf16[12,4,1,128]{3,0,2,1:T(8,128)(2,1)S(1)}, bf16[12,4,1,128]{3,0,2,1:T(8,128)(2,1)S(1)}, u32[]{:S(2)}, u32[]{:S(2)}) collective-permute-start(bf16[12,4,1,128]{3,0,2,1:T(8,128)(2,1)S(1)} %get-tuple-element.131), channel_id=1, source_target_pairs={{0,1},{1,2},{2,3},{3,4},{4,5},{5,6},{6,7},{8,9},{9,10},{10,11},{11... | collective-permute-start | bytes 36872 | tf_op jit(solution)/shard_map/ppermute | solution.py:20
  16.2 6.0 %collective-permute-start.3 = (bf16[12,4,1,128]{3,0,2,1:T(8,128)(2,1)S(1)}, bf16[12,4,1,128]{3,0,2,1:T(8,128)(2,1)S(1)}, u32[]{:S(2)}, u32[]{:S(2)}) collective-permute-start(bf16[12,4,1,128]{3,0,2,1:T(8,128)(2,1)S(1)} %get-tuple-element.132), channel_id=1, source_target_pairs={{1,0},{2,1},{3,2},{4,3},{5,4},{6,5},{7,6},{9,8},{10,9},{11,10},{12... | collective-permute-start | bytes 36872 | tf_op jit(solution)/shard_map/ppermute | solution.py:22
  29.7 7.6 %collective-permute-start.4 = (bf16[64,1,4,128]{3,0,2,1:T(8,128)(2,1)S(1)}, bf16[64,1,4,128]{3,0,2,1:T(8,128)(2,1)S(1)}, u32[]{:S(2)}, u32[]{:S(2)}) collective-permute-start(bf16[64,1,4,128]{3,0,2,1:T(8,128)(2,1)S(1)} %get-tuple-element.94), channel_id=1, source_target_pairs={{0,8},{8,16},{16,24},{24,32},{32,40},{40,48},{48,56},{56,64},{64,7... | collective-permute-start | bytes 196616 | tf_op jit(solution)/shard_map/ppermute | solution.py:20
  34.6 7.1 %collective-permute-start.5 = (bf16[64,1,4,128]{3,0,2,1:T(8,128)(2,1)S(1)}, bf16[64,1,4,128]{3,0,2,1:T(8,128)(2,1)S(1)}, u32[]{:S(2)}, u32[]{:S(2)}) collective-permute-start(bf16[64,1,4,128]{3,0,2,1:T(8,128)(2,1)S(1)} %get-tuple-element.95), channel_id=1, source_target_pairs={{8,0},{16,8},{24,16},{32,24},{40,32},{48,40},{56,48},{64,56},{72,6... | collective-permute-start | bytes 196616 | tf_op jit(solution)/shard_map/ppermute | solution.py:22
  41.6 6.5 %collective-permute-start.6 = (bf16[64,4,1,128]{3,0,2,1:T(8,128)(2,1)S(1)}, bf16[64,4,1,128]{3,0,2,1:T(8,128)(2,1)S(1)}, u32[]{:S(2)}, u32[]{:S(2)}) collective-permute-start(bf16[64,4,1,128]{3,0,2,1:T(8,128)(2,1)S(1)} %get-tuple-element.70), channel_id=1, source_target_pairs={{0,1},{1,2},{2,3},{3,4},{4,5},{5,6},{6,7},{8,9},{9,10},{10,11},{11... | collective-permute-start | bytes 196616 | tf_op jit(solution)/shard_map/ppermute | solution.py:20
  43.6 6.4 %collective-permute-start.7 = (bf16[64,4,1,128]{3,0,2,1:T(8,128)(2,1)S(1)}, bf16[64,4,1,128]{3,0,2,1:T(8,128)(2,1)S(1)}, u32[]{:S(2)}, u32[]{:S(2)}) collective-permute-start(bf16[64,4,1,128]{3,0,2,1:T(8,128)(2,1)S(1)} %get-tuple-element.71), channel_id=1, source_target_pairs={{1,0},{2,1},{3,2},{4,3},{5,4},{6,5},{7,6},{9,8},{10,9},{11,10},{12... | collective-permute-start | bytes 196616 | tf_op jit(solution)/shard_map/ppermute | solution.py:22
  57.6 8.7 %copy-start.35 = (f32[8,8,1,1]{1,0,3,2:T(8,128)S(1)}, f32[8,8,1,1]{1,0,3,2:T(8,128)}, u32[]{:S(2)}) copy-start(f32[8,8,1,1]{1,0,3,2:T(8,128)} %constant.33) | copy-start | bytes 772
  58.5 10.7 %collective-permute-start.8 = (bf16[8,1,4,128]{3,0,2,1:T(8,128)(2,1)}, bf16[8,1,4,128]{3,0,2,1:T(8,128)(2,1)S(1)}, u32[]{:S(2)}, u32[]{:S(2)}) collective-permute-start(bf16[8,1,4,128]{3,0,2,1:T(8,128)(2,1)} %get-tuple-element.147), channel_id=1, source_target_pairs={{0,8},{8,16},{16,24},{24,32},{32,40},{40,48},{48,56},{56,64},{64,7... | collective-permute-start | bytes 24584 | tf_op jit(solution)/shard_map/ppermute | solution.py:20
  61.4 7.9 %collective-permute-start.9 = (bf16[8,1,4,128]{3,0,2,1:T(8,128)(2,1)}, bf16[8,1,4,128]{3,0,2,1:T(8,128)(2,1)S(1)}, u32[]{:S(2)}, u32[]{:S(2)}) collective-permute-start(bf16[8,1,4,128]{3,0,2,1:T(8,128)(2,1)} %get-tuple-element.148), channel_id=1, source_target_pairs={{8,0},{16,8},{24,16},{32,24},{40,32},{48,40},{56,48},{64,56},{72,6... | collective-permute-start | bytes 24584 | tf_op jit(solution)/shard_map/ppermute | solution.py:22
  69.3 6.2 %collective-permute-start.11 = (bf16[8,4,1,128]{3,0,2,1:T(8,128)(2,1)S(1)}, bf16[8,4,1,128]{3,0,2,1:T(8,128)(2,1)S(1)}, u32[]{:S(2)}, u32[]{:S(2)}) collective-permute-start(bf16[8,4,1,128]{3,0,2,1:T(8,128)(2,1)S(1)} %get-tuple-element.139), channel_id=1, source_target_pairs={{1,0},{2,1},{3,2},{4,3},{5,4},{6,5},{7,6},{9,8},{10,9},{11,10},{12... | collective-permute-start | bytes 24584 | tf_op jit(solution)/shard_map/ppermute | solution.py:22
  73.3 5.9 %collective-permute-start.10 = (bf16[8,4,1,128]{3,0,2,1:T(8,128)(2,1)S(1)}, bf16[8,4,1,128]{3,0,2,1:T(8,128)(2,1)S(1)}, u32[]{:S(2)}, u32[]{:S(2)}) collective-permute-start(bf16[8,4,1,128]{3,0,2,1:T(8,128)(2,1)S(1)} %get-tuple-element.138), channel_id=1, source_target_pairs={{0,1},{1,2},{2,3},{3,4},{4,5},{5,6},{6,7},{8,9},{9,10},{10,11},{11... | collective-permute-start | bytes 24584 | tf_op jit(solution)/shard_map/ppermute | solution.py:20
  85.9 8.6 %copy-start.7 = (bf16[12,2,4,128]{3,0,2,1:T(8,128)(2,1)S(1)}, bf16[12,2,4,128]{3,0,2,1:T(8,128)(2,1)}, u32[]{:S(2)}) copy-start(bf16[12,2,4,128]{3,0,2,1:T(8,128)(2,1)} %get-tuple-element.79) | copy-start | bytes 73732
  86.0 8.6 %copy-start.21 = (bf16[12,2,4,128]{3,0,2,1:T(8,128)(2,1)S(1)}, bf16[12,2,4,128]{3,0,2,1:T(8,128)(2,1)}, u32[]{:S(2)}) copy-start(bf16[12,2,4,128]{3,0,2,1:T(8,128)(2,1)} %get-tuple-element.124) | copy-start | bytes 73732
  86.0 11.4 %collective-permute-start.12 = (bf16[64,1,4,128]{3,0,2,1:T(8,128)(2,1)S(1)}, bf16[64,1,4,128]{3,0,2,1:T(8,128)(2,1)S(1)}, u32[]{:S(2)}, u32[]{:S(2)}) collective-permute-start(bf16[64,1,4,128]{3,0,2,1:T(8,128)(2,1)S(1)} %get-tuple-element.92), channel_id=1, source_target_pairs={{0,8},{8,16},{16,24},{24,32},{32,40},{40,48},{48,56},{56,64},{64,7... | collective-permute-start | bytes 196616 | tf_op jit(solution)/shard_map/ppermute | solution.py:20
  90.2 7.3 %collective-permute-start.13 = (bf16[64,1,4,128]{3,0,2,1:T(8,128)(2,1)S(1)}, bf16[64,1,4,128]{3,0,2,1:T(8,128)(2,1)S(1)}, u32[]{:S(2)}, u32[]{:S(2)}) collective-permute-start(bf16[64,1,4,128]{3,0,2,1:T(8,128)(2,1)S(1)} %get-tuple-element.93), channel_id=1, source_target_pairs={{8,0},{16,8},{24,16},{32,24},{40,32},{48,40},{56,48},{64,56},{72,6... | collective-permute-start | bytes 196616 | tf_op jit(solution)/shard_map/ppermute | solution.py:22
  97.5 25.6 %collective-permute-start.15 = (bf16[64,4,1,128]{3,0,2,1:T(8,128)(2,1)S(1)}, bf16[64,4,1,128]{3,0,2,1:T(8,128)(2,1)S(1)}, u32[]{:S(2)}, u32[]{:S(2)}) collective-permute-start(bf16[64,4,1,128]{3,0,2,1:T(8,128)(2,1)S(1)} %get-tuple-element.67), channel_id=1, source_target_pairs={{1,0},{2,1},{3,2},{4,3},{5,4},{6,5},{7,6},{9,8},{10,9},{11,10},{12... | collective-permute-start | bytes 196616 | tf_op jit(solution)/shard_map/ppermute | solution.py:22
  101.7 21.4 %collective-permute-start.14 = (bf16[64,4,1,128]{3,0,2,1:T(8,128)(2,1)S(1)}, bf16[64,4,1,128]{3,0,2,1:T(8,128)(2,1)S(1)}, u32[]{:S(2)}, u32[]{:S(2)}) collective-permute-start(bf16[64,4,1,128]{3,0,2,1:T(8,128)(2,1)S(1)} %get-tuple-element.66), channel_id=1, source_target_pairs={{0,1},{1,2},{2,3},{3,4},{4,5},{5,6},{6,7},{8,9},{9,10},{10,11},{11... | collective-permute-start | bytes 196616 | tf_op jit(solution)/shard_map/ppermute | solution.py:20
  105.0 28.6 %all-to-all-start = ((f32[64,1,607]{2,1,0:T(1,128)}), f32[64,1,607]{2,1,0:T(1,128)S(1)}, u32[]{:S(2)}, u32[]{:S(2)}) async-start(f32[64,1,607]{2,1,0:T(1,128)} %all_to_all.10), calls=%async_computation | async-start | bytes 327680 | tf_op jit(solution)/shard_map/all_to_all | solution.py:128
  127.0 25.5 %copy-start.26 = (bf16[1,64,12]{1,0,2:T(2,128)(2,1)S(1)}, bf16[1,64,12]{1,0,2:T(2,128)(2,1)}, u32[]{:S(2)}) copy-start(bf16[1,64,12]{1,0,2:T(2,128)(2,1)} %copy-done.25) | copy-start | bytes 4612
  127.6 34.6 %copy-start.36 = (f32[8,8,1,1]{1,0,3,2:T(8,128)S(1)}, f32[8,8,1,1]{1,0,3,2:T(8,128)}, u32[]{:S(2)}) copy-start(f32[8,8,1,1]{1,0,3,2:T(8,128)} %constant.33) | copy-start | bytes 772
  133.8 3.1 %collective-permute-start.16 = (f32[607]{0:T(1024)S(1)}, f32[607]{0:T(1024)S(1)}, u32[]{:S(2)}, u32[]{:S(2)}) collective-permute-start(f32[607]{0:T(1024)S(1)} %reduce_sum.39), channel_id=1, source_target_pairs={{0,1},{1,0},{2,3},{3,2},{4,5},{5,4},{6,7},{7,6},{8,9},{9,8},{10,11... | collective-permute-start | bytes 7292 | tf_op jit(solution)/shard_map/ppermute | solution.py:119
  136.8 9.6 %collective-permute-start.17 = (f32[607]{0:T(1024)S(1)}, f32[607]{0:T(1024)S(1)}, u32[]{:S(2)}, u32[]{:S(2)}) collective-permute-start(f32[607]{0:T(1024)S(1)} %add.520), channel_id=1, source_target_pairs={{0,2},{1,3},{2,0},{3,1},{4,6},{5,7},{6,4},{7,5},{8,10},{9,11},{10,... | collective-permute-start | bytes 7292 | tf_op jit(solution)/shard_map/ppermute | solution.py:119
  146.5 9.4 %collective-permute-start.18 = (f32[607]{0:T(1024)S(1)}, f32[607]{0:T(1024)S(1)}, u32[]{:S(2)}, u32[]{:S(2)}) collective-permute-start(f32[607]{0:T(1024)S(1)} %add.521), channel_id=1, source_target_pairs={{0,4},{1,5},{2,6},{3,7},{4,0},{5,1},{6,2},{7,3},{8,12},{9,13},{10,... | collective-permute-start | bytes 7292 | tf_op jit(solution)/shard_map/ppermute | solution.py:119
  156.6 16.0 %all-to-all-start.1 = ((f32[64,1,607]{2,1,0:T(1,128)}), f32[64,1,607]{2,1,0:T(1,128)S(1)}, u32[]{:S(2)}, u32[]{:S(2)}) async-start(f32[64,1,607]{2,1,0:T(1,128)} %broadcast_in_dim.2), calls=%async_computation.1 | async-start | bytes 327680 | tf_op jit(solution)/shard_map/all_to_all | solution.py:130
  (26 other events, 136.8 us)

commit v3 on v2

--- a/solution.py
+++ b/solution.py
@@ -140,15 +140,25 @@
     mixing_offset = offsets[hidden_width : 2 * hidden_width][:, None, None, None]
     project_offset = offsets[2 * hidden_width :][:, None, None, None]
     inputs = jnp.concatenate([upper_half.astype(jnp.bfloat16), condition], axis=0)
-    framed = frame_cols(extended(inputs, (("gz", 1), ("gx", 2)), 1))
-    pre_one = forward_taps(framed, expand_kernel, planes, x_rows) + expand_offset
-    act_one = jax.nn.silu(pre_one).astype(jnp.bfloat16)
-    pre_two = (
-        jnp.einsum("oc,czxy->ozxy", mixing_matrix, act_one, preferred_element_type=jnp.float32)
+    wide = frame_cols(extended(inputs, (("gz", 1), ("gx", 2)), 2))
+    framed = wide[:, 1:-1, 1:-1]
+    pre_wide = forward_taps(wide, expand_kernel, planes + 2, x_rows + 2) + expand_offset
+    act_wide = jax.nn.silu(pre_wide).astype(jnp.bfloat16)
+    pre_two_wide = (
+        jnp.einsum("oc,czxy->ozxy", mixing_matrix, act_wide, preferred_element_type=jnp.float32)
         + mixing_offset
     )
-    act_two = jax.nn.silu(pre_two).astype(jnp.bfloat16)
-    act_frame = frame_cols(extended(act_two, (("gz", 1), ("gx", 2)), 1))
+    plane_at = lax.axis_index("gz") * planes - 1 + jnp.arange(planes + 2)
+    row_at = lax.axis_index("gx") * x_rows - 1 + jnp.arange(x_rows + 2)
+    inside = (
+        ((plane_at >= 0) & (plane_at < planes * lax.axis_size("gz")))[:, None]
+        & ((row_at >= 0) & (row_at < x_rows * lax.axis_size("gx")))[None, :]
+    )
+    act_two_wide = jnp.where(inside[None, :, :, None], jax.nn.silu(pre_two_wide), 0.0).astype(jnp.bfloat16)
+    act_frame = frame_cols(act_two_wide)
+    pre_one = pre_wide[:, 1:-1, 1:-1]
+    act_one = act_wide[:, 1:-1, 1:-1]
+    pre_two = pre_two_wide[:, 1:-1, 1:-1]
     scores = forward_taps(act_frame, project_kernel, planes, x_rows) + project_offset
     log_scale = jnp.tanh(scores[:CH])
     centered = lower_half - scores[CH:]

time: 181 us -> 170 us (0.939)
  the two profiles are of different devices: /device:TPU:56 before, /device:TPU:16 now
where the time goes in v3:
time: 170 us; the launch traced here: 169 us
  starting transfers between devices  74.5 us (44%)
  matrix products  36.1 us (21%)
  waiting for transfers between devices  31.1 us (18%)
  local copies, waits for them, and re-layouts  20.7 us (12%)
  other arithmetic  4.6 us (3%)
  between operations  2.27 us (1%)
    ppermute x6, starting transfers between devices, extended(): lax.ppermute(tail, axis, [(i, (i + 1) % count) for i in range(ends)])  22.5 us
    all_to_all x1, starting transfers between devices, replicated_sum(): owned = lax.all_to_all(chunks, scatter_axis, 0, 0, tiled=False).sum(0)  19.2 us
    ppermute x6, starting transfers between devices, extended(): lax.ppermute(head, axis, [((i + 1) % count, i) for i in range(ends)])  14.5 us
    dot_general x54, matrix products, forward_taps(): jnp.einsum('oc,czxy->ozxy', weight[tap_index], sliced, preferred_element_...  14.1 us
    ppermute x3, starting transfers between devices, butterfly_sum(): flat = flat + lax.ppermute(flat, axis, [(i, i ^ bit) for i in range(count)])  11.7 us
    dot_general x54, matrix products, backward_taps(): jnp.einsum('oc,ozxy->czxy', weight[tap_index], sliced, preferred_element_...  10.8 us
    ppermute x3, waiting for transfers between devices, butterfly_sum(): flat = flat + lax.ppermute(flat, axis, [(i, i ^ bit) for i in range(count)])  10.7 us
    dot_general x54, matrix products, weight_taps(): jnp.einsum('ozxy,czxy->oc', grad, sliced, preferred_element_type=jnp.floa...  8.11 us
  transfers between devices with their start and end apart: 17, of which 9 were waited for; matrix products, arithmetic and copies ran while one was open for 12% of the time, Pallas kernels for 0%

profile of v3, /device:TPU:16, one launch (start us, length us, event | category | flops | bytes accessed | tf_op | source)
XLA Modules:
  0.0 169.2 jit_solution(14927358016659484397)
XLA Ops:
  2.2 3.5 %collective-permute-start = (bf16[12,2,4,128]{3,0,2,1:T(8,128)(2,1)S(1)}, bf16[12,2,4,128]{3,0,2,1:T(8,128)(2,1)S(1)}, u32[]{:S(2)}, u32[]{:S(2)}) collective-permute-start(bf16[12,2,4,128]{3,0,2,1:T(8,128)(2,1)S(1)} %pad_maximum_fusion.18), channel_id=1, source_target_pairs={{0,8},{8,16},{16,24},{24,32},{32,40},{40,48},{48,56},{56,64},{64,7... | collective-permute-start | bytes 73736 | tf_op jit(solution)/shard_map/ppermute | solution.py:20
  5.7 1.3 collective-permute-start.1
  7.0 1.4 fusion.512
  8.5 1.2 fusion.513
  10.6 1.1 collective-permute-done.1
  11.8 1.9 %collective-permute-start.2 = (bf16[12,6,2,128]{3,0,2,1:T(8,128)(2,1)S(1)}, bf16[12,6,2,128]{3,0,2,1:T(8,128)(2,1)S(1)}, u32[]{:S(2)}, u32[]{:S(2)}) collective-permute-start(bf16[12,6,2,128]{3,0,2,1:T(8,128)(2,1)S(1)} %get-tuple-element.124), channel_id=1, source_target_pairs={{0,1},{1,2},{2,3},{3,4},{4,5},{5,6},{6,7},{8,9},{9,10},{10,11},{11... | collective-permute-start | bytes 110600 | tf_op jit(solution)/shard_map/ppermute | solution.py:20
  13.7 4.5 %collective-permute-start.3 = (bf16[12,6,2,128]{3,0,2,1:T(8,128)(2,1)S(1)}, bf16[12,6,2,128]{3,0,2,1:T(8,128)(2,1)S(1)}, u32[]{:S(2)}, u32[]{:S(2)}) collective-permute-start(bf16[12,6,2,128]{3,0,2,1:T(8,128)(2,1)S(1)} %get-tuple-element.125), channel_id=1, source_target_pairs={{1,0},{2,1},{3,2},{4,3},{5,4},{6,5},{7,6},{9,8},{10,9},{11,10},{12... | collective-permute-start | bytes 110600 | tf_op jit(solution)/shard_map/ppermute | solution.py:22
  19.0 1.2 collective-permute-done.3
  29.8 1.3 multiply_convert_fusion
  43.0 4.8 %collective-permute-start.4 = (bf16[8,1,4,128]{3,0,2,1:T(8,128)(2,1)}, bf16[8,1,4,128]{3,0,2,1:T(8,128)(2,1)S(1)}, u32[]{:S(2)}, u32[]{:S(2)}) collective-permute-start(bf16[8,1,4,128]{3,0,2,1:T(8,128)(2,1)} %get-tuple-element.137), channel_id=1, source_target_pairs={{0,8},{8,16},{16,24},{24,32},{32,40},{40,48},{48,56},{56,64},{64,7... | collective-permute-start | bytes 24584 | tf_op jit(solution)/shard_map/ppermute | solution.py:20
  47.8 1.5 collective-permute-start.5
  51.5 1.8 %reshape.105 = f32[4,8,256]{2,1,0:T(8,128)} reshape(f32[2,2,4,2,128,2]{5,4,3,2,1,0:T(8,128)S(1)} %bitcast.1138) | data formatting | bytes 65536 | tf_op jit(solution)/shard_map/reshape | solution.py:50
  53.6 4.0 %collective-permute-start.7 = (bf16[8,4,1,128]{3,0,2,1:T(8,128)(2,1)S(1)}, bf16[8,4,1,128]{3,0,2,1:T(8,128)(2,1)S(1)}, u32[]{:S(2)}, u32[]{:S(2)}) collective-permute-start(bf16[8,4,1,128]{3,0,2,1:T(8,128)(2,1)S(1)} %get-tuple-element.134), channel_id=1, source_target_pairs={{1,0},{2,1},{3,2},{4,3},{5,4},{6,5},{7,6},{9,8},{10,9},{11,10},{12... | collective-permute-start | bytes 24584 | tf_op jit(solution)/shard_map/ppermute | solution.py:22
  57.6 4.4 %collective-permute-start.6 = (bf16[8,4,1,128]{3,0,2,1:T(8,128)(2,1)S(1)}, bf16[8,4,1,128]{3,0,2,1:T(8,128)(2,1)S(1)}, u32[]{:S(2)}, u32[]{:S(2)}) collective-permute-start(bf16[8,4,1,128]{3,0,2,1:T(8,128)(2,1)S(1)} %get-tuple-element.133), channel_id=1, source_target_pairs={{0,1},{1,2},{2,3},{3,4},{4,5},{5,6},{6,7},{8,9},{9,10},{10,11},{11... | collective-permute-start | bytes 24584 | tf_op jit(solution)/shard_map/ppermute | solution.py:20
  62.2 1.2 collective-permute-done.6
  69.8 1.3 convert_reduce_fusion.1
  73.4 4.4 %collective-permute-start.8 = (bf16[64,1,4,128]{3,0,2,1:T(8,128)(2,1)S(1)}, bf16[64,1,4,128]{3,0,2,1:T(8,128)(2,1)S(1)}, u32[]{:S(2)}, u32[]{:S(2)}) collective-permute-start(bf16[64,1,4,128]{3,0,2,1:T(8,128)(2,1)S(1)} %get-tuple-element.95), channel_id=1, source_target_pairs={{0,8},{8,16},{16,24},{24,32},{32,40},{40,48},{48,56},{56,64},{64,7... | collective-permute-start | bytes 196616 | tf_op jit(solution)/shard_map/ppermute | solution.py:20
  77.8 1.3 collective-permute-start.9
  81.1 3.9 %collective-permute-done.9 = bf16[64,1,4,128]{3,0,2,1:T(8,128)(2,1)S(1)} collective-permute-done((bf16[64,1,4,128]{3,0,2,1:T(8,128)(2,1)S(1)}, bf16[64,1,4,128]{3,0,2,1:T(8,128)(2,1)S(1)}, u32[]{:S(2)}, u32[]{:S(2)}) %collective-permute-start.9) | collective-permute-done | bytes 65568 | tf_op jit(solution)/shard_map/ppermute | solution.py:22
  85.0 1.9 %collective-permute-start.11 = (bf16[64,4,1,128]{3,0,2,1:T(8,128)(2,1)S(1)}, bf16[64,4,1,128]{3,0,2,1:T(8,128)(2,1)S(1)}, u32[]{:S(2)}, u32[]{:S(2)}) collective-permute-start(bf16[64,4,1,128]{3,0,2,1:T(8,128)(2,1)S(1)} %get-tuple-element.70), channel_id=1, source_target_pairs={{1,0},{2,1},{3,2},{4,3},{5,4},{6,5},{7,6},{9,8},{10,9},{11,10},{12... | collective-permute-start | bytes 196616 | tf_op jit(solution)/shard_map/ppermute | solution.py:22
  86.9 3.5 %collective-permute-start.10 = (bf16[64,4,1,128]{3,0,2,1:T(8,128)(2,1)S(1)}, bf16[64,4,1,128]{3,0,2,1:T(8,128)(2,1)S(1)}, u32[]{:S(2)}, u32[]{:S(2)}) collective-permute-start(bf16[64,4,1,128]{3,0,2,1:T(8,128)(2,1)S(1)} %get-tuple-element.69), channel_id=1, source_target_pairs={{0,1},{1,2},{2,3},{3,4},{4,5},{5,6},{6,7},{8,9},{9,10},{10,11},{11... | collective-permute-start | bytes 196616 | tf_op jit(solution)/shard_map/ppermute | solution.py:20
  90.4 1.1 convolution_bitcast_fusion.34
  93.8 19.2 %all-to-all-start = ((f32[64,1,607]{2,1,0:T(1,128)}), f32[64,1,607]{2,1,0:T(1,128)S(1)}, u32[]{:S(2)}, u32[]{:S(2)}) async-start(f32[64,1,607]{2,1,0:T(1,128)} %all_to_all.10), calls=%async_computation | async-start | bytes 327680 | tf_op jit(solution)/shard_map/all_to_all | solution.py:128
  117.8 5.8 %all-to-all-done = f32[64,1,607]{2,1,0:T(1,128)S(1)} async-done(((f32[64,1,607]{2,1,0:T(1,128)}), f32[64,1,607]{2,1,0:T(1,128)S(1)}, u32[]{:S(2)}, u32[]{:S(2)}) %all-to-all-start) | async-done | bytes 155424 | tf_op jit(solution)/shard_map/all_to_all | solution.py:128
  123.8 6.3 %collective-permute-start.12 = (f32[607]{0:T(1024)S(1)}, f32[607]{0:T(1024)S(1)}, u32[]{:S(2)}, u32[]{:S(2)}) collective-permute-start(f32[607]{0:T(1024)S(1)} %reduce_sum.39), channel_id=1, source_target_pairs={{0,1},{1,0},{2,3},{3,2},{4,5},{5,4},{6,7},{7,6},{8,9},{9,8},{10,11... | collective-permute-start | bytes 7292 | tf_op jit(solution)/shard_map/ppermute | solution.py:119
  130.9 1.9 %collective-permute-start.13 = (f32[607]{0:T(1024)S(1)}, f32[607]{0:T(1024)S(1)}, u32[]{:S(2)}, u32[]{:S(2)}) collective-permute-start(f32[607]{0:T(1024)S(1)} %add.552), channel_id=1, source_target_pairs={{0,2},{1,3},{2,0},{3,1},{4,6},{5,7},{6,4},{7,5},{8,10},{9,11},{10,... | collective-permute-start | bytes 7292 | tf_op jit(solution)/shard_map/ppermute | solution.py:119
  132.9 4.3 %collective-permute-done.13 = f32[607]{0:T(1024)S(1)} collective-permute-done((f32[607]{0:T(1024)S(1)}, f32[607]{0:T(1024)S(1)}, u32[]{:S(2)}, u32[]{:S(2)}) %collective-permute-start.13) | collective-permute-done | bytes 2460 | tf_op jit(solution)/shard_map/ppermute | solution.py:119
  137.3 3.5 %collective-permute-start.14 = (f32[607]{0:T(1024)S(1)}, f32[607]{0:T(1024)S(1)}, u32[]{:S(2)}, u32[]{:S(2)}) collective-permute-start(f32[607]{0:T(1024)S(1)} %add.553), channel_id=1, source_target_pairs={{0,4},{1,5},{2,6},{3,7},{4,0},{5,1},{6,2},{7,3},{8,12},{9,13},{10,... | collective-permute-start | bytes 7292 | tf_op jit(solution)/shard_map/ppermute | solution.py:119
  141.0 5.7 %collective-permute-done.14 = f32[607]{0:T(1024)S(1)} collective-permute-done((f32[607]{0:T(1024)S(1)}, f32[607]{0:T(1024)S(1)}, u32[]{:S(2)}, u32[]{:S(2)}) %collective-permute-start.14) | collective-permute-done | bytes 2460 | tf_op jit(solution)/shard_map/ppermute | solution.py:119
  147.4 6.5 %all-to-all-start.1 = ((f32[64,1,607]{2,1,0:T(1,128)}), f32[64,1,607]{2,1,0:T(1,128)S(1)}, u32[]{:S(2)}, u32[]{:S(2)}) async-start(f32[64,1,607]{2,1,0:T(1,128)} %broadcast_in_dim.23), calls=%async_computation.1 | async-start | bytes 327680 | tf_op jit(solution)/shard_map/all_to_all | solution.py:130
  154.8 1.8 %reshape.107 = f32[4,8,256]{2,1,0:T(8,128)} reshape(f32[2,2,4,2,128,2]{5,4,3,2,1,0:T(8,128)S(1)} %bitcast.1139) | data formatting | bytes 65536 | tf_op jit(solution)/shard_map/reshape | solution.py:50
  157.3 7.1 %all-to-all-done.1 = f32[64,1,607]{2,1,0:T(1,128)S(1)} async-done(((f32[64,1,607]{2,1,0:T(1,128)}), f32[64,1,607]{2,1,0:T(1,128)S(1)}, u32[]{:S(2)}, u32[]{:S(2)}) %all-to-all-start.1) | async-done | bytes 155424 | tf_op jit(solution)/shard_map/all_to_all | solution.py:130
  (375 shorter events, 52.1 us)
Async XLA Ops:
  0.6 30.5 %copy-start = (bf16[64,64]{1,0:T(8,128)(2,1)S(1)}, bf16[64,64]{1,0:T(8,128)(2,1)}, u32[]{:S(2)}) copy-start(bf16[64,64]{1,0:T(8,128)(2,1)} %param.13) | copy-start | bytes 24580
  2.2 8.5 %collective-permute-start = (bf16[12,2,4,128]{3,0,2,1:T(8,128)(2,1)S(1)}, bf16[12,2,4,128]{3,0,2,1:T(8,128)(2,1)S(1)}, u32[]{:S(2)}, u32[]{:S(2)}) collective-permute-start(bf16[12,2,4,128]{3,0,2,1:T(8,128)(2,1)S(1)} %pad_maximum_fusion.18), channel_id=1, source_target_pairs={{0,8},{8,16},{16,24},{24,32},{32,40},{40,48},{48,56},{56,64},{64,7... | collective-permute-start | bytes 73736 | tf_op jit(solution)/shard_map/ppermute | solution.py:20
  5.7 6.1 %collective-permute-start.1 = (bf16[12,2,4,128]{3,0,2,1:T(8,128)(2,1)S(1)}, bf16[12,2,4,128]{3,0,2,1:T(8,128)(2,1)S(1)}, u32[]{:S(2)}, u32[]{:S(2)}) collective-permute-start(bf16[12,2,4,128]{3,0,2,1:T(8,128)(2,1)S(1)} %pad_maximum_fusion.18), channel_id=1, source_target_pairs={{8,0},{16,8},{24,16},{32,24},{40,32},{48,40},{56,48},{64,56},{72,6... | collective-permute-start | bytes 73736 | tf_op jit(solution)/shard_map/ppermute | solution.py:22
  8.5 18.5 %copy-start.64 = (bf16[1,64,12]{1,0,2:T(2,128)(2,1)}, bf16[1,64,12]{1,0,2:T(2,128)(2,1)S(1)}, u32[]{:S(2)}) copy-start(bf16[1,64,12]{1,0,2:T(2,128)(2,1)S(1)} %get-tuple-element.106) | copy-start | bytes 4612
  8.5 20.2 %copy-start.22 = (bf16[1,64,12]{1,0,2:T(2,128)(2,1)}, bf16[1,64,12]{1,0,2:T(2,128)(2,1)S(1)}, u32[]{:S(2)}) copy-start(bf16[1,64,12]{1,0,2:T(2,128)(2,1)S(1)} %get-tuple-element.104) | copy-start | bytes 4612
  8.5 20.5 %copy-start.62 = (bf16[1,64,12]{1,0,2:T(2,128)(2,1)}, bf16[1,64,12]{1,0,2:T(2,128)(2,1)S(1)}, u32[]{:S(2)}) copy-start(bf16[1,64,12]{1,0,2:T(2,128)(2,1)S(1)} %get-tuple-element.103) | copy-start | bytes 4612
  8.5 21.2 %copy-start.71 = (bf16[1,64,12]{1,0,2:T(2,128)(2,1)}, bf16[1,64,12]{1,0,2:T(2,128)(2,1)S(1)}, u32[]{:S(2)}) copy-start(bf16[1,64,12]{1,0,2:T(2,128)(2,1)S(1)} %get-tuple-element.97) | copy-start | bytes 4612
  11.8 7.3 %collective-permute-start.2 = (bf16[12,6,2,128]{3,0,2,1:T(8,128)(2,1)S(1)}, bf16[12,6,2,128]{3,0,2,1:T(8,128)(2,1)S(1)}, u32[]{:S(2)}, u32[]{:S(2)}) collective-permute-start(bf16[12,6,2,128]{3,0,2,1:T(8,128)(2,1)S(1)} %get-tuple-element.124), channel_id=1, source_target_pairs={{0,1},{1,2},{2,3},{3,4},{4,5},{5,6},{6,7},{8,9},{9,10},{10,11},{11... | collective-permute-start | bytes 110600 | tf_op jit(solution)/shard_map/ppermute | solution.py:20
  13.7 6.5 %collective-permute-start.3 = (bf16[12,6,2,128]{3,0,2,1:T(8,128)(2,1)S(1)}, bf16[12,6,2,128]{3,0,2,1:T(8,128)(2,1)S(1)}, u32[]{:S(2)}, u32[]{:S(2)}) collective-permute-start(bf16[12,6,2,128]{3,0,2,1:T(8,128)(2,1)S(1)} %get-tuple-element.125), channel_id=1, source_target_pairs={{1,0},{2,1},{3,2},{4,3},{5,4},{6,5},{7,6},{9,8},{10,9},{11,10},{12... | collective-permute-start | bytes 110600 | tf_op jit(solution)/shard_map/ppermute | solution.py:22
  43.0 10.5 %collective-permute-start.4 = (bf16[8,1,4,128]{3,0,2,1:T(8,128)(2,1)}, bf16[8,1,4,128]{3,0,2,1:T(8,128)(2,1)S(1)}, u32[]{:S(2)}, u32[]{:S(2)}) collective-permute-start(bf16[8,1,4,128]{3,0,2,1:T(8,128)(2,1)} %get-tuple-element.137), channel_id=1, source_target_pairs={{0,8},{8,16},{16,24},{24,32},{32,40},{40,48},{48,56},{56,64},{64,7... | collective-permute-start | bytes 24584 | tf_op jit(solution)/shard_map/ppermute | solution.py:20
  47.8 5.8 %collective-permute-start.5 = (bf16[8,1,4,128]{3,0,2,1:T(8,128)(2,1)}, bf16[8,1,4,128]{3,0,2,1:T(8,128)(2,1)S(1)}, u32[]{:S(2)}, u32[]{:S(2)}) collective-permute-start(bf16[8,1,4,128]{3,0,2,1:T(8,128)(2,1)} %get-tuple-element.138), channel_id=1, source_target_pairs={{8,0},{16,8},{24,16},{32,24},{40,32},{48,40},{56,48},{64,56},{72,6... | collective-permute-start | bytes 24584 | tf_op jit(solution)/shard_map/ppermute | solution.py:22
  53.6 8.7 %collective-permute-start.7 = (bf16[8,4,1,128]{3,0,2,1:T(8,128)(2,1)S(1)}, bf16[8,4,1,128]{3,0,2,1:T(8,128)(2,1)S(1)}, u32[]{:S(2)}, u32[]{:S(2)}) collective-permute-start(bf16[8,4,1,128]{3,0,2,1:T(8,128)(2,1)S(1)} %get-tuple-element.134), channel_id=1, source_target_pairs={{1,0},{2,1},{3,2},{4,3},{5,4},{6,5},{7,6},{9,8},{10,9},{11,10},{12... | collective-permute-start | bytes 24584 | tf_op jit(solution)/shard_map/ppermute | solution.py:22
  57.6 5.9 %collective-permute-start.6 = (bf16[8,4,1,128]{3,0,2,1:T(8,128)(2,1)S(1)}, bf16[8,4,1,128]{3,0,2,1:T(8,128)(2,1)S(1)}, u32[]{:S(2)}, u32[]{:S(2)}) collective-permute-start(bf16[8,4,1,128]{3,0,2,1:T(8,128)(2,1)S(1)} %get-tuple-element.133), channel_id=1, source_target_pairs={{0,1},{1,2},{2,3},{3,4},{4,5},{5,6},{6,7},{8,9},{9,10},{10,11},{11... | collective-permute-start | bytes 24584 | tf_op jit(solution)/shard_map/ppermute | solution.py:20
  73.4 7.7 %collective-permute-start.8 = (bf16[64,1,4,128]{3,0,2,1:T(8,128)(2,1)S(1)}, bf16[64,1,4,128]{3,0,2,1:T(8,128)(2,1)S(1)}, u32[]{:S(2)}, u32[]{:S(2)}) collective-permute-start(bf16[64,1,4,128]{3,0,2,1:T(8,128)(2,1)S(1)} %get-tuple-element.95), channel_id=1, source_target_pairs={{0,8},{8,16},{16,24},{24,32},{32,40},{40,48},{48,56},{56,64},{64,7... | collective-permute-start | bytes 196616 | tf_op jit(solution)/shard_map/ppermute | solution.py:20
  77.8 7.2 %collective-permute-start.9 = (bf16[64,1,4,128]{3,0,2,1:T(8,128)(2,1)S(1)}, bf16[64,1,4,128]{3,0,2,1:T(8,128)(2,1)S(1)}, u32[]{:S(2)}, u32[]{:S(2)}) collective-permute-start(bf16[64,1,4,128]{3,0,2,1:T(8,128)(2,1)S(1)} %get-tuple-element.96), channel_id=1, source_target_pairs={{8,0},{16,8},{24,16},{32,24},{40,32},{48,40},{56,48},{64,56},{72,6... | collective-permute-start | bytes 196616 | tf_op jit(solution)/shard_map/ppermute | solution.py:22
  85.0 28.1 %collective-permute-start.11 = (bf16[64,4,1,128]{3,0,2,1:T(8,128)(2,1)S(1)}, bf16[64,4,1,128]{3,0,2,1:T(8,128)(2,1)S(1)}, u32[]{:S(2)}, u32[]{:S(2)}) collective-permute-start(bf16[64,4,1,128]{3,0,2,1:T(8,128)(2,1)S(1)} %get-tuple-element.70), channel_id=1, source_target_pairs={{1,0},{2,1},{3,2},{4,3},{5,4},{6,5},{7,6},{9,8},{10,9},{11,10},{12... | collective-permute-start | bytes 196616 | tf_op jit(solution)/shard_map/ppermute | solution.py:22
  86.9 26.1 %collective-permute-start.10 = (bf16[64,4,1,128]{3,0,2,1:T(8,128)(2,1)S(1)}, bf16[64,4,1,128]{3,0,2,1:T(8,128)(2,1)S(1)}, u32[]{:S(2)}, u32[]{:S(2)}) collective-permute-start(bf16[64,4,1,128]{3,0,2,1:T(8,128)(2,1)S(1)} %get-tuple-element.69), channel_id=1, source_target_pairs={{0,1},{1,2},{2,3},{3,4},{4,5},{5,6},{6,7},{8,9},{9,10},{10,11},{11... | collective-permute-start | bytes 196616 | tf_op jit(solution)/shard_map/ppermute | solution.py:20
  91.9 21.6 %copy-start.11 = (bf16[1,64,12]{1,0,2:T(2,128)(2,1)S(1)}, bf16[1,64,12]{1,0,2:T(2,128)(2,1)}, u32[]{:S(2)}) copy-start(bf16[1,64,12]{1,0,2:T(2,128)(2,1)} %copy-done.10) | copy-start | bytes 4612
  91.9 21.8 %copy-start.9 = (bf16[1,64,12]{1,0,2:T(2,128)(2,1)S(1)}, bf16[1,64,12]{1,0,2:T(2,128)(2,1)}, u32[]{:S(2)}) copy-start(bf16[1,64,12]{1,0,2:T(2,128)(2,1)} %copy-done.8) | copy-start | bytes 4612
  92.7 21.2 %copy-start.31 = (bf16[1,64,12]{1,0,2:T(2,128)(2,1)S(1)}, bf16[1,64,12]{1,0,2:T(2,128)(2,1)}, u32[]{:S(2)}) copy-start(bf16[1,64,12]{1,0,2:T(2,128)(2,1)} %copy-done.30) | copy-start | bytes 4612
  92.7 21.4 %copy-start.29 = (bf16[1,64,12]{1,0,2:T(2,128)(2,1)S(1)}, bf16[1,64,12]{1,0,2:T(2,128)(2,1)}, u32[]{:S(2)}) copy-start(bf16[1,64,12]{1,0,2:T(2,128)(2,1)} %copy-done.28) | copy-start | bytes 4612
  92.7 21.6 %copy-start.27 = (bf16[1,64,12]{1,0,2:T(2,128)(2,1)S(1)}, bf16[1,64,12]{1,0,2:T(2,128)(2,1)}, u32[]{:S(2)}) copy-start(bf16[1,64,12]{1,0,2:T(2,128)(2,1)} %copy-done.26) | copy-start | bytes 4612
  92.8 21.7 %copy-start.25 = (bf16[1,64,12]{1,0,2:T(2,128)(2,1)S(1)}, bf16[1,64,12]{1,0,2:T(2,128)(2,1)}, u32[]{:S(2)}) copy-start(bf16[1,64,12]{1,0,2:T(2,128)(2,1)} %copy-done.24) | copy-start | bytes 4612
  92.8 21.8 %copy-start.23 = (bf16[1,64,12]{1,0,2:T(2,128)(2,1)S(1)}, bf16[1,64,12]{1,0,2:T(2,128)(2,1)}, u32[]{:S(2)}) copy-start(bf16[1,64,12]{1,0,2:T(2,128)(2,1)} %copy-done.22) | copy-start | bytes 4612
  92.8 22.0 %copy-start.21 = (bf16[1,64,12]{1,0,2:T(2,128)(2,1)S(1)}, bf16[1,64,12]{1,0,2:T(2,128)(2,1)}, u32[]{:S(2)}) copy-start(bf16[1,64,12]{1,0,2:T(2,128)(2,1)} %copy-done.20) | copy-start | bytes 4612
  93.8 21.2 %copy-start.19 = (bf16[1,64,12]{1,0,2:T(2,128)(2,1)S(1)}, bf16[1,64,12]{1,0,2:T(2,128)(2,1)}, u32[]{:S(2)}) copy-start(bf16[1,64,12]{1,0,2:T(2,128)(2,1)} %copy-done.18) | copy-start | bytes 4612
  93.8 29.8 %all-to-all-start = ((f32[64,1,607]{2,1,0:T(1,128)}), f32[64,1,607]{2,1,0:T(1,128)S(1)}, u32[]{:S(2)}, u32[]{:S(2)}) async-start(f32[64,1,607]{2,1,0:T(1,128)} %all_to_all.10), calls=%async_computation | async-start | bytes 327680 | tf_op jit(solution)/shard_map/all_to_all | solution.py:128
  117.0 23.8 %copy-start.72 = (bf16[1,64,12]{1,0,2:T(2,128)(2,1)S(1)}, bf16[1,64,12]{1,0,2:T(2,128)(2,1)}, u32[]{:S(2)}) copy-start(bf16[1,64,12]{1,0,2:T(2,128)(2,1)} %copy-done.71) | copy-start | bytes 4612
  123.8 7.1 %collective-permute-start.12 = (f32[607]{0:T(1024)S(1)}, f32[607]{0:T(1024)S(1)}, u32[]{:S(2)}, u32[]{:S(2)}) collective-permute-start(f32[607]{0:T(1024)S(1)} %reduce_sum.39), channel_id=1, source_target_pairs={{0,1},{1,0},{2,3},{3,2},{4,5},{5,4},{6,7},{7,6},{8,9},{9,8},{10,11... | collective-permute-start | bytes 7292 | tf_op jit(solution)/shard_map/ppermute | solution.py:119
  130.9 6.4 %collective-permute-start.13 = (f32[607]{0:T(1024)S(1)}, f32[607]{0:T(1024)S(1)}, u32[]{:S(2)}, u32[]{:S(2)}) collective-permute-start(f32[607]{0:T(1024)S(1)} %add.552), channel_id=1, source_target_pairs={{0,2},{1,3},{2,0},{3,1},{4,6},{5,7},{6,4},{7,5},{8,10},{9,11},{10,... | collective-permute-start | bytes 7292 | tf_op jit(solution)/shard_map/ppermute | solution.py:119
  137.3 9.4 %collective-permute-start.14 = (f32[607]{0:T(1024)S(1)}, f32[607]{0:T(1024)S(1)}, u32[]{:S(2)}, u32[]{:S(2)}) collective-permute-start(f32[607]{0:T(1024)S(1)} %add.553), channel_id=1, source_target_pairs={{0,4},{1,5},{2,6},{3,7},{4,0},{5,1},{6,2},{7,3},{8,12},{9,13},{10,... | collective-permute-start | bytes 7292 | tf_op jit(solution)/shard_map/ppermute | solution.py:119
  147.4 16.9 %all-to-all-start.1 = ((f32[64,1,607]{2,1,0:T(1,128)}), f32[64,1,607]{2,1,0:T(1,128)S(1)}, u32[]{:S(2)}, u32[]{:S(2)}) async-start(f32[64,1,607]{2,1,0:T(1,128)} %broadcast_in_dim.23), calls=%async_computation.1 | async-start | bytes 327680 | tf_op jit(solution)/shard_map/all_to_all | solution.py:130
  (59 other events, 451.3 us)

commit v4 on v3

--- a/solution.py
+++ b/solution.py
@@ -174,8 +174,6 @@
         "oc,ozxy->czxy", mixing_matrix, mix_grad, preferred_element_type=jnp.float32
     )
     first_grad = (back_one * silu_slope(pre_one)).astype(jnp.bfloat16)
-    first_frame = frame_cols(extended(first_grad, (("gz", 1), ("gx", 2)), 1))
-    input_grad = backward_taps(first_frame, expand_kernel, planes, x_rows)
     inner_first, inner_mix, inner_act = (first_grad, mix_grad, act_one)
     expand_term = weight_taps(inner_first, framed)
     mixing_term = jnp.einsum(
@@ -186,7 +184,17 @@
         [channel_sums(inner_first), channel_sums(inner_mix), channel_sums(score_grad)]
     )
     terms = (expand_term, mixing_term, project_term, offset_term)
-    flat = replicated_sum(jnp.concatenate([t.reshape(-1) for t in terms]), "gz", ("gx",))
+    flat = jnp.concatenate([t.reshape(-1) for t in terms])
+    total = flat.shape[0]
+    count = lax.axis_size("gz")
+    chunks = jnp.pad(flat, (0, (-total) % count)).reshape(count, -1)
+    owned = lax.all_to_all(chunks, "gz", 0, 0, tiled=False).sum(0)
+    owned, first_grad = lax.optimization_barrier((owned, first_grad))
+    owned = butterfly_sum(owned, ("gx",))
+    first_frame = frame_cols(extended(first_grad, (("gz", 1), ("gx", 2)), 1))
+    input_grad = backward_taps(first_frame, expand_kernel, planes, x_rows)
+    spread = lax.all_to_all(jnp.broadcast_to(owned, (count,) + owned.shape), "gz", 0, 0, tiled=False)
+    flat = spread.reshape(-1)[:total]
     pieces, start = [], 0
     for t in terms:
         pieces.append(flat[start : start + t.size].reshape(t.shape))

time: 170 us -> 156 us (0.918)
  the two profiles are of different devices: /device:TPU:16 before, /device:TPU:56 now
where the time goes in v4:
time: 156 us; the launch traced here: 154 us
  starting transfers between devices  55.6 us (36%)
  matrix products  34.2 us (22%)
  blocking collectives  26.1 us (17%)
  local copies, waits for them, and re-layouts  19 us (12%)
  waiting for transfers between devices  14.8 us (9%)
  other arithmetic  2.64 us (2%)
  between operations  1.62 us (1%)
    all_to_all x1, blocking collectives, per_device(): owned = lax.all_to_all(chunks, 'gz', 0, 0, tiled=False).sum(0)  26.1 us
    ppermute x6, starting transfers between devices, extended(): lax.ppermute(tail, axis, [(i, (i + 1) % count) for i in range(ends)])  17.6 us
    ppermute x6, starting transfers between devices, extended(): lax.ppermute(head, axis, [((i + 1) % count, i) for i in range(ends)])  17.1 us
    dot_general x54, matrix products, forward_taps(): jnp.einsum('oc,czxy->ozxy', weight[tap_index], sliced, preferred_element_...  13.1 us
    ppermute x3, starting transfers between devices, butterfly_sum(): flat = flat + lax.ppermute(flat, axis, [(i, i ^ bit) for i in range(count)])  11.5 us
    dot_general x54, matrix products, backward_taps(): jnp.einsum('oc,ozxy->czxy', weight[tap_index], sliced, preferred_element_...  10.8 us
    all_to_all x1, starting transfers between devices, per_device(): lax.all_to_all(jnp.broadcast_to(owned, (count,) + owned.shape), 'gz', 0,...  9.36 us
    dot_general x54, matrix products, weight_taps(): jnp.einsum('ozxy,czxy->oc', grad, sliced, preferred_element_type=jnp.floa...  8.16 us
  transfers between devices with their start and end apart: 16, of which 7 were waited for; matrix products, arithmetic and copies ran while one was open for 11% of the time, Pallas kernels for 0%

profile of v4, /device:TPU:56, one launch (start us, length us, event | category | flops | bytes accessed | tf_op | source)
XLA Modules:
  0.0 154.0 jit_solution(16940093560066601332)
XLA Ops:
  2.2 5.1 %collective-permute-start = (bf16[12,2,4,128]{3,0,2,1:T(8,128)(2,1)S(1)}, bf16[12,2,4,128]{3,0,2,1:T(8,128)(2,1)S(1)}, u32[]{:S(2)}, u32[]{:S(2)}) collective-permute-start(bf16[12,2,4,128]{3,0,2,1:T(8,128)(2,1)S(1)} %pad_maximum_fusion.22), channel_id=1, source_target_pairs={{0,8},{8,16},{16,24},{24,32},{32,40},{40,48},{48,56},{56,64},{64,7... | collective-permute-start | bytes 73736 | tf_op jit(solution)/shard_map/ppermute | solution.py:20
  7.3 1.9 %collective-permute-start.1 = (bf16[12,2,4,128]{3,0,2,1:T(8,128)(2,1)S(1)}, bf16[12,2,4,128]{3,0,2,1:T(8,128)(2,1)S(1)}, u32[]{:S(2)}, u32[]{:S(2)}) collective-permute-start(bf16[12,2,4,128]{3,0,2,1:T(8,128)(2,1)S(1)} %pad_maximum_fusion.22), channel_id=1, source_target_pairs={{8,0},{16,8},{24,16},{32,24},{40,32},{48,40},{56,48},{64,56},{72,6... | collective-permute-start | bytes 73736 | tf_op jit(solution)/shard_map/ppermute | solution.py:22
  9.2 1.4 fusion.519
  10.6 1.2 fusion.520
  12.6 1.4 collective-permute-done.1
  14.0 1.9 %collective-permute-start.2 = (bf16[12,6,2,128]{3,0,2,1:T(8,128)(2,1)S(1)}, bf16[12,6,2,128]{3,0,2,1:T(8,128)(2,1)S(1)}, u32[]{:S(2)}, u32[]{:S(2)}) collective-permute-start(bf16[12,6,2,128]{3,0,2,1:T(8,128)(2,1)S(1)} %get-tuple-element.128), channel_id=1, source_target_pairs={{0,1},{1,2},{2,3},{3,4},{4,5},{5,6},{6,7},{8,9},{9,10},{10,11},{11... | collective-permute-start | bytes 110600 | tf_op jit(solution)/shard_map/ppermute | solution.py:20
  15.9 4.5 %collective-permute-start.3 = (bf16[12,6,2,128]{3,0,2,1:T(8,128)(2,1)S(1)}, bf16[12,6,2,128]{3,0,2,1:T(8,128)(2,1)S(1)}, u32[]{:S(2)}, u32[]{:S(2)}) collective-permute-start(bf16[12,6,2,128]{3,0,2,1:T(8,128)(2,1)S(1)} %get-tuple-element.129), channel_id=1, source_target_pairs={{1,0},{2,1},{3,2},{4,3},{5,4},{6,5},{7,6},{9,8},{10,9},{11,10},{12... | collective-permute-start | bytes 110600 | tf_op jit(solution)/shard_map/ppermute | solution.py:22
  21.3 1.0 collective-permute-done.3
  29.4 1.0 fusion.28
  42.4 3.5 %collective-permute-start.4 = (bf16[8,1,4,128]{3,0,2,1:T(8,128)(2,1)S(1)}, bf16[8,1,4,128]{3,0,2,1:T(8,128)(2,1)S(1)}, u32[]{:S(2)}, u32[]{:S(2)}) collective-permute-start(bf16[8,1,4,128]{3,0,2,1:T(8,128)(2,1)S(1)} %get-tuple-element.141), channel_id=1, source_target_pairs={{0,8},{8,16},{16,24},{24,32},{32,40},{40,48},{48,56},{56,64},{64,7... | collective-permute-start | bytes 24584 | tf_op jit(solution)/shard_map/ppermute | solution.py:20
  45.9 2.4 %collective-permute-start.5 = (bf16[8,1,4,128]{3,0,2,1:T(8,128)(2,1)S(1)}, bf16[8,1,4,128]{3,0,2,1:T(8,128)(2,1)S(1)}, u32[]{:S(2)}, u32[]{:S(2)}) collective-permute-start(bf16[8,1,4,128]{3,0,2,1:T(8,128)(2,1)S(1)} %get-tuple-element.142), channel_id=1, source_target_pairs={{8,0},{16,8},{24,16},{32,24},{40,32},{48,40},{56,48},{64,56},{72,6... | collective-permute-start | bytes 24584 | tf_op jit(solution)/shard_map/ppermute | solution.py:22
  48.5 3.8 %collective-permute-done.5 = bf16[8,1,4,128]{3,0,2,1:T(8,128)(2,1)S(1)} collective-permute-done((bf16[8,1,4,128]{3,0,2,1:T(8,128)(2,1)S(1)}, bf16[8,1,4,128]{3,0,2,1:T(8,128)(2,1)S(1)}, u32[]{:S(2)}, u32[]{:S(2)}) %collective-permute-start.5) | collective-permute-done | bytes 8224 | tf_op jit(solution)/shard_map/ppermute | solution.py:22
  52.3 3.1 %collective-permute-start.7 = (bf16[8,4,1,128]{3,0,2,1:T(8,128)(2,1)S(1)}, bf16[8,4,1,128]{3,0,2,1:T(8,128)(2,1)S(1)}, u32[]{:S(2)}, u32[]{:S(2)}) collective-permute-start(bf16[8,4,1,128]{3,0,2,1:T(8,128)(2,1)S(1)} %get-tuple-element.138), channel_id=1, source_target_pairs={{1,0},{2,1},{3,2},{4,3},{5,4},{6,5},{7,6},{9,8},{10,9},{11,10},{12... | collective-permute-start | bytes 24584 | tf_op jit(solution)/shard_map/ppermute | solution.py:22
  55.5 2.1 %collective-permute-start.6 = (bf16[8,4,1,128]{3,0,2,1:T(8,128)(2,1)S(1)}, bf16[8,4,1,128]{3,0,2,1:T(8,128)(2,1)S(1)}, u32[]{:S(2)}, u32[]{:S(2)}) collective-permute-start(bf16[8,4,1,128]{3,0,2,1:T(8,128)(2,1)S(1)} %get-tuple-element.137), channel_id=1, source_target_pairs={{0,1},{1,2},{2,3},{3,4},{4,5},{5,6},{6,7},{8,9},{9,10},{10,11},{11... | collective-permute-start | bytes 24584 | tf_op jit(solution)/shard_map/ppermute | solution.py:20
  57.8 3.5 %collective-permute-done.6 = bf16[8,4,1,128]{3,0,2,1:T(8,128)(2,1)S(1)} collective-permute-done((bf16[8,4,1,128]{3,0,2,1:T(8,128)(2,1)S(1)}, bf16[8,4,1,128]{3,0,2,1:T(8,128)(2,1)S(1)}, u32[]{:S(2)}, u32[]{:S(2)}) %collective-permute-start.6) | collective-permute-done | bytes 8224 | tf_op jit(solution)/shard_map/ppermute | solution.py:20
  67.6 1.1 convolution_bitcast_fusion.34
  74.7 26.1 %all_to_all.15 = f32[64,1,607]{2,1,0:T(1,128)S(1)} all-to-all(f32[64,1,607]{2,1,0:T(1,128)S(1)} %all_to_all.10), channel_id=1, replica_groups=mesh['gz'=64,'gx'=8] {'gz'}, dimensions={0} | all-to-all | bytes 310784 | tf_op jit(solution)/shard_map/all_to_all | solution.py:191
  101.0 2.6 %collective-permute-start.8 = (bf16[64,1,4,128]{3,0,2,1:T(8,128)(2,1)S(1)}, bf16[64,1,4,128]{3,0,2,1:T(8,128)(2,1)S(1)}, u32[]{:S(2)}, u32[]{:S(2)}) collective-permute-start(bf16[64,1,4,128]{3,0,2,1:T(8,128)(2,1)S(1)} %get-tuple-element.100), channel_id=1, source_target_pairs={{0,8},{8,16},{16,24},{24,32},{32,40},{40,48},{48,56},{56,64},{64,7... | collective-permute-start | bytes 196616 | tf_op jit(solution)/shard_map/ppermute | solution.py:20
  103.6 1.9 %collective-permute-start.12 = (f32[607]{0:T(1024)S(1)}, f32[607]{0:T(1024)S(1)}, u32[]{:S(2)}, u32[]{:S(2)}) collective-permute-start(f32[607]{0:T(1024)S(1)} %reduce_sum.39), channel_id=1, source_target_pairs={{0,1},{1,0},{2,3},{3,2},{4,5},{5,4},{6,7},{7,6},{8,9},{9,8},{10,11... | collective-permute-start | bytes 7292 | tf_op jit(solution)/shard_map/ppermute | solution.py:119
  105.6 1.1 collective-permute-done.12
  106.7 7.7 %collective-permute-start.13 = (f32[607]{0:T(1024)S(1)}, f32[607]{0:T(1024)S(1)}, u32[]{:S(2)}, u32[]{:S(2)}) collective-permute-start(f32[607]{0:T(1024)S(1)} %add.552), channel_id=1, source_target_pairs={{0,2},{1,3},{2,0},{3,1},{4,6},{5,7},{6,4},{7,5},{8,10},{9,11},{10,... | collective-permute-start | bytes 7292 | tf_op jit(solution)/shard_map/ppermute | solution.py:119
  114.4 3.2 %collective-permute-start.9 = (bf16[64,1,4,128]{3,0,2,1:T(8,128)(2,1)S(1)}, bf16[64,1,4,128]{3,0,2,1:T(8,128)(2,1)S(1)}, u32[]{:S(2)}, u32[]{:S(2)}) collective-permute-start(bf16[64,1,4,128]{3,0,2,1:T(8,128)(2,1)S(1)} %get-tuple-element.99), channel_id=1, source_target_pairs={{8,0},{16,8},{24,16},{32,24},{40,32},{48,40},{56,48},{64,56},{72,6... | collective-permute-start | bytes 196616 | tf_op jit(solution)/shard_map/ppermute | solution.py:22
  117.6 1.9 %collective-permute-start.14 = (f32[607]{0:T(1024)S(1)}, f32[607]{0:T(1024)S(1)}, u32[]{:S(2)}, u32[]{:S(2)}) collective-permute-start(f32[607]{0:T(1024)S(1)} %add.553), channel_id=1, source_target_pairs={{0,4},{1,5},{2,6},{3,7},{4,0},{5,1},{6,2},{7,3},{8,12},{9,13},{10,... | collective-permute-start | bytes 7292 | tf_op jit(solution)/shard_map/ppermute | solution.py:119
  119.6 1.8 %collective-permute-done.9 = bf16[64,1,4,128]{3,0,2,1:T(8,128)(2,1)S(1)} collective-permute-done((bf16[64,1,4,128]{3,0,2,1:T(8,128)(2,1)S(1)}, bf16[64,1,4,128]{3,0,2,1:T(8,128)(2,1)S(1)}, u32[]{:S(2)}, u32[]{:S(2)}) %collective-permute-start.9) | collective-permute-done | bytes 65568 | tf_op jit(solution)/shard_map/ppermute | solution.py:22
  121.5 1.9 %collective-permute-start.11 = (bf16[64,4,1,128]{3,0,2,1:T(8,128)(2,1)S(1)}, bf16[64,4,1,128]{3,0,2,1:T(8,128)(2,1)S(1)}, u32[]{:S(2)}, u32[]{:S(2)}) collective-permute-start(bf16[64,4,1,128]{3,0,2,1:T(8,128)(2,1)S(1)} %get-tuple-element.74), channel_id=1, source_target_pairs={{1,0},{2,1},{3,2},{4,3},{5,4},{6,5},{7,6},{9,8},{10,9},{11,10},{12... | collective-permute-start | bytes 196616 | tf_op jit(solution)/shard_map/ppermute | solution.py:22
  123.4 2.4 %collective-permute-start.10 = (bf16[64,4,1,128]{3,0,2,1:T(8,128)(2,1)S(1)}, bf16[64,4,1,128]{3,0,2,1:T(8,128)(2,1)S(1)}, u32[]{:S(2)}, u32[]{:S(2)}) collective-permute-start(bf16[64,4,1,128]{3,0,2,1:T(8,128)(2,1)S(1)} %get-tuple-element.73), channel_id=1, source_target_pairs={{0,1},{1,2},{2,3},{3,4},{4,5},{5,6},{6,7},{8,9},{9,10},{10,11},{11... | collective-permute-start | bytes 196616 | tf_op jit(solution)/shard_map/ppermute | solution.py:20
  126.7 1.8 %reshape.105 = f32[4,8,256]{2,1,0:T(8,128)} reshape(f32[2,2,4,2,128,2]{5,4,3,2,1,0:T(8,128)S(1)} %bitcast.1138) | data formatting | bytes 65536 | tf_op jit(solution)/shard_map/reshape | solution.py:50
  129.3 9.4 %all-to-all-start.1 = ((f32[64,1,607]{2,1,0:T(1,128)}), f32[64,1,607]{2,1,0:T(1,128)S(1)}, u32[]{:S(2)}, u32[]{:S(2)}) async-start(f32[64,1,607]{2,1,0:T(1,128)} %broadcast_in_dim.23), calls=%async_computation.1 | async-start | bytes 327680 | tf_op jit(solution)/shard_map/all_to_all | solution.py:196
  144.4 1.8 %reshape.110 = f32[4,8,256]{2,1,0:T(8,128)} reshape(f32[2,2,4,2,128,2]{5,4,3,2,1,0:T(8,128)S(1)} %bitcast.1139) | data formatting | bytes 65536 | tf_op jit(solution)/shard_map/reshape | solution.py:50
  146.9 2.2 %all-to-all-done.1 = f32[64,1,607]{2,1,0:T(1,128)S(1)} async-done(((f32[64,1,607]{2,1,0:T(1,128)}), f32[64,1,607]{2,1,0:T(1,128)S(1)}, u32[]{:S(2)}, u32[]{:S(2)}) %all-to-all-start.1) | async-done | bytes 155424 | tf_op jit(solution)/shard_map/all_to_all | solution.py:196
  150.6 1.0 mul.93
  151.5 1.1 copy.754
  (237 shorter events, 45.5 us)
Async XLA Ops:
  0.6 31.3 %copy-start = (bf16[64,64]{1,0:T(8,128)(2,1)S(1)}, bf16[64,64]{1,0:T(8,128)(2,1)}, u32[]{:S(2)}) copy-start(bf16[64,64]{1,0:T(8,128)(2,1)} %param.13) | copy-start | bytes 24580
  2.2 10.4 %collective-permute-start = (bf16[12,2,4,128]{3,0,2,1:T(8,128)(2,1)S(1)}, bf16[12,2,4,128]{3,0,2,1:T(8,128)(2,1)S(1)}, u32[]{:S(2)}, u32[]{:S(2)}) collective-permute-start(bf16[12,2,4,128]{3,0,2,1:T(8,128)(2,1)S(1)} %pad_maximum_fusion.22), channel_id=1, source_target_pairs={{0,8},{8,16},{16,24},{24,32},{32,40},{40,48},{48,56},{56,64},{64,7... | collective-permute-start | bytes 73736 | tf_op jit(solution)/shard_map/ppermute | solution.py:20
  7.3 6.7 %collective-permute-start.1 = (bf16[12,2,4,128]{3,0,2,1:T(8,128)(2,1)S(1)}, bf16[12,2,4,128]{3,0,2,1:T(8,128)(2,1)S(1)}, u32[]{:S(2)}, u32[]{:S(2)}) collective-permute-start(bf16[12,2,4,128]{3,0,2,1:T(8,128)(2,1)S(1)} %pad_maximum_fusion.22), channel_id=1, source_target_pairs={{8,0},{16,8},{24,16},{32,24},{40,32},{48,40},{56,48},{64,56},{72,6... | collective-permute-start | bytes 73736 | tf_op jit(solution)/shard_map/ppermute | solution.py:22
  14.0 7.2 %collective-permute-start.2 = (bf16[12,6,2,128]{3,0,2,1:T(8,128)(2,1)S(1)}, bf16[12,6,2,128]{3,0,2,1:T(8,128)(2,1)S(1)}, u32[]{:S(2)}, u32[]{:S(2)}) collective-permute-start(bf16[12,6,2,128]{3,0,2,1:T(8,128)(2,1)S(1)} %get-tuple-element.128), channel_id=1, source_target_pairs={{0,1},{1,2},{2,3},{3,4},{4,5},{5,6},{6,7},{8,9},{9,10},{10,11},{11... | collective-permute-start | bytes 110600 | tf_op jit(solution)/shard_map/ppermute | solution.py:20
  15.9 6.3 %collective-permute-start.3 = (bf16[12,6,2,128]{3,0,2,1:T(8,128)(2,1)S(1)}, bf16[12,6,2,128]{3,0,2,1:T(8,128)(2,1)S(1)}, u32[]{:S(2)}, u32[]{:S(2)}) collective-permute-start(bf16[12,6,2,128]{3,0,2,1:T(8,128)(2,1)S(1)} %get-tuple-element.129), channel_id=1, source_target_pairs={{1,0},{2,1},{3,2},{4,3},{5,4},{6,5},{7,6},{9,8},{10,9},{11,10},{12... | collective-permute-start | bytes 110600 | tf_op jit(solution)/shard_map/ppermute | solution.py:22
  31.9 0.7 copy-start.3
  33.3 0.8 copy-start.1
  42.4 6.1 %collective-permute-start.4 = (bf16[8,1,4,128]{3,0,2,1:T(8,128)(2,1)S(1)}, bf16[8,1,4,128]{3,0,2,1:T(8,128)(2,1)S(1)}, u32[]{:S(2)}, u32[]{:S(2)}) collective-permute-start(bf16[8,1,4,128]{3,0,2,1:T(8,128)(2,1)S(1)} %get-tuple-element.141), channel_id=1, source_target_pairs={{0,8},{8,16},{16,24},{24,32},{32,40},{40,48},{48,56},{56,64},{64,7... | collective-permute-start | bytes 24584 | tf_op jit(solution)/shard_map/ppermute | solution.py:20
  45.9 6.4 %collective-permute-start.5 = (bf16[8,1,4,128]{3,0,2,1:T(8,128)(2,1)S(1)}, bf16[8,1,4,128]{3,0,2,1:T(8,128)(2,1)S(1)}, u32[]{:S(2)}, u32[]{:S(2)}) collective-permute-start(bf16[8,1,4,128]{3,0,2,1:T(8,128)(2,1)S(1)} %get-tuple-element.142), channel_id=1, source_target_pairs={{8,0},{16,8},{24,16},{32,24},{40,32},{48,40},{56,48},{64,56},{72,6... | collective-permute-start | bytes 24584 | tf_op jit(solution)/shard_map/ppermute | solution.py:22
  52.3 5.5 %collective-permute-start.7 = (bf16[8,4,1,128]{3,0,2,1:T(8,128)(2,1)S(1)}, bf16[8,4,1,128]{3,0,2,1:T(8,128)(2,1)S(1)}, u32[]{:S(2)}, u32[]{:S(2)}) collective-permute-start(bf16[8,4,1,128]{3,0,2,1:T(8,128)(2,1)S(1)} %get-tuple-element.138), channel_id=1, source_target_pairs={{1,0},{2,1},{3,2},{4,3},{5,4},{6,5},{7,6},{9,8},{10,9},{11,10},{12... | collective-permute-start | bytes 24584 | tf_op jit(solution)/shard_map/ppermute | solution.py:22
  55.5 5.9 %collective-permute-start.6 = (bf16[8,4,1,128]{3,0,2,1:T(8,128)(2,1)S(1)}, bf16[8,4,1,128]{3,0,2,1:T(8,128)(2,1)S(1)}, u32[]{:S(2)}, u32[]{:S(2)}) collective-permute-start(bf16[8,4,1,128]{3,0,2,1:T(8,128)(2,1)S(1)} %get-tuple-element.137), channel_id=1, source_target_pairs={{0,1},{1,2},{2,3},{3,4},{4,5},{5,6},{6,7},{8,9},{9,10},{10,11},{11... | collective-permute-start | bytes 24584 | tf_op jit(solution)/shard_map/ppermute | solution.py:20
  73.5 52.3 %copy-start.2 = (f32[8,8,1,1]{1,0,3,2:T(8,128)S(1)}, f32[8,8,1,1]{1,0,3,2:T(8,128)}, u32[]{:S(2)}) copy-start(f32[8,8,1,1]{1,0,3,2:T(8,128)} %constant.57) | copy-start | bytes 772
  101.0 18.6 %collective-permute-start.8 = (bf16[64,1,4,128]{3,0,2,1:T(8,128)(2,1)S(1)}, bf16[64,1,4,128]{3,0,2,1:T(8,128)(2,1)S(1)}, u32[]{:S(2)}, u32[]{:S(2)}) collective-permute-start(bf16[64,1,4,128]{3,0,2,1:T(8,128)(2,1)S(1)} %get-tuple-element.100), channel_id=1, source_target_pairs={{0,8},{8,16},{16,24},{24,32},{32,40},{40,48},{48,56},{56,64},{64,7... | collective-permute-start | bytes 196616 | tf_op jit(solution)/shard_map/ppermute | solution.py:20
  103.6 3.1 %collective-permute-start.12 = (f32[607]{0:T(1024)S(1)}, f32[607]{0:T(1024)S(1)}, u32[]{:S(2)}, u32[]{:S(2)}) collective-permute-start(f32[607]{0:T(1024)S(1)} %reduce_sum.39), channel_id=1, source_target_pairs={{0,1},{1,0},{2,3},{3,2},{4,5},{5,4},{6,7},{7,6},{8,9},{9,8},{10,11... | collective-permute-start | bytes 7292 | tf_op jit(solution)/shard_map/ppermute | solution.py:119
  106.7 10.9 %collective-permute-start.13 = (f32[607]{0:T(1024)S(1)}, f32[607]{0:T(1024)S(1)}, u32[]{:S(2)}, u32[]{:S(2)}) collective-permute-start(f32[607]{0:T(1024)S(1)} %add.552), channel_id=1, source_target_pairs={{0,2},{1,3},{2,0},{3,1},{4,6},{5,7},{6,4},{7,5},{8,10},{9,11},{10,... | collective-permute-start | bytes 7292 | tf_op jit(solution)/shard_map/ppermute | solution.py:119
  114.4 7.1 %collective-permute-start.9 = (bf16[64,1,4,128]{3,0,2,1:T(8,128)(2,1)S(1)}, bf16[64,1,4,128]{3,0,2,1:T(8,128)(2,1)S(1)}, u32[]{:S(2)}, u32[]{:S(2)}) collective-permute-start(bf16[64,1,4,128]{3,0,2,1:T(8,128)(2,1)S(1)} %get-tuple-element.99), channel_id=1, source_target_pairs={{8,0},{16,8},{24,16},{32,24},{40,32},{48,40},{56,48},{64,56},{72,6... | collective-permute-start | bytes 196616 | tf_op jit(solution)/shard_map/ppermute | solution.py:22
  117.6 10.9 %collective-permute-start.14 = (f32[607]{0:T(1024)S(1)}, f32[607]{0:T(1024)S(1)}, u32[]{:S(2)}, u32[]{:S(2)}) collective-permute-start(f32[607]{0:T(1024)S(1)} %add.553), channel_id=1, source_target_pairs={{0,4},{1,5},{2,6},{3,7},{4,0},{5,1},{6,2},{7,3},{8,12},{9,13},{10,... | collective-permute-start | bytes 7292 | tf_op jit(solution)/shard_map/ppermute | solution.py:119
  121.5 17.1 %collective-permute-start.11 = (bf16[64,4,1,128]{3,0,2,1:T(8,128)(2,1)S(1)}, bf16[64,4,1,128]{3,0,2,1:T(8,128)(2,1)S(1)}, u32[]{:S(2)}, u32[]{:S(2)}) collective-permute-start(bf16[64,4,1,128]{3,0,2,1:T(8,128)(2,1)S(1)} %get-tuple-element.74), channel_id=1, source_target_pairs={{1,0},{2,1},{3,2},{4,3},{5,4},{6,5},{7,6},{9,8},{10,9},{11,10},{12... | collective-permute-start | bytes 196616 | tf_op jit(solution)/shard_map/ppermute | solution.py:22
  123.4 15.2 %collective-permute-start.10 = (bf16[64,4,1,128]{3,0,2,1:T(8,128)(2,1)S(1)}, bf16[64,4,1,128]{3,0,2,1:T(8,128)(2,1)S(1)}, u32[]{:S(2)}, u32[]{:S(2)}) collective-permute-start(bf16[64,4,1,128]{3,0,2,1:T(8,128)(2,1)S(1)} %get-tuple-element.73), channel_id=1, source_target_pairs={{0,1},{1,2},{2,3},{3,4},{4,5},{5,6},{6,7},{8,9},{9,10},{10,11},{11... | collective-permute-start | bytes 196616 | tf_op jit(solution)/shard_map/ppermute | solution.py:20
  129.3 19.8 %all-to-all-start.1 = ((f32[64,1,607]{2,1,0:T(1,128)}), f32[64,1,607]{2,1,0:T(1,128)S(1)}, u32[]{:S(2)}, u32[]{:S(2)}) async-start(f32[64,1,607]{2,1,0:T(1,128)} %broadcast_in_dim.23), calls=%async_computation.1 | async-start | bytes 327680 | tf_op jit(solution)/shard_map/all_to_all | solution.py:196

commit v5 on v4

--- a/solution.py
+++ b/solution.py
@@ -55,49 +55,39 @@
     return sigma * (1.0 + preact * (1.0 - sigma))
 
 
-def forward_taps(padded, weight, planes, x_rows):
+def shifted(padded, planes, x_rows, flip):
     y_cols = padded.shape[3] - 2
-    summed = None
+    slices = []
     for tap_index in range(27):
         z_step, x_step, y_step = (tap_index // 9, tap_index // 3 % 3, tap_index % 3)
-        sliced = padded[
-            :, z_step : z_step + planes, x_step : x_step + x_rows, y_step : y_step + y_cols
-        ]
-        product = jnp.einsum(
-            "oc,czxy->ozxy", weight[tap_index], sliced, preferred_element_type=jnp.float32
+        if flip:
+            z_step, x_step, y_step = (2 - z_step, 2 - x_step, 2 - y_step)
+        slices.append(
+            padded[:, z_step : z_step + planes, x_step : x_step + x_rows, y_step : y_step + y_cols]
         )
-        summed = product if summed is None else summed + product
-    return summed
+    return jnp.stack(slices)
+
+
+def forward_taps(padded, weight, planes, x_rows):
+    return jnp.einsum(
+        "toc,tczxy->ozxy", weight, shifted(padded, planes, x_rows, False),
+        preferred_element_type=jnp.float32,
+    )
 
 
 def backward_taps(padded, weight, planes, x_rows):
-    y_cols = padded.shape[3] - 2
-    summed = None
-    for tap_index in range(27):
-        z_step, x_step, y_step = (tap_index // 9, tap_index // 3 % 3, tap_index % 3)
-        sliced = padded[
-            :,
-            2 - z_step : 2 - z_step + planes,
-            2 - x_step : 2 - x_step + x_rows,
-            2 - y_step : 2 - y_step + y_cols,
-        ]
-        product = jnp.einsum(
-            "oc,ozxy->czxy", weight[tap_index], sliced, preferred_element_type=jnp.float32
-        )
-        summed = product if summed is None else summed + product
-    return summed
+    return jnp.einsum(
+        "toc,tozxy->czxy", weight, shifted(padded, planes, x_rows, True),
+        preferred_element_type=jnp.float32,
+    )
 
 
 def weight_taps(grad, padded):
-    planes, x_rows, y_cols = (grad.shape[1], grad.shape[2], grad.shape[3])
-    result = []
-    for tap_index in range(27):
-        z_step, x_step, y_step = (tap_index // 9, tap_index // 3 % 3, tap_index % 3)
-        sliced = padded[
-            :, z_step : z_step + planes, x_step : x_step + x_rows, y_step : y_step + y_cols
-        ]
-        result.append(jnp.einsum("ozxy,czxy->oc", grad, sliced, preferred_element_type=jnp.float32))
-    return jnp.stack(result)
+    planes, x_rows = (grad.shape[1], grad.shape[2])
+    return jnp.einsum(
+        "ozxy,tczxy->toc", grad, shifted(padded, planes, x_rows, False),
+        preferred_element_type=jnp.float32,
+    )
 
 
 def frame_cols(tensor):

time: 156 us -> 176 us (1.13)
  local copies, waits for them, and re-layouts: 19 us -> 63.1 us
  matrix products: 34.2 us -> 8.5 us
  starting transfers between devices: 55.6 us -> 59.3 us
  waiting for transfers between devices: 14.8 us -> 11.5 us
    another operation x1 -> x64, local copies, waits for them, and re-layouts: 0.37 us -> 41.7 us  [shifted(): return jnp.stack(slices)]
    dot_general x162 -> x6, matrix products: 32 us -> 5.42 us  [the longest x2 2.76 us: forward_taps(): jnp.einsum('toc,tczxy->ozxy', weight, shifted(padded, planes, x_rows, Fal...]
    ppermute x6, starting transfers between devices: 17.1 us -> 20.9 us  [extended(): lax.ppermute(head, axis, [((i + 1) % count, i) for i in range(ends)])]
    ppermute x6, waiting for transfers between devices: 3.53 us -> 0.02 us  [extended(): lax.ppermute(tail, axis, [(i, (i + 1) % count) for i in range(ends)])]
    unnamed x16 -> x102, local copies, waits for them, and re-layouts: 3.38 us -> 6.37 us
    slice x5 -> x1, local copies, waits for them, and re-layouts: 3.72 us -> 1.38 us  [per_device(): upper_half, lower_half = (latent[:CH], latent[CH:])]
    all_to_all x1, waiting for transfers between devices: 2.21 us -> 4.34 us  [per_device(): lax.all_to_all(jnp.broadcast_to(owned, (count,) + owned.shape), 'gz', 0,...]
    ppermute x6, waiting for transfers between devices: 7.95 us -> 5.99 us  [extended(): lax.ppermute(head, axis, [((i + 1) % count, i) for i in range(ends)])]
  transfers between devices with their start and end apart: 16 -> 16, of which waited for: 7 -> 6; matrix products, arithmetic and copies ran while one was open for 11% -> 11% of each run, Pallas kernels for 0% -> 0%
where the time goes in v5:
time: 176 us; the launch traced here: 174 us
  local copies, waits for them, and re-layouts  63.1 us (36%)
  starting transfers between devices  59.3 us (34%)
  blocking collectives  26.1 us (15%)
  waiting for transfers between devices  11.5 us (7%)
  matrix products  8.5 us (5%)
  other arithmetic  3.94 us (2%)
  between operations  1.95 us (1%)
    another operation x64, local copies, waits for them, and re-layouts, shifted(): return jnp.stack(slices)  41.7 us
    all_to_all x1, blocking collectives, per_device(): owned = lax.all_to_all(chunks, 'gz', 0, 0, tiled=False).sum(0)  26.1 us
    ppermute x6, starting transfers between devices, extended(): lax.ppermute(head, axis, [((i + 1) % count, i) for i in range(ends)])  20.9 us
    ppermute x6, starting transfers between devices, extended(): lax.ppermute(tail, axis, [(i, (i + 1) % count) for i in range(ends)])  18.1 us
    ppermute x3, starting transfers between devices, butterfly_sum(): flat = flat + lax.ppermute(flat, axis, [(i, i ^ bit) for i in range(count)])  11 us
    all_to_all x1, starting transfers between devices, per_device(): lax.all_to_all(jnp.broadcast_to(owned, (count,) + owned.shape), 'gz', 0,...  9.35 us
    unnamed x102, local copies, waits for them, and re-layouts  6.37 us
    ppermute x6, waiting for transfers between devices, extended(): lax.ppermute(head, axis, [((i + 1) % count, i) for i in range(ends)])  5.99 us
  transfers between devices with their start and end apart: 16, of which 6 were waited for; matrix products, arithmetic and copies ran while one was open for 11% of the time, Pallas kernels for 0%

profile of v5, /device:TPU:56, one launch (start us, length us, event | category | flops | bytes accessed | tf_op | source)
XLA Modules:
  0.0 174.4 jit_solution(5681768181510020148)
XLA Ops:
  0.6 1.4 fusion.120
  2.8 5.1 %collective-permute-start = (bf16[12,2,4,128]{3,2,1,0:T(4,128)(2,1)S(1)}, bf16[12,2,4,128]{3,2,1,0:T(4,128)(2,1)S(1)}, u32[]{:S(2)}, u32[]{:S(2)}) collective-permute-start(bf16[12,2,4,128]{3,2,1,0:T(4,128)(2,1)S(1)} %constant_dynamic-update-slice_fusion), channel_id=1, source_target_pairs={{0,8},{8,16},{16,24},{24,32},{32,40},{40,48},{48,56},{56,64},{64,7... | collective-permute-start | bytes 73736 | tf_op jit(solution)/shard_map/ppermute | solution.py:20
  7.8 1.9 %collective-permute-start.1 = (bf16[12,2,4,128]{3,2,1,0:T(4,128)(2,1)S(1)}, bf16[12,2,4,128]{3,2,1,0:T(4,128)(2,1)S(1)}, u32[]{:S(2)}, u32[]{:S(2)}) collective-permute-start(bf16[12,2,4,128]{3,2,1,0:T(4,128)(2,1)S(1)} %constant_dynamic-update-slice_fusion), channel_id=1, source_target_pairs={{8,0},{16,8},{24,16},{32,24},{40,32},{48,40},{56,48},{64,56},{72,6... | collective-permute-start | bytes 73736 | tf_op jit(solution)/shard_map/ppermute | solution.py:22
  9.8 1.3 fusion.121
  12.5 1.2 slice.690
  14.6 1.9 %collective-permute-start.2 = (bf16[12,6,2,128]{3,2,1,0:T(2,128)(2,1)S(1)}, bf16[12,6,2,128]{3,2,1,0:T(2,128)(2,1)S(1)}, u32[]{:S(2)}, u32[]{:S(2)}) collective-permute-start(bf16[12,6,2,128]{3,2,1,0:T(2,128)(2,1)S(1)} %get-tuple-element.301), channel_id=1, source_target_pairs={{0,1},{1,2},{2,3},{3,4},{4,5},{5,6},{6,7},{8,9},{9,10},{10,11},{11... | collective-permute-start | bytes 110600 | tf_op jit(solution)/shard_map/ppermute | solution.py:20
  16.5 4.5 %collective-permute-start.3 = (bf16[12,6,2,128]{3,2,1,0:T(2,128)(2,1)S(1)}, bf16[12,6,2,128]{3,2,1,0:T(2,128)(2,1)S(1)}, u32[]{:S(2)}, u32[]{:S(2)}) collective-permute-start(bf16[12,6,2,128]{3,2,1,0:T(2,128)(2,1)S(1)} %get-tuple-element.302), channel_id=1, source_target_pairs={{1,0},{2,1},{3,2},{4,3},{5,4},{6,5},{7,6},{9,8},{10,9},{11,10},{12... | collective-permute-start | bytes 110600 | tf_op jit(solution)/shard_map/ppermute | solution.py:22
  42.0 17.0 %stack.473 = bf16[27,12,4,6,128]{4,0,1,3,2:T(8,128)(2,1)S(1)} concatenate(bf16[1,12,4,6,128]{4,0,1,3,2:T(2,128)(2,1)} %copy.2200, bf16[1,12,4,6,128]{4,0,1,3,2:T(2,128)(2,1)S(1)} %copy.2201, bf16[1,12,4,6,128]{4,0,1,3,2:T(2,128)(2,1)} %copy.2202, bf16[1,12,4,6,128]{4,0,1,3,2:T(2,128)(2,1)} %copy.2203, bf16[1,12,4,6,128]{4,0,1,3,2:T(2,128)(2,1)} %copy.2204, ...), dimensions={0} | concatenate | bytes 3981312 | tf_op jit(solution)/shard_map/stack | solution.py:68
  59.0 2.2 %multiply_convert_fusion = (bf16[64,4,6,128]{3,0,2,1:T(8,128)(2,1)S(1)}, f32[64,4,6,128]{3,0,2,1:T(8,128)}) fusion(f32[64]{0:T(128)} %get-tuple-element.319, bf16[27,12,4,6,128]{4,0,1,3,2:T(8,128)(2,1)S(1)} %stack.473, bf16[27,64,12]{1,0,2:T(8,128)(2,1)S(1)} %copy-done), kind=kOutput, calls=%fused_computation.77 | convolution fusion | flops 128581632 | bytes 3212032 | tf_op jit(solution)/shard_map/toc,tczxy->ozxy/dot_general | solution.py:72
  65.0 1.5 fusion.8
  66.5 4.7 %collective-permute-start.4 = (bf16[8,1,4,128]{3,0,1,2:T(8,128)(2,1)S(1)}, bf16[8,1,4,128]{3,0,1,2:T(8,128)(2,1)S(1)}, u32[]{:S(2)}, u32[]{:S(2)}) collective-permute-start(bf16[8,1,4,128]{3,0,1,2:T(8,128)(2,1)S(1)} %get-tuple-element.316), channel_id=1, source_target_pairs={{0,8},{8,16},{16,24},{24,32},{32,40},{40,48},{48,56},{56,64},{64,7... | collective-permute-start | bytes 24584 | tf_op jit(solution)/shard_map/ppermute | solution.py:20
  71.1 1.9 %collective-permute-start.5 = (bf16[8,1,4,128]{3,0,1,2:T(8,128)(2,1)S(1)}, bf16[8,1,4,128]{3,0,1,2:T(8,128)(2,1)S(1)}, u32[]{:S(2)}, u32[]{:S(2)}) collective-permute-start(bf16[8,1,4,128]{3,0,1,2:T(8,128)(2,1)S(1)} %get-tuple-element.317), channel_id=1, source_target_pairs={{8,0},{16,8},{24,16},{32,24},{40,32},{48,40},{56,48},{64,56},{72,6... | collective-permute-start | bytes 24584 | tf_op jit(solution)/shard_map/ppermute | solution.py:22
  73.2 4.4 %collective-permute-done.5 = bf16[8,1,4,128]{3,0,1,2:T(8,128)(2,1)S(1)} collective-permute-done((bf16[8,1,4,128]{3,0,1,2:T(8,128)(2,1)S(1)}, bf16[8,1,4,128]{3,0,1,2:T(8,128)(2,1)S(1)}, u32[]{:S(2)}, u32[]{:S(2)}) %collective-permute-start.5) | collective-permute-done | bytes 8224 | tf_op jit(solution)/shard_map/ppermute | solution.py:22
  77.6 1.9 %collective-permute-start.6 = (bf16[8,4,1,128]{3,0,1,2:T(8,128)(2,1)S(1)}, bf16[8,4,1,128]{3,0,1,2:T(8,128)(2,1)S(1)}, u32[]{:S(2)}, u32[]{:S(2)}) collective-permute-start(bf16[8,4,1,128]{3,0,1,2:T(8,128)(2,1)S(1)} %get-tuple-element.310), channel_id=1, source_target_pairs={{0,1},{1,2},{2,3},{3,4},{4,5},{5,6},{6,7},{8,9},{9,10},{10,11},{11... | collective-permute-start | bytes 24584 | tf_op jit(solution)/shard_map/ppermute | solution.py:20
  79.5 4.7 %collective-permute-start.7 = (bf16[8,4,1,128]{3,0,1,2:T(8,128)(2,1)S(1)}, bf16[8,4,1,128]{3,0,1,2:T(8,128)(2,1)S(1)}, u32[]{:S(2)}, u32[]{:S(2)}) collective-permute-start(bf16[8,4,1,128]{3,0,1,2:T(8,128)(2,1)S(1)} %get-tuple-element.311), channel_id=1, source_target_pairs={{1,0},{2,1},{3,2},{4,3},{5,4},{6,5},{7,6},{9,8},{10,9},{11,10},{12... | collective-permute-start | bytes 24584 | tf_op jit(solution)/shard_map/ppermute | solution.py:22
  85.8 2.3 %stack.529 = bf16[27,12,2,4,128]{4,0,2,1,3:T(8,128)(2,1)S(1)} concatenate(bf16[1,12,2,4,128]{4,0,2,1,3:T(2,128)(2,1)S(1)} %copy.2280, bf16[1,12,2,4,128]{4,0,2,1,3:T(2,128)(2,1)S(1)} %copy.2281, bf16[1,12,2,4,128]{4,0,2,1,3:T(2,128)(2,1)S(1)} %copy.2282, bf16[1,12,2,4,128]{4,0,2,1,3:T(2,128)(2,1)S(1)} %copy.2283, bf16[1,12,2,4,128]{4,0,2,1,3:T(2,128)(2,1)S(1)} %copy-done.3, ...), dimensions={0} | concatenate | bytes 1327104 | tf_op jit(solution)/shard_map/stack | solution.py:68
  89.9 1.1 convolution_bitcast_fusion.4
  91.1 1.3 convert_reduce_fusion.1
  94.3 26.1 %all_to_all.15 = f32[64,1,607]{2,1,0:T(1,128)S(1)} all-to-all(f32[64,1,607]{2,1,0:T(1,128)S(1)} %all_to_all.10), channel_id=1, replica_groups=mesh['gz'=64,'gx'=8] {'gz'}, dimensions={0} | all-to-all | bytes 310784 | tf_op jit(solution)/shard_map/all_to_all | solution.py:181
  120.5 2.6 %collective-permute-start.8 = (bf16[64,1,4,128]{3,0,2,1:T(8,128)(2,1)S(1)}, bf16[64,1,4,128]{3,0,2,1:T(8,128)(2,1)S(1)}, u32[]{:S(2)}, u32[]{:S(2)}) collective-permute-start(bf16[64,1,4,128]{3,0,2,1:T(8,128)(2,1)S(1)} %get-tuple-element.298), channel_id=1, source_target_pairs={{0,8},{8,16},{16,24},{24,32},{32,40},{40,48},{48,56},{56,64},{64,7... | collective-permute-start | bytes 196616 | tf_op jit(solution)/shard_map/ppermute | solution.py:20
  123.2 1.9 %collective-permute-start.12 = (f32[607]{0:T(1024)S(1)}, f32[607]{0:T(1024)S(1)}, u32[]{:S(2)}, u32[]{:S(2)}) collective-permute-start(f32[607]{0:T(1024)S(1)} %reduce_sum.39), channel_id=1, source_target_pairs={{0,1},{1,0},{2,3},{3,2},{4,5},{5,4},{6,7},{7,6},{8,9},{9,8},{10,11... | collective-permute-start | bytes 7292 | tf_op jit(solution)/shard_map/ppermute | solution.py:109
  125.1 1.1 collective-permute-done.12
  126.2 6.5 %collective-permute-start.13 = (f32[607]{0:T(1024)S(1)}, f32[607]{0:T(1024)S(1)}, u32[]{:S(2)}, u32[]{:S(2)}) collective-permute-start(f32[607]{0:T(1024)S(1)} %add.116), channel_id=1, source_target_pairs={{0,2},{1,3},{2,0},{3,1},{4,6},{5,7},{6,4},{7,5},{8,10},{9,11},{10,... | collective-permute-start | bytes 7292 | tf_op jit(solution)/shard_map/ppermute | solution.py:109
  132.7 3.2 %collective-permute-start.9 = (bf16[64,1,4,128]{3,0,2,1:T(8,128)(2,1)S(1)}, bf16[64,1,4,128]{3,0,2,1:T(8,128)(2,1)S(1)}, u32[]{:S(2)}, u32[]{:S(2)}) collective-permute-start(bf16[64,1,4,128]{3,0,2,1:T(8,128)(2,1)S(1)} %get-tuple-element.297), channel_id=1, source_target_pairs={{8,0},{16,8},{24,16},{32,24},{40,32},{48,40},{56,48},{64,56},{72,6... | collective-permute-start | bytes 196616 | tf_op jit(solution)/shard_map/ppermute | solution.py:22
  136.0 2.6 %collective-permute-start.14 = (f32[607]{0:T(1024)S(1)}, f32[607]{0:T(1024)S(1)}, u32[]{:S(2)}, u32[]{:S(2)}) collective-permute-start(f32[607]{0:T(1024)S(1)} %add.117), channel_id=1, source_target_pairs={{0,4},{1,5},{2,6},{3,7},{4,0},{5,1},{6,2},{7,3},{8,12},{9,13},{10,... | collective-permute-start | bytes 7292 | tf_op jit(solution)/shard_map/ppermute | solution.py:109
  138.6 1.2 collective-permute-done.9
  139.8 1.9 %collective-permute-start.10 = (bf16[64,4,1,128]{3,0,2,1:T(8,128)(2,1)S(1)}, bf16[64,4,1,128]{3,0,2,1:T(8,128)(2,1)S(1)}, u32[]{:S(2)}, u32[]{:S(2)}) collective-permute-start(bf16[64,4,1,128]{3,0,2,1:T(8,128)(2,1)S(1)} %get-tuple-element.244), channel_id=1, source_target_pairs={{0,1},{1,2},{2,3},{3,4},{4,5},{5,6},{6,7},{8,9},{9,10},{10,11},{11... | collective-permute-start | bytes 196616 | tf_op jit(solution)/shard_map/ppermute | solution.py:20
  141.7 4.5 %collective-permute-start.11 = (bf16[64,4,1,128]{3,0,2,1:T(8,128)(2,1)S(1)}, bf16[64,4,1,128]{3,0,2,1:T(8,128)(2,1)S(1)}, u32[]{:S(2)}, u32[]{:S(2)}) collective-permute-start(bf16[64,4,1,128]{3,0,2,1:T(8,128)(2,1)S(1)} %get-tuple-element.245), channel_id=1, source_target_pairs={{1,0},{2,1},{3,2},{4,3},{5,4},{6,5},{7,6},{9,8},{10,9},{11,10},{12... | collective-permute-start | bytes 196616 | tf_op jit(solution)/shard_map/ppermute | solution.py:22
  147.1 1.8 %reshape.127 = f32[4,8,256]{2,1,0:T(8,128)} reshape(f32[2,2,4,2,128,2]{5,4,3,2,1,0:T(8,128)S(1)} %copy.2255) | data formatting | bytes 65536 | tf_op jit(solution)/shard_map/reshape | solution.py:50
  149.7 9.4 %all-to-all-start.1 = ((f32[64,1,607]{2,1,0:T(1,128)}), f32[64,1,607]{2,1,0:T(1,128)S(1)}, u32[]{:S(2)}, u32[]{:S(2)}) async-start(f32[64,1,607]{2,1,0:T(1,128)} %broadcast_in_dim.23), calls=%async_computation.1 | async-start | bytes 327680 | tf_op jit(solution)/shard_map/all_to_all | solution.py:186
  162.7 1.8 %reshape.132 = f32[4,8,256]{2,1,0:T(8,128)} reshape(f32[2,2,4,2,128,2]{5,4,3,2,1,0:T(8,128)S(1)} %copy.2345) | data formatting | bytes 65536 | tf_op jit(solution)/shard_map/reshape | solution.py:50
  165.2 4.3 %all-to-all-done.1 = f32[64,1,607]{2,1,0:T(1,128)S(1)} async-done(((f32[64,1,607]{2,1,0:T(1,128)}), f32[64,1,607]{2,1,0:T(1,128)S(1)}, u32[]{:S(2)}, u32[]{:S(2)}) %all-to-all-start.1) | async-done | bytes 155424 | tf_op jit(solution)/shard_map/all_to_all | solution.py:186
  (242 shorter events, 43.1 us)
Async XLA Ops:
  0.6 58.3 %copy-start = (bf16[27,64,12]{1,0,2:T(8,128)(2,1)S(1)}, bf16[27,64,12]{1,0,2:T(8,128)(2,1)}, u32[]{:S(2)}) copy-start(bf16[27,64,12]{1,0,2:T(8,128)(2,1)} %param.12) | copy-start | bytes 124420
  2.8 11.6 %collective-permute-start = (bf16[12,2,4,128]{3,2,1,0:T(4,128)(2,1)S(1)}, bf16[12,2,4,128]{3,2,1,0:T(4,128)(2,1)S(1)}, u32[]{:S(2)}, u32[]{:S(2)}) collective-permute-start(bf16[12,2,4,128]{3,2,1,0:T(4,128)(2,1)S(1)} %constant_dynamic-update-slice_fusion), channel_id=1, source_target_pairs={{0,8},{8,16},{16,24},{24,32},{32,40},{40,48},{48,56},{56,64},{64,7... | collective-permute-start | bytes 73736 | tf_op jit(solution)/shard_map/ppermute | solution.py:20
  7.8 6.6 %collective-permute-start.1 = (bf16[12,2,4,128]{3,2,1,0:T(4,128)(2,1)S(1)}, bf16[12,2,4,128]{3,2,1,0:T(4,128)(2,1)S(1)}, u32[]{:S(2)}, u32[]{:S(2)}) collective-permute-start(bf16[12,2,4,128]{3,2,1,0:T(4,128)(2,1)S(1)} %constant_dynamic-update-slice_fusion), channel_id=1, source_target_pairs={{8,0},{16,8},{24,16},{32,24},{40,32},{48,40},{56,48},{64,56},{72,6... | collective-permute-start | bytes 73736 | tf_op jit(solution)/shard_map/ppermute | solution.py:22
  14.6 7.8 %collective-permute-start.2 = (bf16[12,6,2,128]{3,2,1,0:T(2,128)(2,1)S(1)}, bf16[12,6,2,128]{3,2,1,0:T(2,128)(2,1)S(1)}, u32[]{:S(2)}, u32[]{:S(2)}) collective-permute-start(bf16[12,6,2,128]{3,2,1,0:T(2,128)(2,1)S(1)} %get-tuple-element.301), channel_id=1, source_target_pairs={{0,1},{1,2},{2,3},{3,4},{4,5},{5,6},{6,7},{8,9},{9,10},{10,11},{11... | collective-permute-start | bytes 110600 | tf_op jit(solution)/shard_map/ppermute | solution.py:20
  16.5 6.2 %collective-permute-start.3 = (bf16[12,6,2,128]{3,2,1,0:T(2,128)(2,1)S(1)}, bf16[12,6,2,128]{3,2,1,0:T(2,128)(2,1)S(1)}, u32[]{:S(2)}, u32[]{:S(2)}) collective-permute-start(bf16[12,6,2,128]{3,2,1,0:T(2,128)(2,1)S(1)} %get-tuple-element.302), channel_id=1, source_target_pairs={{1,0},{2,1},{3,2},{4,3},{5,4},{6,5},{7,6},{9,8},{10,9},{11,10},{12... | collective-permute-start | bytes 110600 | tf_op jit(solution)/shard_map/ppermute | solution.py:22
  59.0 2.2 %copy-start.8 = (f32[64]{0:T(128)S(1)}, f32[64]{0:T(128)}, u32[]{:S(2)}) copy-start(f32[64]{0:T(128)} %get-tuple-element.318) | copy-start | bytes 772
  59.0 2.2 %copy-start.9 = (bf16[64,64]{1,0:T(8,128)(2,1)S(1)}, bf16[64,64]{1,0:T(8,128)(2,1)}, u32[]{:S(2)}) copy-start(bf16[64,64]{1,0:T(8,128)(2,1)} %param.13) | copy-start | bytes 24580
  59.0 2.2 %copy-start.11 = (pred[4,6]{1,0:T(4,128)(4,1)S(1)}, pred[4,6]{1,0:T(4,128)(4,1)}, u32[]{:S(2)}) copy-start(pred[4,6]{1,0:T(4,128)(4,1)} %broadcast_and_fusion) | copy-start | bytes 76
  61.2 1.1 copy-start.12
  62.6 1.6 copy-start.1
  63.4 1.4 copy-start.7
  63.4 1.4 copy-start.5
  64.9 20.9 %copy-start.2 = (bf16[1,12,2,4,128]{4,0,2,1,3:T(2,128)(2,1)S(1)}, bf16[1,12,2,4,128]{4,0,2,1,3:T(2,128)(2,1)}, u32[]{:S(2)}) copy-start(bf16[1,12,2,4,128]{4,0,2,1,3:T(2,128)(2,1)} %copy.2293) | copy-start | bytes 73732
  64.9 20.9 %copy-start.3 = (bf16[1,12,2,4,128]{4,0,2,1,3:T(2,128)(2,1)S(1)}, bf16[1,12,2,4,128]{4,0,2,1,3:T(2,128)(2,1)}, u32[]{:S(2)}) copy-start(bf16[1,12,2,4,128]{4,0,2,1,3:T(2,128)(2,1)} %copy.2284) | copy-start | bytes 73732
  64.9 20.9 %copy-start.4 = (bf16[1,12,2,4,128]{4,0,2,1,3:T(2,128)(2,1)S(1)}, bf16[1,12,2,4,128]{4,0,2,1,3:T(2,128)(2,1)}, u32[]{:S(2)}) copy-start(bf16[1,12,2,4,128]{4,0,2,1,3:T(2,128)(2,1)} %copy.2302) | copy-start | bytes 73732
  66.5 6.7 %collective-permute-start.4 = (bf16[8,1,4,128]{3,0,1,2:T(8,128)(2,1)S(1)}, bf16[8,1,4,128]{3,0,1,2:T(8,128)(2,1)S(1)}, u32[]{:S(2)}, u32[]{:S(2)}) collective-permute-start(bf16[8,1,4,128]{3,0,1,2:T(8,128)(2,1)S(1)} %get-tuple-element.316), channel_id=1, source_target_pairs={{0,8},{8,16},{16,24},{24,32},{32,40},{40,48},{48,56},{56,64},{64,7... | collective-permute-start | bytes 24584 | tf_op jit(solution)/shard_map/ppermute | solution.py:20
  71.1 6.4 %collective-permute-start.5 = (bf16[8,1,4,128]{3,0,1,2:T(8,128)(2,1)S(1)}, bf16[8,1,4,128]{3,0,1,2:T(8,128)(2,1)S(1)}, u32[]{:S(2)}, u32[]{:S(2)}) collective-permute-start(bf16[8,1,4,128]{3,0,1,2:T(8,128)(2,1)S(1)} %get-tuple-element.317), channel_id=1, source_target_pairs={{8,0},{16,8},{24,16},{32,24},{40,32},{48,40},{56,48},{64,56},{72,6... | collective-permute-start | bytes 24584 | tf_op jit(solution)/shard_map/ppermute | solution.py:22
  77.6 10.7 %collective-permute-start.6 = (bf16[8,4,1,128]{3,0,1,2:T(8,128)(2,1)S(1)}, bf16[8,4,1,128]{3,0,1,2:T(8,128)(2,1)S(1)}, u32[]{:S(2)}, u32[]{:S(2)}) collective-permute-start(bf16[8,4,1,128]{3,0,1,2:T(8,128)(2,1)S(1)} %get-tuple-element.310), channel_id=1, source_target_pairs={{0,1},{1,2},{2,3},{3,4},{4,5},{5,6},{6,7},{8,9},{9,10},{10,11},{11... | collective-permute-start | bytes 24584 | tf_op jit(solution)/shard_map/ppermute | solution.py:20
  79.5 8.8 %collective-permute-start.7 = (bf16[8,4,1,128]{3,0,1,2:T(8,128)(2,1)S(1)}, bf16[8,4,1,128]{3,0,1,2:T(8,128)(2,1)S(1)}, u32[]{:S(2)}, u32[]{:S(2)}) collective-permute-start(bf16[8,4,1,128]{3,0,1,2:T(8,128)(2,1)S(1)} %get-tuple-element.311), channel_id=1, source_target_pairs={{1,0},{2,1},{3,2},{4,3},{5,4},{6,5},{7,6},{9,8},{10,9},{11,10},{12... | collective-permute-start | bytes 24584 | tf_op jit(solution)/shard_map/ppermute | solution.py:22
  84.7 6.4 %copy-start.10 = (bf16[64,64]{1,0:T(8,128)(2,1)S(1)}, bf16[64,64]{1,0:T(8,128)(2,1)}, u32[]{:S(2)}) copy-start(bf16[64,64]{1,0:T(8,128)(2,1)} %param.13) | copy-start | bytes 24580
  91.1 55.2 %copy-start.6 = (f32[8,8,1,1]{1,0,3,2:T(8,128)S(1)}, f32[8,8,1,1]{1,0,3,2:T(8,128)}, u32[]{:S(2)}) copy-start(f32[8,8,1,1]{1,0,3,2:T(8,128)} %constant.57) | copy-start | bytes 772
  120.5 18.0 %collective-permute-start.8 = (bf16[64,1,4,128]{3,0,2,1:T(8,128)(2,1)S(1)}, bf16[64,1,4,128]{3,0,2,1:T(8,128)(2,1)S(1)}, u32[]{:S(2)}, u32[]{:S(2)}) collective-permute-start(bf16[64,1,4,128]{3,0,2,1:T(8,128)(2,1)S(1)} %get-tuple-element.298), channel_id=1, source_target_pairs={{0,8},{8,16},{16,24},{24,32},{32,40},{40,48},{48,56},{56,64},{64,7... | collective-permute-start | bytes 196616 | tf_op jit(solution)/shard_map/ppermute | solution.py:20
  123.2 3.1 %collective-permute-start.12 = (f32[607]{0:T(1024)S(1)}, f32[607]{0:T(1024)S(1)}, u32[]{:S(2)}, u32[]{:S(2)}) collective-permute-start(f32[607]{0:T(1024)S(1)} %reduce_sum.39), channel_id=1, source_target_pairs={{0,1},{1,0},{2,3},{3,2},{4,5},{5,4},{6,7},{7,6},{8,9},{9,8},{10,11... | collective-permute-start | bytes 7292 | tf_op jit(solution)/shard_map/ppermute | solution.py:109
  126.2 9.7 %collective-permute-start.13 = (f32[607]{0:T(1024)S(1)}, f32[607]{0:T(1024)S(1)}, u32[]{:S(2)}, u32[]{:S(2)}) collective-permute-start(f32[607]{0:T(1024)S(1)} %add.116), channel_id=1, source_target_pairs={{0,2},{1,3},{2,0},{3,1},{4,6},{5,7},{6,4},{7,5},{8,10},{9,11},{10,... | collective-permute-start | bytes 7292 | tf_op jit(solution)/shard_map/ppermute | solution.py:109
  132.7 7.1 %collective-permute-start.9 = (bf16[64,1,4,128]{3,0,2,1:T(8,128)(2,1)S(1)}, bf16[64,1,4,128]{3,0,2,1:T(8,128)(2,1)S(1)}, u32[]{:S(2)}, u32[]{:S(2)}) collective-permute-start(bf16[64,1,4,128]{3,0,2,1:T(8,128)(2,1)S(1)} %get-tuple-element.297), channel_id=1, source_target_pairs={{8,0},{16,8},{24,16},{32,24},{40,32},{48,40},{56,48},{64,56},{72,6... | collective-permute-start | bytes 196616 | tf_op jit(solution)/shard_map/ppermute | solution.py:22
  136.0 13.0 %collective-permute-start.14 = (f32[607]{0:T(1024)S(1)}, f32[607]{0:T(1024)S(1)}, u32[]{:S(2)}, u32[]{:S(2)}) collective-permute-start(f32[607]{0:T(1024)S(1)} %add.117), channel_id=1, source_target_pairs={{0,4},{1,5},{2,6},{3,7},{4,0},{5,1},{6,2},{7,3},{8,12},{9,13},{10,... | collective-permute-start | bytes 7292 | tf_op jit(solution)/shard_map/ppermute | solution.py:109
  139.8 19.3 %collective-permute-start.10 = (bf16[64,4,1,128]{3,0,2,1:T(8,128)(2,1)S(1)}, bf16[64,4,1,128]{3,0,2,1:T(8,128)(2,1)S(1)}, u32[]{:S(2)}, u32[]{:S(2)}) collective-permute-start(bf16[64,4,1,128]{3,0,2,1:T(8,128)(2,1)S(1)} %get-tuple-element.244), channel_id=1, source_target_pairs={{0,1},{1,2},{2,3},{3,4},{4,5},{5,6},{6,7},{8,9},{9,10},{10,11},{11... | collective-permute-start | bytes 196616 | tf_op jit(solution)/shard_map/ppermute | solution.py:20
  141.7 17.4 %collective-permute-start.11 = (bf16[64,4,1,128]{3,0,2,1:T(8,128)(2,1)S(1)}, bf16[64,4,1,128]{3,0,2,1:T(8,128)(2,1)S(1)}, u32[]{:S(2)}, u32[]{:S(2)}) collective-permute-start(bf16[64,4,1,128]{3,0,2,1:T(8,128)(2,1)S(1)} %get-tuple-element.245), channel_id=1, source_target_pairs={{1,0},{2,1},{3,2},{4,3},{5,4},{6,5},{7,6},{9,8},{10,9},{11,10},{12... | collective-permute-start | bytes 196616 | tf_op jit(solution)/shard_map/ppermute | solution.py:22
  149.7 19.8 %all-to-all-start.1 = ((f32[64,1,607]{2,1,0:T(1,128)}), f32[64,1,607]{2,1,0:T(1,128)S(1)}, u32[]{:S(2)}, u32[]{:S(2)}) async-start(f32[64,1,607]{2,1,0:T(1,128)} %broadcast_in_dim.23), calls=%async_computation.1 | async-start | bytes 327680 | tf_op jit(solution)/shard_map/all_to_all | solution.py:186

commit v6 on v4

--- a/solution.py
+++ b/solution.py
@@ -190,7 +190,8 @@
     chunks = jnp.pad(flat, (0, (-total) % count)).reshape(count, -1)
     owned = lax.all_to_all(chunks, "gz", 0, 0, tiled=False).sum(0)
     owned, first_grad = lax.optimization_barrier((owned, first_grad))
-    owned = butterfly_sum(owned, ("gx",))
+    factor = 1.0 / math.sqrt(float(planes * x_rows * y_cols))
+    owned = butterfly_sum(owned, ("gx",)) * factor
     first_frame = frame_cols(extended(first_grad, (("gz", 1), ("gx", 2)), 1))
     input_grad = backward_taps(first_frame, expand_kernel, planes, x_rows)
     spread = lax.all_to_all(jnp.broadcast_to(owned, (count,) + owned.shape), "gz", 0, 0, tiled=False)
@@ -203,15 +204,14 @@
     restored = unsqueeze(jnp.concatenate([upper_half, recovered], axis=0))
     field_grad = unsqueeze(jnp.concatenate([cot_upper + input_grad[:CH], lower_grad], axis=0))
     condition_grad = input_grad[CH:]
-    factor = 1.0 / math.sqrt(float(planes * x_rows * y_cols))
     return (
         restored,
         field_grad,
         condition_grad,
-        expand_sum * factor,
-        mixing_sum * factor,
-        project_sum * factor,
-        offset_sum * factor,
+        expand_sum,
+        mixing_sum,
+        project_sum,
+        offset_sum,
     )
 
 

time: 156 us -> 156 us (level)
  blocking collectives: 26.1 us -> 0 us
  starting transfers between devices: 55.6 us -> 70.1 us
  waiting for transfers between devices: 14.8 us -> 25.5 us
    all_to_all x1 -> x0, blocking collectives: 26.1 us -> none  [per_device(): owned = lax.all_to_all(chunks, 'gz', 0, 0, tiled=False).sum(0)]
    all_to_all x0 -> x1, starting transfers between devices: none -> 15.9 us  [per_device(): owned = lax.all_to_all(chunks, 'gz', 0, 0, tiled=False).sum(0)]
    all_to_all x0 -> x1, waiting for transfers between devices: none -> 10.4 us  [per_device(): owned = lax.all_to_all(chunks, 'gz', 0, 0, tiled=False).sum(0)]
    mul x2 -> x0, local copies, waits for them, and re-layouts: 1.69 us -> none  [the longest x1 0.96 us: per_device(): expand_sum * factor]
    reshape x0 -> x2, local copies, waits for them, and re-layouts: none -> 1.69 us  [per_device(): pieces.append(flat[start:start + t.size].reshape(t.shape))]
    unnamed x16 -> x14, local copies, waits for them, and re-layouts: 3.38 us -> 3.05 us
  transfers between devices with their start and end apart: 16 -> 17, of which waited for: 7 -> 8; matrix products, arithmetic and copies ran while one was open for 11% -> 11% of each run, Pallas kernels for 0% -> 0%
where the time goes in v6:
time: 156 us; the launch traced here: 154 us
  starting transfers between devices  70.1 us (45%)
  matrix products  35.1 us (22%)
  waiting for transfers between devices  25.5 us (16%)
  local copies, waits for them, and re-layouts  20.5 us (13%)
  between operations  1.62 us (1%)
    ppermute x6, starting transfers between devices, extended(): lax.ppermute(tail, axis, [(i, (i + 1) % count) for i in range(ends)])  17.6 us
    ppermute x6, starting transfers between devices, extended(): lax.ppermute(head, axis, [((i + 1) % count, i) for i in range(ends)])  17.1 us
    all_to_all x1, starting transfers between devices, per_device(): owned = lax.all_to_all(chunks, 'gz', 0, 0, tiled=False).sum(0)  15.9 us
    dot_general x54, matrix products, forward_taps(): jnp.einsum('oc,czxy->ozxy', weight[tap_index], sliced, preferred_element_...  14 us
    ppermute x3, starting transfers between devices, butterfly_sum(): flat = flat + lax.ppermute(flat, axis, [(i, i ^ bit) for i in range(count)])  11.5 us
    dot_general x54, matrix products, backward_taps(): jnp.einsum('oc,ozxy->czxy', weight[tap_index], sliced, preferred_element_...  10.8 us
    all_to_all x1, waiting for transfers between devices, per_device(): owned = lax.all_to_all(chunks, 'gz', 0, 0, tiled=False).sum(0)  10.4 us
    dot_general x54, matrix products, weight_taps(): jnp.einsum('ozxy,czxy->oc', grad, sliced, preferred_element_type=jnp.floa...  8.16 us
  transfers between devices with their start and end apart: 17, of which 8 were waited for; matrix products, arithmetic and copies ran while one was open for 11% of the time, Pallas kernels for 0%

profile of v6, /device:TPU:56, one launch (start us, length us, event | category | flops | bytes accessed | tf_op | source)
XLA Modules:
  0.0 154.3 jit_solution(9297030216356223717)
XLA Ops:
  2.2 5.1 %collective-permute-start = (bf16[12,2,4,128]{3,0,2,1:T(8,128)(2,1)S(1)}, bf16[12,2,4,128]{3,0,2,1:T(8,128)(2,1)S(1)}, u32[]{:S(2)}, u32[]{:S(2)}) collective-permute-start(bf16[12,2,4,128]{3,0,2,1:T(8,128)(2,1)S(1)} %pad_maximum_fusion.22), channel_id=1, source_target_pairs={{0,8},{8,16},{16,24},{24,32},{32,40},{40,48},{48,56},{56,64},{64,7... | collective-permute-start | bytes 73736 | tf_op jit(solution)/shard_map/ppermute | solution.py:20
  7.3 1.9 %collective-permute-start.1 = (bf16[12,2,4,128]{3,0,2,1:T(8,128)(2,1)S(1)}, bf16[12,2,4,128]{3,0,2,1:T(8,128)(2,1)S(1)}, u32[]{:S(2)}, u32[]{:S(2)}) collective-permute-start(bf16[12,2,4,128]{3,0,2,1:T(8,128)(2,1)S(1)} %pad_maximum_fusion.22), channel_id=1, source_target_pairs={{8,0},{16,8},{24,16},{32,24},{40,32},{48,40},{56,48},{64,56},{72,6... | collective-permute-start | bytes 73736 | tf_op jit(solution)/shard_map/ppermute | solution.py:22
  9.2 1.4 fusion.519
  10.6 1.2 fusion.520
  12.6 1.4 collective-permute-done.1
  14.0 1.9 %collective-permute-start.2 = (bf16[12,6,2,128]{3,0,2,1:T(8,128)(2,1)S(1)}, bf16[12,6,2,128]{3,0,2,1:T(8,128)(2,1)S(1)}, u32[]{:S(2)}, u32[]{:S(2)}) collective-permute-start(bf16[12,6,2,128]{3,0,2,1:T(8,128)(2,1)S(1)} %get-tuple-element.128), channel_id=1, source_target_pairs={{0,1},{1,2},{2,3},{3,4},{4,5},{5,6},{6,7},{8,9},{9,10},{10,11},{11... | collective-permute-start | bytes 110600 | tf_op jit(solution)/shard_map/ppermute | solution.py:20
  15.9 4.5 %collective-permute-start.3 = (bf16[12,6,2,128]{3,0,2,1:T(8,128)(2,1)S(1)}, bf16[12,6,2,128]{3,0,2,1:T(8,128)(2,1)S(1)}, u32[]{:S(2)}, u32[]{:S(2)}) collective-permute-start(bf16[12,6,2,128]{3,0,2,1:T(8,128)(2,1)S(1)} %get-tuple-element.129), channel_id=1, source_target_pairs={{1,0},{2,1},{3,2},{4,3},{5,4},{6,5},{7,6},{9,8},{10,9},{11,10},{12... | collective-permute-start | bytes 110600 | tf_op jit(solution)/shard_map/ppermute | solution.py:22
  29.4 1.0 fusion.28
  31.4 1.3 multiply_convert_fusion
  42.9 3.5 %collective-permute-start.4 = (bf16[8,1,4,128]{3,0,2,1:T(8,128)(2,1)S(1)}, bf16[8,1,4,128]{3,0,2,1:T(8,128)(2,1)S(1)}, u32[]{:S(2)}, u32[]{:S(2)}) collective-permute-start(bf16[8,1,4,128]{3,0,2,1:T(8,128)(2,1)S(1)} %get-tuple-element.141), channel_id=1, source_target_pairs={{0,8},{8,16},{16,24},{24,32},{32,40},{40,48},{48,56},{56,64},{64,7... | collective-permute-start | bytes 24584 | tf_op jit(solution)/shard_map/ppermute | solution.py:20
  46.4 2.4 %collective-permute-start.5 = (bf16[8,1,4,128]{3,0,2,1:T(8,128)(2,1)S(1)}, bf16[8,1,4,128]{3,0,2,1:T(8,128)(2,1)S(1)}, u32[]{:S(2)}, u32[]{:S(2)}) collective-permute-start(bf16[8,1,4,128]{3,0,2,1:T(8,128)(2,1)S(1)} %get-tuple-element.142), channel_id=1, source_target_pairs={{8,0},{16,8},{24,16},{32,24},{40,32},{48,40},{56,48},{64,56},{72,6... | collective-permute-start | bytes 24584 | tf_op jit(solution)/shard_map/ppermute | solution.py:22
  49.1 3.8 %collective-permute-done.5 = bf16[8,1,4,128]{3,0,2,1:T(8,128)(2,1)S(1)} collective-permute-done((bf16[8,1,4,128]{3,0,2,1:T(8,128)(2,1)S(1)}, bf16[8,1,4,128]{3,0,2,1:T(8,128)(2,1)S(1)}, u32[]{:S(2)}, u32[]{:S(2)}) %collective-permute-start.5) | collective-permute-done | bytes 8224 | tf_op jit(solution)/shard_map/ppermute | solution.py:22
  52.9 3.1 %collective-permute-start.7 = (bf16[8,4,1,128]{3,0,2,1:T(8,128)(2,1)S(1)}, bf16[8,4,1,128]{3,0,2,1:T(8,128)(2,1)S(1)}, u32[]{:S(2)}, u32[]{:S(2)}) collective-permute-start(bf16[8,4,1,128]{3,0,2,1:T(8,128)(2,1)S(1)} %get-tuple-element.138), channel_id=1, source_target_pairs={{1,0},{2,1},{3,2},{4,3},{5,4},{6,5},{7,6},{9,8},{10,9},{11,10},{12... | collective-permute-start | bytes 24584 | tf_op jit(solution)/shard_map/ppermute | solution.py:22
  56.0 2.1 %collective-permute-start.6 = (bf16[8,4,1,128]{3,0,2,1:T(8,128)(2,1)S(1)}, bf16[8,4,1,128]{3,0,2,1:T(8,128)(2,1)S(1)}, u32[]{:S(2)}, u32[]{:S(2)}) collective-permute-start(bf16[8,4,1,128]{3,0,2,1:T(8,128)(2,1)S(1)} %get-tuple-element.137), channel_id=1, source_target_pairs={{0,1},{1,2},{2,3},{3,4},{4,5},{5,6},{6,7},{8,9},{9,10},{10,11},{11... | collective-permute-start | bytes 24584 | tf_op jit(solution)/shard_map/ppermute | solution.py:20
  58.4 3.5 %collective-permute-done.6 = bf16[8,4,1,128]{3,0,2,1:T(8,128)(2,1)S(1)} collective-permute-done((bf16[8,4,1,128]{3,0,2,1:T(8,128)(2,1)S(1)}, bf16[8,4,1,128]{3,0,2,1:T(8,128)(2,1)S(1)}, u32[]{:S(2)}, u32[]{:S(2)}) %collective-permute-start.6) | collective-permute-done | bytes 8224 | tf_op jit(solution)/shard_map/ppermute | solution.py:20
  68.3 1.3 convert_reduce_fusion.1
  76.0 15.9 %all-to-all-start = ((f32[64,1,607]{2,1,0:T(1,128)}), f32[64,1,607]{2,1,0:T(1,128)S(1)}, u32[]{:S(2)}, u32[]{:S(2)}) async-start(f32[64,1,607]{2,1,0:T(1,128)} %all_to_all.10), calls=%async_computation | async-start | bytes 327680 | tf_op jit(solution)/shard_map/all_to_all | solution.py:191
  91.9 10.4 %all-to-all-done = f32[64,1,607]{2,1,0:T(1,128)S(1)} async-done(((f32[64,1,607]{2,1,0:T(1,128)}), f32[64,1,607]{2,1,0:T(1,128)S(1)}, u32[]{:S(2)}, u32[]{:S(2)}) %all-to-all-start) | async-done | bytes 155424 | tf_op jit(solution)/shard_map/all_to_all | solution.py:191
  102.4 1.9 %collective-permute-start.12 = (f32[607]{0:T(1024)S(1)}, f32[607]{0:T(1024)S(1)}, u32[]{:S(2)}, u32[]{:S(2)}) collective-permute-start(f32[607]{0:T(1024)S(1)} %reduce_sum.39), channel_id=1, source_target_pairs={{0,1},{1,0},{2,3},{3,2},{4,5},{5,4},{6,7},{7,6},{8,9},{9,8},{10,11... | collective-permute-start | bytes 7292 | tf_op jit(solution)/shard_map/ppermute | solution.py:119
  104.4 2.6 %collective-permute-start.8 = (bf16[64,1,4,128]{3,0,2,1:T(8,128)(2,1)S(1)}, bf16[64,1,4,128]{3,0,2,1:T(8,128)(2,1)S(1)}, u32[]{:S(2)}, u32[]{:S(2)}) collective-permute-start(bf16[64,1,4,128]{3,0,2,1:T(8,128)(2,1)S(1)} %get-tuple-element.100), channel_id=1, source_target_pairs={{0,8},{8,16},{16,24},{24,32},{32,40},{40,48},{48,56},{56,64},{64,7... | collective-permute-start | bytes 196616 | tf_op jit(solution)/shard_map/ppermute | solution.py:20
  107.0 7.7 %collective-permute-start.13 = (f32[607]{0:T(1024)S(1)}, f32[607]{0:T(1024)S(1)}, u32[]{:S(2)}, u32[]{:S(2)}) collective-permute-start(f32[607]{0:T(1024)S(1)} %add.552), channel_id=1, source_target_pairs={{0,2},{1,3},{2,0},{3,1},{4,6},{5,7},{6,4},{7,5},{8,10},{9,11},{10,... | collective-permute-start | bytes 7292 | tf_op jit(solution)/shard_map/ppermute | solution.py:119
  115.6 1.8 %reshape.105 = f32[4,8,256]{2,1,0:T(8,128)} reshape(f32[2,2,4,2,128,2]{5,4,3,2,1,0:T(8,128)S(1)} %bitcast.1138) | data formatting | bytes 65536 | tf_op jit(solution)/shard_map/reshape | solution.py:50
  117.4 3.2 %collective-permute-start.9 = (bf16[64,1,4,128]{3,0,2,1:T(8,128)(2,1)S(1)}, bf16[64,1,4,128]{3,0,2,1:T(8,128)(2,1)S(1)}, u32[]{:S(2)}, u32[]{:S(2)}) collective-permute-start(bf16[64,1,4,128]{3,0,2,1:T(8,128)(2,1)S(1)} %get-tuple-element.99), channel_id=1, source_target_pairs={{8,0},{16,8},{24,16},{32,24},{40,32},{48,40},{56,48},{64,56},{72,6... | collective-permute-start | bytes 196616 | tf_op jit(solution)/shard_map/ppermute | solution.py:22
  120.6 1.9 %collective-permute-start.14 = (f32[607]{0:T(1024)S(1)}, f32[607]{0:T(1024)S(1)}, u32[]{:S(2)}, u32[]{:S(2)}) collective-permute-start(f32[607]{0:T(1024)S(1)} %add.553), channel_id=1, source_target_pairs={{0,4},{1,5},{2,6},{3,7},{4,0},{5,1},{6,2},{7,3},{8,12},{9,13},{10,... | collective-permute-start | bytes 7292 | tf_op jit(solution)/shard_map/ppermute | solution.py:119
  122.6 1.8 %collective-permute-done.9 = bf16[64,1,4,128]{3,0,2,1:T(8,128)(2,1)S(1)} collective-permute-done((bf16[64,1,4,128]{3,0,2,1:T(8,128)(2,1)S(1)}, bf16[64,1,4,128]{3,0,2,1:T(8,128)(2,1)S(1)}, u32[]{:S(2)}, u32[]{:S(2)}) %collective-permute-start.9) | collective-permute-done | bytes 65568 | tf_op jit(solution)/shard_map/ppermute | solution.py:22
  124.5 1.9 %collective-permute-start.11 = (bf16[64,4,1,128]{3,0,2,1:T(8,128)(2,1)S(1)}, bf16[64,4,1,128]{3,0,2,1:T(8,128)(2,1)S(1)}, u32[]{:S(2)}, u32[]{:S(2)}) collective-permute-start(bf16[64,4,1,128]{3,0,2,1:T(8,128)(2,1)S(1)} %get-tuple-element.74), channel_id=1, source_target_pairs={{1,0},{2,1},{3,2},{4,3},{5,4},{6,5},{7,6},{9,8},{10,9},{11,10},{12... | collective-permute-start | bytes 196616 | tf_op jit(solution)/shard_map/ppermute | solution.py:22
  126.4 2.4 %collective-permute-start.10 = (bf16[64,4,1,128]{3,0,2,1:T(8,128)(2,1)S(1)}, bf16[64,4,1,128]{3,0,2,1:T(8,128)(2,1)S(1)}, u32[]{:S(2)}, u32[]{:S(2)}) collective-permute-start(bf16[64,4,1,128]{3,0,2,1:T(8,128)(2,1)S(1)} %get-tuple-element.73), channel_id=1, source_target_pairs={{0,1},{1,2},{2,3},{3,4},{4,5},{5,6},{6,7},{8,9},{9,10},{10,11},{11... | collective-permute-start | bytes 196616 | tf_op jit(solution)/shard_map/ppermute | solution.py:20
  128.8 1.3 collective-permute-done.14
  130.9 8.1 %all-to-all-start.1 = ((f32[64,1,607]{2,1,0:T(1,128)}), f32[64,1,607]{2,1,0:T(1,128)S(1)}, u32[]{:S(2)}, u32[]{:S(2)}) async-start(f32[64,1,607]{2,1,0:T(1,128)} %broadcast_in_dim.23), calls=%async_computation.1 | async-start | bytes 327680 | tf_op jit(solution)/shard_map/all_to_all | solution.py:197
  144.8 1.8 %reshape.110 = f32[4,8,256]{2,1,0:T(8,128)} reshape(f32[2,2,4,2,128,2]{5,4,3,2,1,0:T(8,128)S(1)} %bitcast.1139) | data formatting | bytes 65536 | tf_op jit(solution)/shard_map/reshape | solution.py:50
  147.2 2.2 %all-to-all-done.1 = f32[64,1,607]{2,1,0:T(1,128)S(1)} async-done(((f32[64,1,607]{2,1,0:T(1,128)}), f32[64,1,607]{2,1,0:T(1,128)S(1)}, u32[]{:S(2)}, u32[]{:S(2)}) %all-to-all-start.1) | async-done | bytes 155424 | tf_op jit(solution)/shard_map/all_to_all | solution.py:197
  151.9 1.1 copy.754
  (236 shorter events, 47.1 us)
Async XLA Ops:
  0.6 32.1 %copy-start = (bf16[64,64]{1,0:T(8,128)(2,1)S(1)}, bf16[64,64]{1,0:T(8,128)(2,1)}, u32[]{:S(2)}) copy-start(bf16[64,64]{1,0:T(8,128)(2,1)} %param.13) | copy-start | bytes 24580
  2.2 10.4 %collective-permute-start = (bf16[12,2,4,128]{3,0,2,1:T(8,128)(2,1)S(1)}, bf16[12,2,4,128]{3,0,2,1:T(8,128)(2,1)S(1)}, u32[]{:S(2)}, u32[]{:S(2)}) collective-permute-start(bf16[12,2,4,128]{3,0,2,1:T(8,128)(2,1)S(1)} %pad_maximum_fusion.22), channel_id=1, source_target_pairs={{0,8},{8,16},{16,24},{24,32},{32,40},{40,48},{48,56},{56,64},{64,7... | collective-permute-start | bytes 73736 | tf_op jit(solution)/shard_map/ppermute | solution.py:20
  7.3 6.7 %collective-permute-start.1 = (bf16[12,2,4,128]{3,0,2,1:T(8,128)(2,1)S(1)}, bf16[12,2,4,128]{3,0,2,1:T(8,128)(2,1)S(1)}, u32[]{:S(2)}, u32[]{:S(2)}) collective-permute-start(bf16[12,2,4,128]{3,0,2,1:T(8,128)(2,1)S(1)} %pad_maximum_fusion.22), channel_id=1, source_target_pairs={{8,0},{16,8},{24,16},{32,24},{40,32},{48,40},{56,48},{64,56},{72,6... | collective-permute-start | bytes 73736 | tf_op jit(solution)/shard_map/ppermute | solution.py:22
  14.0 7.2 %collective-permute-start.2 = (bf16[12,6,2,128]{3,0,2,1:T(8,128)(2,1)S(1)}, bf16[12,6,2,128]{3,0,2,1:T(8,128)(2,1)S(1)}, u32[]{:S(2)}, u32[]{:S(2)}) collective-permute-start(bf16[12,6,2,128]{3,0,2,1:T(8,128)(2,1)S(1)} %get-tuple-element.128), channel_id=1, source_target_pairs={{0,1},{1,2},{2,3},{3,4},{4,5},{5,6},{6,7},{8,9},{9,10},{10,11},{11... | collective-permute-start | bytes 110600 | tf_op jit(solution)/shard_map/ppermute | solution.py:20
  15.9 6.3 %collective-permute-start.3 = (bf16[12,6,2,128]{3,0,2,1:T(8,128)(2,1)S(1)}, bf16[12,6,2,128]{3,0,2,1:T(8,128)(2,1)S(1)}, u32[]{:S(2)}, u32[]{:S(2)}) collective-permute-start(bf16[12,6,2,128]{3,0,2,1:T(8,128)(2,1)S(1)} %get-tuple-element.129), channel_id=1, source_target_pairs={{1,0},{2,1},{3,2},{4,3},{5,4},{6,5},{7,6},{9,8},{10,9},{11,10},{12... | collective-permute-start | bytes 110600 | tf_op jit(solution)/shard_map/ppermute | solution.py:22
  33.9 0.8 copy-start.1
  42.9 6.1 %collective-permute-start.4 = (bf16[8,1,4,128]{3,0,2,1:T(8,128)(2,1)S(1)}, bf16[8,1,4,128]{3,0,2,1:T(8,128)(2,1)S(1)}, u32[]{:S(2)}, u32[]{:S(2)}) collective-permute-start(bf16[8,1,4,128]{3,0,2,1:T(8,128)(2,1)S(1)} %get-tuple-element.141), channel_id=1, source_target_pairs={{0,8},{8,16},{16,24},{24,32},{32,40},{40,48},{48,56},{56,64},{64,7... | collective-permute-start | bytes 24584 | tf_op jit(solution)/shard_map/ppermute | solution.py:20
  46.4 6.4 %collective-permute-start.5 = (bf16[8,1,4,128]{3,0,2,1:T(8,128)(2,1)S(1)}, bf16[8,1,4,128]{3,0,2,1:T(8,128)(2,1)S(1)}, u32[]{:S(2)}, u32[]{:S(2)}) collective-permute-start(bf16[8,1,4,128]{3,0,2,1:T(8,128)(2,1)S(1)} %get-tuple-element.142), channel_id=1, source_target_pairs={{8,0},{16,8},{24,16},{32,24},{40,32},{48,40},{56,48},{64,56},{72,6... | collective-permute-start | bytes 24584 | tf_op jit(solution)/shard_map/ppermute | solution.py:22
  52.9 5.5 %collective-permute-start.7 = (bf16[8,4,1,128]{3,0,2,1:T(8,128)(2,1)S(1)}, bf16[8,4,1,128]{3,0,2,1:T(8,128)(2,1)S(1)}, u32[]{:S(2)}, u32[]{:S(2)}) collective-permute-start(bf16[8,4,1,128]{3,0,2,1:T(8,128)(2,1)S(1)} %get-tuple-element.138), channel_id=1, source_target_pairs={{1,0},{2,1},{3,2},{4,3},{5,4},{6,5},{7,6},{9,8},{10,9},{11,10},{12... | collective-permute-start | bytes 24584 | tf_op jit(solution)/shard_map/ppermute | solution.py:22
  56.0 5.9 %collective-permute-start.6 = (bf16[8,4,1,128]{3,0,2,1:T(8,128)(2,1)S(1)}, bf16[8,4,1,128]{3,0,2,1:T(8,128)(2,1)S(1)}, u32[]{:S(2)}, u32[]{:S(2)}) collective-permute-start(bf16[8,4,1,128]{3,0,2,1:T(8,128)(2,1)S(1)} %get-tuple-element.137), channel_id=1, source_target_pairs={{0,1},{1,2},{2,3},{3,4},{4,5},{5,6},{6,7},{8,9},{9,10},{10,11},{11... | collective-permute-start | bytes 24584 | tf_op jit(solution)/shard_map/ppermute | solution.py:20
  74.1 40.6 %copy-start.2 = (f32[8,8,1,1]{1,0,3,2:T(8,128)S(1)}, f32[8,8,1,1]{1,0,3,2:T(8,128)}, u32[]{:S(2)}) copy-start(f32[8,8,1,1]{1,0,3,2:T(8,128)} %constant.54) | copy-start | bytes 772
  76.0 26.3 %all-to-all-start = ((f32[64,1,607]{2,1,0:T(1,128)}), f32[64,1,607]{2,1,0:T(1,128)S(1)}, u32[]{:S(2)}, u32[]{:S(2)}) async-start(f32[64,1,607]{2,1,0:T(1,128)} %all_to_all.10), calls=%async_computation | async-start | bytes 327680 | tf_op jit(solution)/shard_map/all_to_all | solution.py:191
  102.4 4.6 %collective-permute-start.12 = (f32[607]{0:T(1024)S(1)}, f32[607]{0:T(1024)S(1)}, u32[]{:S(2)}, u32[]{:S(2)}) collective-permute-start(f32[607]{0:T(1024)S(1)} %reduce_sum.39), channel_id=1, source_target_pairs={{0,1},{1,0},{2,3},{3,2},{4,5},{5,4},{6,7},{7,6},{8,9},{9,8},{10,11... | collective-permute-start | bytes 7292 | tf_op jit(solution)/shard_map/ppermute | solution.py:119
  104.4 18.2 %collective-permute-start.8 = (bf16[64,1,4,128]{3,0,2,1:T(8,128)(2,1)S(1)}, bf16[64,1,4,128]{3,0,2,1:T(8,128)(2,1)S(1)}, u32[]{:S(2)}, u32[]{:S(2)}) collective-permute-start(bf16[64,1,4,128]{3,0,2,1:T(8,128)(2,1)S(1)} %get-tuple-element.100), channel_id=1, source_target_pairs={{0,8},{8,16},{16,24},{24,32},{32,40},{40,48},{48,56},{56,64},{64,7... | collective-permute-start | bytes 196616 | tf_op jit(solution)/shard_map/ppermute | solution.py:20
  107.0 13.6 %collective-permute-start.13 = (f32[607]{0:T(1024)S(1)}, f32[607]{0:T(1024)S(1)}, u32[]{:S(2)}, u32[]{:S(2)}) collective-permute-start(f32[607]{0:T(1024)S(1)} %add.552), channel_id=1, source_target_pairs={{0,2},{1,3},{2,0},{3,1},{4,6},{5,7},{6,4},{7,5},{8,10},{9,11},{10,... | collective-permute-start | bytes 7292 | tf_op jit(solution)/shard_map/ppermute | solution.py:119
  117.4 7.0 %collective-permute-start.9 = (bf16[64,1,4,128]{3,0,2,1:T(8,128)(2,1)S(1)}, bf16[64,1,4,128]{3,0,2,1:T(8,128)(2,1)S(1)}, u32[]{:S(2)}, u32[]{:S(2)}) collective-permute-start(bf16[64,1,4,128]{3,0,2,1:T(8,128)(2,1)S(1)} %get-tuple-element.99), channel_id=1, source_target_pairs={{8,0},{16,8},{24,16},{32,24},{40,32},{48,40},{56,48},{64,56},{72,6... | collective-permute-start | bytes 196616 | tf_op jit(solution)/shard_map/ppermute | solution.py:22
  120.6 9.5 %collective-permute-start.14 = (f32[607]{0:T(1024)S(1)}, f32[607]{0:T(1024)S(1)}, u32[]{:S(2)}, u32[]{:S(2)}) collective-permute-start(f32[607]{0:T(1024)S(1)} %add.553), channel_id=1, source_target_pairs={{0,4},{1,5},{2,6},{3,7},{4,0},{5,1},{6,2},{7,3},{8,12},{9,13},{10,... | collective-permute-start | bytes 7292 | tf_op jit(solution)/shard_map/ppermute | solution.py:119
  124.5 14.5 %collective-permute-start.11 = (bf16[64,4,1,128]{3,0,2,1:T(8,128)(2,1)S(1)}, bf16[64,4,1,128]{3,0,2,1:T(8,128)(2,1)S(1)}, u32[]{:S(2)}, u32[]{:S(2)}) collective-permute-start(bf16[64,4,1,128]{3,0,2,1:T(8,128)(2,1)S(1)} %get-tuple-element.74), channel_id=1, source_target_pairs={{1,0},{2,1},{3,2},{4,3},{5,4},{6,5},{7,6},{9,8},{10,9},{11,10},{12... | collective-permute-start | bytes 196616 | tf_op jit(solution)/shard_map/ppermute | solution.py:22
  126.4 12.6 %collective-permute-start.10 = (bf16[64,4,1,128]{3,0,2,1:T(8,128)(2,1)S(1)}, bf16[64,4,1,128]{3,0,2,1:T(8,128)(2,1)S(1)}, u32[]{:S(2)}, u32[]{:S(2)}) collective-permute-start(bf16[64,4,1,128]{3,0,2,1:T(8,128)(2,1)S(1)} %get-tuple-element.73), channel_id=1, source_target_pairs={{0,1},{1,2},{2,3},{3,4},{4,5},{5,6},{6,7},{8,9},{9,10},{10,11},{11... | collective-permute-start | bytes 196616 | tf_op jit(solution)/shard_map/ppermute | solution.py:20
  130.9 18.5 %all-to-all-start.1 = ((f32[64,1,607]{2,1,0:T(1,128)}), f32[64,1,607]{2,1,0:T(1,128)S(1)}, u32[]{:S(2)}, u32[]{:S(2)}) async-start(f32[64,1,607]{2,1,0:T(1,128)} %broadcast_in_dim.23), calls=%async_computation.1 | async-start | bytes 327680 | tf_op jit(solution)/shard_map/all_to_all | solution.py:197

commit v7 on v6

--- a/solution.py
+++ b/solution.py
@@ -55,49 +55,58 @@
     return sigma * (1.0 + preact * (1.0 - sigma))
 
 
+def y_shifts(padded):
+    y_cols = padded.shape[3] - 2
+    return jnp.stack([padded[..., y_step : y_step + y_cols] for y_step in range(3)])
+
+
 def forward_taps(padded, weight, planes, x_rows):
-    y_cols = padded.shape[3] - 2
+    stacked = y_shifts(padded)
+    kernel = weight.reshape((3, 3, 3) + weight.shape[1:])
     summed = None
-    for tap_index in range(27):
-        z_step, x_step, y_step = (tap_index // 9, tap_index // 3 % 3, tap_index % 3)
-        sliced = padded[
-            :, z_step : z_step + planes, x_step : x_step + x_rows, y_step : y_step + y_cols
-        ]
-        product = jnp.einsum(
-            "oc,czxy->ozxy", weight[tap_index], sliced, preferred_element_type=jnp.float32
-        )
-        summed = product if summed is None else summed + product
+    for z_step in range(3):
+        for x_step in range(3):
+            product = jnp.einsum(
+                "eoc,eczxy->ozxy",
+                kernel[z_step, x_step],
+                stacked[:, :, z_step : z_step + planes, x_step : x_step + x_rows],
+                preferred_element_type=jnp.float32,
+            )
+            summed = product if summed is None else summed + product
     return summed
 
 
 def backward_taps(padded, weight, planes, x_rows):
-    y_cols = padded.shape[3] - 2
+    stacked = y_shifts(padded)
+    kernel = weight.reshape((3, 3, 3) + weight.shape[1:])
     summed = None
-    for tap_index in range(27):
-        z_step, x_step, y_step = (tap_index // 9, tap_index // 3 % 3, tap_index % 3)
-        sliced = padded[
-            :,
-            2 - z_step : 2 - z_step + planes,
-            2 - x_step : 2 - x_step + x_rows,
-            2 - y_step : 2 - y_step + y_cols,
-        ]
-        product = jnp.einsum(
-            "oc,ozxy->czxy", weight[tap_index], sliced, preferred_element_type=jnp.float32
-        )
-        summed = product if summed is None else summed + product
+    for z_step in range(3):
+        for x_step in range(3):
+            product = jnp.einsum(
+                "eoc,eozxy->czxy",
+                kernel[z_step, x_step, ::-1],
+                stacked[:, :, 2 - z_step : 2 - z_step + planes, 2 - x_step : 2 - x_step + x_rows],
+                preferred_element_type=jnp.float32,
+            )
+            summed = product if summed is None else summed + product
     return summed
 
 
 def weight_taps(grad, padded):
-    planes, x_rows, y_cols = (grad.shape[1], grad.shape[2], grad.shape[3])
+    planes, x_rows = (grad.shape[1], grad.shape[2])
+    stacked = y_shifts(padded)
     result = []
-    for tap_index in range(27):
-        z_step, x_step, y_step = (tap_index // 9, tap_index // 3 % 3, tap_index % 3)
-        sliced = padded[
-            :, z_step : z_step + planes, x_step : x_step + x_rows, y_step : y_step + y_cols
-        ]
-        result.append(jnp.einsum("ozxy,czxy->oc", grad, sliced, preferred_element_type=jnp.float32))
-    return jnp.stack(result)
+    for z_step in range(3):
+        for x_step in range(3):
+            result.append(
+                jnp.einsum(
+                    "ozxy,eczxy->eoc",
+                    grad,
+                    stacked[:, :, z_step : z_step + planes, x_step : x_step + x_rows],
+                    preferred_element_type=jnp.float32,
+                )
+            )
+    return jnp.concatenate(result)
 
 
 def frame_cols(tensor):

time: 156 us -> 135 us (0.87)
  matrix products: 35.1 us -> 13.8 us
  starting transfers between devices: 70.1 us -> 74.7 us
  waiting for transfers between devices: 25.5 us -> 21.7 us
    dot_general x162 -> x54, matrix products: 32.9 us -> 12.6 us  [the longest x18 5 us: forward_taps(): jnp.einsum('eoc,eczxy->ozxy', kernel[z_step, x_step], stacked[:, :, z_ste...]
    ppermute x6, starting transfers between devices: 17.1 us -> 21.7 us  [extended(): lax.ppermute(head, axis, [((i + 1) % count, i) for i in range(ends)])]
    ppermute x6, waiting for transfers between devices: 3.53 us -> 0.02 us  [extended(): lax.ppermute(tail, axis, [(i, (i + 1) % count) for i in range(ends)])]
    all_to_all x1, waiting for transfers between devices: 2.22 us -> 4.05 us  [per_device(): lax.all_to_all(jnp.broadcast_to(owned, (count,) + owned.shape), 'gz', 0,...]
    unnamed x14 -> x15, local copies, waits for them, and re-layouts: 3.05 us -> 3.42 us
  transfers between devices with their start and end apart: 17 -> 17, of which waited for: 8 -> 5; matrix products, arithmetic and copies ran while one was open for 11% -> 10% of each run, Pallas kernels for 0% -> 0%
where the time goes in v7:
time: 135 us; the launch traced here: 134 us
  starting transfers between devices  74.7 us (55%)
  waiting for transfers between devices  21.7 us (16%)
  local copies, waits for them, and re-layouts  20.6 us (15%)
  matrix products  13.8 us (10%)
  other arithmetic  1.83 us (1%)
  between operations  1.71 us (1%)
    ppermute x6, starting transfers between devices, extended(): lax.ppermute(head, axis, [((i + 1) % count, i) for i in range(ends)])  21.7 us
    ppermute x6, starting transfers between devices, extended(): lax.ppermute(tail, axis, [(i, (i + 1) % count) for i in range(ends)])  16.3 us
    all_to_all x1, starting transfers between devices, per_device(): owned = lax.all_to_all(chunks, 'gz', 0, 0, tiled=False).sum(0)  14.9 us
    ppermute x3, starting transfers between devices, butterfly_sum(): flat = flat + lax.ppermute(flat, axis, [(i, i ^ bit) for i in range(count)])  12.7 us
    all_to_all x1, waiting for transfers between devices, per_device(): owned = lax.all_to_all(chunks, 'gz', 0, 0, tiled=False).sum(0)  10.3 us
    all_to_all x1, starting transfers between devices, per_device(): lax.all_to_all(jnp.broadcast_to(owned, (count,) + owned.shape), 'gz', 0,...  8.96 us
    ppermute x6, waiting for transfers between devices, extended(): lax.ppermute(head, axis, [((i + 1) % count, i) for i in range(ends)])  7.29 us
    dot_general x18, matrix products, forward_taps(): jnp.einsum('eoc,eczxy->ozxy', kernel[z_step, x_step], stacked[:, :, z_ste...  5 us
  transfers between devices with their start and end apart: 17, of which 5 were waited for; matrix products, arithmetic and copies ran while one was open for 10% of the time, Pallas kernels for 0%

profile of v7, /device:TPU:56, one launch (start us, length us, event | category | flops | bytes accessed | tf_op | source)
XLA Modules:
  0.0 134.3 jit_solution(18065339724872838465)
XLA Ops:
  0.6 0.8 fusion.170
  2.2 5.1 %collective-permute-start = (bf16[12,2,4,128]{3,0,2,1:T(8,128)(2,1)S(1)}, bf16[12,2,4,128]{3,0,2,1:T(8,128)(2,1)S(1)}, u32[]{:S(2)}, u32[]{:S(2)}) collective-permute-start(bf16[12,2,4,128]{3,0,2,1:T(8,128)(2,1)S(1)} %pad_maximum_fusion.9), channel_id=1, source_target_pairs={{0,8},{8,16},{16,24},{24,32},{32,40},{40,48},{48,56},{56,64},{64,7... | collective-permute-start | bytes 73736 | tf_op jit(solution)/shard_map/ppermute | solution.py:20
  7.3 1.9 %collective-permute-start.1 = (bf16[12,2,4,128]{3,0,2,1:T(8,128)(2,1)S(1)}, bf16[12,2,4,128]{3,0,2,1:T(8,128)(2,1)S(1)}, u32[]{:S(2)}, u32[]{:S(2)}) collective-permute-start(bf16[12,2,4,128]{3,0,2,1:T(8,128)(2,1)S(1)} %pad_maximum_fusion.9), channel_id=1, source_target_pairs={{8,0},{16,8},{24,16},{32,24},{40,32},{48,40},{56,48},{64,56},{72,6... | collective-permute-start | bytes 73736 | tf_op jit(solution)/shard_map/ppermute | solution.py:22
  9.2 0.8 fusion.172
  10.0 0.8 fusion.169
  10.9 3.1 %collective-permute-done.1 = bf16[12,2,4,128]{3,0,2,1:T(8,128)(2,1)S(1)} collective-permute-done((bf16[12,2,4,128]{3,0,2,1:T(8,128)(2,1)S(1)}, bf16[12,2,4,128]{3,0,2,1:T(8,128)(2,1)S(1)}, u32[]{:S(2)}, u32[]{:S(2)}) %collective-permute-start.1) | collective-permute-done | bytes 24608 | tf_op jit(solution)/shard_map/ppermute | solution.py:22
  14.0 1.9 %collective-permute-start.2 = (bf16[12,6,2,128]{3,0,2,1:T(8,128)(2,1)S(1)}, bf16[12,6,2,128]{3,0,2,1:T(8,128)(2,1)S(1)}, u32[]{:S(2)}, u32[]{:S(2)}) collective-permute-start(bf16[12,6,2,128]{3,0,2,1:T(8,128)(2,1)S(1)} %get-tuple-element.99), channel_id=1, source_target_pairs={{0,1},{1,2},{2,3},{3,4},{4,5},{5,6},{6,7},{8,9},{9,10},{10,11},{11... | collective-permute-start | bytes 110600 | tf_op jit(solution)/shard_map/ppermute | solution.py:20
  15.9 4.5 %collective-permute-start.3 = (bf16[12,6,2,128]{3,0,2,1:T(8,128)(2,1)S(1)}, bf16[12,6,2,128]{3,0,2,1:T(8,128)(2,1)S(1)}, u32[]{:S(2)}, u32[]{:S(2)}) collective-permute-start(bf16[12,6,2,128]{3,0,2,1:T(8,128)(2,1)S(1)} %get-tuple-element.100), channel_id=1, source_target_pairs={{1,0},{2,1},{3,2},{4,3},{5,4},{6,5},{7,6},{9,8},{10,9},{11,10},{12... | collective-permute-start | bytes 110600 | tf_op jit(solution)/shard_map/ppermute | solution.py:22
  21.2 0.9 copy.299
  26.6 0.9 fusion.163
  31.7 2.9 %collective-permute-start.4 = (bf16[8,1,4,128]{3,0,2,1:T(8,128)(2,1)S(1)}, bf16[8,1,4,128]{3,0,2,1:T(8,128)(2,1)S(1)}, u32[]{:S(2)}, u32[]{:S(2)}) collective-permute-start(bf16[8,1,4,128]{3,0,2,1:T(8,128)(2,1)S(1)} %get-tuple-element.121), channel_id=1, source_target_pairs={{0,8},{8,16},{16,24},{24,32},{32,40},{40,48},{48,56},{56,64},{64,7... | collective-permute-start | bytes 24584 | tf_op jit(solution)/shard_map/ppermute | solution.py:20
  34.5 3.0 %collective-permute-start.5 = (bf16[8,1,4,128]{3,0,2,1:T(8,128)(2,1)S(1)}, bf16[8,1,4,128]{3,0,2,1:T(8,128)(2,1)S(1)}, u32[]{:S(2)}, u32[]{:S(2)}) collective-permute-start(bf16[8,1,4,128]{3,0,2,1:T(8,128)(2,1)S(1)} %get-tuple-element.122), channel_id=1, source_target_pairs={{8,0},{16,8},{24,16},{32,24},{40,32},{48,40},{56,48},{64,56},{72,6... | collective-permute-start | bytes 24584 | tf_op jit(solution)/shard_map/ppermute | solution.py:22
  37.8 3.2 %collective-permute-done.5 = bf16[8,1,4,128]{3,0,2,1:T(8,128)(2,1)S(1)} collective-permute-done((bf16[8,1,4,128]{3,0,2,1:T(8,128)(2,1)S(1)}, bf16[8,1,4,128]{3,0,2,1:T(8,128)(2,1)S(1)}, u32[]{:S(2)}, u32[]{:S(2)}) %collective-permute-start.5) | collective-permute-done | bytes 8224 | tf_op jit(solution)/shard_map/ppermute | solution.py:22
  41.0 1.9 %collective-permute-start.6 = (bf16[8,4,1,128]{3,0,2,1:T(8,128)(2,1)S(1)}, bf16[8,4,1,128]{3,0,2,1:T(8,128)(2,1)S(1)}, u32[]{:S(2)}, u32[]{:S(2)}) collective-permute-start(bf16[8,4,1,128]{3,0,2,1:T(8,128)(2,1)S(1)} %get-tuple-element.117), channel_id=1, source_target_pairs={{0,1},{1,2},{2,3},{3,4},{4,5},{5,6},{6,7},{8,9},{9,10},{10,11},{11... | collective-permute-start | bytes 24584 | tf_op jit(solution)/shard_map/ppermute | solution.py:20
  42.9 4.5 %collective-permute-start.7 = (bf16[8,4,1,128]{3,0,2,1:T(8,128)(2,1)S(1)}, bf16[8,4,1,128]{3,0,2,1:T(8,128)(2,1)S(1)}, u32[]{:S(2)}, u32[]{:S(2)}) collective-permute-start(bf16[8,4,1,128]{3,0,2,1:T(8,128)(2,1)S(1)} %get-tuple-element.118), channel_id=1, source_target_pairs={{1,0},{2,1},{3,2},{4,3},{5,4},{6,5},{7,6},{9,8},{10,9},{11,10},{12... | collective-permute-start | bytes 24584 | tf_op jit(solution)/shard_map/ppermute | solution.py:22
  47.8 1.0 collective-permute-done.7
  54.8 1.0 all_to_all.10
  55.8 14.9 %all-to-all-start = ((f32[64,1,607]{2,1,0:T(1,128)}), f32[64,1,607]{2,1,0:T(1,128)S(1)}, u32[]{:S(2)}, u32[]{:S(2)}) async-start(f32[64,1,607]{2,1,0:T(1,128)} %all_to_all.10), calls=%async_computation | async-start | bytes 327680 | tf_op jit(solution)/shard_map/all_to_all | solution.py:200
  70.9 10.3 %all-to-all-done = f32[64,1,607]{2,1,0:T(1,128)S(1)} async-done(((f32[64,1,607]{2,1,0:T(1,128)}), f32[64,1,607]{2,1,0:T(1,128)S(1)}, u32[]{:S(2)}, u32[]{:S(2)}) %all-to-all-start) | async-done | bytes 155424 | tf_op jit(solution)/shard_map/all_to_all | solution.py:200
  81.4 1.9 %collective-permute-start.12 = (f32[607]{0:T(1024)S(1)}, f32[607]{0:T(1024)S(1)}, u32[]{:S(2)}, u32[]{:S(2)}) collective-permute-start(f32[607]{0:T(1024)S(1)} %reduce_sum.39), channel_id=1, source_target_pairs={{0,1},{1,0},{2,3},{3,2},{4,5},{5,4},{6,7},{7,6},{8,9},{9,8},{10,11... | collective-permute-start | bytes 7292 | tf_op jit(solution)/shard_map/ppermute | solution.py:128
  83.3 2.6 %collective-permute-start.8 = (bf16[64,1,4,128]{3,0,2,1:T(8,128)(2,1)S(1)}, bf16[64,1,4,128]{3,0,2,1:T(8,128)(2,1)S(1)}, u32[]{:S(2)}, u32[]{:S(2)}) collective-permute-start(bf16[64,1,4,128]{3,0,2,1:T(8,128)(2,1)S(1)} %get-tuple-element.89), channel_id=1, source_target_pairs={{0,8},{8,16},{16,24},{24,32},{32,40},{40,48},{48,56},{56,64},{64,7... | collective-permute-start | bytes 196616 | tf_op jit(solution)/shard_map/ppermute | solution.py:20
  86.0 6.7 %collective-permute-start.13 = (f32[607]{0:T(1024)S(1)}, f32[607]{0:T(1024)S(1)}, u32[]{:S(2)}, u32[]{:S(2)}) collective-permute-start(f32[607]{0:T(1024)S(1)} %add.264), channel_id=1, source_target_pairs={{0,2},{1,3},{2,0},{3,1},{4,6},{5,7},{6,4},{7,5},{8,10},{9,11},{10,... | collective-permute-start | bytes 7292 | tf_op jit(solution)/shard_map/ppermute | solution.py:128
  93.5 1.8 %reshape.115 = f32[4,8,256]{2,1,0:T(8,128)} reshape(f32[2,2,4,2,128,2]{5,4,3,2,1,0:T(8,128)S(1)} %bitcast.691) | data formatting | bytes 65536 | tf_op jit(solution)/shard_map/reshape | solution.py:50
  95.3 3.2 %collective-permute-start.9 = (bf16[64,1,4,128]{3,0,2,1:T(8,128)(2,1)S(1)}, bf16[64,1,4,128]{3,0,2,1:T(8,128)(2,1)S(1)}, u32[]{:S(2)}, u32[]{:S(2)}) collective-permute-start(bf16[64,1,4,128]{3,0,2,1:T(8,128)(2,1)S(1)} %get-tuple-element.88), channel_id=1, source_target_pairs={{8,0},{16,8},{24,16},{32,24},{40,32},{48,40},{56,48},{64,56},{72,6... | collective-permute-start | bytes 196616 | tf_op jit(solution)/shard_map/ppermute | solution.py:22
  98.5 4.1 %collective-permute-start.14 = (f32[607]{0:T(1024)S(1)}, f32[607]{0:T(1024)S(1)}, u32[]{:S(2)}, u32[]{:S(2)}) collective-permute-start(f32[607]{0:T(1024)S(1)} %add.265), channel_id=1, source_target_pairs={{0,4},{1,5},{2,6},{3,7},{4,0},{5,1},{6,2},{7,3},{8,12},{9,13},{10,... | collective-permute-start | bytes 7292 | tf_op jit(solution)/shard_map/ppermute | solution.py:128
  102.8 1.9 %collective-permute-start.10 = (bf16[64,4,1,128]{3,0,2,1:T(8,128)(2,1)S(1)}, bf16[64,4,1,128]{3,0,2,1:T(8,128)(2,1)S(1)}, u32[]{:S(2)}, u32[]{:S(2)}) collective-permute-start(bf16[64,4,1,128]{3,0,2,1:T(8,128)(2,1)S(1)} %get-tuple-element.72), channel_id=1, source_target_pairs={{0,1},{1,2},{2,3},{3,4},{4,5},{5,6},{6,7},{8,9},{9,10},{10,11},{11... | collective-permute-start | bytes 196616 | tf_op jit(solution)/shard_map/ppermute | solution.py:20
  104.7 4.5 %collective-permute-start.11 = (bf16[64,4,1,128]{3,0,2,1:T(8,128)(2,1)S(1)}, bf16[64,4,1,128]{3,0,2,1:T(8,128)(2,1)S(1)}, u32[]{:S(2)}, u32[]{:S(2)}) collective-permute-start(bf16[64,4,1,128]{3,0,2,1:T(8,128)(2,1)S(1)} %get-tuple-element.73), channel_id=1, source_target_pairs={{1,0},{2,1},{3,2},{4,3},{5,4},{6,5},{7,6},{9,8},{10,9},{11,10},{12... | collective-permute-start | bytes 196616 | tf_op jit(solution)/shard_map/ppermute | solution.py:22
  110.0 9.0 %all-to-all-start.1 = ((f32[64,1,607]{2,1,0:T(1,128)}), f32[64,1,607]{2,1,0:T(1,128)S(1)}, u32[]{:S(2)}, u32[]{:S(2)}) async-start(f32[64,1,607]{2,1,0:T(1,128)} %broadcast_in_dim.23), calls=%async_computation.1 | async-start | bytes 327680 | tf_op jit(solution)/shard_map/all_to_all | solution.py:206
  123.0 1.8 %reshape.120 = f32[4,8,256]{2,1,0:T(8,128)} reshape(f32[2,2,4,2,128,2]{5,4,3,2,1,0:T(8,128)S(1)} %bitcast.692) | data formatting | bytes 65536 | tf_op jit(solution)/shard_map/reshape | solution.py:50
  125.4 4.1 %all-to-all-done.1 = f32[64,1,607]{2,1,0:T(1,128)S(1)} async-done(((f32[64,1,607]{2,1,0:T(1,128)}), f32[64,1,607]{2,1,0:T(1,128)S(1)}, u32[]{:S(2)}, u32[]{:S(2)}) %all-to-all-start.1) | async-done | bytes 155424 | tf_op jit(solution)/shard_map/all_to_all | solution.py:206
  130.9 1.0 reshape.122
  131.9 1.1 copy.382
  (158 shorter events, 25.3 us)
Async XLA Ops:
  0.6 25.1 %copy-start = (bf16[64,64]{1,0:T(8,128)(2,1)S(1)}, bf16[64,64]{1,0:T(8,128)(2,1)}, u32[]{:S(2)}) copy-start(bf16[64,64]{1,0:T(8,128)(2,1)} %param.13) | copy-start | bytes 24580
  2.2 8.7 %collective-permute-start = (bf16[12,2,4,128]{3,0,2,1:T(8,128)(2,1)S(1)}, bf16[12,2,4,128]{3,0,2,1:T(8,128)(2,1)S(1)}, u32[]{:S(2)}, u32[]{:S(2)}) collective-permute-start(bf16[12,2,4,128]{3,0,2,1:T(8,128)(2,1)S(1)} %pad_maximum_fusion.9), channel_id=1, source_target_pairs={{0,8},{8,16},{16,24},{24,32},{32,40},{40,48},{48,56},{56,64},{64,7... | collective-permute-start | bytes 73736 | tf_op jit(solution)/shard_map/ppermute | solution.py:20
  7.3 6.7 %collective-permute-start.1 = (bf16[12,2,4,128]{3,0,2,1:T(8,128)(2,1)S(1)}, bf16[12,2,4,128]{3,0,2,1:T(8,128)(2,1)S(1)}, u32[]{:S(2)}, u32[]{:S(2)}) collective-permute-start(bf16[12,2,4,128]{3,0,2,1:T(8,128)(2,1)S(1)} %pad_maximum_fusion.9), channel_id=1, source_target_pairs={{8,0},{16,8},{24,16},{32,24},{40,32},{48,40},{56,48},{64,56},{72,6... | collective-permute-start | bytes 73736 | tf_op jit(solution)/shard_map/ppermute | solution.py:22
  14.0 8.3 %collective-permute-start.2 = (bf16[12,6,2,128]{3,0,2,1:T(8,128)(2,1)S(1)}, bf16[12,6,2,128]{3,0,2,1:T(8,128)(2,1)S(1)}, u32[]{:S(2)}, u32[]{:S(2)}) collective-permute-start(bf16[12,6,2,128]{3,0,2,1:T(8,128)(2,1)S(1)} %get-tuple-element.99), channel_id=1, source_target_pairs={{0,1},{1,2},{2,3},{3,4},{4,5},{5,6},{6,7},{8,9},{9,10},{10,11},{11... | collective-permute-start | bytes 110600 | tf_op jit(solution)/shard_map/ppermute | solution.py:20
  15.9 6.4 %collective-permute-start.3 = (bf16[12,6,2,128]{3,0,2,1:T(8,128)(2,1)S(1)}, bf16[12,6,2,128]{3,0,2,1:T(8,128)(2,1)S(1)}, u32[]{:S(2)}, u32[]{:S(2)}) collective-permute-start(bf16[12,6,2,128]{3,0,2,1:T(8,128)(2,1)S(1)} %get-tuple-element.100), channel_id=1, source_target_pairs={{1,0},{2,1},{3,2},{4,3},{5,4},{6,5},{7,6},{9,8},{10,9},{11,10},{12... | collective-permute-start | bytes 110600 | tf_op jit(solution)/shard_map/ppermute | solution.py:22
  26.6 0.9 copy-start.1
  31.7 6.1 %collective-permute-start.4 = (bf16[8,1,4,128]{3,0,2,1:T(8,128)(2,1)S(1)}, bf16[8,1,4,128]{3,0,2,1:T(8,128)(2,1)S(1)}, u32[]{:S(2)}, u32[]{:S(2)}) collective-permute-start(bf16[8,1,4,128]{3,0,2,1:T(8,128)(2,1)S(1)} %get-tuple-element.121), channel_id=1, source_target_pairs={{0,8},{8,16},{16,24},{24,32},{32,40},{40,48},{48,56},{56,64},{64,7... | collective-permute-start | bytes 24584 | tf_op jit(solution)/shard_map/ppermute | solution.py:20
  34.5 6.4 %collective-permute-start.5 = (bf16[8,1,4,128]{3,0,2,1:T(8,128)(2,1)S(1)}, bf16[8,1,4,128]{3,0,2,1:T(8,128)(2,1)S(1)}, u32[]{:S(2)}, u32[]{:S(2)}) collective-permute-start(bf16[8,1,4,128]{3,0,2,1:T(8,128)(2,1)S(1)} %get-tuple-element.122), channel_id=1, source_target_pairs={{8,0},{16,8},{24,16},{32,24},{40,32},{48,40},{56,48},{64,56},{72,6... | collective-permute-start | bytes 24584 | tf_op jit(solution)/shard_map/ppermute | solution.py:22
  41.0 6.8 %collective-permute-start.6 = (bf16[8,4,1,128]{3,0,2,1:T(8,128)(2,1)S(1)}, bf16[8,4,1,128]{3,0,2,1:T(8,128)(2,1)S(1)}, u32[]{:S(2)}, u32[]{:S(2)}) collective-permute-start(bf16[8,4,1,128]{3,0,2,1:T(8,128)(2,1)S(1)} %get-tuple-element.117), channel_id=1, source_target_pairs={{0,1},{1,2},{2,3},{3,4},{4,5},{5,6},{6,7},{8,9},{9,10},{10,11},{11... | collective-permute-start | bytes 24584 | tf_op jit(solution)/shard_map/ppermute | solution.py:20
  42.9 5.9 %collective-permute-start.7 = (bf16[8,4,1,128]{3,0,2,1:T(8,128)(2,1)S(1)}, bf16[8,4,1,128]{3,0,2,1:T(8,128)(2,1)S(1)}, u32[]{:S(2)}, u32[]{:S(2)}) collective-permute-start(bf16[8,4,1,128]{3,0,2,1:T(8,128)(2,1)S(1)} %get-tuple-element.118), channel_id=1, source_target_pairs={{1,0},{2,1},{3,2},{4,3},{5,4},{6,5},{7,6},{9,8},{10,9},{11,10},{12... | collective-permute-start | bytes 24584 | tf_op jit(solution)/shard_map/ppermute | solution.py:22
  54.7 37.9 %copy-start.2 = (f32[8,8,1,1]{1,0,3,2:T(8,128)S(1)}, f32[8,8,1,1]{1,0,3,2:T(8,128)}, u32[]{:S(2)}) copy-start(f32[8,8,1,1]{1,0,3,2:T(8,128)} %constant.54) | copy-start | bytes 772
  55.8 25.4 %all-to-all-start = ((f32[64,1,607]{2,1,0:T(1,128)}), f32[64,1,607]{2,1,0:T(1,128)S(1)}, u32[]{:S(2)}, u32[]{:S(2)}) async-start(f32[64,1,607]{2,1,0:T(1,128)} %all_to_all.10), calls=%async_computation | async-start | bytes 327680 | tf_op jit(solution)/shard_map/all_to_all | solution.py:200
  81.4 4.6 %collective-permute-start.12 = (f32[607]{0:T(1024)S(1)}, f32[607]{0:T(1024)S(1)}, u32[]{:S(2)}, u32[]{:S(2)}) collective-permute-start(f32[607]{0:T(1024)S(1)} %reduce_sum.39), channel_id=1, source_target_pairs={{0,1},{1,0},{2,3},{3,2},{4,5},{5,4},{6,7},{7,6},{8,9},{9,8},{10,11... | collective-permute-start | bytes 7292 | tf_op jit(solution)/shard_map/ppermute | solution.py:128
  83.3 19.4 %collective-permute-start.8 = (bf16[64,1,4,128]{3,0,2,1:T(8,128)(2,1)S(1)}, bf16[64,1,4,128]{3,0,2,1:T(8,128)(2,1)S(1)}, u32[]{:S(2)}, u32[]{:S(2)}) collective-permute-start(bf16[64,1,4,128]{3,0,2,1:T(8,128)(2,1)S(1)} %get-tuple-element.89), channel_id=1, source_target_pairs={{0,8},{8,16},{16,24},{24,32},{32,40},{40,48},{48,56},{56,64},{64,7... | collective-permute-start | bytes 196616 | tf_op jit(solution)/shard_map/ppermute | solution.py:20
  86.0 12.5 %collective-permute-start.13 = (f32[607]{0:T(1024)S(1)}, f32[607]{0:T(1024)S(1)}, u32[]{:S(2)}, u32[]{:S(2)}) collective-permute-start(f32[607]{0:T(1024)S(1)} %add.264), channel_id=1, source_target_pairs={{0,2},{1,3},{2,0},{3,1},{4,6},{5,7},{6,4},{7,5},{8,10},{9,11},{10,... | collective-permute-start | bytes 7292 | tf_op jit(solution)/shard_map/ppermute | solution.py:128
  95.3 7.4 %collective-permute-start.9 = (bf16[64,1,4,128]{3,0,2,1:T(8,128)(2,1)S(1)}, bf16[64,1,4,128]{3,0,2,1:T(8,128)(2,1)S(1)}, u32[]{:S(2)}, u32[]{:S(2)}) collective-permute-start(bf16[64,1,4,128]{3,0,2,1:T(8,128)(2,1)S(1)} %get-tuple-element.88), channel_id=1, source_target_pairs={{8,0},{16,8},{24,16},{32,24},{40,32},{48,40},{56,48},{64,56},{72,6... | collective-permute-start | bytes 196616 | tf_op jit(solution)/shard_map/ppermute | solution.py:22
  98.5 10.7 %collective-permute-start.14 = (f32[607]{0:T(1024)S(1)}, f32[607]{0:T(1024)S(1)}, u32[]{:S(2)}, u32[]{:S(2)}) collective-permute-start(f32[607]{0:T(1024)S(1)} %add.265), channel_id=1, source_target_pairs={{0,4},{1,5},{2,6},{3,7},{4,0},{5,1},{6,2},{7,3},{8,12},{9,13},{10,... | collective-permute-start | bytes 7292 | tf_op jit(solution)/shard_map/ppermute | solution.py:128
  102.8 16.2 %collective-permute-start.10 = (bf16[64,4,1,128]{3,0,2,1:T(8,128)(2,1)S(1)}, bf16[64,4,1,128]{3,0,2,1:T(8,128)(2,1)S(1)}, u32[]{:S(2)}, u32[]{:S(2)}) collective-permute-start(bf16[64,4,1,128]{3,0,2,1:T(8,128)(2,1)S(1)} %get-tuple-element.72), channel_id=1, source_target_pairs={{0,1},{1,2},{2,3},{3,4},{4,5},{5,6},{6,7},{8,9},{9,10},{10,11},{11... | collective-permute-start | bytes 196616 | tf_op jit(solution)/shard_map/ppermute | solution.py:20
  104.7 14.3 %collective-permute-start.11 = (bf16[64,4,1,128]{3,0,2,1:T(8,128)(2,1)S(1)}, bf16[64,4,1,128]{3,0,2,1:T(8,128)(2,1)S(1)}, u32[]{:S(2)}, u32[]{:S(2)}) collective-permute-start(bf16[64,4,1,128]{3,0,2,1:T(8,128)(2,1)S(1)} %get-tuple-element.73), channel_id=1, source_target_pairs={{1,0},{2,1},{3,2},{4,3},{5,4},{6,5},{7,6},{9,8},{10,9},{11,10},{12... | collective-permute-start | bytes 196616 | tf_op jit(solution)/shard_map/ppermute | solution.py:22
  110.0 19.4 %all-to-all-start.1 = ((f32[64,1,607]{2,1,0:T(1,128)}), f32[64,1,607]{2,1,0:T(1,128)S(1)}, u32[]{:S(2)}, u32[]{:S(2)}) async-start(f32[64,1,607]{2,1,0:T(1,128)} %broadcast_in_dim.23), calls=%async_computation.1 | async-start | bytes 327680 | tf_op jit(solution)/shard_map/all_to_all | solution.py:206

commit v8 on v7

--- a/solution.py
+++ b/solution.py
@@ -200,7 +200,10 @@
     owned = lax.all_to_all(chunks, "gz", 0, 0, tiled=False).sum(0)
     owned, first_grad = lax.optimization_barrier((owned, first_grad))
     factor = 1.0 / math.sqrt(float(planes * x_rows * y_cols))
-    owned = butterfly_sum(owned, ("gx",)) * factor
+    members = lax.axis_size("gx")
+    owned = lax.all_to_all(
+        jnp.broadcast_to(owned, (members,) + owned.shape), "gx", 0, 0, tiled=False
+    ).sum(0) * factor
     first_frame = frame_cols(extended(first_grad, (("gz", 1), ("gx", 2)), 1))
     input_grad = backward_taps(first_frame, expand_kernel, planes, x_rows)
     spread = lax.all_to_all(jnp.broadcast_to(owned, (count,) + owned.shape), "gz", 0, 0, tiled=False)

time: 135 us -> 138 us (1.022); the launches traced: 134 us -> 136 us
  waiting for transfers between devices: 21.7 us -> 25.4 us
  starting transfers between devices: 74.7 us -> 71.8 us
    ppermute x3 -> x0, starting transfers between devices: 12.7 us -> none  [butterfly_sum(): flat = flat + lax.ppermute(flat, axis, [(i, i ^ bit) for i in range(count)])]
    all_to_all x0 -> x1, starting transfers between devices: none -> 9.41 us  [per_device(): lax.all_to_all(jnp.broadcast_to(owned, (members,) + owned.shape), 'gx', 0...]
    ppermute x6, waiting for transfers between devices: 7.29 us -> 11 us  [extended(): lax.ppermute(head, axis, [((i + 1) % count, i) for i in range(ends)])]
  transfers between devices with their start and end apart: 17 -> 15, of which waited for: 5 -> 6; matrix products, arithmetic and copies ran while one was open for 10% -> 11% of each run, Pallas kernels for 0% -> 0%
where the time goes in v8:
time: 138 us; the launch traced here: 136 us
  starting transfers between devices  71.8 us (52%)
  waiting for transfers between devices  25.4 us (18%)
  local copies, waits for them, and re-layouts  21.2 us (15%)
  matrix products  13.8 us (10%)
  other arithmetic  1.85 us (1%)
  between operations  1.64 us (1%)
    ppermute x6, starting transfers between devices, extended(): lax.ppermute(head, axis, [((i + 1) % count, i) for i in range(ends)])  21.8 us
    ppermute x6, starting transfers between devices, extended(): lax.ppermute(tail, axis, [(i, (i + 1) % count) for i in range(ends)])  16.3 us
    all_to_all x1, starting transfers between devices, per_device(): owned = lax.all_to_all(chunks, 'gz', 0, 0, tiled=False).sum(0)  14.9 us
    ppermute x6, waiting for transfers between devices, extended(): lax.ppermute(head, axis, [((i + 1) % count, i) for i in range(ends)])  11 us
    all_to_all x1, waiting for transfers between devices, per_device(): owned = lax.all_to_all(chunks, 'gz', 0, 0, tiled=False).sum(0)  10.3 us
    all_to_all x1, starting transfers between devices, per_device(): lax.all_to_all(jnp.broadcast_to(owned, (members,) + owned.shape), 'gx', 0...  9.41 us
    all_to_all x1, starting transfers between devices, per_device(): lax.all_to_all(jnp.broadcast_to(owned, (count,) + owned.shape), 'gz', 0,...  9.35 us
    dot_general x18, matrix products, forward_taps(): jnp.einsum('eoc,eczxy->ozxy', kernel[z_step, x_step], stacked[:, :, z_ste...  5 us
  transfers between devices with their start and end apart: 15, of which 6 were waited for; matrix products, arithmetic and copies ran while one was open for 11% of the time, Pallas kernels for 0%

profile of v8, /device:TPU:56, one launch (start us, length us, event | category | flops | bytes accessed | tf_op | source)
XLA Modules:
  0.0 135.7 jit_solution(17443672501710498931)
XLA Ops:
  0.6 0.8 fusion.170
  2.2 5.1 %collective-permute-start = (bf16[12,2,4,128]{3,0,2,1:T(8,128)(2,1)S(1)}, bf16[12,2,4,128]{3,0,2,1:T(8,128)(2,1)S(1)}, u32[]{:S(2)}, u32[]{:S(2)}) collective-permute-start(bf16[12,2,4,128]{3,0,2,1:T(8,128)(2,1)S(1)} %pad_maximum_fusion.9), channel_id=1, source_target_pairs={{0,8},{8,16},{16,24},{24,32},{32,40},{40,48},{48,56},{56,64},{64,7... | collective-permute-start | bytes 73736 | tf_op jit(solution)/shard_map/ppermute | solution.py:20
  7.3 1.9 %collective-permute-start.1 = (bf16[12,2,4,128]{3,0,2,1:T(8,128)(2,1)S(1)}, bf16[12,2,4,128]{3,0,2,1:T(8,128)(2,1)S(1)}, u32[]{:S(2)}, u32[]{:S(2)}) collective-permute-start(bf16[12,2,4,128]{3,0,2,1:T(8,128)(2,1)S(1)} %pad_maximum_fusion.9), channel_id=1, source_target_pairs={{8,0},{16,8},{24,16},{32,24},{40,32},{48,40},{56,48},{64,56},{72,6... | collective-permute-start | bytes 73736 | tf_op jit(solution)/shard_map/ppermute | solution.py:22
  9.2 0.8 fusion.172
  10.0 0.8 fusion.169
  10.9 3.1 %collective-permute-done.1 = bf16[12,2,4,128]{3,0,2,1:T(8,128)(2,1)S(1)} collective-permute-done((bf16[12,2,4,128]{3,0,2,1:T(8,128)(2,1)S(1)}, bf16[12,2,4,128]{3,0,2,1:T(8,128)(2,1)S(1)}, u32[]{:S(2)}, u32[]{:S(2)}) %collective-permute-start.1) | collective-permute-done | bytes 24608 | tf_op jit(solution)/shard_map/ppermute | solution.py:22
  14.0 1.9 %collective-permute-start.2 = (bf16[12,6,2,128]{3,0,2,1:T(8,128)(2,1)S(1)}, bf16[12,6,2,128]{3,0,2,1:T(8,128)(2,1)S(1)}, u32[]{:S(2)}, u32[]{:S(2)}) collective-permute-start(bf16[12,6,2,128]{3,0,2,1:T(8,128)(2,1)S(1)} %get-tuple-element.99), channel_id=1, source_target_pairs={{0,1},{1,2},{2,3},{3,4},{4,5},{5,6},{6,7},{8,9},{9,10},{10,11},{11... | collective-permute-start | bytes 110600 | tf_op jit(solution)/shard_map/ppermute | solution.py:20
  15.9 4.5 %collective-permute-start.3 = (bf16[12,6,2,128]{3,0,2,1:T(8,128)(2,1)S(1)}, bf16[12,6,2,128]{3,0,2,1:T(8,128)(2,1)S(1)}, u32[]{:S(2)}, u32[]{:S(2)}) collective-permute-start(bf16[12,6,2,128]{3,0,2,1:T(8,128)(2,1)S(1)} %get-tuple-element.100), channel_id=1, source_target_pairs={{1,0},{2,1},{3,2},{4,3},{5,4},{6,5},{7,6},{9,8},{10,9},{11,10},{12... | collective-permute-start | bytes 110600 | tf_op jit(solution)/shard_map/ppermute | solution.py:22
  21.2 0.9 copy.299
  26.6 0.9 fusion.163
  31.7 2.9 %collective-permute-start.4 = (bf16[8,1,4,128]{3,0,2,1:T(8,128)(2,1)S(1)}, bf16[8,1,4,128]{3,0,2,1:T(8,128)(2,1)S(1)}, u32[]{:S(2)}, u32[]{:S(2)}) collective-permute-start(bf16[8,1,4,128]{3,0,2,1:T(8,128)(2,1)S(1)} %get-tuple-element.121), channel_id=1, source_target_pairs={{0,8},{8,16},{16,24},{24,32},{32,40},{40,48},{48,56},{56,64},{64,7... | collective-permute-start | bytes 24584 | tf_op jit(solution)/shard_map/ppermute | solution.py:20
  34.5 3.0 %collective-permute-start.5 = (bf16[8,1,4,128]{3,0,2,1:T(8,128)(2,1)S(1)}, bf16[8,1,4,128]{3,0,2,1:T(8,128)(2,1)S(1)}, u32[]{:S(2)}, u32[]{:S(2)}) collective-permute-start(bf16[8,1,4,128]{3,0,2,1:T(8,128)(2,1)S(1)} %get-tuple-element.122), channel_id=1, source_target_pairs={{8,0},{16,8},{24,16},{32,24},{40,32},{48,40},{56,48},{64,56},{72,6... | collective-permute-start | bytes 24584 | tf_op jit(solution)/shard_map/ppermute | solution.py:22
  37.8 3.2 %collective-permute-done.5 = bf16[8,1,4,128]{3,0,2,1:T(8,128)(2,1)S(1)} collective-permute-done((bf16[8,1,4,128]{3,0,2,1:T(8,128)(2,1)S(1)}, bf16[8,1,4,128]{3,0,2,1:T(8,128)(2,1)S(1)}, u32[]{:S(2)}, u32[]{:S(2)}) %collective-permute-start.5) | collective-permute-done | bytes 8224 | tf_op jit(solution)/shard_map/ppermute | solution.py:22
  41.0 1.9 %collective-permute-start.6 = (bf16[8,4,1,128]{3,0,2,1:T(8,128)(2,1)S(1)}, bf16[8,4,1,128]{3,0,2,1:T(8,128)(2,1)S(1)}, u32[]{:S(2)}, u32[]{:S(2)}) collective-permute-start(bf16[8,4,1,128]{3,0,2,1:T(8,128)(2,1)S(1)} %get-tuple-element.117), channel_id=1, source_target_pairs={{0,1},{1,2},{2,3},{3,4},{4,5},{5,6},{6,7},{8,9},{9,10},{10,11},{11... | collective-permute-start | bytes 24584 | tf_op jit(solution)/shard_map/ppermute | solution.py:20
  42.9 4.5 %collective-permute-start.7 = (bf16[8,4,1,128]{3,0,2,1:T(8,128)(2,1)S(1)}, bf16[8,4,1,128]{3,0,2,1:T(8,128)(2,1)S(1)}, u32[]{:S(2)}, u32[]{:S(2)}) collective-permute-start(bf16[8,4,1,128]{3,0,2,1:T(8,128)(2,1)S(1)} %get-tuple-element.118), channel_id=1, source_target_pairs={{1,0},{2,1},{3,2},{4,3},{5,4},{6,5},{7,6},{9,8},{10,9},{11,10},{12... | collective-permute-start | bytes 24584 | tf_op jit(solution)/shard_map/ppermute | solution.py:22
  47.8 1.0 collective-permute-done.7
  54.8 1.0 all_to_all.14
  55.8 14.9 %all-to-all-start = ((f32[64,1,607]{2,1,0:T(1,128)}), f32[64,1,607]{2,1,0:T(1,128)S(1)}, u32[]{:S(2)}, u32[]{:S(2)}) async-start(f32[64,1,607]{2,1,0:T(1,128)} %all_to_all.14), calls=%async_computation | async-start | bytes 327680 | tf_op jit(solution)/shard_map/all_to_all | solution.py:200
  70.9 10.3 %all-to-all-done = f32[64,1,607]{2,1,0:T(1,128)S(1)} async-done(((f32[64,1,607]{2,1,0:T(1,128)}), f32[64,1,607]{2,1,0:T(1,128)S(1)}, u32[]{:S(2)}, u32[]{:S(2)}) %all-to-all-start) | async-done | bytes 155424 | tf_op jit(solution)/shard_map/all_to_all | solution.py:200
  81.4 2.6 %collective-permute-start.8 = (bf16[64,1,4,128]{3,0,2,1:T(8,128)(2,1)S(1)}, bf16[64,1,4,128]{3,0,2,1:T(8,128)(2,1)S(1)}, u32[]{:S(2)}, u32[]{:S(2)}) collective-permute-start(bf16[64,1,4,128]{3,0,2,1:T(8,128)(2,1)S(1)} %get-tuple-element.89), channel_id=1, source_target_pairs={{0,8},{8,16},{16,24},{24,32},{32,40},{40,48},{48,56},{56,64},{64,7... | collective-permute-start | bytes 196616 | tf_op jit(solution)/shard_map/ppermute | solution.py:20
  84.7 9.4 %all-to-all-start.1 = ((f32[8,1,607]{2,1,0:T(1,128)}), f32[8,1,607]{2,1,0:T(1,128)S(1)}, u32[]{:S(2)}, u32[]{:S(2)}) async-start(f32[8,1,607]{2,1,0:T(1,128)} %broadcast_in_dim.26), calls=%async_computation.1 | async-start | bytes 40960 | tf_op jit(solution)/shard_map/all_to_all | solution.py:204
  94.9 1.8 %reshape.119 = f32[4,8,256]{2,1,0:T(8,128)} reshape(f32[2,2,4,2,128,2]{5,4,3,2,1,0:T(8,128)S(1)} %bitcast.691) | data formatting | bytes 65536 | tf_op jit(solution)/shard_map/reshape | solution.py:50
  96.7 3.2 %collective-permute-start.9 = (bf16[64,1,4,128]{3,0,2,1:T(8,128)(2,1)S(1)}, bf16[64,1,4,128]{3,0,2,1:T(8,128)(2,1)S(1)}, u32[]{:S(2)}, u32[]{:S(2)}) collective-permute-start(bf16[64,1,4,128]{3,0,2,1:T(8,128)(2,1)S(1)} %get-tuple-element.88), channel_id=1, source_target_pairs={{8,0},{16,8},{24,16},{32,24},{40,32},{48,40},{56,48},{64,56},{72,6... | collective-permute-start | bytes 196616 | tf_op jit(solution)/shard_map/ppermute | solution.py:22
  100.0 3.7 %collective-permute-done.9 = bf16[64,1,4,128]{3,0,2,1:T(8,128)(2,1)S(1)} collective-permute-done((bf16[64,1,4,128]{3,0,2,1:T(8,128)(2,1)S(1)}, bf16[64,1,4,128]{3,0,2,1:T(8,128)(2,1)S(1)}, u32[]{:S(2)}, u32[]{:S(2)}) %collective-permute-start.9) | collective-permute-done | bytes 65568 | tf_op jit(solution)/shard_map/ppermute | solution.py:22
  103.8 1.9 %collective-permute-start.10 = (bf16[64,4,1,128]{3,0,2,1:T(8,128)(2,1)S(1)}, bf16[64,4,1,128]{3,0,2,1:T(8,128)(2,1)S(1)}, u32[]{:S(2)}, u32[]{:S(2)}) collective-permute-start(bf16[64,4,1,128]{3,0,2,1:T(8,128)(2,1)S(1)} %get-tuple-element.72), channel_id=1, source_target_pairs={{0,1},{1,2},{2,3},{3,4},{4,5},{5,6},{6,7},{8,9},{9,10},{10,11},{11... | collective-permute-start | bytes 196616 | tf_op jit(solution)/shard_map/ppermute | solution.py:20
  105.7 4.5 %collective-permute-start.11 = (bf16[64,4,1,128]{3,0,2,1:T(8,128)(2,1)S(1)}, bf16[64,4,1,128]{3,0,2,1:T(8,128)(2,1)S(1)}, u32[]{:S(2)}, u32[]{:S(2)}) collective-permute-start(bf16[64,4,1,128]{3,0,2,1:T(8,128)(2,1)S(1)} %get-tuple-element.73), channel_id=1, source_target_pairs={{1,0},{2,1},{3,2},{4,3},{5,4},{6,5},{7,6},{9,8},{10,9},{11,10},{12... | collective-permute-start | bytes 196616 | tf_op jit(solution)/shard_map/ppermute | solution.py:22
  110.3 0.8 broadcast_in_dim.27
  111.0 9.3 %all-to-all-start.2 = ((f32[64,1,607]{2,1,0:T(1,128)}), f32[64,1,607]{2,1,0:T(1,128)S(1)}, u32[]{:S(2)}, u32[]{:S(2)}) async-start(f32[64,1,607]{2,1,0:T(1,128)} %broadcast_in_dim.27), calls=%async_computation.2 | async-start | bytes 327680 | tf_op jit(solution)/shard_map/all_to_all | solution.py:209
  124.4 1.8 %reshape.124 = f32[4,8,256]{2,1,0:T(8,128)} reshape(f32[2,2,4,2,128,2]{5,4,3,2,1,0:T(8,128)S(1)} %bitcast.692) | data formatting | bytes 65536 | tf_op jit(solution)/shard_map/reshape | solution.py:50
  126.8 4.0 %all-to-all-done.2 = f32[64,1,607]{2,1,0:T(1,128)S(1)} async-done(((f32[64,1,607]{2,1,0:T(1,128)}), f32[64,1,607]{2,1,0:T(1,128)S(1)}, u32[]{:S(2)}, u32[]{:S(2)}) %all-to-all-start.2) | async-done | bytes 155424 | tf_op jit(solution)/shard_map/all_to_all | solution.py:209
  132.3 1.0 reshape.126
  133.3 1.1 copy.383
  (154 shorter events, 25.2 us)
Async XLA Ops:
  0.6 25.1 %copy-start = (bf16[64,64]{1,0:T(8,128)(2,1)S(1)}, bf16[64,64]{1,0:T(8,128)(2,1)}, u32[]{:S(2)}) copy-start(bf16[64,64]{1,0:T(8,128)(2,1)} %param.13) | copy-start | bytes 24580
  2.2 8.7 %collective-permute-start = (bf16[12,2,4,128]{3,0,2,1:T(8,128)(2,1)S(1)}, bf16[12,2,4,128]{3,0,2,1:T(8,128)(2,1)S(1)}, u32[]{:S(2)}, u32[]{:S(2)}) collective-permute-start(bf16[12,2,4,128]{3,0,2,1:T(8,128)(2,1)S(1)} %pad_maximum_fusion.9), channel_id=1, source_target_pairs={{0,8},{8,16},{16,24},{24,32},{32,40},{40,48},{48,56},{56,64},{64,7... | collective-permute-start | bytes 73736 | tf_op jit(solution)/shard_map/ppermute | solution.py:20
  7.3 6.7 %collective-permute-start.1 = (bf16[12,2,4,128]{3,0,2,1:T(8,128)(2,1)S(1)}, bf16[12,2,4,128]{3,0,2,1:T(8,128)(2,1)S(1)}, u32[]{:S(2)}, u32[]{:S(2)}) collective-permute-start(bf16[12,2,4,128]{3,0,2,1:T(8,128)(2,1)S(1)} %pad_maximum_fusion.9), channel_id=1, source_target_pairs={{8,0},{16,8},{24,16},{32,24},{40,32},{48,40},{56,48},{64,56},{72,6... | collective-permute-start | bytes 73736 | tf_op jit(solution)/shard_map/ppermute | solution.py:22
  14.0 8.3 %collective-permute-start.2 = (bf16[12,6,2,128]{3,0,2,1:T(8,128)(2,1)S(1)}, bf16[12,6,2,128]{3,0,2,1:T(8,128)(2,1)S(1)}, u32[]{:S(2)}, u32[]{:S(2)}) collective-permute-start(bf16[12,6,2,128]{3,0,2,1:T(8,128)(2,1)S(1)} %get-tuple-element.99), channel_id=1, source_target_pairs={{0,1},{1,2},{2,3},{3,4},{4,5},{5,6},{6,7},{8,9},{9,10},{10,11},{11... | collective-permute-start | bytes 110600 | tf_op jit(solution)/shard_map/ppermute | solution.py:20
  15.9 6.4 %collective-permute-start.3 = (bf16[12,6,2,128]{3,0,2,1:T(8,128)(2,1)S(1)}, bf16[12,6,2,128]{3,0,2,1:T(8,128)(2,1)S(1)}, u32[]{:S(2)}, u32[]{:S(2)}) collective-permute-start(bf16[12,6,2,128]{3,0,2,1:T(8,128)(2,1)S(1)} %get-tuple-element.100), channel_id=1, source_target_pairs={{1,0},{2,1},{3,2},{4,3},{5,4},{6,5},{7,6},{9,8},{10,9},{11,10},{12... | collective-permute-start | bytes 110600 | tf_op jit(solution)/shard_map/ppermute | solution.py:22
  26.6 0.9 copy-start.1
  31.7 6.1 %collective-permute-start.4 = (bf16[8,1,4,128]{3,0,2,1:T(8,128)(2,1)S(1)}, bf16[8,1,4,128]{3,0,2,1:T(8,128)(2,1)S(1)}, u32[]{:S(2)}, u32[]{:S(2)}) collective-permute-start(bf16[8,1,4,128]{3,0,2,1:T(8,128)(2,1)S(1)} %get-tuple-element.121), channel_id=1, source_target_pairs={{0,8},{8,16},{16,24},{24,32},{32,40},{40,48},{48,56},{56,64},{64,7... | collective-permute-start | bytes 24584 | tf_op jit(solution)/shard_map/ppermute | solution.py:20
  34.5 6.4 %collective-permute-start.5 = (bf16[8,1,4,128]{3,0,2,1:T(8,128)(2,1)S(1)}, bf16[8,1,4,128]{3,0,2,1:T(8,128)(2,1)S(1)}, u32[]{:S(2)}, u32[]{:S(2)}) collective-permute-start(bf16[8,1,4,128]{3,0,2,1:T(8,128)(2,1)S(1)} %get-tuple-element.122), channel_id=1, source_target_pairs={{8,0},{16,8},{24,16},{32,24},{40,32},{48,40},{56,48},{64,56},{72,6... | collective-permute-start | bytes 24584 | tf_op jit(solution)/shard_map/ppermute | solution.py:22
  41.0 6.8 %collective-permute-start.6 = (bf16[8,4,1,128]{3,0,2,1:T(8,128)(2,1)S(1)}, bf16[8,4,1,128]{3,0,2,1:T(8,128)(2,1)S(1)}, u32[]{:S(2)}, u32[]{:S(2)}) collective-permute-start(bf16[8,4,1,128]{3,0,2,1:T(8,128)(2,1)S(1)} %get-tuple-element.117), channel_id=1, source_target_pairs={{0,1},{1,2},{2,3},{3,4},{4,5},{5,6},{6,7},{8,9},{9,10},{10,11},{11... | collective-permute-start | bytes 24584 | tf_op jit(solution)/shard_map/ppermute | solution.py:20
  42.9 5.9 %collective-permute-start.7 = (bf16[8,4,1,128]{3,0,2,1:T(8,128)(2,1)S(1)}, bf16[8,4,1,128]{3,0,2,1:T(8,128)(2,1)S(1)}, u32[]{:S(2)}, u32[]{:S(2)}) collective-permute-start(bf16[8,4,1,128]{3,0,2,1:T(8,128)(2,1)S(1)} %get-tuple-element.118), channel_id=1, source_target_pairs={{1,0},{2,1},{3,2},{4,3},{5,4},{6,5},{7,6},{9,8},{10,9},{11,10},{12... | collective-permute-start | bytes 24584 | tf_op jit(solution)/shard_map/ppermute | solution.py:22
  54.7 39.3 %copy-start.2 = (f32[8,8,1,1]{1,0,3,2:T(8,128)S(1)}, f32[8,8,1,1]{1,0,3,2:T(8,128)}, u32[]{:S(2)}) copy-start(f32[8,8,1,1]{1,0,3,2:T(8,128)} %constant.54) | copy-start | bytes 772
  55.8 25.4 %all-to-all-start = ((f32[64,1,607]{2,1,0:T(1,128)}), f32[64,1,607]{2,1,0:T(1,128)S(1)}, u32[]{:S(2)}, u32[]{:S(2)}) async-start(f32[64,1,607]{2,1,0:T(1,128)} %all_to_all.14), calls=%async_computation | async-start | bytes 327680 | tf_op jit(solution)/shard_map/all_to_all | solution.py:200
  81.4 18.6 %collective-permute-start.8 = (bf16[64,1,4,128]{3,0,2,1:T(8,128)(2,1)S(1)}, bf16[64,1,4,128]{3,0,2,1:T(8,128)(2,1)S(1)}, u32[]{:S(2)}, u32[]{:S(2)}) collective-permute-start(bf16[64,1,4,128]{3,0,2,1:T(8,128)(2,1)S(1)} %get-tuple-element.89), channel_id=1, source_target_pairs={{0,8},{8,16},{16,24},{24,32},{32,40},{40,48},{48,56},{56,64},{64,7... | collective-permute-start | bytes 196616 | tf_op jit(solution)/shard_map/ppermute | solution.py:20
  84.7 15.3 %all-to-all-start.1 = ((f32[8,1,607]{2,1,0:T(1,128)}), f32[8,1,607]{2,1,0:T(1,128)S(1)}, u32[]{:S(2)}, u32[]{:S(2)}) async-start(f32[8,1,607]{2,1,0:T(1,128)} %broadcast_in_dim.26), calls=%async_computation.1 | async-start | bytes 40960 | tf_op jit(solution)/shard_map/all_to_all | solution.py:204
  96.7 7.0 %collective-permute-start.9 = (bf16[64,1,4,128]{3,0,2,1:T(8,128)(2,1)S(1)}, bf16[64,1,4,128]{3,0,2,1:T(8,128)(2,1)S(1)}, u32[]{:S(2)}, u32[]{:S(2)}) collective-permute-start(bf16[64,1,4,128]{3,0,2,1:T(8,128)(2,1)S(1)} %get-tuple-element.88), channel_id=1, source_target_pairs={{8,0},{16,8},{24,16},{32,24},{40,32},{48,40},{56,48},{64,56},{72,6... | collective-permute-start | bytes 196616 | tf_op jit(solution)/shard_map/ppermute | solution.py:22
  103.8 16.6 %collective-permute-start.10 = (bf16[64,4,1,128]{3,0,2,1:T(8,128)(2,1)S(1)}, bf16[64,4,1,128]{3,0,2,1:T(8,128)(2,1)S(1)}, u32[]{:S(2)}, u32[]{:S(2)}) collective-permute-start(bf16[64,4,1,128]{3,0,2,1:T(8,128)(2,1)S(1)} %get-tuple-element.72), channel_id=1, source_target_pairs={{0,1},{1,2},{2,3},{3,4},{4,5},{5,6},{6,7},{8,9},{9,10},{10,11},{11... | collective-permute-start | bytes 196616 | tf_op jit(solution)/shard_map/ppermute | solution.py:20
  105.7 14.7 %collective-permute-start.11 = (bf16[64,4,1,128]{3,0,2,1:T(8,128)(2,1)S(1)}, bf16[64,4,1,128]{3,0,2,1:T(8,128)(2,1)S(1)}, u32[]{:S(2)}, u32[]{:S(2)}) collective-permute-start(bf16[64,4,1,128]{3,0,2,1:T(8,128)(2,1)S(1)} %get-tuple-element.73), channel_id=1, source_target_pairs={{1,0},{2,1},{3,2},{4,3},{5,4},{6,5},{7,6},{9,8},{10,9},{11,10},{12... | collective-permute-start | bytes 196616 | tf_op jit(solution)/shard_map/ppermute | solution.py:22
  111.0 19.8 %all-to-all-start.2 = ((f32[64,1,607]{2,1,0:T(1,128)}), f32[64,1,607]{2,1,0:T(1,128)S(1)}, u32[]{:S(2)}, u32[]{:S(2)}) async-start(f32[64,1,607]{2,1,0:T(1,128)} %broadcast_in_dim.27), calls=%async_computation.2 | async-start | bytes 327680 | tf_op jit(solution)/shard_map/all_to_all | solution.py:209

commit v9 on v7

--- a/solution.py
+++ b/solution.py
@@ -55,38 +55,56 @@
     return sigma * (1.0 + preact * (1.0 - sigma))
 
 
-def y_shifts(padded):
+def shift_stack(padded, x_rows):
     y_cols = padded.shape[3] - 2
-    return jnp.stack([padded[..., y_step : y_step + y_cols] for y_step in range(3)])
+    if padded.shape[0] > 16:
+        steps = [(None, y_step) for y_step in range(3)]
+    else:
+        steps = [(x_step, y_step) for x_step in range(3) for y_step in range(3)]
+    slices = []
+    for x_step, y_step in steps:
+        cut = padded[..., y_step : y_step + y_cols]
+        if x_step is not None:
+            cut = cut[:, :, x_step : x_step + x_rows]
+        slices.append(cut)
+    return jnp.stack(slices), len(steps) == 9
 
 
 def forward_taps(padded, weight, planes, x_rows):
-    stacked = y_shifts(padded)
+    stacked, full = shift_stack(padded, x_rows)
     kernel = weight.reshape((3, 3, 3) + weight.shape[1:])
     summed = None
     for z_step in range(3):
-        for x_step in range(3):
+        for x_step in [None] if full else range(3):
+            if full:
+                taps = kernel[z_step].reshape((9,) + weight.shape[1:])
+                window = stacked[:, :, z_step : z_step + planes]
+            else:
+                taps = kernel[z_step, x_step]
+                window = stacked[:, :, z_step : z_step + planes, x_step : x_step + x_rows]
             product = jnp.einsum(
-                "eoc,eczxy->ozxy",
-                kernel[z_step, x_step],
-                stacked[:, :, z_step : z_step + planes, x_step : x_step + x_rows],
-                preferred_element_type=jnp.float32,
+                "eoc,eczxy->ozxy", taps, window, preferred_element_type=jnp.float32
             )
             summed = product if summed is None else summed + product
     return summed
 
 
 def backward_taps(padded, weight, planes, x_rows):
-    stacked = y_shifts(padded)
+    stacked, full = shift_stack(padded, x_rows)
     kernel = weight.reshape((3, 3, 3) + weight.shape[1:])
     summed = None
     for z_step in range(3):
-        for x_step in range(3):
+        for x_step in [None] if full else range(3):
+            if full:
+                taps = kernel[z_step, ::-1, ::-1].reshape((9,) + weight.shape[1:])
+                window = stacked[:, :, 2 - z_step : 2 - z_step + planes]
+            else:
+                taps = kernel[z_step, x_step, ::-1]
+                window = stacked[
+                    :, :, 2 - z_step : 2 - z_step + planes, 2 - x_step : 2 - x_step + x_rows
+                ]
             product = jnp.einsum(
-                "eoc,eozxy->czxy",
-                kernel[z_step, x_step, ::-1],
-                stacked[:, :, 2 - z_step : 2 - z_step + planes, 2 - x_step : 2 - x_step + x_rows],
-                preferred_element_type=jnp.float32,
+                "eoc,eozxy->czxy", taps, window, preferred_element_type=jnp.float32
             )
             summed = product if summed is None else summed + product
     return summed
@@ -94,17 +112,16 @@
 
 def weight_taps(grad, padded):
     planes, x_rows = (grad.shape[1], grad.shape[2])
-    stacked = y_shifts(padded)
+    stacked, full = shift_stack(padded, x_rows)
     result = []
     for z_step in range(3):
-        for x_step in range(3):
+        for x_step in [None] if full else range(3):
+            if full:
+                window = stacked[:, :, z_step : z_step + planes]
+            else:
+                window = stacked[:, :, z_step : z_step + planes, x_step : x_step + x_rows]
             result.append(
-                jnp.einsum(
-                    "ozxy,eczxy->eoc",
-                    grad,
-                    stacked[:, :, z_step : z_step + planes, x_step : x_step + x_rows],
-                    preferred_element_type=jnp.float32,
-                )
+                jnp.einsum("ozxy,eczxy->eoc", grad, window, preferred_element_type=jnp.float32)
             )
     return jnp.concatenate(result)
 

time: 135 us -> 134 us (level)
  matrix products: 13.8 us -> 11.6 us
    dot_general x54 -> x36, matrix products: 12.6 us -> 9.44 us  [the longest x12 3.86 us: forward_taps(): jnp.einsum('eoc,eczxy->ozxy', taps, window, preferred_element_type=jnp.fl...]
    unnamed x15 -> x34, local copies, waits for them, and re-layouts: 3.42 us -> 4.83 us
  transfers between devices with their start and end apart: 17 -> 17, of which waited for: 5 -> 5; matrix products, arithmetic and copies ran while one was open for 10% -> 11% of each run, Pallas kernels for 0% -> 0%
where the time goes in v9:
time: 134 us; the launch traced here: 133 us
  starting transfers between devices  74.5 us (56%)
  local copies, waits for them, and re-layouts  21.8 us (16%)
  waiting for transfers between devices  21.5 us (16%)
  matrix products  11.6 us (9%)
  other arithmetic  1.99 us (1%)
  between operations  1.54 us (1%)
    ppermute x6, starting transfers between devices, extended(): lax.ppermute(head, axis, [((i + 1) % count, i) for i in range(ends)])  21.8 us
    ppermute x6, starting transfers between devices, extended(): lax.ppermute(tail, axis, [(i, (i + 1) % count) for i in range(ends)])  16.3 us
    all_to_all x1, starting transfers between devices, per_device(): owned = lax.all_to_all(chunks, 'gz', 0, 0, tiled=False).sum(0)  15 us
    ppermute x3, starting transfers between devices, butterfly_sum(): flat = flat + lax.ppermute(flat, axis, [(i, i ^ bit) for i in range(count)])  12.5 us
    all_to_all x1, waiting for transfers between devices, per_device(): owned = lax.all_to_all(chunks, 'gz', 0, 0, tiled=False).sum(0)  10.3 us
    all_to_all x1, starting transfers between devices, per_device(): lax.all_to_all(jnp.broadcast_to(owned, (count,) + owned.shape), 'gz', 0,...  8.96 us
    ppermute x6, waiting for transfers between devices, extended(): lax.ppermute(head, axis, [((i + 1) % count, i) for i in range(ends)])  7.07 us
    unnamed x34, local copies, waits for them, and re-layouts  4.83 us
  transfers between devices with their start and end apart: 17, of which 5 were waited for; matrix products, arithmetic and copies ran while one was open for 11% of the time, Pallas kernels for 0%

profile of v9, /device:TPU:56, one launch (start us, length us, event | category | flops | bytes accessed | tf_op | source)
XLA Modules:
  0.0 132.9 jit_solution(8662908234691562863)
XLA Ops:
  2.2 5.1 %collective-permute-start = (bf16[12,2,4,128]{3,0,2,1:T(8,128)(2,1)S(1)}, bf16[12,2,4,128]{3,0,2,1:T(8,128)(2,1)S(1)}, u32[]{:S(2)}, u32[]{:S(2)}) collective-permute-start(bf16[12,2,4,128]{3,0,2,1:T(8,128)(2,1)S(1)} %pad_maximum_fusion.15), channel_id=1, source_target_pairs={{0,8},{8,16},{16,24},{24,32},{32,40},{40,48},{48,56},{56,64},{64,7... | collective-permute-start | bytes 73736 | tf_op jit(solution)/shard_map/ppermute | solution.py:20
  7.3 1.9 %collective-permute-start.1 = (bf16[12,2,4,128]{3,0,2,1:T(8,128)(2,1)S(1)}, bf16[12,2,4,128]{3,0,2,1:T(8,128)(2,1)S(1)}, u32[]{:S(2)}, u32[]{:S(2)}) collective-permute-start(bf16[12,2,4,128]{3,0,2,1:T(8,128)(2,1)S(1)} %pad_maximum_fusion.15), channel_id=1, source_target_pairs={{8,0},{16,8},{24,16},{32,24},{40,32},{48,40},{56,48},{64,56},{72,6... | collective-permute-start | bytes 73736 | tf_op jit(solution)/shard_map/ppermute | solution.py:22
  9.2 0.8 fusion.124
  10.8 3.2 %collective-permute-done.1 = bf16[12,2,4,128]{3,0,2,1:T(8,128)(2,1)S(1)} collective-permute-done((bf16[12,2,4,128]{3,0,2,1:T(8,128)(2,1)S(1)}, bf16[12,2,4,128]{3,0,2,1:T(8,128)(2,1)S(1)}, u32[]{:S(2)}, u32[]{:S(2)}) %collective-permute-start.1) | collective-permute-done | bytes 24608 | tf_op jit(solution)/shard_map/ppermute | solution.py:22
  14.0 1.9 %collective-permute-start.2 = (bf16[12,6,2,128]{3,0,2,1:T(8,128)(2,1)S(1)}, bf16[12,6,2,128]{3,0,2,1:T(8,128)(2,1)S(1)}, u32[]{:S(2)}, u32[]{:S(2)}) collective-permute-start(bf16[12,6,2,128]{3,0,2,1:T(8,128)(2,1)S(1)} %get-tuple-element.88), channel_id=1, source_target_pairs={{0,1},{1,2},{2,3},{3,4},{4,5},{5,6},{6,7},{8,9},{9,10},{10,11},{11... | collective-permute-start | bytes 110600 | tf_op jit(solution)/shard_map/ppermute | solution.py:20
  15.9 4.5 %collective-permute-start.3 = (bf16[12,6,2,128]{3,0,2,1:T(8,128)(2,1)S(1)}, bf16[12,6,2,128]{3,0,2,1:T(8,128)(2,1)S(1)}, u32[]{:S(2)}, u32[]{:S(2)}) collective-permute-start(bf16[12,6,2,128]{3,0,2,1:T(8,128)(2,1)S(1)} %get-tuple-element.89), channel_id=1, source_target_pairs={{1,0},{2,1},{3,2},{4,3},{5,4},{6,5},{7,6},{9,8},{10,9},{11,10},{12... | collective-permute-start | bytes 110600 | tf_op jit(solution)/shard_map/ppermute | solution.py:22
  21.2 0.9 copy.319
  23.9 1.3 %multiply_convert_fusion = (bf16[64,4,6,128]{3,0,2,1:T(8,128)(2,1)S(1)}, f32[64,4,6,128]{3,0,2,1:T(8,128)}) fusion(f32[64]{0:T(128)S(1)} %get-tuple-element.107, f32[4,6,128,64]{2,3,1,0:T(8,128)S(1)} %convolution_bitcast_fusion, f32[4,6,128,64]{2,3,1,0:T(8,128)S(1)} %convolution_bitcast_fusion.1, bf16[9,12,6,6,128]{4,1,0,3,2:T(8,128)(2,1)S(1)} %fusion.51, ...), kind=kOutput, calls=%fused_computation.74 | convolution fusion | flops 44040192 | bytes 4116992 | tf_op jit(solution)/shard_map/eoc,eczxy->ozxy/dot_general | solution.py:85
  26.0 0.8 fusion.114
  31.4 2.9 %collective-permute-start.4 = (bf16[8,1,4,128]{3,0,2,1:T(8,128)(2,1)S(1)}, bf16[8,1,4,128]{3,0,2,1:T(8,128)(2,1)S(1)}, u32[]{:S(2)}, u32[]{:S(2)}) collective-permute-start(bf16[8,1,4,128]{3,0,2,1:T(8,128)(2,1)S(1)} %get-tuple-element.104), channel_id=1, source_target_pairs={{0,8},{8,16},{16,24},{24,32},{32,40},{40,48},{48,56},{56,64},{64,7... | collective-permute-start | bytes 24584 | tf_op jit(solution)/shard_map/ppermute | solution.py:20
  34.3 3.0 %collective-permute-start.5 = (bf16[8,1,4,128]{3,0,2,1:T(8,128)(2,1)S(1)}, bf16[8,1,4,128]{3,0,2,1:T(8,128)(2,1)S(1)}, u32[]{:S(2)}, u32[]{:S(2)}) collective-permute-start(bf16[8,1,4,128]{3,0,2,1:T(8,128)(2,1)S(1)} %get-tuple-element.105), channel_id=1, source_target_pairs={{8,0},{16,8},{24,16},{32,24},{40,32},{48,40},{56,48},{64,56},{72,6... | collective-permute-start | bytes 24584 | tf_op jit(solution)/shard_map/ppermute | solution.py:22
  37.9 2.9 %collective-permute-done.5 = bf16[8,1,4,128]{3,0,2,1:T(8,128)(2,1)S(1)} collective-permute-done((bf16[8,1,4,128]{3,0,2,1:T(8,128)(2,1)S(1)}, bf16[8,1,4,128]{3,0,2,1:T(8,128)(2,1)S(1)}, u32[]{:S(2)}, u32[]{:S(2)}) %collective-permute-start.5) | collective-permute-done | bytes 8224 | tf_op jit(solution)/shard_map/ppermute | solution.py:22
  40.8 1.9 %collective-permute-start.6 = (bf16[8,4,1,128]{3,0,2,1:T(8,128)(2,1)S(1)}, bf16[8,4,1,128]{3,0,2,1:T(8,128)(2,1)S(1)}, u32[]{:S(2)}, u32[]{:S(2)}) collective-permute-start(bf16[8,4,1,128]{3,0,2,1:T(8,128)(2,1)S(1)} %get-tuple-element.100), channel_id=1, source_target_pairs={{0,1},{1,2},{2,3},{3,4},{4,5},{5,6},{6,7},{8,9},{9,10},{10,11},{11... | collective-permute-start | bytes 24584 | tf_op jit(solution)/shard_map/ppermute | solution.py:20
  42.7 4.5 %collective-permute-start.7 = (bf16[8,4,1,128]{3,0,2,1:T(8,128)(2,1)S(1)}, bf16[8,4,1,128]{3,0,2,1:T(8,128)(2,1)S(1)}, u32[]{:S(2)}, u32[]{:S(2)}) collective-permute-start(bf16[8,4,1,128]{3,0,2,1:T(8,128)(2,1)S(1)} %get-tuple-element.101), channel_id=1, source_target_pairs={{1,0},{2,1},{3,2},{4,3},{5,4},{6,5},{7,6},{9,8},{10,9},{11,10},{12... | collective-permute-start | bytes 24584 | tf_op jit(solution)/shard_map/ppermute | solution.py:22
  47.6 1.0 collective-permute-done.7
  50.3 1.3 convert_reduce_fusion.1
  53.6 1.0 all_to_all.10
  54.6 15.0 %all-to-all-start = ((f32[64,1,607]{2,1,0:T(1,128)}), f32[64,1,607]{2,1,0:T(1,128)S(1)}, u32[]{:S(2)}, u32[]{:S(2)}) async-start(f32[64,1,607]{2,1,0:T(1,128)} %all_to_all.10), calls=%async_computation | async-start | bytes 327680 | tf_op jit(solution)/shard_map/all_to_all | solution.py:217
  69.7 10.3 %all-to-all-done = f32[64,1,607]{2,1,0:T(1,128)S(1)} async-done(((f32[64,1,607]{2,1,0:T(1,128)}), f32[64,1,607]{2,1,0:T(1,128)S(1)}, u32[]{:S(2)}, u32[]{:S(2)}) %all-to-all-start) | async-done | bytes 155424 | tf_op jit(solution)/shard_map/all_to_all | solution.py:217
  80.1 1.9 %collective-permute-start.12 = (f32[607]{0:T(1024)S(1)}, f32[607]{0:T(1024)S(1)}, u32[]{:S(2)}, u32[]{:S(2)}) collective-permute-start(f32[607]{0:T(1024)S(1)} %reduce_sum.39), channel_id=1, source_target_pairs={{0,1},{1,0},{2,3},{3,2},{4,5},{5,4},{6,7},{7,6},{8,9},{9,8},{10,11... | collective-permute-start | bytes 7292 | tf_op jit(solution)/shard_map/ppermute | solution.py:145
  82.1 2.6 %collective-permute-start.8 = (bf16[64,1,4,128]{3,0,2,1:T(8,128)(2,1)S(1)}, bf16[64,1,4,128]{3,0,2,1:T(8,128)(2,1)S(1)}, u32[]{:S(2)}, u32[]{:S(2)}) collective-permute-start(bf16[64,1,4,128]{3,0,2,1:T(8,128)(2,1)S(1)} %get-tuple-element.78), channel_id=1, source_target_pairs={{0,8},{8,16},{16,24},{24,32},{32,40},{40,48},{48,56},{56,64},{64,7... | collective-permute-start | bytes 196616 | tf_op jit(solution)/shard_map/ppermute | solution.py:20
  84.7 6.5 %collective-permute-start.13 = (f32[607]{0:T(1024)S(1)}, f32[607]{0:T(1024)S(1)}, u32[]{:S(2)}, u32[]{:S(2)}) collective-permute-start(f32[607]{0:T(1024)S(1)} %add.213), channel_id=1, source_target_pairs={{0,2},{1,3},{2,0},{3,1},{4,6},{5,7},{6,4},{7,5},{8,10},{9,11},{10,... | collective-permute-start | bytes 7292 | tf_op jit(solution)/shard_map/ppermute | solution.py:145
  92.0 1.8 %reshape.123 = f32[4,8,256]{2,1,0:T(8,128)} reshape(f32[2,2,4,2,128,2]{5,4,3,2,1,0:T(8,128)S(1)} %bitcast.577) | data formatting | bytes 65536 | tf_op jit(solution)/shard_map/reshape | solution.py:50
  93.9 3.2 %collective-permute-start.9 = (bf16[64,1,4,128]{3,0,2,1:T(8,128)(2,1)S(1)}, bf16[64,1,4,128]{3,0,2,1:T(8,128)(2,1)S(1)}, u32[]{:S(2)}, u32[]{:S(2)}) collective-permute-start(bf16[64,1,4,128]{3,0,2,1:T(8,128)(2,1)S(1)} %get-tuple-element.77), channel_id=1, source_target_pairs={{8,0},{16,8},{24,16},{32,24},{40,32},{48,40},{56,48},{64,56},{72,6... | collective-permute-start | bytes 196616 | tf_op jit(solution)/shard_map/ppermute | solution.py:22
  97.1 4.1 %collective-permute-start.14 = (f32[607]{0:T(1024)S(1)}, f32[607]{0:T(1024)S(1)}, u32[]{:S(2)}, u32[]{:S(2)}) collective-permute-start(f32[607]{0:T(1024)S(1)} %add.214), channel_id=1, source_target_pairs={{0,4},{1,5},{2,6},{3,7},{4,0},{5,1},{6,2},{7,3},{8,12},{9,13},{10,... | collective-permute-start | bytes 7292 | tf_op jit(solution)/shard_map/ppermute | solution.py:145
  101.3 1.9 %collective-permute-start.10 = (bf16[64,4,1,128]{3,0,2,1:T(8,128)(2,1)S(1)}, bf16[64,4,1,128]{3,0,2,1:T(8,128)(2,1)S(1)}, u32[]{:S(2)}, u32[]{:S(2)}) collective-permute-start(bf16[64,4,1,128]{3,0,2,1:T(8,128)(2,1)S(1)} %get-tuple-element.75), channel_id=1, source_target_pairs={{0,1},{1,2},{2,3},{3,4},{4,5},{5,6},{6,7},{8,9},{9,10},{10,11},{11... | collective-permute-start | bytes 196616 | tf_op jit(solution)/shard_map/ppermute | solution.py:20
  103.3 4.5 %collective-permute-start.11 = (bf16[64,4,1,128]{3,0,2,1:T(8,128)(2,1)S(1)}, bf16[64,4,1,128]{3,0,2,1:T(8,128)(2,1)S(1)}, u32[]{:S(2)}, u32[]{:S(2)}) collective-permute-start(bf16[64,4,1,128]{3,0,2,1:T(8,128)(2,1)S(1)} %get-tuple-element.76), channel_id=1, source_target_pairs={{1,0},{2,1},{3,2},{4,3},{5,4},{6,5},{7,6},{9,8},{10,9},{11,10},{12... | collective-permute-start | bytes 196616 | tf_op jit(solution)/shard_map/ppermute | solution.py:22
  108.6 9.0 %all-to-all-start.1 = ((f32[64,1,607]{2,1,0:T(1,128)}), f32[64,1,607]{2,1,0:T(1,128)S(1)}, u32[]{:S(2)}, u32[]{:S(2)}) async-start(f32[64,1,607]{2,1,0:T(1,128)} %broadcast_in_dim.23), calls=%async_computation.1 | async-start | bytes 327680 | tf_op jit(solution)/shard_map/all_to_all | solution.py:223
  121.5 1.8 %reshape.129 = f32[4,8,256]{2,1,0:T(8,128)} reshape(f32[2,2,4,2,128,2]{5,4,3,2,1,0:T(8,128)S(1)} %bitcast.578) | data formatting | bytes 65536 | tf_op jit(solution)/shard_map/reshape | solution.py:50
  124.0 4.0 %all-to-all-done.1 = f32[64,1,607]{2,1,0:T(1,128)S(1)} async-done(((f32[64,1,607]{2,1,0:T(1,128)}), f32[64,1,607]{2,1,0:T(1,128)S(1)}, u32[]{:S(2)}, u32[]{:S(2)}) %all-to-all-start.1) | async-done | bytes 155424 | tf_op jit(solution)/shard_map/all_to_all | solution.py:223
  129.5 1.0 reshape.131
  130.5 1.1 copy.395
  (158 shorter events, 23.5 us)
Async XLA Ops:
  0.6 24.6 %copy-start = (bf16[64,64]{1,0:T(8,128)(2,1)S(1)}, bf16[64,64]{1,0:T(8,128)(2,1)}, u32[]{:S(2)}) copy-start(bf16[64,64]{1,0:T(8,128)(2,1)} %param.13) | copy-start | bytes 24580
  2.2 8.6 %collective-permute-start = (bf16[12,2,4,128]{3,0,2,1:T(8,128)(2,1)S(1)}, bf16[12,2,4,128]{3,0,2,1:T(8,128)(2,1)S(1)}, u32[]{:S(2)}, u32[]{:S(2)}) collective-permute-start(bf16[12,2,4,128]{3,0,2,1:T(8,128)(2,1)S(1)} %pad_maximum_fusion.15), channel_id=1, source_target_pairs={{0,8},{8,16},{16,24},{24,32},{32,40},{40,48},{48,56},{56,64},{64,7... | collective-permute-start | bytes 73736 | tf_op jit(solution)/shard_map/ppermute | solution.py:20
  7.3 6.7 %collective-permute-start.1 = (bf16[12,2,4,128]{3,0,2,1:T(8,128)(2,1)S(1)}, bf16[12,2,4,128]{3,0,2,1:T(8,128)(2,1)S(1)}, u32[]{:S(2)}, u32[]{:S(2)}) collective-permute-start(bf16[12,2,4,128]{3,0,2,1:T(8,128)(2,1)S(1)} %pad_maximum_fusion.15), channel_id=1, source_target_pairs={{8,0},{16,8},{24,16},{32,24},{40,32},{48,40},{56,48},{64,56},{72,6... | collective-permute-start | bytes 73736 | tf_op jit(solution)/shard_map/ppermute | solution.py:22
  14.0 8.2 %collective-permute-start.2 = (bf16[12,6,2,128]{3,0,2,1:T(8,128)(2,1)S(1)}, bf16[12,6,2,128]{3,0,2,1:T(8,128)(2,1)S(1)}, u32[]{:S(2)}, u32[]{:S(2)}) collective-permute-start(bf16[12,6,2,128]{3,0,2,1:T(8,128)(2,1)S(1)} %get-tuple-element.88), channel_id=1, source_target_pairs={{0,1},{1,2},{2,3},{3,4},{4,5},{5,6},{6,7},{8,9},{9,10},{10,11},{11... | collective-permute-start | bytes 110600 | tf_op jit(solution)/shard_map/ppermute | solution.py:20
  15.9 6.3 %collective-permute-start.3 = (bf16[12,6,2,128]{3,0,2,1:T(8,128)(2,1)S(1)}, bf16[12,6,2,128]{3,0,2,1:T(8,128)(2,1)S(1)}, u32[]{:S(2)}, u32[]{:S(2)}) collective-permute-start(bf16[12,6,2,128]{3,0,2,1:T(8,128)(2,1)S(1)} %get-tuple-element.89), channel_id=1, source_target_pairs={{1,0},{2,1},{3,2},{4,3},{5,4},{6,5},{7,6},{9,8},{10,9},{11,10},{12... | collective-permute-start | bytes 110600 | tf_op jit(solution)/shard_map/ppermute | solution.py:22
  26.0 0.9 copy-start.1
  31.4 6.4 %collective-permute-start.4 = (bf16[8,1,4,128]{3,0,2,1:T(8,128)(2,1)S(1)}, bf16[8,1,4,128]{3,0,2,1:T(8,128)(2,1)S(1)}, u32[]{:S(2)}, u32[]{:S(2)}) collective-permute-start(bf16[8,1,4,128]{3,0,2,1:T(8,128)(2,1)S(1)} %get-tuple-element.104), channel_id=1, source_target_pairs={{0,8},{8,16},{16,24},{24,32},{32,40},{40,48},{48,56},{56,64},{64,7... | collective-permute-start | bytes 24584 | tf_op jit(solution)/shard_map/ppermute | solution.py:20
  34.3 6.4 %collective-permute-start.5 = (bf16[8,1,4,128]{3,0,2,1:T(8,128)(2,1)S(1)}, bf16[8,1,4,128]{3,0,2,1:T(8,128)(2,1)S(1)}, u32[]{:S(2)}, u32[]{:S(2)}) collective-permute-start(bf16[8,1,4,128]{3,0,2,1:T(8,128)(2,1)S(1)} %get-tuple-element.105), channel_id=1, source_target_pairs={{8,0},{16,8},{24,16},{32,24},{40,32},{48,40},{56,48},{64,56},{72,6... | collective-permute-start | bytes 24584 | tf_op jit(solution)/shard_map/ppermute | solution.py:22
  40.8 6.8 %collective-permute-start.6 = (bf16[8,4,1,128]{3,0,2,1:T(8,128)(2,1)S(1)}, bf16[8,4,1,128]{3,0,2,1:T(8,128)(2,1)S(1)}, u32[]{:S(2)}, u32[]{:S(2)}) collective-permute-start(bf16[8,4,1,128]{3,0,2,1:T(8,128)(2,1)S(1)} %get-tuple-element.100), channel_id=1, source_target_pairs={{0,1},{1,2},{2,3},{3,4},{4,5},{5,6},{6,7},{8,9},{9,10},{10,11},{11... | collective-permute-start | bytes 24584 | tf_op jit(solution)/shard_map/ppermute | solution.py:20
  42.7 5.9 %collective-permute-start.7 = (bf16[8,4,1,128]{3,0,2,1:T(8,128)(2,1)S(1)}, bf16[8,4,1,128]{3,0,2,1:T(8,128)(2,1)S(1)}, u32[]{:S(2)}, u32[]{:S(2)}) collective-permute-start(bf16[8,4,1,128]{3,0,2,1:T(8,128)(2,1)S(1)} %get-tuple-element.101), channel_id=1, source_target_pairs={{1,0},{2,1},{3,2},{4,3},{5,4},{6,5},{7,6},{9,8},{10,9},{11,10},{12... | collective-permute-start | bytes 24584 | tf_op jit(solution)/shard_map/ppermute | solution.py:22
  53.5 37.8 %copy-start.2 = (f32[8,8,1,1]{1,0,3,2:T(8,128)S(1)}, f32[8,8,1,1]{1,0,3,2:T(8,128)}, u32[]{:S(2)}) copy-start(f32[8,8,1,1]{1,0,3,2:T(8,128)} %constant.54) | copy-start | bytes 772
  54.6 25.4 %all-to-all-start = ((f32[64,1,607]{2,1,0:T(1,128)}), f32[64,1,607]{2,1,0:T(1,128)S(1)}, u32[]{:S(2)}, u32[]{:S(2)}) async-start(f32[64,1,607]{2,1,0:T(1,128)} %all_to_all.10), calls=%async_computation | async-start | bytes 327680 | tf_op jit(solution)/shard_map/all_to_all | solution.py:217
  80.1 4.6 %collective-permute-start.12 = (f32[607]{0:T(1024)S(1)}, f32[607]{0:T(1024)S(1)}, u32[]{:S(2)}, u32[]{:S(2)}) collective-permute-start(f32[607]{0:T(1024)S(1)} %reduce_sum.39), channel_id=1, source_target_pairs={{0,1},{1,0},{2,3},{3,2},{4,5},{5,4},{6,7},{7,6},{8,9},{9,8},{10,11... | collective-permute-start | bytes 7292 | tf_op jit(solution)/shard_map/ppermute | solution.py:145
  82.1 19.2 %collective-permute-start.8 = (bf16[64,1,4,128]{3,0,2,1:T(8,128)(2,1)S(1)}, bf16[64,1,4,128]{3,0,2,1:T(8,128)(2,1)S(1)}, u32[]{:S(2)}, u32[]{:S(2)}) collective-permute-start(bf16[64,1,4,128]{3,0,2,1:T(8,128)(2,1)S(1)} %get-tuple-element.78), channel_id=1, source_target_pairs={{0,8},{8,16},{16,24},{24,32},{32,40},{40,48},{48,56},{56,64},{64,7... | collective-permute-start | bytes 196616 | tf_op jit(solution)/shard_map/ppermute | solution.py:20
  84.7 12.4 %collective-permute-start.13 = (f32[607]{0:T(1024)S(1)}, f32[607]{0:T(1024)S(1)}, u32[]{:S(2)}, u32[]{:S(2)}) collective-permute-start(f32[607]{0:T(1024)S(1)} %add.213), channel_id=1, source_target_pairs={{0,2},{1,3},{2,0},{3,1},{4,6},{5,7},{6,4},{7,5},{8,10},{9,11},{10,... | collective-permute-start | bytes 7292 | tf_op jit(solution)/shard_map/ppermute | solution.py:145
  93.9 7.4 %collective-permute-start.9 = (bf16[64,1,4,128]{3,0,2,1:T(8,128)(2,1)S(1)}, bf16[64,1,4,128]{3,0,2,1:T(8,128)(2,1)S(1)}, u32[]{:S(2)}, u32[]{:S(2)}) collective-permute-start(bf16[64,1,4,128]{3,0,2,1:T(8,128)(2,1)S(1)} %get-tuple-element.77), channel_id=1, source_target_pairs={{8,0},{16,8},{24,16},{32,24},{40,32},{48,40},{56,48},{64,56},{72,6... | collective-permute-start | bytes 196616 | tf_op jit(solution)/shard_map/ppermute | solution.py:22
  97.1 10.7 %collective-permute-start.14 = (f32[607]{0:T(1024)S(1)}, f32[607]{0:T(1024)S(1)}, u32[]{:S(2)}, u32[]{:S(2)}) collective-permute-start(f32[607]{0:T(1024)S(1)} %add.214), channel_id=1, source_target_pairs={{0,4},{1,5},{2,6},{3,7},{4,0},{5,1},{6,2},{7,3},{8,12},{9,13},{10,... | collective-permute-start | bytes 7292 | tf_op jit(solution)/shard_map/ppermute | solution.py:145
  101.3 16.2 %collective-permute-start.10 = (bf16[64,4,1,128]{3,0,2,1:T(8,128)(2,1)S(1)}, bf16[64,4,1,128]{3,0,2,1:T(8,128)(2,1)S(1)}, u32[]{:S(2)}, u32[]{:S(2)}) collective-permute-start(bf16[64,4,1,128]{3,0,2,1:T(8,128)(2,1)S(1)} %get-tuple-element.75), channel_id=1, source_target_pairs={{0,1},{1,2},{2,3},{3,4},{4,5},{5,6},{6,7},{8,9},{9,10},{10,11},{11... | collective-permute-start | bytes 196616 | tf_op jit(solution)/shard_map/ppermute | solution.py:20
  103.3 14.3 %collective-permute-start.11 = (bf16[64,4,1,128]{3,0,2,1:T(8,128)(2,1)S(1)}, bf16[64,4,1,128]{3,0,2,1:T(8,128)(2,1)S(1)}, u32[]{:S(2)}, u32[]{:S(2)}) collective-permute-start(bf16[64,4,1,128]{3,0,2,1:T(8,128)(2,1)S(1)} %get-tuple-element.76), channel_id=1, source_target_pairs={{1,0},{2,1},{3,2},{4,3},{5,4},{6,5},{7,6},{9,8},{10,9},{11,10},{12... | collective-permute-start | bytes 196616 | tf_op jit(solution)/shard_map/ppermute | solution.py:22
  108.6 19.4 %all-to-all-start.1 = ((f32[64,1,607]{2,1,0:T(1,128)}), f32[64,1,607]{2,1,0:T(1,128)S(1)}, u32[]{:S(2)}, u32[]{:S(2)}) async-start(f32[64,1,607]{2,1,0:T(1,128)} %broadcast_in_dim.23), calls=%async_computation.1 | async-start | bytes 327680 | tf_op jit(solution)/shard_map/all_to_all | solution.py:223

commit v10 on v9

--- a/solution.py
+++ b/solution.py
@@ -57,7 +57,7 @@
 
 def shift_stack(padded, x_rows):
     y_cols = padded.shape[3] - 2
-    if padded.shape[0] > 16:
+    if padded.shape[0] > 64:
         steps = [(None, y_step) for y_step in range(3)]
     else:
         steps = [(x_step, y_step) for x_step in range(3) for y_step in range(3)]

time: 134 us -> 134 us (level)
  local copies, waits for them, and re-layouts: 21.8 us -> 24.6 us
  matrix products: 11.6 us -> 8.98 us
    dot_general x12 -> x6, matrix products: 3.86 us -> 2.88 us  [forward_taps(): jnp.einsum('eoc,eczxy->ozxy', taps, window, preferred_element_type=jnp.fl...]
    unnamed x34 -> x50, local copies, waits for them, and re-layouts: 4.83 us -> 5.7 us
    slice x4 -> x3, local copies, waits for them, and re-layouts: 2.24 us -> 3.03 us  [the longest x2 1.76 us: forward_taps(): taps = kernel[z_step].reshape((9,) + weight.shape[1:])]
    dot_general x12 -> x6, matrix products: 3.02 us -> 2.34 us  [weight_taps(): jnp.einsum('ozxy,eczxy->eoc', grad, window, preferred_element_type=jnp.fl...]
  transfers between devices with their start and end apart: 17 -> 17, of which waited for: 5 -> 6; matrix products, arithmetic and copies ran while one was open for 11% -> 11% of each run, Pallas kernels for 0% -> 0%
where the time goes in v10:
time: 134 us; the launch traced here: 133 us
  starting transfers between devices  75.4 us (56%)
  local copies, waits for them, and re-layouts  24.6 us (18%)
  waiting for transfers between devices  20.8 us (16%)
  matrix products  8.98 us (7%)
  other arithmetic  2.07 us (2%)
  between operations  1.6 us (1%)
    ppermute x6, starting transfers between devices, extended(): lax.ppermute(head, axis, [((i + 1) % count, i) for i in range(ends)])  21.9 us
    ppermute x6, starting transfers between devices, extended(): lax.ppermute(tail, axis, [(i, (i + 1) % count) for i in range(ends)])  16.3 us
    all_to_all x1, starting transfers between devices, per_device(): owned = lax.all_to_all(chunks, 'gz', 0, 0, tiled=False).sum(0)  15.7 us
    ppermute x3, starting transfers between devices, butterfly_sum(): flat = flat + lax.ppermute(flat, axis, [(i, i ^ bit) for i in range(count)])  12.5 us
    all_to_all x1, waiting for transfers between devices, per_device(): owned = lax.all_to_all(chunks, 'gz', 0, 0, tiled=False).sum(0)  10.4 us
    all_to_all x1, starting transfers between devices, per_device(): lax.all_to_all(jnp.broadcast_to(owned, (count,) + owned.shape), 'gz', 0,...  8.97 us
    ppermute x6, waiting for transfers between devices, extended(): lax.ppermute(head, axis, [((i + 1) % count, i) for i in range(ends)])  6.91 us
    unnamed x50, local copies, waits for them, and re-layouts  5.7 us
  transfers between devices with their start and end apart: 17, of which 6 were waited for; matrix products, arithmetic and copies ran while one was open for 11% of the time, Pallas kernels for 0%

profile of v10, /device:TPU:56, one launch (start us, length us, event | category | flops | bytes accessed | tf_op | source)
XLA Modules:
  0.0 133.5 jit_solution(13153251058709333686)
XLA Ops:
  2.2 5.1 %collective-permute-start = (bf16[12,2,4,128]{3,0,2,1:T(8,128)(2,1)S(1)}, bf16[12,2,4,128]{3,0,2,1:T(8,128)(2,1)S(1)}, u32[]{:S(2)}, u32[]{:S(2)}) collective-permute-start(bf16[12,2,4,128]{3,0,2,1:T(8,128)(2,1)S(1)} %pad_maximum_fusion.15), channel_id=1, source_target_pairs={{0,8},{8,16},{16,24},{24,32},{32,40},{40,48},{48,56},{56,64},{64,7... | collective-permute-start | bytes 73736 | tf_op jit(solution)/shard_map/ppermute | solution.py:20
  7.3 1.9 %collective-permute-start.1 = (bf16[12,2,4,128]{3,0,2,1:T(8,128)(2,1)S(1)}, bf16[12,2,4,128]{3,0,2,1:T(8,128)(2,1)S(1)}, u32[]{:S(2)}, u32[]{:S(2)}) collective-permute-start(bf16[12,2,4,128]{3,0,2,1:T(8,128)(2,1)S(1)} %pad_maximum_fusion.15), channel_id=1, source_target_pairs={{8,0},{16,8},{24,16},{32,24},{40,32},{48,40},{56,48},{64,56},{72,6... | collective-permute-start | bytes 73736 | tf_op jit(solution)/shard_map/ppermute | solution.py:22
  9.2 1.0 fusion.141
  11.8 2.2 %collective-permute-done.1 = bf16[12,2,4,128]{3,0,2,1:T(8,128)(2,1)S(1)} collective-permute-done((bf16[12,2,4,128]{3,0,2,1:T(8,128)(2,1)S(1)}, bf16[12,2,4,128]{3,0,2,1:T(8,128)(2,1)S(1)}, u32[]{:S(2)}, u32[]{:S(2)}) %collective-permute-start.1) | collective-permute-done | bytes 24608 | tf_op jit(solution)/shard_map/ppermute | solution.py:22
  14.0 1.9 %collective-permute-start.2 = (bf16[12,6,2,128]{3,0,2,1:T(8,128)(2,1)S(1)}, bf16[12,6,2,128]{3,0,2,1:T(8,128)(2,1)S(1)}, u32[]{:S(2)}, u32[]{:S(2)}) collective-permute-start(bf16[12,6,2,128]{3,0,2,1:T(8,128)(2,1)S(1)} %get-tuple-element.64), channel_id=1, source_target_pairs={{0,1},{1,2},{2,3},{3,4},{4,5},{5,6},{6,7},{8,9},{9,10},{10,11},{11... | collective-permute-start | bytes 110600 | tf_op jit(solution)/shard_map/ppermute | solution.py:20
  15.9 4.5 %collective-permute-start.3 = (bf16[12,6,2,128]{3,0,2,1:T(8,128)(2,1)S(1)}, bf16[12,6,2,128]{3,0,2,1:T(8,128)(2,1)S(1)}, u32[]{:S(2)}, u32[]{:S(2)}) collective-permute-start(bf16[12,6,2,128]{3,0,2,1:T(8,128)(2,1)S(1)} %get-tuple-element.65), channel_id=1, source_target_pairs={{1,0},{2,1},{3,2},{4,3},{5,4},{6,5},{7,6},{9,8},{10,9},{11,10},{12... | collective-permute-start | bytes 110600 | tf_op jit(solution)/shard_map/ppermute | solution.py:22
  23.8 1.3 multiply_convert_fusion
  27.0 1.3 fusion.137
  31.1 2.8 %collective-permute-start.4 = (bf16[8,1,4,128]{3,0,2,1:T(8,128)(2,1)S(1)}, bf16[8,1,4,128]{3,0,2,1:T(8,128)(2,1)S(1)}, u32[]{:S(2)}, u32[]{:S(2)}) collective-permute-start(bf16[8,1,4,128]{3,0,2,1:T(8,128)(2,1)S(1)} %get-tuple-element.80), channel_id=1, source_target_pairs={{0,8},{8,16},{16,24},{24,32},{32,40},{40,48},{48,56},{56,64},{64,7... | collective-permute-start | bytes 24584 | tf_op jit(solution)/shard_map/ppermute | solution.py:20
  33.9 3.0 %collective-permute-start.5 = (bf16[8,1,4,128]{3,0,2,1:T(8,128)(2,1)S(1)}, bf16[8,1,4,128]{3,0,2,1:T(8,128)(2,1)S(1)}, u32[]{:S(2)}, u32[]{:S(2)}) collective-permute-start(bf16[8,1,4,128]{3,0,2,1:T(8,128)(2,1)S(1)} %get-tuple-element.81), channel_id=1, source_target_pairs={{8,0},{16,8},{24,16},{32,24},{40,32},{48,40},{56,48},{64,56},{72,6... | collective-permute-start | bytes 24584 | tf_op jit(solution)/shard_map/ppermute | solution.py:22
  37.5 2.9 %collective-permute-done.5 = bf16[8,1,4,128]{3,0,2,1:T(8,128)(2,1)S(1)} collective-permute-done((bf16[8,1,4,128]{3,0,2,1:T(8,128)(2,1)S(1)}, bf16[8,1,4,128]{3,0,2,1:T(8,128)(2,1)S(1)}, u32[]{:S(2)}, u32[]{:S(2)}) %collective-permute-start.5) | collective-permute-done | bytes 8224 | tf_op jit(solution)/shard_map/ppermute | solution.py:22
  40.4 1.9 %collective-permute-start.6 = (bf16[8,4,1,128]{3,0,2,1:T(8,128)(2,1)S(1)}, bf16[8,4,1,128]{3,0,2,1:T(8,128)(2,1)S(1)}, u32[]{:S(2)}, u32[]{:S(2)}) collective-permute-start(bf16[8,4,1,128]{3,0,2,1:T(8,128)(2,1)S(1)} %get-tuple-element.76), channel_id=1, source_target_pairs={{0,1},{1,2},{2,3},{3,4},{4,5},{5,6},{6,7},{8,9},{9,10},{10,11},{11... | collective-permute-start | bytes 24584 | tf_op jit(solution)/shard_map/ppermute | solution.py:20
  42.3 4.5 %collective-permute-start.7 = (bf16[8,4,1,128]{3,0,2,1:T(8,128)(2,1)S(1)}, bf16[8,4,1,128]{3,0,2,1:T(8,128)(2,1)S(1)}, u32[]{:S(2)}, u32[]{:S(2)}) collective-permute-start(bf16[8,4,1,128]{3,0,2,1:T(8,128)(2,1)S(1)} %get-tuple-element.77), channel_id=1, source_target_pairs={{1,0},{2,1},{3,2},{4,3},{5,4},{6,5},{7,6},{9,8},{10,9},{11,10},{12... | collective-permute-start | bytes 24584 | tf_op jit(solution)/shard_map/ppermute | solution.py:22
  47.2 1.0 collective-permute-done.7
  49.9 1.3 convert_reduce_fusion.1
  53.2 1.0 all_to_all.10
  54.2 15.7 %all-to-all-start = ((f32[64,1,607]{2,1,0:T(1,128)}), f32[64,1,607]{2,1,0:T(1,128)S(1)}, u32[]{:S(2)}, u32[]{:S(2)}) async-start(f32[64,1,607]{2,1,0:T(1,128)} %all_to_all.10), calls=%async_computation | async-start | bytes 327680 | tf_op jit(solution)/shard_map/all_to_all | solution.py:217
  70.0 10.4 %all-to-all-done = f32[64,1,607]{2,1,0:T(1,128)S(1)} async-done(((f32[64,1,607]{2,1,0:T(1,128)}), f32[64,1,607]{2,1,0:T(1,128)S(1)}, u32[]{:S(2)}, u32[]{:S(2)}) %all-to-all-start) | async-done | bytes 155424 | tf_op jit(solution)/shard_map/all_to_all | solution.py:217
  80.5 1.9 %collective-permute-start.12 = (f32[607]{0:T(1024)S(1)}, f32[607]{0:T(1024)S(1)}, u32[]{:S(2)}, u32[]{:S(2)}) collective-permute-start(f32[607]{0:T(1024)S(1)} %reduce_sum.39), channel_id=1, source_target_pairs={{0,1},{1,0},{2,3},{3,2},{4,5},{5,4},{6,7},{7,6},{8,9},{9,8},{10,11... | collective-permute-start | bytes 7292 | tf_op jit(solution)/shard_map/ppermute | solution.py:145
  82.5 2.6 %collective-permute-start.8 = (bf16[64,1,4,128]{3,0,2,1:T(8,128)(2,1)S(1)}, bf16[64,1,4,128]{3,0,2,1:T(8,128)(2,1)S(1)}, u32[]{:S(2)}, u32[]{:S(2)}) collective-permute-start(bf16[64,1,4,128]{3,0,2,1:T(8,128)(2,1)S(1)} %get-tuple-element.60), channel_id=1, source_target_pairs={{0,8},{8,16},{16,24},{24,32},{32,40},{40,48},{48,56},{56,64},{64,7... | collective-permute-start | bytes 196616 | tf_op jit(solution)/shard_map/ppermute | solution.py:20
  85.1 6.5 %collective-permute-start.13 = (f32[607]{0:T(1024)S(1)}, f32[607]{0:T(1024)S(1)}, u32[]{:S(2)}, u32[]{:S(2)}) collective-permute-start(f32[607]{0:T(1024)S(1)} %add.162), channel_id=1, source_target_pairs={{0,2},{1,3},{2,0},{3,1},{4,6},{5,7},{6,4},{7,5},{8,10},{9,11},{10,... | collective-permute-start | bytes 7292 | tf_op jit(solution)/shard_map/ppermute | solution.py:145
  92.4 1.8 %reshape.121 = f32[4,8,256]{2,1,0:T(8,128)} reshape(f32[2,2,4,2,128,2]{5,4,3,2,1,0:T(8,128)S(1)} %bitcast.430) | data formatting | bytes 65536 | tf_op jit(solution)/shard_map/reshape | solution.py:50
  94.3 3.2 %collective-permute-start.9 = (bf16[64,1,4,128]{3,0,2,1:T(8,128)(2,1)S(1)}, bf16[64,1,4,128]{3,0,2,1:T(8,128)(2,1)S(1)}, u32[]{:S(2)}, u32[]{:S(2)}) collective-permute-start(bf16[64,1,4,128]{3,0,2,1:T(8,128)(2,1)S(1)} %get-tuple-element.59), channel_id=1, source_target_pairs={{8,0},{16,8},{24,16},{32,24},{40,32},{48,40},{56,48},{64,56},{72,6... | collective-permute-start | bytes 196616 | tf_op jit(solution)/shard_map/ppermute | solution.py:22
  97.5 4.1 %collective-permute-start.14 = (f32[607]{0:T(1024)S(1)}, f32[607]{0:T(1024)S(1)}, u32[]{:S(2)}, u32[]{:S(2)}) collective-permute-start(f32[607]{0:T(1024)S(1)} %add.163), channel_id=1, source_target_pairs={{0,4},{1,5},{2,6},{3,7},{4,0},{5,1},{6,2},{7,3},{8,12},{9,13},{10,... | collective-permute-start | bytes 7292 | tf_op jit(solution)/shard_map/ppermute | solution.py:145
  101.7 1.9 %collective-permute-start.10 = (bf16[64,4,1,128]{3,0,2,1:T(8,128)(2,1)S(1)}, bf16[64,4,1,128]{3,0,2,1:T(8,128)(2,1)S(1)}, u32[]{:S(2)}, u32[]{:S(2)}) collective-permute-start(bf16[64,4,1,128]{3,0,2,1:T(8,128)(2,1)S(1)} %get-tuple-element.57), channel_id=1, source_target_pairs={{0,1},{1,2},{2,3},{3,4},{4,5},{5,6},{6,7},{8,9},{9,10},{10,11},{11... | collective-permute-start | bytes 196616 | tf_op jit(solution)/shard_map/ppermute | solution.py:20
  103.7 4.7 %collective-permute-start.11 = (bf16[64,4,1,128]{3,0,2,1:T(8,128)(2,1)S(1)}, bf16[64,4,1,128]{3,0,2,1:T(8,128)(2,1)S(1)}, u32[]{:S(2)}, u32[]{:S(2)}) collective-permute-start(bf16[64,4,1,128]{3,0,2,1:T(8,128)(2,1)S(1)} %get-tuple-element.58), channel_id=1, source_target_pairs={{1,0},{2,1},{3,2},{4,3},{5,4},{6,5},{7,6},{9,8},{10,9},{11,10},{12... | collective-permute-start | bytes 196616 | tf_op jit(solution)/shard_map/ppermute | solution.py:22
  109.2 9.0 %all-to-all-start.1 = ((f32[64,1,607]{2,1,0:T(1,128)}), f32[64,1,607]{2,1,0:T(1,128)S(1)}, u32[]{:S(2)}, u32[]{:S(2)}) async-start(f32[64,1,607]{2,1,0:T(1,128)} %broadcast_in_dim.23), calls=%async_computation.1 | async-start | bytes 327680 | tf_op jit(solution)/shard_map/all_to_all | solution.py:223
  119.6 1.3 fusion.136
  122.7 1.8 %reshape.126 = f32[4,8,256]{2,1,0:T(8,128)} reshape(f32[2,2,4,2,128,2]{5,4,3,2,1,0:T(8,128)S(1)} %bitcast.431) | data formatting | bytes 65536 | tf_op jit(solution)/shard_map/reshape | solution.py:50
  125.2 3.5 %all-to-all-done.1 = f32[64,1,607]{2,1,0:T(1,128)S(1)} async-done(((f32[64,1,607]{2,1,0:T(1,128)}), f32[64,1,607]{2,1,0:T(1,128)S(1)}, u32[]{:S(2)}, u32[]{:S(2)}) %all-to-all-start.1) | async-done | bytes 155424 | tf_op jit(solution)/shard_map/all_to_all | solution.py:223
  130.1 1.0 reshape.128
  131.1 1.1 copy.236
  (151 shorter events, 23.7 us)
Async XLA Ops:
  0.6 24.5 %copy-start = (bf16[64,64]{1,0:T(8,128)(2,1)S(1)}, bf16[64,64]{1,0:T(8,128)(2,1)}, u32[]{:S(2)}) copy-start(bf16[64,64]{1,0:T(8,128)(2,1)} %param.13) | copy-start | bytes 24580
  2.2 9.6 %collective-permute-start = (bf16[12,2,4,128]{3,0,2,1:T(8,128)(2,1)S(1)}, bf16[12,2,4,128]{3,0,2,1:T(8,128)(2,1)S(1)}, u32[]{:S(2)}, u32[]{:S(2)}) collective-permute-start(bf16[12,2,4,128]{3,0,2,1:T(8,128)(2,1)S(1)} %pad_maximum_fusion.15), channel_id=1, source_target_pairs={{0,8},{8,16},{16,24},{24,32},{32,40},{40,48},{48,56},{56,64},{64,7... | collective-permute-start | bytes 73736 | tf_op jit(solution)/shard_map/ppermute | solution.py:20
  7.3 6.7 %collective-permute-start.1 = (bf16[12,2,4,128]{3,0,2,1:T(8,128)(2,1)S(1)}, bf16[12,2,4,128]{3,0,2,1:T(8,128)(2,1)S(1)}, u32[]{:S(2)}, u32[]{:S(2)}) collective-permute-start(bf16[12,2,4,128]{3,0,2,1:T(8,128)(2,1)S(1)} %pad_maximum_fusion.15), channel_id=1, source_target_pairs={{8,0},{16,8},{24,16},{32,24},{40,32},{48,40},{56,48},{64,56},{72,6... | collective-permute-start | bytes 73736 | tf_op jit(solution)/shard_map/ppermute | solution.py:22
  14.0 7.3 %collective-permute-start.2 = (bf16[12,6,2,128]{3,0,2,1:T(8,128)(2,1)S(1)}, bf16[12,6,2,128]{3,0,2,1:T(8,128)(2,1)S(1)}, u32[]{:S(2)}, u32[]{:S(2)}) collective-permute-start(bf16[12,6,2,128]{3,0,2,1:T(8,128)(2,1)S(1)} %get-tuple-element.64), channel_id=1, source_target_pairs={{0,1},{1,2},{2,3},{3,4},{4,5},{5,6},{6,7},{8,9},{9,10},{10,11},{11... | collective-permute-start | bytes 110600 | tf_op jit(solution)/shard_map/ppermute | solution.py:20
  15.9 6.3 %collective-permute-start.3 = (bf16[12,6,2,128]{3,0,2,1:T(8,128)(2,1)S(1)}, bf16[12,6,2,128]{3,0,2,1:T(8,128)(2,1)S(1)}, u32[]{:S(2)}, u32[]{:S(2)}) collective-permute-start(bf16[12,6,2,128]{3,0,2,1:T(8,128)(2,1)S(1)} %get-tuple-element.65), channel_id=1, source_target_pairs={{1,0},{2,1},{3,2},{4,3},{5,4},{6,5},{7,6},{9,8},{10,9},{11,10},{12... | collective-permute-start | bytes 110600 | tf_op jit(solution)/shard_map/ppermute | solution.py:22
  27.0 1.3 copy-start.1
  31.1 6.4 %collective-permute-start.4 = (bf16[8,1,4,128]{3,0,2,1:T(8,128)(2,1)S(1)}, bf16[8,1,4,128]{3,0,2,1:T(8,128)(2,1)S(1)}, u32[]{:S(2)}, u32[]{:S(2)}) collective-permute-start(bf16[8,1,4,128]{3,0,2,1:T(8,128)(2,1)S(1)} %get-tuple-element.80), channel_id=1, source_target_pairs={{0,8},{8,16},{16,24},{24,32},{32,40},{40,48},{48,56},{56,64},{64,7... | collective-permute-start | bytes 24584 | tf_op jit(solution)/shard_map/ppermute | solution.py:20
  33.9 6.4 %collective-permute-start.5 = (bf16[8,1,4,128]{3,0,2,1:T(8,128)(2,1)S(1)}, bf16[8,1,4,128]{3,0,2,1:T(8,128)(2,1)S(1)}, u32[]{:S(2)}, u32[]{:S(2)}) collective-permute-start(bf16[8,1,4,128]{3,0,2,1:T(8,128)(2,1)S(1)} %get-tuple-element.81), channel_id=1, source_target_pairs={{8,0},{16,8},{24,16},{32,24},{40,32},{48,40},{56,48},{64,56},{72,6... | collective-permute-start | bytes 24584 | tf_op jit(solution)/shard_map/ppermute | solution.py:22
  40.4 6.8 %collective-permute-start.6 = (bf16[8,4,1,128]{3,0,2,1:T(8,128)(2,1)S(1)}, bf16[8,4,1,128]{3,0,2,1:T(8,128)(2,1)S(1)}, u32[]{:S(2)}, u32[]{:S(2)}) collective-permute-start(bf16[8,4,1,128]{3,0,2,1:T(8,128)(2,1)S(1)} %get-tuple-element.76), channel_id=1, source_target_pairs={{0,1},{1,2},{2,3},{3,4},{4,5},{5,6},{6,7},{8,9},{9,10},{10,11},{11... | collective-permute-start | bytes 24584 | tf_op jit(solution)/shard_map/ppermute | solution.py:20
  42.3 5.9 %collective-permute-start.7 = (bf16[8,4,1,128]{3,0,2,1:T(8,128)(2,1)S(1)}, bf16[8,4,1,128]{3,0,2,1:T(8,128)(2,1)S(1)}, u32[]{:S(2)}, u32[]{:S(2)}) collective-permute-start(bf16[8,4,1,128]{3,0,2,1:T(8,128)(2,1)S(1)} %get-tuple-element.77), channel_id=1, source_target_pairs={{1,0},{2,1},{3,2},{4,3},{5,4},{6,5},{7,6},{9,8},{10,9},{11,10},{12... | collective-permute-start | bytes 24584 | tf_op jit(solution)/shard_map/ppermute | solution.py:22
  52.4 39.2 %copy-start.2 = (f32[8,8,1,1]{1,0,3,2:T(8,128)S(1)}, f32[8,8,1,1]{1,0,3,2:T(8,128)}, u32[]{:S(2)}) copy-start(f32[8,8,1,1]{1,0,3,2:T(8,128)} %constant.54) | copy-start | bytes 772
  54.2 26.2 %all-to-all-start = ((f32[64,1,607]{2,1,0:T(1,128)}), f32[64,1,607]{2,1,0:T(1,128)S(1)}, u32[]{:S(2)}, u32[]{:S(2)}) async-start(f32[64,1,607]{2,1,0:T(1,128)} %all_to_all.10), calls=%async_computation | async-start | bytes 327680 | tf_op jit(solution)/shard_map/all_to_all | solution.py:217
  80.5 4.6 %collective-permute-start.12 = (f32[607]{0:T(1024)S(1)}, f32[607]{0:T(1024)S(1)}, u32[]{:S(2)}, u32[]{:S(2)}) collective-permute-start(f32[607]{0:T(1024)S(1)} %reduce_sum.39), channel_id=1, source_target_pairs={{0,1},{1,0},{2,3},{3,2},{4,5},{5,4},{6,7},{7,6},{8,9},{9,8},{10,11... | collective-permute-start | bytes 7292 | tf_op jit(solution)/shard_map/ppermute | solution.py:145
  82.5 19.2 %collective-permute-start.8 = (bf16[64,1,4,128]{3,0,2,1:T(8,128)(2,1)S(1)}, bf16[64,1,4,128]{3,0,2,1:T(8,128)(2,1)S(1)}, u32[]{:S(2)}, u32[]{:S(2)}) collective-permute-start(bf16[64,1,4,128]{3,0,2,1:T(8,128)(2,1)S(1)} %get-tuple-element.60), channel_id=1, source_target_pairs={{0,8},{8,16},{16,24},{24,32},{32,40},{40,48},{48,56},{56,64},{64,7... | collective-permute-start | bytes 196616 | tf_op jit(solution)/shard_map/ppermute | solution.py:20
  85.1 12.4 %collective-permute-start.13 = (f32[607]{0:T(1024)S(1)}, f32[607]{0:T(1024)S(1)}, u32[]{:S(2)}, u32[]{:S(2)}) collective-permute-start(f32[607]{0:T(1024)S(1)} %add.162), channel_id=1, source_target_pairs={{0,2},{1,3},{2,0},{3,1},{4,6},{5,7},{6,4},{7,5},{8,10},{9,11},{10,... | collective-permute-start | bytes 7292 | tf_op jit(solution)/shard_map/ppermute | solution.py:145
  94.3 7.4 %collective-permute-start.9 = (bf16[64,1,4,128]{3,0,2,1:T(8,128)(2,1)S(1)}, bf16[64,1,4,128]{3,0,2,1:T(8,128)(2,1)S(1)}, u32[]{:S(2)}, u32[]{:S(2)}) collective-permute-start(bf16[64,1,4,128]{3,0,2,1:T(8,128)(2,1)S(1)} %get-tuple-element.59), channel_id=1, source_target_pairs={{8,0},{16,8},{24,16},{32,24},{40,32},{48,40},{56,48},{64,56},{72,6... | collective-permute-start | bytes 196616 | tf_op jit(solution)/shard_map/ppermute | solution.py:22
  97.5 10.9 %collective-permute-start.14 = (f32[607]{0:T(1024)S(1)}, f32[607]{0:T(1024)S(1)}, u32[]{:S(2)}, u32[]{:S(2)}) collective-permute-start(f32[607]{0:T(1024)S(1)} %add.163), channel_id=1, source_target_pairs={{0,4},{1,5},{2,6},{3,7},{4,0},{5,1},{6,2},{7,3},{8,12},{9,13},{10,... | collective-permute-start | bytes 7292 | tf_op jit(solution)/shard_map/ppermute | solution.py:145
  101.7 16.4 %collective-permute-start.10 = (bf16[64,4,1,128]{3,0,2,1:T(8,128)(2,1)S(1)}, bf16[64,4,1,128]{3,0,2,1:T(8,128)(2,1)S(1)}, u32[]{:S(2)}, u32[]{:S(2)}) collective-permute-start(bf16[64,4,1,128]{3,0,2,1:T(8,128)(2,1)S(1)} %get-tuple-element.57), channel_id=1, source_target_pairs={{0,1},{1,2},{2,3},{3,4},{4,5},{5,6},{6,7},{8,9},{9,10},{10,11},{11... | collective-permute-start | bytes 196616 | tf_op jit(solution)/shard_map/ppermute | solution.py:20
  103.7 14.5 %collective-permute-start.11 = (bf16[64,4,1,128]{3,0,2,1:T(8,128)(2,1)S(1)}, bf16[64,4,1,128]{3,0,2,1:T(8,128)(2,1)S(1)}, u32[]{:S(2)}, u32[]{:S(2)}) collective-permute-start(bf16[64,4,1,128]{3,0,2,1:T(8,128)(2,1)S(1)} %get-tuple-element.58), channel_id=1, source_target_pairs={{1,0},{2,1},{3,2},{4,3},{5,4},{6,5},{7,6},{9,8},{10,9},{11,10},{12... | collective-permute-start | bytes 196616 | tf_op jit(solution)/shard_map/ppermute | solution.py:22
  109.2 19.4 %all-to-all-start.1 = ((f32[64,1,607]{2,1,0:T(1,128)}), f32[64,1,607]{2,1,0:T(1,128)S(1)}, u32[]{:S(2)}, u32[]{:S(2)}) async-start(f32[64,1,607]{2,1,0:T(1,128)} %broadcast_in_dim.23), calls=%async_computation.1 | async-start | bytes 327680 | tf_op jit(solution)/shard_map/all_to_all | solution.py:223

commit v11 on v9

--- a/solution.py
+++ b/solution.py
@@ -123,6 +123,19 @@
             result.append(
                 jnp.einsum("ozxy,eczxy->eoc", grad, window, preferred_element_type=jnp.float32)
             )
+    return jnp.concatenate(result)
+
+
+def weight_taps_swapped(grad, padded):
+    planes, x_rows = (padded.shape[1], padded.shape[2])
+    spread = jnp.pad(grad, ((0, 0), (2, 2), (2, 2), (2, 2)))
+    stacked, _ = shift_stack(spread, x_rows)
+    result = []
+    for z_step in range(3):
+        window = stacked[:, :, 2 - z_step : 2 - z_step + planes]
+        result.append(
+            jnp.einsum("eozxy,czxy->eoc", window, padded, preferred_element_type=jnp.float32)[::-1]
+        )
     return jnp.concatenate(result)
 
 
@@ -205,7 +218,7 @@
     mixing_term = jnp.einsum(
         "ozxy,czxy->oc", inner_mix, inner_act, preferred_element_type=jnp.float32
     )
-    project_term = weight_taps(score_grad, act_frame)
+    project_term = weight_taps_swapped(score_grad, act_frame)
     offset_term = jnp.concatenate(
         [channel_sums(inner_first), channel_sums(inner_mix), channel_sums(score_grad)]
     )

time: 134 us -> 134 us (level)
    dot_general x12 -> x3, matrix products: 3.02 us -> 0.66 us  [weight_taps(): jnp.einsum('ozxy,eczxy->eoc', grad, window, preferred_element_type=jnp.fl...]
    dot_general x0 -> x3, matrix products: none -> 1.39 us  [weight_taps_swapped(): jnp.einsum('eozxy,czxy->eoc', window, padded, preferred_element_type=jnp....]
    unnamed x34 -> x42, local copies, waits for them, and re-layouts: 4.83 us -> 5.33 us
where the time goes in v11:
time: 134 us; the launch traced here: 133 us
  starting transfers between devices  74.7 us (56%)
  local copies, waits for them, and re-layouts  22.3 us (17%)
  waiting for transfers between devices  21.4 us (16%)
  matrix products  10.6 us (8%)
  other arithmetic  1.98 us (1%)
  between operations  1.62 us (1%)
    ppermute x6, starting transfers between devices, extended(): lax.ppermute(head, axis, [((i + 1) % count, i) for i in range(ends)])  22 us
    ppermute x6, starting transfers between devices, extended(): lax.ppermute(tail, axis, [(i, (i + 1) % count) for i in range(ends)])  16.3 us
    all_to_all x1, starting transfers between devices, per_device(): owned = lax.all_to_all(chunks, 'gz', 0, 0, tiled=False).sum(0)  14.9 us
    ppermute x3, starting transfers between devices, butterfly_sum(): flat = flat + lax.ppermute(flat, axis, [(i, i ^ bit) for i in range(count)])  12.5 us
    all_to_all x1, waiting for transfers between devices, per_device(): owned = lax.all_to_all(chunks, 'gz', 0, 0, tiled=False).sum(0)  10.3 us
    all_to_all x1, starting transfers between devices, per_device(): lax.all_to_all(jnp.broadcast_to(owned, (count,) + owned.shape), 'gz', 0,...  8.96 us
    ppermute x6, waiting for transfers between devices, extended(): lax.ppermute(head, axis, [((i + 1) % count, i) for i in range(ends)])  7.05 us
    unnamed x42, local copies, waits for them, and re-layouts  5.33 us
  transfers between devices with their start and end apart: 17, of which 5 were waited for; matrix products, arithmetic and copies ran while one was open for 11% of the time, Pallas kernels for 0%

profile of v11, /device:TPU:56, one launch (start us, length us, event | category | flops | bytes accessed | tf_op | source)
XLA Modules:
  0.0 132.6 jit_solution(17695560380759855478)
XLA Ops:
  2.2 5.1 %collective-permute-start = (bf16[12,2,4,128]{3,0,2,1:T(8,128)(2,1)S(1)}, bf16[12,2,4,128]{3,0,2,1:T(8,128)(2,1)S(1)}, u32[]{:S(2)}, u32[]{:S(2)}) collective-permute-start(bf16[12,2,4,128]{3,0,2,1:T(8,128)(2,1)S(1)} %pad_maximum_fusion.16), channel_id=1, source_target_pairs={{0,8},{8,16},{16,24},{24,32},{32,40},{40,48},{48,56},{56,64},{64,7... | collective-permute-start | bytes 73736 | tf_op jit(solution)/shard_map/ppermute | solution.py:20
  7.3 1.9 %collective-permute-start.1 = (bf16[12,2,4,128]{3,0,2,1:T(8,128)(2,1)S(1)}, bf16[12,2,4,128]{3,0,2,1:T(8,128)(2,1)S(1)}, u32[]{:S(2)}, u32[]{:S(2)}) collective-permute-start(bf16[12,2,4,128]{3,0,2,1:T(8,128)(2,1)S(1)} %pad_maximum_fusion.16), channel_id=1, source_target_pairs={{8,0},{16,8},{24,16},{32,24},{40,32},{48,40},{56,48},{64,56},{72,6... | collective-permute-start | bytes 73736 | tf_op jit(solution)/shard_map/ppermute | solution.py:22
  9.2 0.8 fusion.127
  10.8 3.2 %collective-permute-done.1 = bf16[12,2,4,128]{3,0,2,1:T(8,128)(2,1)S(1)} collective-permute-done((bf16[12,2,4,128]{3,0,2,1:T(8,128)(2,1)S(1)}, bf16[12,2,4,128]{3,0,2,1:T(8,128)(2,1)S(1)}, u32[]{:S(2)}, u32[]{:S(2)}) %collective-permute-start.1) | collective-permute-done | bytes 24608 | tf_op jit(solution)/shard_map/ppermute | solution.py:22
  14.0 1.9 %collective-permute-start.2 = (bf16[12,6,2,128]{3,0,2,1:T(8,128)(2,1)S(1)}, bf16[12,6,2,128]{3,0,2,1:T(8,128)(2,1)S(1)}, u32[]{:S(2)}, u32[]{:S(2)}) collective-permute-start(bf16[12,6,2,128]{3,0,2,1:T(8,128)(2,1)S(1)} %get-tuple-element.88), channel_id=1, source_target_pairs={{0,1},{1,2},{2,3},{3,4},{4,5},{5,6},{6,7},{8,9},{9,10},{10,11},{11... | collective-permute-start | bytes 110600 | tf_op jit(solution)/shard_map/ppermute | solution.py:20
  15.9 4.5 %collective-permute-start.3 = (bf16[12,6,2,128]{3,0,2,1:T(8,128)(2,1)S(1)}, bf16[12,6,2,128]{3,0,2,1:T(8,128)(2,1)S(1)}, u32[]{:S(2)}, u32[]{:S(2)}) collective-permute-start(bf16[12,6,2,128]{3,0,2,1:T(8,128)(2,1)S(1)} %get-tuple-element.89), channel_id=1, source_target_pairs={{1,0},{2,1},{3,2},{4,3},{5,4},{6,5},{7,6},{9,8},{10,9},{11,10},{12... | collective-permute-start | bytes 110600 | tf_op jit(solution)/shard_map/ppermute | solution.py:22
  21.2 0.9 copy.283
  23.9 1.3 %multiply_convert_fusion = (bf16[64,4,6,128]{3,0,2,1:T(8,128)(2,1)S(1)}, f32[64,4,6,128]{3,0,2,1:T(8,128)}) fusion(f32[64]{0:T(128)S(1)} %get-tuple-element.107, f32[4,6,128,64]{2,3,1,0:T(8,128)S(1)} %convolution_bitcast_fusion, f32[4,6,128,64]{2,3,1,0:T(8,128)S(1)} %convolution_bitcast_fusion.1, bf16[9,12,6,6,128]{4,1,0,3,2:T(8,128)(2,1)S(1)} %fusion.60, ...), kind=kOutput, calls=%fused_computation.60 | convolution fusion | flops 44040192 | bytes 4116992 | tf_op jit(solution)/shard_map/eoc,eczxy->ozxy/dot_general | solution.py:85
  26.1 0.8 fusion.117
  31.0 2.8 %collective-permute-start.4 = (bf16[8,1,4,128]{3,0,2,1:T(8,128)(2,1)S(1)}, bf16[8,1,4,128]{3,0,2,1:T(8,128)(2,1)S(1)}, u32[]{:S(2)}, u32[]{:S(2)}) collective-permute-start(bf16[8,1,4,128]{3,0,2,1:T(8,128)(2,1)S(1)} %get-tuple-element.104), channel_id=1, source_target_pairs={{0,8},{8,16},{16,24},{24,32},{32,40},{40,48},{48,56},{56,64},{64,7... | collective-permute-start | bytes 24584 | tf_op jit(solution)/shard_map/ppermute | solution.py:20
  33.9 3.0 %collective-permute-start.5 = (bf16[8,1,4,128]{3,0,2,1:T(8,128)(2,1)S(1)}, bf16[8,1,4,128]{3,0,2,1:T(8,128)(2,1)S(1)}, u32[]{:S(2)}, u32[]{:S(2)}) collective-permute-start(bf16[8,1,4,128]{3,0,2,1:T(8,128)(2,1)S(1)} %get-tuple-element.105), channel_id=1, source_target_pairs={{8,0},{16,8},{24,16},{32,24},{40,32},{48,40},{56,48},{64,56},{72,6... | collective-permute-start | bytes 24584 | tf_op jit(solution)/shard_map/ppermute | solution.py:22
  37.5 2.9 %collective-permute-done.5 = bf16[8,1,4,128]{3,0,2,1:T(8,128)(2,1)S(1)} collective-permute-done((bf16[8,1,4,128]{3,0,2,1:T(8,128)(2,1)S(1)}, bf16[8,1,4,128]{3,0,2,1:T(8,128)(2,1)S(1)}, u32[]{:S(2)}, u32[]{:S(2)}) %collective-permute-start.5) | collective-permute-done | bytes 8224 | tf_op jit(solution)/shard_map/ppermute | solution.py:22
  40.3 1.9 %collective-permute-start.6 = (bf16[8,4,1,128]{3,0,2,1:T(8,128)(2,1)S(1)}, bf16[8,4,1,128]{3,0,2,1:T(8,128)(2,1)S(1)}, u32[]{:S(2)}, u32[]{:S(2)}) collective-permute-start(bf16[8,4,1,128]{3,0,2,1:T(8,128)(2,1)S(1)} %get-tuple-element.100), channel_id=1, source_target_pairs={{0,1},{1,2},{2,3},{3,4},{4,5},{5,6},{6,7},{8,9},{9,10},{10,11},{11... | collective-permute-start | bytes 24584 | tf_op jit(solution)/shard_map/ppermute | solution.py:20
  42.3 4.5 %collective-permute-start.7 = (bf16[8,4,1,128]{3,0,2,1:T(8,128)(2,1)S(1)}, bf16[8,4,1,128]{3,0,2,1:T(8,128)(2,1)S(1)}, u32[]{:S(2)}, u32[]{:S(2)}) collective-permute-start(bf16[8,4,1,128]{3,0,2,1:T(8,128)(2,1)S(1)} %get-tuple-element.101), channel_id=1, source_target_pairs={{1,0},{2,1},{3,2},{4,3},{5,4},{6,5},{7,6},{9,8},{10,9},{11,10},{12... | collective-permute-start | bytes 24584 | tf_op jit(solution)/shard_map/ppermute | solution.py:22
  47.1 1.0 collective-permute-done.7
  49.9 1.3 convert_reduce_fusion.1
  53.1 1.0 all_to_all.10
  54.1 14.9 %all-to-all-start = ((f32[64,1,607]{2,1,0:T(1,128)}), f32[64,1,607]{2,1,0:T(1,128)S(1)}, u32[]{:S(2)}, u32[]{:S(2)}) async-start(f32[64,1,607]{2,1,0:T(1,128)} %all_to_all.10), calls=%async_computation | async-start | bytes 327680 | tf_op jit(solution)/shard_map/all_to_all | solution.py:230
  69.2 10.3 %all-to-all-done = f32[64,1,607]{2,1,0:T(1,128)S(1)} async-done(((f32[64,1,607]{2,1,0:T(1,128)}), f32[64,1,607]{2,1,0:T(1,128)S(1)}, u32[]{:S(2)}, u32[]{:S(2)}) %all-to-all-start) | async-done | bytes 155424 | tf_op jit(solution)/shard_map/all_to_all | solution.py:230
  79.7 1.9 %collective-permute-start.12 = (f32[607]{0:T(1024)S(1)}, f32[607]{0:T(1024)S(1)}, u32[]{:S(2)}, u32[]{:S(2)}) collective-permute-start(f32[607]{0:T(1024)S(1)} %reduce_sum.39), channel_id=1, source_target_pairs={{0,1},{1,0},{2,3},{3,2},{4,5},{5,4},{6,7},{7,6},{8,9},{9,8},{10,11... | collective-permute-start | bytes 7292 | tf_op jit(solution)/shard_map/ppermute | solution.py:158
  81.6 2.6 %collective-permute-start.8 = (bf16[64,1,4,128]{3,0,2,1:T(8,128)(2,1)S(1)}, bf16[64,1,4,128]{3,0,2,1:T(8,128)(2,1)S(1)}, u32[]{:S(2)}, u32[]{:S(2)}) collective-permute-start(bf16[64,1,4,128]{3,0,2,1:T(8,128)(2,1)S(1)} %get-tuple-element.78), channel_id=1, source_target_pairs={{0,8},{8,16},{16,24},{24,32},{32,40},{40,48},{48,56},{56,64},{64,7... | collective-permute-start | bytes 196616 | tf_op jit(solution)/shard_map/ppermute | solution.py:20
  84.3 6.5 %collective-permute-start.13 = (f32[607]{0:T(1024)S(1)}, f32[607]{0:T(1024)S(1)}, u32[]{:S(2)}, u32[]{:S(2)}) collective-permute-start(f32[607]{0:T(1024)S(1)} %add.215), channel_id=1, source_target_pairs={{0,2},{1,3},{2,0},{3,1},{4,6},{5,7},{6,4},{7,5},{8,10},{9,11},{10,... | collective-permute-start | bytes 7292 | tf_op jit(solution)/shard_map/ppermute | solution.py:158
  91.6 1.8 %reshape.123 = f32[4,8,256]{2,1,0:T(8,128)} reshape(f32[2,2,4,2,128,2]{5,4,3,2,1,0:T(8,128)S(1)} %bitcast.516) | data formatting | bytes 65536 | tf_op jit(solution)/shard_map/reshape | solution.py:50
  93.4 3.2 %collective-permute-start.9 = (bf16[64,1,4,128]{3,0,2,1:T(8,128)(2,1)S(1)}, bf16[64,1,4,128]{3,0,2,1:T(8,128)(2,1)S(1)}, u32[]{:S(2)}, u32[]{:S(2)}) collective-permute-start(bf16[64,1,4,128]{3,0,2,1:T(8,128)(2,1)S(1)} %get-tuple-element.77), channel_id=1, source_target_pairs={{8,0},{16,8},{24,16},{32,24},{40,32},{48,40},{56,48},{64,56},{72,6... | collective-permute-start | bytes 196616 | tf_op jit(solution)/shard_map/ppermute | solution.py:22
  96.7 4.1 %collective-permute-start.14 = (f32[607]{0:T(1024)S(1)}, f32[607]{0:T(1024)S(1)}, u32[]{:S(2)}, u32[]{:S(2)}) collective-permute-start(f32[607]{0:T(1024)S(1)} %add.216), channel_id=1, source_target_pairs={{0,4},{1,5},{2,6},{3,7},{4,0},{5,1},{6,2},{7,3},{8,12},{9,13},{10,... | collective-permute-start | bytes 7292 | tf_op jit(solution)/shard_map/ppermute | solution.py:158
  100.9 1.9 %collective-permute-start.10 = (bf16[64,4,1,128]{3,0,2,1:T(8,128)(2,1)S(1)}, bf16[64,4,1,128]{3,0,2,1:T(8,128)(2,1)S(1)}, u32[]{:S(2)}, u32[]{:S(2)}) collective-permute-start(bf16[64,4,1,128]{3,0,2,1:T(8,128)(2,1)S(1)} %get-tuple-element.75), channel_id=1, source_target_pairs={{0,1},{1,2},{2,3},{3,4},{4,5},{5,6},{6,7},{8,9},{9,10},{10,11},{11... | collective-permute-start | bytes 196616 | tf_op jit(solution)/shard_map/ppermute | solution.py:20
  102.8 4.7 %collective-permute-start.11 = (bf16[64,4,1,128]{3,0,2,1:T(8,128)(2,1)S(1)}, bf16[64,4,1,128]{3,0,2,1:T(8,128)(2,1)S(1)}, u32[]{:S(2)}, u32[]{:S(2)}) collective-permute-start(bf16[64,4,1,128]{3,0,2,1:T(8,128)(2,1)S(1)} %get-tuple-element.76), channel_id=1, source_target_pairs={{1,0},{2,1},{3,2},{4,3},{5,4},{6,5},{7,6},{9,8},{10,9},{11,10},{12... | collective-permute-start | bytes 196616 | tf_op jit(solution)/shard_map/ppermute | solution.py:22
  108.3 9.0 %all-to-all-start.1 = ((f32[64,1,607]{2,1,0:T(1,128)}), f32[64,1,607]{2,1,0:T(1,128)S(1)}, u32[]{:S(2)}, u32[]{:S(2)}) async-start(f32[64,1,607]{2,1,0:T(1,128)} %broadcast_in_dim.23), calls=%async_computation.1 | async-start | bytes 327680 | tf_op jit(solution)/shard_map/all_to_all | solution.py:236
  121.3 1.8 %reshape.129 = f32[4,8,256]{2,1,0:T(8,128)} reshape(f32[2,2,4,2,128,2]{5,4,3,2,1,0:T(8,128)S(1)} %bitcast.517) | data formatting | bytes 65536 | tf_op jit(solution)/shard_map/reshape | solution.py:50
  123.7 4.0 %all-to-all-done.1 = f32[64,1,607]{2,1,0:T(1,128)S(1)} async-done(((f32[64,1,607]{2,1,0:T(1,128)}), f32[64,1,607]{2,1,0:T(1,128)S(1)}, u32[]{:S(2)}, u32[]{:S(2)}) %all-to-all-start.1) | async-done | bytes 155424 | tf_op jit(solution)/shard_map/all_to_all | solution.py:236
  129.2 1.0 reshape.131
  130.2 1.1 copy.353
  (166 shorter events, 23.0 us)
Async XLA Ops:
  0.6 24.6 %copy-start = (bf16[64,64]{1,0:T(8,128)(2,1)S(1)}, bf16[64,64]{1,0:T(8,128)(2,1)}, u32[]{:S(2)}) copy-start(bf16[64,64]{1,0:T(8,128)(2,1)} %param.13) | copy-start | bytes 24580
  2.2 8.6 %collective-permute-start = (bf16[12,2,4,128]{3,0,2,1:T(8,128)(2,1)S(1)}, bf16[12,2,4,128]{3,0,2,1:T(8,128)(2,1)S(1)}, u32[]{:S(2)}, u32[]{:S(2)}) collective-permute-start(bf16[12,2,4,128]{3,0,2,1:T(8,128)(2,1)S(1)} %pad_maximum_fusion.16), channel_id=1, source_target_pairs={{0,8},{8,16},{16,24},{24,32},{32,40},{40,48},{48,56},{56,64},{64,7... | collective-permute-start | bytes 73736 | tf_op jit(solution)/shard_map/ppermute | solution.py:20
  7.3 6.7 %collective-permute-start.1 = (bf16[12,2,4,128]{3,0,2,1:T(8,128)(2,1)S(1)}, bf16[12,2,4,128]{3,0,2,1:T(8,128)(2,1)S(1)}, u32[]{:S(2)}, u32[]{:S(2)}) collective-permute-start(bf16[12,2,4,128]{3,0,2,1:T(8,128)(2,1)S(1)} %pad_maximum_fusion.16), channel_id=1, source_target_pairs={{8,0},{16,8},{24,16},{32,24},{40,32},{48,40},{56,48},{64,56},{72,6... | collective-permute-start | bytes 73736 | tf_op jit(solution)/shard_map/ppermute | solution.py:22
  14.0 8.2 %collective-permute-start.2 = (bf16[12,6,2,128]{3,0,2,1:T(8,128)(2,1)S(1)}, bf16[12,6,2,128]{3,0,2,1:T(8,128)(2,1)S(1)}, u32[]{:S(2)}, u32[]{:S(2)}) collective-permute-start(bf16[12,6,2,128]{3,0,2,1:T(8,128)(2,1)S(1)} %get-tuple-element.88), channel_id=1, source_target_pairs={{0,1},{1,2},{2,3},{3,4},{4,5},{5,6},{6,7},{8,9},{9,10},{10,11},{11... | collective-permute-start | bytes 110600 | tf_op jit(solution)/shard_map/ppermute | solution.py:20
  15.9 6.3 %collective-permute-start.3 = (bf16[12,6,2,128]{3,0,2,1:T(8,128)(2,1)S(1)}, bf16[12,6,2,128]{3,0,2,1:T(8,128)(2,1)S(1)}, u32[]{:S(2)}, u32[]{:S(2)}) collective-permute-start(bf16[12,6,2,128]{3,0,2,1:T(8,128)(2,1)S(1)} %get-tuple-element.89), channel_id=1, source_target_pairs={{1,0},{2,1},{3,2},{4,3},{5,4},{6,5},{7,6},{9,8},{10,9},{11,10},{12... | collective-permute-start | bytes 110600 | tf_op jit(solution)/shard_map/ppermute | solution.py:22
  26.0 0.9 copy-start.1
  31.0 6.4 %collective-permute-start.4 = (bf16[8,1,4,128]{3,0,2,1:T(8,128)(2,1)S(1)}, bf16[8,1,4,128]{3,0,2,1:T(8,128)(2,1)S(1)}, u32[]{:S(2)}, u32[]{:S(2)}) collective-permute-start(bf16[8,1,4,128]{3,0,2,1:T(8,128)(2,1)S(1)} %get-tuple-element.104), channel_id=1, source_target_pairs={{0,8},{8,16},{16,24},{24,32},{32,40},{40,48},{48,56},{56,64},{64,7... | collective-permute-start | bytes 24584 | tf_op jit(solution)/shard_map/ppermute | solution.py:20
  33.9 6.5 %collective-permute-start.5 = (bf16[8,1,4,128]{3,0,2,1:T(8,128)(2,1)S(1)}, bf16[8,1,4,128]{3,0,2,1:T(8,128)(2,1)S(1)}, u32[]{:S(2)}, u32[]{:S(2)}) collective-permute-start(bf16[8,1,4,128]{3,0,2,1:T(8,128)(2,1)S(1)} %get-tuple-element.105), channel_id=1, source_target_pairs={{8,0},{16,8},{24,16},{32,24},{40,32},{48,40},{56,48},{64,56},{72,6... | collective-permute-start | bytes 24584 | tf_op jit(solution)/shard_map/ppermute | solution.py:22
  40.3 6.8 %collective-permute-start.6 = (bf16[8,4,1,128]{3,0,2,1:T(8,128)(2,1)S(1)}, bf16[8,4,1,128]{3,0,2,1:T(8,128)(2,1)S(1)}, u32[]{:S(2)}, u32[]{:S(2)}) collective-permute-start(bf16[8,4,1,128]{3,0,2,1:T(8,128)(2,1)S(1)} %get-tuple-element.100), channel_id=1, source_target_pairs={{0,1},{1,2},{2,3},{3,4},{4,5},{5,6},{6,7},{8,9},{9,10},{10,11},{11... | collective-permute-start | bytes 24584 | tf_op jit(solution)/shard_map/ppermute | solution.py:20
  42.3 5.9 %collective-permute-start.7 = (bf16[8,4,1,128]{3,0,2,1:T(8,128)(2,1)S(1)}, bf16[8,4,1,128]{3,0,2,1:T(8,128)(2,1)S(1)}, u32[]{:S(2)}, u32[]{:S(2)}) collective-permute-start(bf16[8,4,1,128]{3,0,2,1:T(8,128)(2,1)S(1)} %get-tuple-element.101), channel_id=1, source_target_pairs={{1,0},{2,1},{3,2},{4,3},{5,4},{6,5},{7,6},{9,8},{10,9},{11,10},{12... | collective-permute-start | bytes 24584 | tf_op jit(solution)/shard_map/ppermute | solution.py:22
  53.0 37.8 %copy-start.2 = (f32[8,8,1,1]{1,0,3,2:T(8,128)S(1)}, f32[8,8,1,1]{1,0,3,2:T(8,128)}, u32[]{:S(2)}) copy-start(f32[8,8,1,1]{1,0,3,2:T(8,128)} %constant.56) | copy-start | bytes 772
  54.1 25.4 %all-to-all-start = ((f32[64,1,607]{2,1,0:T(1,128)}), f32[64,1,607]{2,1,0:T(1,128)S(1)}, u32[]{:S(2)}, u32[]{:S(2)}) async-start(f32[64,1,607]{2,1,0:T(1,128)} %all_to_all.10), calls=%async_computation | async-start | bytes 327680 | tf_op jit(solution)/shard_map/all_to_all | solution.py:230
  79.7 4.6 %collective-permute-start.12 = (f32[607]{0:T(1024)S(1)}, f32[607]{0:T(1024)S(1)}, u32[]{:S(2)}, u32[]{:S(2)}) collective-permute-start(f32[607]{0:T(1024)S(1)} %reduce_sum.39), channel_id=1, source_target_pairs={{0,1},{1,0},{2,3},{3,2},{4,5},{5,4},{6,7},{7,6},{8,9},{9,8},{10,11... | collective-permute-start | bytes 7292 | tf_op jit(solution)/shard_map/ppermute | solution.py:158
  81.6 19.2 %collective-permute-start.8 = (bf16[64,1,4,128]{3,0,2,1:T(8,128)(2,1)S(1)}, bf16[64,1,4,128]{3,0,2,1:T(8,128)(2,1)S(1)}, u32[]{:S(2)}, u32[]{:S(2)}) collective-permute-start(bf16[64,1,4,128]{3,0,2,1:T(8,128)(2,1)S(1)} %get-tuple-element.78), channel_id=1, source_target_pairs={{0,8},{8,16},{16,24},{24,32},{32,40},{40,48},{48,56},{56,64},{64,7... | collective-permute-start | bytes 196616 | tf_op jit(solution)/shard_map/ppermute | solution.py:20
  84.3 12.4 %collective-permute-start.13 = (f32[607]{0:T(1024)S(1)}, f32[607]{0:T(1024)S(1)}, u32[]{:S(2)}, u32[]{:S(2)}) collective-permute-start(f32[607]{0:T(1024)S(1)} %add.215), channel_id=1, source_target_pairs={{0,2},{1,3},{2,0},{3,1},{4,6},{5,7},{6,4},{7,5},{8,10},{9,11},{10,... | collective-permute-start | bytes 7292 | tf_op jit(solution)/shard_map/ppermute | solution.py:158
  93.4 7.4 %collective-permute-start.9 = (bf16[64,1,4,128]{3,0,2,1:T(8,128)(2,1)S(1)}, bf16[64,1,4,128]{3,0,2,1:T(8,128)(2,1)S(1)}, u32[]{:S(2)}, u32[]{:S(2)}) collective-permute-start(bf16[64,1,4,128]{3,0,2,1:T(8,128)(2,1)S(1)} %get-tuple-element.77), channel_id=1, source_target_pairs={{8,0},{16,8},{24,16},{32,24},{40,32},{48,40},{56,48},{64,56},{72,6... | collective-permute-start | bytes 196616 | tf_op jit(solution)/shard_map/ppermute | solution.py:22
  96.7 10.9 %collective-permute-start.14 = (f32[607]{0:T(1024)S(1)}, f32[607]{0:T(1024)S(1)}, u32[]{:S(2)}, u32[]{:S(2)}) collective-permute-start(f32[607]{0:T(1024)S(1)} %add.216), channel_id=1, source_target_pairs={{0,4},{1,5},{2,6},{3,7},{4,0},{5,1},{6,2},{7,3},{8,12},{9,13},{10,... | collective-permute-start | bytes 7292 | tf_op jit(solution)/shard_map/ppermute | solution.py:158
  100.9 16.4 %collective-permute-start.10 = (bf16[64,4,1,128]{3,0,2,1:T(8,128)(2,1)S(1)}, bf16[64,4,1,128]{3,0,2,1:T(8,128)(2,1)S(1)}, u32[]{:S(2)}, u32[]{:S(2)}) collective-permute-start(bf16[64,4,1,128]{3,0,2,1:T(8,128)(2,1)S(1)} %get-tuple-element.75), channel_id=1, source_target_pairs={{0,1},{1,2},{2,3},{3,4},{4,5},{5,6},{6,7},{8,9},{9,10},{10,11},{11... | collective-permute-start | bytes 196616 | tf_op jit(solution)/shard_map/ppermute | solution.py:20
  102.8 14.5 %collective-permute-start.11 = (bf16[64,4,1,128]{3,0,2,1:T(8,128)(2,1)S(1)}, bf16[64,4,1,128]{3,0,2,1:T(8,128)(2,1)S(1)}, u32[]{:S(2)}, u32[]{:S(2)}) collective-permute-start(bf16[64,4,1,128]{3,0,2,1:T(8,128)(2,1)S(1)} %get-tuple-element.76), channel_id=1, source_target_pairs={{1,0},{2,1},{3,2},{4,3},{5,4},{6,5},{7,6},{9,8},{10,9},{11,10},{12... | collective-permute-start | bytes 196616 | tf_op jit(solution)/shard_map/ppermute | solution.py:22
  108.3 19.4 %all-to-all-start.1 = ((f32[64,1,607]{2,1,0:T(1,128)}), f32[64,1,607]{2,1,0:T(1,128)S(1)}, u32[]{:S(2)}, u32[]{:S(2)}) async-start(f32[64,1,607]{2,1,0:T(1,128)} %broadcast_in_dim.23), calls=%async_computation.1 | async-start | bytes 327680 | tf_op jit(solution)/shard_map/all_to_all | solution.py:236

commit v12 on v9

--- a/solution.py
+++ b/solution.py
@@ -140,10 +140,10 @@
         if count & (count - 1):
             flat = lax.psum(flat, axis)
             continue
-        bit = 1
-        while bit < count:
+        bit = count // 2
+        while bit >= 1:
             flat = flat + lax.ppermute(flat, axis, [(i, i ^ bit) for i in range(count)])
-            bit *= 2
+            bit //= 2
     return flat
 
 

time: 134 us -> 137 us (1.022)
  waiting for transfers between devices: 21.5 us -> 25 us
    ppermute x6, waiting for transfers between devices: 7.07 us -> 9.52 us  [extended(): lax.ppermute(head, axis, [((i + 1) % count, i) for i in range(ends)])]
    all_to_all x1, starting transfers between devices: 8.96 us -> 6.99 us  [per_device(): lax.all_to_all(jnp.broadcast_to(owned, (count,) + owned.shape), 'gz', 0,...]
    ppermute x3, starting transfers between devices: 12.5 us -> 14 us  [butterfly_sum(): flat = flat + lax.ppermute(flat, axis, [(i, i ^ bit) for i in range(count)])]
  transfers between devices with their start and end apart: 17 -> 17, of which waited for: 5 -> 7; matrix products, arithmetic and copies ran while one was open for 11% -> 10% of each run, Pallas kernels for 0% -> 0%
where the time goes in v12:
time: 137 us; the launch traced here: 135 us
  starting transfers between devices  73.5 us (54%)
  waiting for transfers between devices  25 us (18%)
  local copies, waits for them, and re-layouts  21.8 us (16%)
  matrix products  11.6 us (8%)
  other arithmetic  1.98 us (1%)
  between operations  1.51 us (1%)
    ppermute x6, starting transfers between devices, extended(): lax.ppermute(head, axis, [((i + 1) % count, i) for i in range(ends)])  21.1 us
    ppermute x6, starting transfers between devices, extended(): lax.ppermute(tail, axis, [(i, (i + 1) % count) for i in range(ends)])  16.4 us
    all_to_all x1, starting transfers between devices, per_device(): owned = lax.all_to_all(chunks, 'gz', 0, 0, tiled=False).sum(0)  15 us
    ppermute x3, starting transfers between devices, butterfly_sum(): flat = flat + lax.ppermute(flat, axis, [(i, i ^ bit) for i in range(count)])  14 us
    all_to_all x1, waiting for transfers between devices, per_device(): owned = lax.all_to_all(chunks, 'gz', 0, 0, tiled=False).sum(0)  10.3 us
    ppermute x6, waiting for transfers between devices, extended(): lax.ppermute(head, axis, [((i + 1) % count, i) for i in range(ends)])  9.52 us
    all_to_all x1, starting transfers between devices, per_device(): lax.all_to_all(jnp.broadcast_to(owned, (count,) + owned.shape), 'gz', 0,...  6.99 us
    unnamed x34, local copies, waits for them, and re-layouts  4.83 us
  transfers between devices with their start and end apart: 17, of which 7 were waited for; matrix products, arithmetic and copies ran while one was open for 10% of the time, Pallas kernels for 0%

profile of v12, /device:TPU:56, one launch (start us, length us, event | category | flops | bytes accessed | tf_op | source)
XLA Modules:
  0.0 135.3 jit_solution(11635084189309402674)
XLA Ops:
  2.2 5.1 %collective-permute-start = (bf16[12,2,4,128]{3,0,2,1:T(8,128)(2,1)S(1)}, bf16[12,2,4,128]{3,0,2,1:T(8,128)(2,1)S(1)}, u32[]{:S(2)}, u32[]{:S(2)}) collective-permute-start(bf16[12,2,4,128]{3,0,2,1:T(8,128)(2,1)S(1)} %pad_maximum_fusion.15), channel_id=1, source_target_pairs={{0,8},{8,16},{16,24},{24,32},{32,40},{40,48},{48,56},{56,64},{64,7... | collective-permute-start | bytes 73736 | tf_op jit(solution)/shard_map/ppermute | solution.py:20
  7.3 1.9 %collective-permute-start.1 = (bf16[12,2,4,128]{3,0,2,1:T(8,128)(2,1)S(1)}, bf16[12,2,4,128]{3,0,2,1:T(8,128)(2,1)S(1)}, u32[]{:S(2)}, u32[]{:S(2)}) collective-permute-start(bf16[12,2,4,128]{3,0,2,1:T(8,128)(2,1)S(1)} %pad_maximum_fusion.15), channel_id=1, source_target_pairs={{8,0},{16,8},{24,16},{32,24},{40,32},{48,40},{56,48},{64,56},{72,6... | collective-permute-start | bytes 73736 | tf_op jit(solution)/shard_map/ppermute | solution.py:22
  10.8 3.2 %collective-permute-done.1 = bf16[12,2,4,128]{3,0,2,1:T(8,128)(2,1)S(1)} collective-permute-done((bf16[12,2,4,128]{3,0,2,1:T(8,128)(2,1)S(1)}, bf16[12,2,4,128]{3,0,2,1:T(8,128)(2,1)S(1)}, u32[]{:S(2)}, u32[]{:S(2)}) %collective-permute-start.1) | collective-permute-done | bytes 24608 | tf_op jit(solution)/shard_map/ppermute | solution.py:22
  14.0 1.9 %collective-permute-start.2 = (bf16[12,6,2,128]{3,0,2,1:T(8,128)(2,1)S(1)}, bf16[12,6,2,128]{3,0,2,1:T(8,128)(2,1)S(1)}, u32[]{:S(2)}, u32[]{:S(2)}) collective-permute-start(bf16[12,6,2,128]{3,0,2,1:T(8,128)(2,1)S(1)} %get-tuple-element.88), channel_id=1, source_target_pairs={{0,1},{1,2},{2,3},{3,4},{4,5},{5,6},{6,7},{8,9},{9,10},{10,11},{11... | collective-permute-start | bytes 110600 | tf_op jit(solution)/shard_map/ppermute | solution.py:20
  15.9 4.5 %collective-permute-start.3 = (bf16[12,6,2,128]{3,0,2,1:T(8,128)(2,1)S(1)}, bf16[12,6,2,128]{3,0,2,1:T(8,128)(2,1)S(1)}, u32[]{:S(2)}, u32[]{:S(2)}) collective-permute-start(bf16[12,6,2,128]{3,0,2,1:T(8,128)(2,1)S(1)} %get-tuple-element.89), channel_id=1, source_target_pairs={{1,0},{2,1},{3,2},{4,3},{5,4},{6,5},{7,6},{9,8},{10,9},{11,10},{12... | collective-permute-start | bytes 110600 | tf_op jit(solution)/shard_map/ppermute | solution.py:22
  21.2 0.9 copy.319
  23.9 1.3 multiply_convert_fusion
  31.4 2.9 %collective-permute-start.4 = (bf16[8,1,4,128]{3,0,2,1:T(8,128)(2,1)S(1)}, bf16[8,1,4,128]{3,0,2,1:T(8,128)(2,1)S(1)}, u32[]{:S(2)}, u32[]{:S(2)}) collective-permute-start(bf16[8,1,4,128]{3,0,2,1:T(8,128)(2,1)S(1)} %get-tuple-element.104), channel_id=1, source_target_pairs={{0,8},{8,16},{16,24},{24,32},{32,40},{40,48},{48,56},{56,64},{64,7... | collective-permute-start | bytes 24584 | tf_op jit(solution)/shard_map/ppermute | solution.py:20
  34.3 3.0 %collective-permute-start.5 = (bf16[8,1,4,128]{3,0,2,1:T(8,128)(2,1)S(1)}, bf16[8,1,4,128]{3,0,2,1:T(8,128)(2,1)S(1)}, u32[]{:S(2)}, u32[]{:S(2)}) collective-permute-start(bf16[8,1,4,128]{3,0,2,1:T(8,128)(2,1)S(1)} %get-tuple-element.105), channel_id=1, source_target_pairs={{8,0},{16,8},{24,16},{32,24},{40,32},{48,40},{56,48},{64,56},{72,6... | collective-permute-start | bytes 24584 | tf_op jit(solution)/shard_map/ppermute | solution.py:22
  37.9 2.9 %collective-permute-done.5 = bf16[8,1,4,128]{3,0,2,1:T(8,128)(2,1)S(1)} collective-permute-done((bf16[8,1,4,128]{3,0,2,1:T(8,128)(2,1)S(1)}, bf16[8,1,4,128]{3,0,2,1:T(8,128)(2,1)S(1)}, u32[]{:S(2)}, u32[]{:S(2)}) %collective-permute-start.5) | collective-permute-done | bytes 8224 | tf_op jit(solution)/shard_map/ppermute | solution.py:22
  40.8 1.9 %collective-permute-start.6 = (bf16[8,4,1,128]{3,0,2,1:T(8,128)(2,1)S(1)}, bf16[8,4,1,128]{3,0,2,1:T(8,128)(2,1)S(1)}, u32[]{:S(2)}, u32[]{:S(2)}) collective-permute-start(bf16[8,4,1,128]{3,0,2,1:T(8,128)(2,1)S(1)} %get-tuple-element.100), channel_id=1, source_target_pairs={{0,1},{1,2},{2,3},{3,4},{4,5},{5,6},{6,7},{8,9},{9,10},{10,11},{11... | collective-permute-start | bytes 24584 | tf_op jit(solution)/shard_map/ppermute | solution.py:20
  42.7 4.5 %collective-permute-start.7 = (bf16[8,4,1,128]{3,0,2,1:T(8,128)(2,1)S(1)}, bf16[8,4,1,128]{3,0,2,1:T(8,128)(2,1)S(1)}, u32[]{:S(2)}, u32[]{:S(2)}) collective-permute-start(bf16[8,4,1,128]{3,0,2,1:T(8,128)(2,1)S(1)} %get-tuple-element.101), channel_id=1, source_target_pairs={{1,0},{2,1},{3,2},{4,3},{5,4},{6,5},{7,6},{9,8},{10,9},{11,10},{12... | collective-permute-start | bytes 24584 | tf_op jit(solution)/shard_map/ppermute | solution.py:22
  47.6 1.0 collective-permute-done.7
  50.3 1.3 convert_reduce_fusion.1
  53.6 1.0 all_to_all.10
  54.6 15.0 %all-to-all-start = ((f32[64,1,607]{2,1,0:T(1,128)}), f32[64,1,607]{2,1,0:T(1,128)S(1)}, u32[]{:S(2)}, u32[]{:S(2)}) async-start(f32[64,1,607]{2,1,0:T(1,128)} %all_to_all.10), calls=%async_computation | async-start | bytes 327680 | tf_op jit(solution)/shard_map/all_to_all | solution.py:217
  69.7 10.3 %all-to-all-done = f32[64,1,607]{2,1,0:T(1,128)S(1)} async-done(((f32[64,1,607]{2,1,0:T(1,128)}), f32[64,1,607]{2,1,0:T(1,128)S(1)}, u32[]{:S(2)}, u32[]{:S(2)}) %all-to-all-start) | async-done | bytes 155424 | tf_op jit(solution)/shard_map/all_to_all | solution.py:217
  80.1 5.6 %collective-permute-start.12 = (f32[607]{0:T(1024)S(1)}, f32[607]{0:T(1024)S(1)}, u32[]{:S(2)}, u32[]{:S(2)}) collective-permute-start(f32[607]{0:T(1024)S(1)} %reduce_sum.39), channel_id=1, source_target_pairs={{0,4},{1,5},{2,6},{3,7},{4,0},{5,1},{6,2},{7,3},{8,12},{9,13},{10,... | collective-permute-start | bytes 7292 | tf_op jit(solution)/shard_map/ppermute | solution.py:145
  85.7 2.7 %collective-permute-start.8 = (bf16[64,1,4,128]{3,0,2,1:T(8,128)(2,1)S(1)}, bf16[64,1,4,128]{3,0,2,1:T(8,128)(2,1)S(1)}, u32[]{:S(2)}, u32[]{:S(2)}) collective-permute-start(bf16[64,1,4,128]{3,0,2,1:T(8,128)(2,1)S(1)} %get-tuple-element.78), channel_id=1, source_target_pairs={{0,8},{8,16},{16,24},{24,32},{32,40},{40,48},{48,56},{56,64},{64,7... | collective-permute-start | bytes 196616 | tf_op jit(solution)/shard_map/ppermute | solution.py:20
  88.5 1.1 collective-permute-done.12
  89.5 6.5 %collective-permute-start.13 = (f32[607]{0:T(1024)S(1)}, f32[607]{0:T(1024)S(1)}, u32[]{:S(2)}, u32[]{:S(2)}) collective-permute-start(f32[607]{0:T(1024)S(1)} %add.213), channel_id=1, source_target_pairs={{0,2},{1,3},{2,0},{3,1},{4,6},{5,7},{6,4},{7,5},{8,10},{9,11},{10,... | collective-permute-start | bytes 7292 | tf_op jit(solution)/shard_map/ppermute | solution.py:145
  96.8 1.8 %reshape.123 = f32[4,8,256]{2,1,0:T(8,128)} reshape(f32[2,2,4,2,128,2]{5,4,3,2,1,0:T(8,128)S(1)} %bitcast.577) | data formatting | bytes 65536 | tf_op jit(solution)/shard_map/reshape | solution.py:50
  98.7 2.6 %collective-permute-start.9 = (bf16[64,1,4,128]{3,0,2,1:T(8,128)(2,1)S(1)}, bf16[64,1,4,128]{3,0,2,1:T(8,128)(2,1)S(1)}, u32[]{:S(2)}, u32[]{:S(2)}) collective-permute-start(bf16[64,1,4,128]{3,0,2,1:T(8,128)(2,1)S(1)} %get-tuple-element.77), channel_id=1, source_target_pairs={{8,0},{16,8},{24,16},{32,24},{40,32},{48,40},{56,48},{64,56},{72,6... | collective-permute-start | bytes 196616 | tf_op jit(solution)/shard_map/ppermute | solution.py:22
  101.3 1.9 %collective-permute-start.14 = (f32[607]{0:T(1024)S(1)}, f32[607]{0:T(1024)S(1)}, u32[]{:S(2)}, u32[]{:S(2)}) collective-permute-start(f32[607]{0:T(1024)S(1)} %add.214), channel_id=1, source_target_pairs={{0,1},{1,0},{2,3},{3,2},{4,5},{5,4},{6,7},{7,6},{8,9},{9,8},{10,11... | collective-permute-start | bytes 7292 | tf_op jit(solution)/shard_map/ppermute | solution.py:145
  103.3 2.5 %collective-permute-done.9 = bf16[64,1,4,128]{3,0,2,1:T(8,128)(2,1)S(1)} collective-permute-done((bf16[64,1,4,128]{3,0,2,1:T(8,128)(2,1)S(1)}, bf16[64,1,4,128]{3,0,2,1:T(8,128)(2,1)S(1)}, u32[]{:S(2)}, u32[]{:S(2)}) %collective-permute-start.9) | collective-permute-done | bytes 65568 | tf_op jit(solution)/shard_map/ppermute | solution.py:22
  105.8 1.9 %collective-permute-start.10 = (bf16[64,4,1,128]{3,0,2,1:T(8,128)(2,1)S(1)}, bf16[64,4,1,128]{3,0,2,1:T(8,128)(2,1)S(1)}, u32[]{:S(2)}, u32[]{:S(2)}) collective-permute-start(bf16[64,4,1,128]{3,0,2,1:T(8,128)(2,1)S(1)} %get-tuple-element.75), channel_id=1, source_target_pairs={{0,1},{1,2},{2,3},{3,4},{4,5},{5,6},{6,7},{8,9},{9,10},{10,11},{11... | collective-permute-start | bytes 196616 | tf_op jit(solution)/shard_map/ppermute | solution.py:20
  107.7 4.5 %collective-permute-start.11 = (bf16[64,4,1,128]{3,0,2,1:T(8,128)(2,1)S(1)}, bf16[64,4,1,128]{3,0,2,1:T(8,128)(2,1)S(1)}, u32[]{:S(2)}, u32[]{:S(2)}) collective-permute-start(bf16[64,4,1,128]{3,0,2,1:T(8,128)(2,1)S(1)} %get-tuple-element.76), channel_id=1, source_target_pairs={{1,0},{2,1},{3,2},{4,3},{5,4},{6,5},{7,6},{9,8},{10,9},{11,10},{12... | collective-permute-start | bytes 196616 | tf_op jit(solution)/shard_map/ppermute | solution.py:22
  113.0 7.0 %all-to-all-start.1 = ((f32[64,1,607]{2,1,0:T(1,128)}), f32[64,1,607]{2,1,0:T(1,128)S(1)}, u32[]{:S(2)}, u32[]{:S(2)}) async-start(f32[64,1,607]{2,1,0:T(1,128)} %broadcast_in_dim.23), calls=%async_computation.1 | async-start | bytes 327680 | tf_op jit(solution)/shard_map/all_to_all | solution.py:223
  124.0 1.8 %reshape.129 = f32[4,8,256]{2,1,0:T(8,128)} reshape(f32[2,2,4,2,128,2]{5,4,3,2,1,0:T(8,128)S(1)} %bitcast.578) | data formatting | bytes 65536 | tf_op jit(solution)/shard_map/reshape | solution.py:50
  126.4 4.0 %all-to-all-done.1 = f32[64,1,607]{2,1,0:T(1,128)S(1)} async-done(((f32[64,1,607]{2,1,0:T(1,128)}), f32[64,1,607]{2,1,0:T(1,128)S(1)}, u32[]{:S(2)}, u32[]{:S(2)}) %all-to-all-start.1) | async-done | bytes 155424 | tf_op jit(solution)/shard_map/all_to_all | solution.py:223
  131.9 1.0 reshape.131
  132.9 1.1 copy.395
  (158 shorter events, 25.1 us)
Async XLA Ops:
  0.6 24.6 %copy-start = (bf16[64,64]{1,0:T(8,128)(2,1)S(1)}, bf16[64,64]{1,0:T(8,128)(2,1)}, u32[]{:S(2)}) copy-start(bf16[64,64]{1,0:T(8,128)(2,1)} %param.13) | copy-start | bytes 24580
  2.2 8.6 %collective-permute-start = (bf16[12,2,4,128]{3,0,2,1:T(8,128)(2,1)S(1)}, bf16[12,2,4,128]{3,0,2,1:T(8,128)(2,1)S(1)}, u32[]{:S(2)}, u32[]{:S(2)}) collective-permute-start(bf16[12,2,4,128]{3,0,2,1:T(8,128)(2,1)S(1)} %pad_maximum_fusion.15), channel_id=1, source_target_pairs={{0,8},{8,16},{16,24},{24,32},{32,40},{40,48},{48,56},{56,64},{64,7... | collective-permute-start | bytes 73736 | tf_op jit(solution)/shard_map/ppermute | solution.py:20
  7.3 6.7 %collective-permute-start.1 = (bf16[12,2,4,128]{3,0,2,1:T(8,128)(2,1)S(1)}, bf16[12,2,4,128]{3,0,2,1:T(8,128)(2,1)S(1)}, u32[]{:S(2)}, u32[]{:S(2)}) collective-permute-start(bf16[12,2,4,128]{3,0,2,1:T(8,128)(2,1)S(1)} %pad_maximum_fusion.15), channel_id=1, source_target_pairs={{8,0},{16,8},{24,16},{32,24},{40,32},{48,40},{56,48},{64,56},{72,6... | collective-permute-start | bytes 73736 | tf_op jit(solution)/shard_map/ppermute | solution.py:22
  14.0 8.2 %collective-permute-start.2 = (bf16[12,6,2,128]{3,0,2,1:T(8,128)(2,1)S(1)}, bf16[12,6,2,128]{3,0,2,1:T(8,128)(2,1)S(1)}, u32[]{:S(2)}, u32[]{:S(2)}) collective-permute-start(bf16[12,6,2,128]{3,0,2,1:T(8,128)(2,1)S(1)} %get-tuple-element.88), channel_id=1, source_target_pairs={{0,1},{1,2},{2,3},{3,4},{4,5},{5,6},{6,7},{8,9},{9,10},{10,11},{11... | collective-permute-start | bytes 110600 | tf_op jit(solution)/shard_map/ppermute | solution.py:20
  15.9 6.3 %collective-permute-start.3 = (bf16[12,6,2,128]{3,0,2,1:T(8,128)(2,1)S(1)}, bf16[12,6,2,128]{3,0,2,1:T(8,128)(2,1)S(1)}, u32[]{:S(2)}, u32[]{:S(2)}) collective-permute-start(bf16[12,6,2,128]{3,0,2,1:T(8,128)(2,1)S(1)} %get-tuple-element.89), channel_id=1, source_target_pairs={{1,0},{2,1},{3,2},{4,3},{5,4},{6,5},{7,6},{9,8},{10,9},{11,10},{12... | collective-permute-start | bytes 110600 | tf_op jit(solution)/shard_map/ppermute | solution.py:22
  26.0 0.9 copy-start.1
  31.4 6.4 %collective-permute-start.4 = (bf16[8,1,4,128]{3,0,2,1:T(8,128)(2,1)S(1)}, bf16[8,1,4,128]{3,0,2,1:T(8,128)(2,1)S(1)}, u32[]{:S(2)}, u32[]{:S(2)}) collective-permute-start(bf16[8,1,4,128]{3,0,2,1:T(8,128)(2,1)S(1)} %get-tuple-element.104), channel_id=1, source_target_pairs={{0,8},{8,16},{16,24},{24,32},{32,40},{40,48},{48,56},{56,64},{64,7... | collective-permute-start | bytes 24584 | tf_op jit(solution)/shard_map/ppermute | solution.py:20
  34.3 6.4 %collective-permute-start.5 = (bf16[8,1,4,128]{3,0,2,1:T(8,128)(2,1)S(1)}, bf16[8,1,4,128]{3,0,2,1:T(8,128)(2,1)S(1)}, u32[]{:S(2)}, u32[]{:S(2)}) collective-permute-start(bf16[8,1,4,128]{3,0,2,1:T(8,128)(2,1)S(1)} %get-tuple-element.105), channel_id=1, source_target_pairs={{8,0},{16,8},{24,16},{32,24},{40,32},{48,40},{56,48},{64,56},{72,6... | collective-permute-start | bytes 24584 | tf_op jit(solution)/shard_map/ppermute | solution.py:22
  40.8 6.8 %collective-permute-start.6 = (bf16[8,4,1,128]{3,0,2,1:T(8,128)(2,1)S(1)}, bf16[8,4,1,128]{3,0,2,1:T(8,128)(2,1)S(1)}, u32[]{:S(2)}, u32[]{:S(2)}) collective-permute-start(bf16[8,4,1,128]{3,0,2,1:T(8,128)(2,1)S(1)} %get-tuple-element.100), channel_id=1, source_target_pairs={{0,1},{1,2},{2,3},{3,4},{4,5},{5,6},{6,7},{8,9},{9,10},{10,11},{11... | collective-permute-start | bytes 24584 | tf_op jit(solution)/shard_map/ppermute | solution.py:20
  42.7 5.9 %collective-permute-start.7 = (bf16[8,4,1,128]{3,0,2,1:T(8,128)(2,1)S(1)}, bf16[8,4,1,128]{3,0,2,1:T(8,128)(2,1)S(1)}, u32[]{:S(2)}, u32[]{:S(2)}) collective-permute-start(bf16[8,4,1,128]{3,0,2,1:T(8,128)(2,1)S(1)} %get-tuple-element.101), channel_id=1, source_target_pairs={{1,0},{2,1},{3,2},{4,3},{5,4},{6,5},{7,6},{9,8},{10,9},{11,10},{12... | collective-permute-start | bytes 24584 | tf_op jit(solution)/shard_map/ppermute | solution.py:22
  53.5 42.6 %copy-start.2 = (f32[8,8,1,1]{1,0,3,2:T(8,128)S(1)}, f32[8,8,1,1]{1,0,3,2:T(8,128)}, u32[]{:S(2)}) copy-start(f32[8,8,1,1]{1,0,3,2:T(8,128)} %constant.54) | copy-start | bytes 772
  54.6 25.4 %all-to-all-start = ((f32[64,1,607]{2,1,0:T(1,128)}), f32[64,1,607]{2,1,0:T(1,128)S(1)}, u32[]{:S(2)}, u32[]{:S(2)}) async-start(f32[64,1,607]{2,1,0:T(1,128)} %all_to_all.10), calls=%async_computation | async-start | bytes 327680 | tf_op jit(solution)/shard_map/all_to_all | solution.py:217
  80.1 9.4 %collective-permute-start.12 = (f32[607]{0:T(1024)S(1)}, f32[607]{0:T(1024)S(1)}, u32[]{:S(2)}, u32[]{:S(2)}) collective-permute-start(f32[607]{0:T(1024)S(1)} %reduce_sum.39), channel_id=1, source_target_pairs={{0,4},{1,5},{2,6},{3,7},{4,0},{5,1},{6,2},{7,3},{8,12},{9,13},{10,... | collective-permute-start | bytes 7292 | tf_op jit(solution)/shard_map/ppermute | solution.py:145
  85.7 17.5 %collective-permute-start.8 = (bf16[64,1,4,128]{3,0,2,1:T(8,128)(2,1)S(1)}, bf16[64,1,4,128]{3,0,2,1:T(8,128)(2,1)S(1)}, u32[]{:S(2)}, u32[]{:S(2)}) collective-permute-start(bf16[64,1,4,128]{3,0,2,1:T(8,128)(2,1)S(1)} %get-tuple-element.78), channel_id=1, source_target_pairs={{0,8},{8,16},{16,24},{24,32},{32,40},{40,48},{48,56},{56,64},{64,7... | collective-permute-start | bytes 196616 | tf_op jit(solution)/shard_map/ppermute | solution.py:20
  89.5 11.7 %collective-permute-start.13 = (f32[607]{0:T(1024)S(1)}, f32[607]{0:T(1024)S(1)}, u32[]{:S(2)}, u32[]{:S(2)}) collective-permute-start(f32[607]{0:T(1024)S(1)} %add.213), channel_id=1, source_target_pairs={{0,2},{1,3},{2,0},{3,1},{4,6},{5,7},{6,4},{7,5},{8,10},{9,11},{10,... | collective-permute-start | bytes 7292 | tf_op jit(solution)/shard_map/ppermute | solution.py:145
  98.7 7.0 %collective-permute-start.9 = (bf16[64,1,4,128]{3,0,2,1:T(8,128)(2,1)S(1)}, bf16[64,1,4,128]{3,0,2,1:T(8,128)(2,1)S(1)}, u32[]{:S(2)}, u32[]{:S(2)}) collective-permute-start(bf16[64,1,4,128]{3,0,2,1:T(8,128)(2,1)S(1)} %get-tuple-element.77), channel_id=1, source_target_pairs={{8,0},{16,8},{24,16},{32,24},{40,32},{48,40},{56,48},{64,56},{72,6... | collective-permute-start | bytes 196616 | tf_op jit(solution)/shard_map/ppermute | solution.py:22
  101.3 10.9 %collective-permute-start.14 = (f32[607]{0:T(1024)S(1)}, f32[607]{0:T(1024)S(1)}, u32[]{:S(2)}, u32[]{:S(2)}) collective-permute-start(f32[607]{0:T(1024)S(1)} %add.214), channel_id=1, source_target_pairs={{0,1},{1,0},{2,3},{3,2},{4,5},{5,4},{6,7},{7,6},{8,9},{9,8},{10,11... | collective-permute-start | bytes 7292 | tf_op jit(solution)/shard_map/ppermute | solution.py:145
  105.8 14.2 %collective-permute-start.10 = (bf16[64,4,1,128]{3,0,2,1:T(8,128)(2,1)S(1)}, bf16[64,4,1,128]{3,0,2,1:T(8,128)(2,1)S(1)}, u32[]{:S(2)}, u32[]{:S(2)}) collective-permute-start(bf16[64,4,1,128]{3,0,2,1:T(8,128)(2,1)S(1)} %get-tuple-element.75), channel_id=1, source_target_pairs={{0,1},{1,2},{2,3},{3,4},{4,5},{5,6},{6,7},{8,9},{9,10},{10,11},{11... | collective-permute-start | bytes 196616 | tf_op jit(solution)/shard_map/ppermute | solution.py:20
  107.7 12.3 %collective-permute-start.11 = (bf16[64,4,1,128]{3,0,2,1:T(8,128)(2,1)S(1)}, bf16[64,4,1,128]{3,0,2,1:T(8,128)(2,1)S(1)}, u32[]{:S(2)}, u32[]{:S(2)}) collective-permute-start(bf16[64,4,1,128]{3,0,2,1:T(8,128)(2,1)S(1)} %get-tuple-element.76), channel_id=1, source_target_pairs={{1,0},{2,1},{3,2},{4,3},{5,4},{6,5},{7,6},{9,8},{10,9},{11,10},{12... | collective-permute-start | bytes 196616 | tf_op jit(solution)/shard_map/ppermute | solution.py:22
  113.0 17.5 %all-to-all-start.1 = ((f32[64,1,607]{2,1,0:T(1,128)}), f32[64,1,607]{2,1,0:T(1,128)S(1)}, u32[]{:S(2)}, u32[]{:S(2)}) async-start(f32[64,1,607]{2,1,0:T(1,128)} %broadcast_in_dim.23), calls=%async_computation.1 | async-start | bytes 327680 | tf_op jit(solution)/shard_map/all_to_all | solution.py:223
